TPU v7x, 32 devices: a whole 2x2x4 slice. The times are simulated.
32 devices in a mesh: gx: 4 (over y, core), gy: 8 (over z, x).
Axes of the slice: x: 2, y: 2, z: 4, core: 2. Of those that a mesh axis runs over, the one named last changes fastest.
Arguments:
- initial_heat_values: float32 [16, 128, 1024], P(None, 'gx', 'gy'), may hold values from -5 to 5
- spreading_coefficients: float32 [16, 128, 1024], P(None, 'gx', 'gy'), may hold values from 1 to 16
Outputs:
- advanced: float32 [16, 128, 1024], P(None, 'gx', 'gy')
All inputs are finite; a program needn't handle non-finite values.
Results may differ from a plain program's by a relative error of at most 0.0003.
Values sent between devices are 32-bit elements; how exact they have to be, the bound alone decides.
No kernel may reach another device: no remote copies, remote signals or barrier semaphores. Data moves between devices by JAX's collectives and lax.ppermute only.
A program may use at most 64 MiB of HBM per device.

v0:
```python
import jax
import jax.numpy as jnp
from jax import lax
from jax.experimental import pallas as pl
from jax.experimental.pallas import tpu as pltpu
from jax.sharding import PartitionSpec as P

diffusion_number = 1000.0
implicit_weight = 0.5


def padded(block, sides, width):
    for axis, dim in sides:
        count = lax.axis_size(axis)
        forward = [(i, i + 1) for i in range(count - 1)]
        backward = [(target, source) for source, target in forward]
        low = lax.ppermute(
            lax.slice_in_dim(block, block.shape[dim] - width, None, axis=dim), axis, forward
        )
        high = lax.ppermute(lax.slice_in_dim(block, 0, width, axis=dim), axis, backward)
        block = jnp.concatenate([low, block, high], axis=dim)
    return block


def partition_kernel(h_ref, d_ref, out_ref, red_ref, ratio_ref):
    n = h_ref.shape[0]
    ratio = jnp.zeros(h_ref.shape[1:], jnp.float32)
    vb = jnp.zeros_like(ratio)
    vf = jnp.zeros_like(ratio)
    for i in range(1, n - 1):
        hi = h_ref[i]
        denom = 1.0 + 2.0 * hi + hi * ratio
        ratio = -hi / denom
        if i == 1:
            vb = d_ref[i] / denom
            vf = hi / denom
        else:
            vb = (d_ref[i] + hi * vb) / denom
            vf = (hi * vf) / denom
        if i == n - 2:
            vl = hi / denom
        ratio_ref[i] = ratio
        out_ref[0, i] = vb
        out_ref[1, i] = vf
    b, f, l = vb, vf, vl
    out_ref[2, n - 2] = l
    for i in range(n - 3, 0, -1):
        r = ratio_ref[i]
        b = out_ref[0, i] - r * b
        f = out_ref[1, i] - r * f
        l = -r * l
        out_ref[0, i] = b
        out_ref[1, i] = f
        out_ref[2, i] = l
    zero = jnp.zeros_like(ratio)
    for k in range(3):
        out_ref[k, 0] = zero
        out_ref[k, n - 1] = zero
    rh = h_ref[0]
    rt = h_ref[n - 1]
    red_ref[0, 0] = -rh
    red_ref[0, 1] = -rt * out_ref[1, n - 2]
    red_ref[1, 0] = 1.0 + 2.0 * rh - rh * out_ref[1, 1]
    red_ref[1, 1] = 1.0 + 2.0 * rt - rt * out_ref[2, n - 2]
    red_ref[2, 0] = -rh * out_ref[2, 1]
    red_ref[2, 1] = -rt
    red_ref[3, 0] = d_ref[0] + rh * out_ref[0, 1]
    red_ref[3, 1] = d_ref[n - 1] + rt * out_ref[0, n - 2]


def partition_call(h_lines, d_lines):
    n = h_lines.shape[0]
    rest = h_lines.shape[1:]
    return pl.pallas_call(
        partition_kernel,
        out_shape=(
            jax.ShapeDtypeStruct((3, n) + rest, jnp.float32),
            jax.ShapeDtypeStruct((4, 2) + rest, jnp.float32),
        ),
        scratch_shapes=[pltpu_vmem((n,) + rest)],
    )(h_lines, d_lines)


def pltpu_vmem(shape):
    return pltpu.VMEM(shape, jnp.float32)


def reduced_kernel(g_ref, out_ref, ratio_ref):
    count = g_ref.shape[0]
    ratio = None
    value = None
    for j in range(2 * count):
        k, q = divmod(j, 2)
        lower = g_ref[k, 0, q]
        centre = g_ref[k, 1, q]
        upper = g_ref[k, 2, q]
        side = g_ref[k, 3, q]
        if j == 0:
            denom = centre
            value = side / denom
        else:
            denom = centre - lower * ratio
            value = (side - lower * value) / denom
        ratio = upper / denom
        ratio_ref[j] = ratio
        out_ref[k, q] = value
    x = value
    for j in range(2 * count - 2, -1, -1):
        k, q = divmod(j, 2)
        x = out_ref[k, q] - ratio_ref[j] * x
        out_ref[k, q] = x


def reduced_call(gathered):
    count = gathered.shape[0]
    rest = gathered.shape[3:]
    return pl.pallas_call(
        reduced_kernel,
        out_shape=jax.ShapeDtypeStruct((count, 2) + rest, jnp.float32),
        scratch_shapes=[pltpu_vmem((2 * count,) + rest)],
    )(gathered)


def sweep_kernel(h_ref, d_ref, out_ref, ratio_ref):
    n = h_ref.shape[0]
    ratio = None
    value = None
    for i in range(n):
        hi = h_ref[i]
        if i == 0:
            denom = 1.0 + 2.0 * hi
            value = d_ref[i] / denom
        else:
            denom = 1.0 + 2.0 * hi + hi * ratio
            value = (d_ref[i] + hi * value) / denom
        ratio = -hi / denom
        ratio_ref[i] = ratio
        out_ref[i] = value
    x = value
    for i in range(n - 2, -1, -1):
        x = out_ref[i] - ratio_ref[i] * x
        out_ref[i] = x


def sweep_call(h_lines, d_lines):
    return pl.pallas_call(
        sweep_kernel,
        out_shape=jax.ShapeDtypeStruct(h_lines.shape, jnp.float32),
        scratch_shapes=[pltpu_vmem(h_lines.shape)],
    )(h_lines, d_lines)


def distributed_solve(h_lines, d_lines, axis):
    responses, reduced = partition_call(h_lines, d_lines)
    gathered = lax.all_gather(reduced, axis)
    ends = reduced_call(gathered)
    head, tail = lax.dynamic_index_in_dim(ends, lax.axis_index(axis), 0, keepdims=False)
    interior = responses[0, 1:-1] + responses[1, 1:-1] * head + responses[2, 1:-1] * tail
    return jnp.concatenate([head[None], interior, tail[None]], 0)


def per_device(initial_heat_values, spreading_coefficients):
    conductivity_map = diffusion_number * spreading_coefficients
    half_rate = implicit_weight * conductivity_map
    plane_count, row_count, column_count = initial_heat_values.shape
    edge_extended_grid = padded(initial_heat_values, (("gx", 1), ("gy", 2)), 1)
    horizontal_implicit_solve = conductivity_map * (
        edge_extended_grid[:, :-2, 1:-1]
        - 2.0 * initial_heat_values
        + edge_extended_grid[:, 2:, 1:-1]
    )
    vertical_implicit_solve = conductivity_map * (
        edge_extended_grid[:, 1:-1, :-2]
        - 2.0 * initial_heat_values
        + edge_extended_grid[:, 1:-1, 2:]
    )
    depth_edge_extension = jnp.pad(initial_heat_values, ((1, 1), (0, 0), (0, 0)))
    depth_implicit_solve = conductivity_map * (
        depth_edge_extension[:-2] - 2.0 * initial_heat_values + depth_edge_extension[2:]
    )
    forward_euler_increment = (
        initial_heat_values
        + horizontal_implicit_solve
        + vertical_implicit_solve
        + depth_implicit_solve
    )
    first_side = jnp.moveaxis(
        forward_euler_increment - implicit_weight * horizontal_implicit_solve, 1, 0
    )
    first_rate = jnp.moveaxis(half_rate, 1, 0)
    first_pass = jnp.moveaxis(distributed_solve(first_rate, first_side, "gx"), 0, 1)
    second_side = first_pass - implicit_weight * vertical_implicit_solve
    lanes = 128
    groups = plane_count * row_count // lanes
    side_lines = jnp.transpose(second_side, (2, 0, 1)).reshape(column_count, groups, lanes)
    rate_lines = jnp.transpose(half_rate, (2, 0, 1)).reshape(column_count, groups, lanes)
    column_lines = distributed_solve(rate_lines, side_lines, "gy")
    second = jnp.transpose(column_lines.reshape(column_count, plane_count, row_count), (1, 2, 0))
    plane_side = second - implicit_weight * depth_implicit_solve
    return sweep_call(half_rate, plane_side)


def solution(mesh):
    in_specs = (P(None, "gx", "gy"), P(None, "gx", "gy"))
    out_specs = P(None, "gx", "gy")
    return jax.shard_map(
        per_device, mesh=mesh, in_specs=in_specs, out_specs=out_specs, check_vma=False
    )
```

profile of v0, /device:TPU:0, one launch (start us, length us, event | category | flops | bytes accessed | tf_op | source)
XLA Modules:
  0.0 90.0 jit_solution(1223604459067411140)
XLA Ops:
  0.0 0.9 fusion.18
  0.9 2.4 %collective-permute-start = (f32[16,1,128]{2,1,0:T(1,128)S(1)}, f32[16,1,128]{2,1,0:T(1,128)S(1)}, u32[]{:S(2)}, u32[]{:S(2)}) collective-permute-start(f32[16,1,128]{2,1,0:T(1,128)S(1)} %get-tuple-element.22), channel_id=1, source_target_pairs={{0,8},{8,16},{16,24},{1,9},{9,17},{17,25},{2,10},{10,18},{18,26},{... | collective-permute-start | bytes 24584 | tf_op jit(solution)/shard_map/ppermute | solution.py:17
  3.3 1.3 %collective-permute-start.1 = (f32[16,1,128]{2,1,0:T(1,128)S(1)}, f32[16,1,128]{2,1,0:T(1,128)S(1)}, u32[]{:S(2)}, u32[]{:S(2)}) collective-permute-start(f32[16,1,128]{2,1,0:T(1,128)S(1)} %get-tuple-element.23), channel_id=1, source_target_pairs={{8,0},{16,8},{24,16},{9,1},{17,9},{25,17},{10,2},{18,10},{26,18},{... | collective-permute-start | bytes 24584 | tf_op jit(solution)/shard_map/ppermute | solution.py:20
  4.6 3.9 %collective-permute-done.1 = f32[16,1,128]{2,1,0:T(1,128)S(1)} collective-permute-done((f32[16,1,128]{2,1,0:T(1,128)S(1)}, f32[16,1,128]{2,1,0:T(1,128)S(1)}, u32[]{:S(2)}, u32[]{:S(2)}) %collective-permute-start.1) | collective-permute-done | bytes 8224 | tf_op jit(solution)/shard_map/ppermute | solution.py:20
  8.5 1.0 %pad_maximum_fusion = f32[16,34,128]{2,1,0:T(8,128)S(1)} fusion(f32[16,1,128]{2,1,0:T(1,128)S(1)} %collective-permute-done.1, f32[16,32,128]{2,1,0:T(8,128)} %param.2, f32[16,1,128]{2,1,0:T(1,128)S(1)} %collective-permute-done), kind=kLoop, calls=%fused_computation | loop fusion | flops 139264 | bytes 557056 | tf_op jit(solution)/shard_map/concatenate | solution.py:21
  9.6 3.4 %collective-permute-start.2 = (f32[16,34,1]{2,1,0:T(8,128)S(1)}, f32[16,34,1]{2,1,0:T(8,128)S(1)}, u32[]{:S(2)}, u32[]{:S(2)}) collective-permute-start(f32[16,34,1]{2,1,0:T(8,128)S(1)} %get-tuple-element.16), channel_id=1, source_target_pairs={{0,1},{1,2},{2,3},{3,4},{4,5},{5,6},{6,7},{8,9},{9,10},{10,11},{11... | collective-permute-start | bytes 6536 | tf_op jit(solution)/shard_map/ppermute | solution.py:17
  13.1 1.3 %collective-permute-start.3 = (f32[16,34,1]{2,1,0:T(8,128)S(1)}, f32[16,34,1]{2,1,0:T(8,128)S(1)}, u32[]{:S(2)}, u32[]{:S(2)}) collective-permute-start(f32[16,34,1]{2,1,0:T(8,128)S(1)} %get-tuple-element.17), channel_id=1, source_target_pairs={{1,0},{2,1},{3,2},{4,3},{5,4},{6,5},{7,6},{9,8},{10,9},{11,10},{12... | collective-permute-start | bytes 6536 | tf_op jit(solution)/shard_map/ppermute | solution.py:20
  14.4 12.3 %collective-permute-done.2 = f32[16,34,1]{2,1,0:T(8,128)S(1)} collective-permute-done((f32[16,34,1]{2,1,0:T(8,128)S(1)}, f32[16,34,1]{2,1,0:T(8,128)S(1)}, u32[]{:S(2)}, u32[]{:S(2)}) %collective-permute-start.2) | collective-permute-done | bytes 2208 | tf_op jit(solution)/shard_map/ppermute | solution.py:17
  26.7 0.4 subtract_bitcast_fusion
  27.1 0.9 copy.27.h_ref
  28.0 0.9 copy.28.d_ref
  28.8 2.3 %shard_map.28 = (f32[3,32,16,128]{3,2,1,0:T(8,128)}, f32[4,2,16,128]{3,2,1,0:T(8,128)}) custom-call(f32[32,16,128]{2,1,0:T(8,128)} %copy.27.h_ref, f32[32,16,128]{2,1,0:T(8,128)} %copy.28.d_ref), custom_call_target="tpu_custom_call" | custom-call | tf_op jit(solution)/shard_map/pallas_call | solution.py:74
  31.1 7.5 %all-gather = f32[16,2,16,128]{3,2,1,0:T(8,128)} all-gather(f32[4,2,16,128]{3,2,1,0:T(8,128)} %get-tuple-element.9), channel_id=2, replica_groups=mesh['gx'=4,'gy'=8] {'gx'}, dimensions={0}, use_global_device_ids=true | all-gather | bytes 327680 | tf_op jit(solution)/shard_map/all_gather | solution.py:155
  38.6 1.7 %shard_map.29 = f32[4,2,16,128]{3,2,1,0:T(8,128)} custom-call(f32[4,4,2,16,128]{4,3,2,1,0:T(8,128)} %bitcast.49), custom_call_target="tpu_custom_call" | custom-call | tf_op jit(solution)/shard_map/pallas_call | solution.py:117
  40.3 1.4 %copy.29 = f32[3,32,16,128]{3,1,2,0:T(8,128)S(1)} copy(f32[3,32,16,128]{3,2,1,0:T(8,128)} %get-tuple-element.10) | data formatting | bytes 1572864 | tf_op jit(solution)/shard_map/pallas_call | solution.py:74
  41.7 0.7 constant_dynamic-slice_fusion.1
  42.9 0.8 copy.33.h_ref
  43.7 0.9 copy.34.d_ref
  44.6 3.3 %shard_map.30 = (f32[3,128,4,128]{3,2,1,0:T(4,128)}, f32[4,2,4,128]{3,2,1,0:T(4,128)}) custom-call(f32[128,4,128]{2,1,0:T(4,128)} %copy.33.h_ref, f32[128,4,128]{2,1,0:T(4,128)} %copy.34.d_ref), custom_call_target="tpu_custom_call" | custom-call | tf_op jit(solution)/shard_map/pallas_call | solution.py:74
  47.9 35.5 %all-gather.1 = f32[32,2,4,128]{3,2,1,0:T(4,128)} all-gather(f32[4,2,4,128]{3,2,1,0:T(4,128)} %get-tuple-element.11), channel_id=3, replica_groups=mesh['gx'=4,'gy'=8] {'gy'}, dimensions={0}, use_global_device_ids=true | all-gather | bytes 147456 | tf_op jit(solution)/shard_map/all_gather | solution.py:155
  83.5 1.7 %shard_map.31 = f32[8,2,4,128]{3,2,1,0:T(4,128)} custom-call(f32[8,4,2,4,128]{4,3,2,1,0:T(4,128)} %bitcast.53), custom_call_target="tpu_custom_call" | custom-call | tf_op jit(solution)/shard_map/pallas_call | solution.py:117
  85.2 0.7 constant_dynamic-slice_fusion
  87.2 0.9 %fusion.14.d_ref = f32[16,32,128]{2,1,0:T(8,128)} fusion(f32[1,16,32]{0,2,1:T(8,128)S(1)} %concatenate.37, f32[126,16,32]{0,2,1:T(8,128)S(1)} %multiply_add_fusion, f32[1,16,32]{0,2,1:T(8,128)S(1)} %concatenate.36, f32[16,32,128]{2,1,0:T(8,128)S(1)} %copy-done, f32[16,32,128]{2,1,0:T(8,128)S(1)} %copy-done.2), kind=kLoop, calls=%fused_computation.30 | loop fusion | flops 589824 | bytes 1048576 | tf_op jit(solution)/shard_map/sub | solution.py:199
  88.1 1.9 %shard_map.32 = f32[16,32,128]{2,1,0:T(8,128)} custom-call(f32[16,32,128]{2,1,0:T(8,128)} %copy-done.1, f32[16,32,128]{2,1,0:T(8,128)} %fusion.14.d_ref), custom_call_target="tpu_custom_call" | custom-call | tf_op jit(solution)/shard_map/pallas_call | solution.py:146
  (22 shorter events, 1.9 us)
Async XLA Ops:
  0.9 3.7 %collective-permute-start = (f32[16,1,128]{2,1,0:T(1,128)S(1)}, f32[16,1,128]{2,1,0:T(1,128)S(1)}, u32[]{:S(2)}, u32[]{:S(2)}) collective-permute-start(f32[16,1,128]{2,1,0:T(1,128)S(1)} %get-tuple-element.22), channel_id=1, source_target_pairs={{0,8},{8,16},{16,24},{1,9},{9,17},{17,25},{2,10},{10,18},{18,26},{... | collective-permute-start | bytes 24584 | tf_op jit(solution)/shard_map/ppermute | solution.py:17
  3.3 5.2 %collective-permute-start.1 = (f32[16,1,128]{2,1,0:T(1,128)S(1)}, f32[16,1,128]{2,1,0:T(1,128)S(1)}, u32[]{:S(2)}, u32[]{:S(2)}) collective-permute-start(f32[16,1,128]{2,1,0:T(1,128)S(1)} %get-tuple-element.23), channel_id=1, source_target_pairs={{8,0},{16,8},{24,16},{9,1},{17,9},{25,17},{10,2},{18,10},{26,18},{... | collective-permute-start | bytes 24584 | tf_op jit(solution)/shard_map/ppermute | solution.py:20
  9.4 17.2 %copy-start = (f32[16,32,128]{2,1,0:T(8,128)S(1)}, f32[16,32,128]{2,1,0:T(8,128)}, u32[]{:S(2)}) copy-start(f32[16,32,128]{2,1,0:T(8,128)} %param.2) | copy-start | bytes 786436
  9.5 17.2 %copy-start.2 = (f32[16,32,128]{2,1,0:T(8,128)S(1)}, f32[16,32,128]{2,1,0:T(8,128)}, u32[]{:S(2)}) copy-start(f32[16,32,128]{2,1,0:T(8,128)} %param.3) | copy-start | bytes 786436
  9.6 17.0 %collective-permute-start.2 = (f32[16,34,1]{2,1,0:T(8,128)S(1)}, f32[16,34,1]{2,1,0:T(8,128)S(1)}, u32[]{:S(2)}, u32[]{:S(2)}) collective-permute-start(f32[16,34,1]{2,1,0:T(8,128)S(1)} %get-tuple-element.16), channel_id=1, source_target_pairs={{0,1},{1,2},{2,3},{3,4},{4,5},{5,6},{6,7},{8,9},{9,10},{10,11},{11... | collective-permute-start | bytes 6536 | tf_op jit(solution)/shard_map/ppermute | solution.py:17
  13.1 13.6 %collective-permute-start.3 = (f32[16,34,1]{2,1,0:T(8,128)S(1)}, f32[16,34,1]{2,1,0:T(8,128)S(1)}, u32[]{:S(2)}, u32[]{:S(2)}) collective-permute-start(f32[16,34,1]{2,1,0:T(8,128)S(1)} %get-tuple-element.17), channel_id=1, source_target_pairs={{1,0},{2,1},{3,2},{4,3},{5,4},{6,5},{7,6},{9,8},{10,9},{11,10},{12... | collective-permute-start | bytes 6536 | tf_op jit(solution)/shard_map/ppermute | solution.py:20
  42.9 0.8 copy-start.1
  47.9 38.5 %copy-start.3 = (f32[3,128,4,128]{3,2,1,0:T(4,128)S(1)}, f32[3,128,4,128]{3,2,1,0:T(4,128)}, u32[]{:S(2)}) copy-start(f32[3,128,4,128]{3,2,1,0:T(4,128)} %get-tuple-element.12) | copy-start | bytes 2359300
where the time goes:
time: 90.5 us; the launch traced here: 90 us
  blocking collectives  43 us (48%)
  waiting for transfers between devices  16.2 us (18%)
  Pallas kernels  10.9 us (12%)
  starting transfers between devices  8.36 us (9%)
  local copies, waits for them, and re-layouts  8.33 us (9%)
  other arithmetic  2.99 us (3%)
    all_gather x2, blocking collectives, distributed_solve(): gathered = lax.all_gather(reduced, axis)  43 us
    ppermute x2, waiting for transfers between devices, padded(): lax.ppermute(lax.slice_in_dim(block, block.shape[dim] - width, None, axis...  12.3 us
    ppermute x2, starting transfers between devices, padded(): lax.ppermute(lax.slice_in_dim(block, block.shape[dim] - width, None, axis...  5.77 us
    pallas_call x2, Pallas kernels, partition_call(): pl.pallas_call(partition_kernel, out_shape=(jax.ShapeDtypeStruct((3, n) +...  5.65 us
    ppermute x2, waiting for transfers between devices, padded(): lax.ppermute(lax.slice_in_dim(block, 0, width, axis=dim), axis, backward)  3.89 us
    pallas_call x2, Pallas kernels, reduced_call(): pl.pallas_call(reduced_kernel, out_shape=jax.ShapeDtypeStruct((count, 2)...  3.36 us
    ppermute x2, starting transfers between devices, padded(): lax.ppermute(lax.slice_in_dim(block, 0, width, axis=dim), axis, backward)  2.58 us
    pallas_call x1, Pallas kernels, sweep_call(): pl.pallas_call(sweep_kernel, out_shape=jax.ShapeDtypeStruct(h_lines.shape...  1.91 us
  transfers between devices with their start and end apart: 4, of which 2 were waited for; matrix products, arithmetic and copies ran while one was open for 0% of the time, Pallas kernels for 0%

commit v1 on v0

--- a/solution.py
+++ b/solution.py
@@ -9,17 +9,15 @@
 implicit_weight = 0.5
 
 
-def padded(block, sides, width):
-    for axis, dim in sides:
-        count = lax.axis_size(axis)
-        forward = [(i, i + 1) for i in range(count - 1)]
-        backward = [(target, source) for source, target in forward]
-        low = lax.ppermute(
-            lax.slice_in_dim(block, block.shape[dim] - width, None, axis=dim), axis, forward
-        )
-        high = lax.ppermute(lax.slice_in_dim(block, 0, width, axis=dim), axis, backward)
-        block = jnp.concatenate([low, block, high], axis=dim)
-    return block
+def halos(block, axis, dim):
+    count = lax.axis_size(axis)
+    forward = [(i, i + 1) for i in range(count - 1)]
+    backward = [(target, source) for source, target in forward]
+    last = lax.index_in_dim(block, block.shape[dim] - 1, dim, keepdims=False)
+    first = lax.index_in_dim(block, 0, dim, keepdims=False)
+    low = lax.ppermute(last, axis, forward)
+    high = lax.ppermute(first, axis, backward)
+    return jnp.expand_dims(low, dim), jnp.expand_dims(high, dim)
 
 
 def partition_kernel(h_ref, d_ref, out_ref, red_ref, ratio_ref):
@@ -163,16 +161,17 @@
     conductivity_map = diffusion_number * spreading_coefficients
     half_rate = implicit_weight * conductivity_map
     plane_count, row_count, column_count = initial_heat_values.shape
-    edge_extended_grid = padded(initial_heat_values, (("gx", 1), ("gy", 2)), 1)
+    x_low, x_high = halos(initial_heat_values, "gx", 1)
+    y_low, y_high = halos(initial_heat_values, "gy", 2)
     horizontal_implicit_solve = conductivity_map * (
-        edge_extended_grid[:, :-2, 1:-1]
+        jnp.concatenate([x_low, initial_heat_values[:, :-1]], 1)
         - 2.0 * initial_heat_values
-        + edge_extended_grid[:, 2:, 1:-1]
+        + jnp.concatenate([initial_heat_values[:, 1:], x_high], 1)
     )
     vertical_implicit_solve = conductivity_map * (
-        edge_extended_grid[:, 1:-1, :-2]
+        jnp.concatenate([y_low, initial_heat_values[:, :, :-1]], 2)
         - 2.0 * initial_heat_values
-        + edge_extended_grid[:, 1:-1, 2:]
+        + jnp.concatenate([initial_heat_values[:, :, 1:], y_high], 2)
     )
     depth_edge_extension = jnp.pad(initial_heat_values, ((1, 1), (0, 0), (0, 0)))
     depth_implicit_solve = conductivity_map * (

time: 90.5 us -> 78 us (0.86)
  waiting for transfers between devices: 16.2 us -> 2.78 us
  other arithmetic: 2.99 us -> 1.62 us
  local copies, waits for them, and re-layouts: 8.33 us -> 9.3 us
    ppermute x4, waiting for transfers between devices: 16.2 us -> 2.78 us  [the longest x2 2.78 us: halos(): high = lax.ppermute(first, axis, backward)]
    concatenate x1 -> x0, other arithmetic: 0.99 us -> none  [padded(): block = jnp.concatenate([low, block, high], axis=dim)]
  transfers between devices with their start and end apart: 4 -> 4, of which waited for: 2 -> 2; matrix products, arithmetic and copies ran while one was open for 0% -> 1% of each run, Pallas kernels for 0% -> 0%
where the time goes in v1:
time: 78 us; the launch traced here: 77.5 us
  blocking collectives  43.8 us (56%)
  Pallas kernels  10.9 us (14%)
  local copies, waits for them, and re-layouts  9.3 us (12%)
  starting transfers between devices  8.89 us (11%)
  waiting for transfers between devices  2.78 us (4%)
  other arithmetic  1.62 us (2%)
    all_gather x2, blocking collectives, distributed_solve(): gathered = lax.all_gather(reduced, axis)  43.8 us
    ppermute x2, starting transfers between devices, halos(): low = lax.ppermute(last, axis, forward)  6.3 us
    pallas_call x2, Pallas kernels, partition_call(): pl.pallas_call(partition_kernel, out_shape=(jax.ShapeDtypeStruct((3, n) +...  5.62 us
    pallas_call x2, Pallas kernels, reduced_call(): pl.pallas_call(reduced_kernel, out_shape=jax.ShapeDtypeStruct((count, 2)...  3.36 us
    ppermute x2, waiting for transfers between devices, halos(): high = lax.ppermute(first, axis, backward)  2.78 us
    ppermute x2, starting transfers between devices, halos(): high = lax.ppermute(first, axis, backward)  2.59 us
    pallas_call x1, Pallas kernels, sweep_call(): pl.pallas_call(sweep_kernel, out_shape=jax.ShapeDtypeStruct(h_lines.shape...  1.91 us
  transfers between devices with their start and end apart: 4, of which 2 were waited for; matrix products, arithmetic and copies ran while one was open for 1% of the time, Pallas kernels for 0%

profile of v1, /device:TPU:0, one launch (start us, length us, event | category | flops | bytes accessed | tf_op | source)
XLA Modules:
  0.0 77.5 jit_solution(2648221673932560007)
XLA Ops:
  0.0 1.2 %fusion.16 = (f32[16,32,1]{2,1,0:T(8,128)S(1)}, f32[16,32,1]{2,1,0:T(8,128)S(1)}) fusion(f32[16,32,128]{2,1,0:T(8,128)} %param.2), kind=kLoop, calls=%fused_computation.31 | loop fusion | bytes 8192 | tf_op jit(solution)/shard_map/slice | solution.py:16
  1.3 4.8 %collective-permute-start.2 = (f32[16,32]{1,0:T(8,128)S(1)}, f32[16,32]{1,0:T(8,128)S(1)}, u32[]{:S(2)}, u32[]{:S(2)}) collective-permute-start(f32[16,32]{1,0:T(8,128)S(1)} %bitcast.72), channel_id=1, source_target_pairs={{0,1},{1,2},{2,3},{3,4},{4,5},{5,6},{6,7},{8,9},{9,10},{10,11},{11... | collective-permute-start | bytes 6152 | tf_op jit(solution)/shard_map/ppermute | solution.py:18
  6.3 1.3 %collective-permute-start.3 = (f32[16,32]{1,0:T(8,128)S(1)}, f32[16,32]{1,0:T(8,128)S(1)}, u32[]{:S(2)}, u32[]{:S(2)}) collective-permute-start(f32[16,32]{1,0:T(8,128)S(1)} %bitcast.74), channel_id=1, source_target_pairs={{1,0},{2,1},{3,2},{4,3},{5,4},{6,5},{7,6},{9,8},{10,9},{11,10},{12... | collective-permute-start | bytes 6152 | tf_op jit(solution)/shard_map/ppermute | solution.py:19
  7.7 1.5 %collective-permute-start = (f32[16,128]{1,0:T(8,128)S(1)}, f32[16,128]{1,0:T(8,128)S(1)}, u32[]{:S(2)}, u32[]{:S(2)}) collective-permute-start(f32[16,128]{1,0:T(8,128)S(1)} %bitcast.77), channel_id=1, source_target_pairs={{0,8},{8,16},{16,24},{1,9},{9,17},{17,25},{2,10},{10,18},{18,26},{... | collective-permute-start | bytes 24584 | tf_op jit(solution)/shard_map/ppermute | solution.py:18
  9.1 1.3 %collective-permute-start.1 = (f32[16,128]{1,0:T(8,128)S(1)}, f32[16,128]{1,0:T(8,128)S(1)}, u32[]{:S(2)}, u32[]{:S(2)}) collective-permute-start(f32[16,128]{1,0:T(8,128)S(1)} %bitcast.76), channel_id=1, source_target_pairs={{8,0},{16,8},{24,16},{9,1},{17,9},{25,17},{10,2},{18,10},{26,18},{... | collective-permute-start | bytes 24584 | tf_op jit(solution)/shard_map/ppermute | solution.py:19
  10.8 1.0 %collective-permute-done.3 = f32[16,32]{1,0:T(8,128)S(1)} collective-permute-done((f32[16,32]{1,0:T(8,128)S(1)}, f32[16,32]{1,0:T(8,128)S(1)}, u32[]{:S(2)}, u32[]{:S(2)}) %collective-permute-start.3) | collective-permute-done | bytes 2080 | tf_op jit(solution)/shard_map/ppermute | solution.py:19
  12.1 1.7 %collective-permute-done.1 = f32[16,128]{1,0:T(8,128)S(1)} collective-permute-done((f32[16,128]{1,0:T(8,128)S(1)}, f32[16,128]{1,0:T(8,128)S(1)}, u32[]{:S(2)}, u32[]{:S(2)}) %collective-permute-start.1) | collective-permute-done | bytes 8224 | tf_op jit(solution)/shard_map/ppermute | solution.py:19
  13.8 0.3 subtract_bitcast_fusion
  14.1 0.9 %copy.43.h_ref = f32[32,16,128]{2,1,0:T(8,128)} copy(f32[32,16,128]{2,0,1:T(8,128)S(1)} %get-tuple-element.18) | data formatting | bytes 524288 | tf_op jit(solution)/shard_map/transpose | solution.py:189
  15.0 0.9 %copy.44.d_ref = f32[32,16,128]{2,1,0:T(8,128)} copy(f32[32,16,128]{2,0,1:T(8,128)S(1)} %get-tuple-element.13) | data formatting | bytes 524288 | tf_op jit(solution)/shard_map/transpose | solution.py:186
  15.9 2.3 %shard_map.28 = (f32[3,32,16,128]{3,2,1,0:T(8,128)}, f32[4,2,16,128]{3,2,1,0:T(8,128)}) custom-call(f32[32,16,128]{2,1,0:T(8,128)} %copy.43.h_ref, f32[32,16,128]{2,1,0:T(8,128)} %copy.44.d_ref), custom_call_target="tpu_custom_call" | custom-call | tf_op jit(solution)/shard_map/pallas_call | solution.py:72
  18.1 8.6 %all-gather = f32[16,2,16,128]{3,2,1,0:T(8,128)} all-gather(f32[4,2,16,128]{3,2,1,0:T(8,128)} %get-tuple-element.9), channel_id=2, replica_groups=mesh['gx'=4,'gy'=8] {'gx'}, dimensions={0}, use_global_device_ids=true | all-gather | bytes 327680 | tf_op jit(solution)/shard_map/all_gather | solution.py:153
  26.7 1.7 %shard_map.29 = f32[4,2,16,128]{3,2,1,0:T(8,128)} custom-call(f32[4,4,2,16,128]{4,3,2,1,0:T(8,128)} %bitcast.61), custom_call_target="tpu_custom_call" | custom-call | tf_op jit(solution)/shard_map/pallas_call | solution.py:115
  28.4 1.4 %copy.45 = f32[3,32,16,128]{3,1,2,0:T(8,128)S(1)} copy(f32[3,32,16,128]{3,2,1,0:T(8,128)} %get-tuple-element.10) | data formatting | bytes 1572864 | tf_op jit(solution)/shard_map/pallas_call | solution.py:72
  29.8 0.7 constant_dynamic-slice_fusion.1
  30.7 0.9 %copy.50.d_ref = f32[128,4,128]{2,1,0:T(4,128)} copy(f32[128,4,128]{0,2,1:T(8,128)S(1)} %bitcast.60) | data formatting | bytes 524288 | tf_op jit(solution)/shard_map/reshape | solution.py:194
  31.5 0.8 %copy.49.h_ref = f32[128,4,128]{2,1,0:T(4,128)} copy(f32[128,4,128]{0,2,1:T(8,128)S(1)} %bitcast.59) | data formatting | bytes 524288 | tf_op jit(solution)/shard_map/reshape | solution.py:195
  32.4 3.3 %shard_map.30 = (f32[3,128,4,128]{3,2,1,0:T(4,128)}, f32[4,2,4,128]{3,2,1,0:T(4,128)}) custom-call(f32[128,4,128]{2,1,0:T(4,128)} %copy.49.h_ref, f32[128,4,128]{2,1,0:T(4,128)} %copy.50.d_ref), custom_call_target="tpu_custom_call" | custom-call | tf_op jit(solution)/shard_map/pallas_call | solution.py:72
  35.7 35.2 %all-gather.1 = f32[32,2,4,128]{3,2,1,0:T(4,128)} all-gather(f32[4,2,4,128]{3,2,1,0:T(4,128)} %get-tuple-element.11), channel_id=3, replica_groups=mesh['gx'=4,'gy'=8] {'gy'}, dimensions={0}, use_global_device_ids=true | all-gather | bytes 147456 | tf_op jit(solution)/shard_map/all_gather | solution.py:153
  71.0 1.7 %shard_map.31 = f32[8,2,4,128]{3,2,1,0:T(4,128)} custom-call(f32[8,4,2,4,128]{4,3,2,1,0:T(4,128)} %bitcast.65), custom_call_target="tpu_custom_call" | custom-call | tf_op jit(solution)/shard_map/pallas_call | solution.py:115
  72.7 0.7 constant_dynamic-slice_fusion
  73.7 0.2 concatenate.32
  74.7 0.9 %fusion.12.d_ref = f32[16,32,128]{2,1,0:T(8,128)} fusion(f32[1,16,32]{0,2,1:T(8,128)S(1)} %concatenate.32, f32[126,16,32]{0,2,1:T(8,128)S(1)} %multiply_add_fusion, f32[1,16,32]{0,2,1:T(8,128)S(1)} %concatenate.31, f32[16,32,128]{2,1,0:T(8,128)S(1)} %copy-done, f32[16,32,128]{2,1,0:T(8,128)S(1)} %copy-done.2), kind=kLoop, calls=%fused_computation.21 | loop fusion | flops 589824 | bytes 1048576 | tf_op jit(solution)/shard_map/sub | solution.py:198
  75.6 1.9 %shard_map.32 = f32[16,32,128]{2,1,0:T(8,128)} custom-call(f32[16,32,128]{2,1,0:T(8,128)} %copy-done.1, f32[16,32,128]{2,1,0:T(8,128)} %fusion.12.d_ref), custom_call_target="tpu_custom_call" | custom-call | tf_op jit(solution)/shard_map/pallas_call | solution.py:144
  (27 shorter events, 2.1 us)
Async XLA Ops:
  1.2 6.5 %copy-start = (f32[16,32,128]{2,1,0:T(8,128)S(1)}, f32[16,32,128]{2,1,0:T(8,128)}, u32[]{:S(2)}) copy-start(f32[16,32,128]{2,1,0:T(8,128)} %param.2) | copy-start | bytes 786436
  1.3 9.3 %collective-permute-start.2 = (f32[16,32]{1,0:T(8,128)S(1)}, f32[16,32]{1,0:T(8,128)S(1)}, u32[]{:S(2)}, u32[]{:S(2)}) collective-permute-start(f32[16,32]{1,0:T(8,128)S(1)} %bitcast.72), channel_id=1, source_target_pairs={{0,1},{1,2},{2,3},{3,4},{4,5},{5,6},{6,7},{8,9},{9,10},{10,11},{11... | collective-permute-start | bytes 6152 | tf_op jit(solution)/shard_map/ppermute | solution.py:18
  6.3 5.5 %collective-permute-start.3 = (f32[16,32]{1,0:T(8,128)S(1)}, f32[16,32]{1,0:T(8,128)S(1)}, u32[]{:S(2)}, u32[]{:S(2)}) collective-permute-start(f32[16,32]{1,0:T(8,128)S(1)} %bitcast.74), channel_id=1, source_target_pairs={{1,0},{2,1},{3,2},{4,3},{5,4},{6,5},{7,6},{9,8},{10,9},{11,10},{12... | collective-permute-start | bytes 6152 | tf_op jit(solution)/shard_map/ppermute | solution.py:19
  7.7 4.4 %collective-permute-start = (f32[16,128]{1,0:T(8,128)S(1)}, f32[16,128]{1,0:T(8,128)S(1)}, u32[]{:S(2)}, u32[]{:S(2)}) collective-permute-start(f32[16,128]{1,0:T(8,128)S(1)} %bitcast.77), channel_id=1, source_target_pairs={{0,8},{8,16},{16,24},{1,9},{9,17},{17,25},{2,10},{10,18},{18,26},{... | collective-permute-start | bytes 24584 | tf_op jit(solution)/shard_map/ppermute | solution.py:18
  9.1 4.7 %collective-permute-start.1 = (f32[16,128]{1,0:T(8,128)S(1)}, f32[16,128]{1,0:T(8,128)S(1)}, u32[]{:S(2)}, u32[]{:S(2)}) collective-permute-start(f32[16,128]{1,0:T(8,128)S(1)} %bitcast.76), channel_id=1, source_target_pairs={{8,0},{16,8},{24,16},{9,1},{17,9},{25,17},{10,2},{18,10},{26,18},{... | collective-permute-start | bytes 24584 | tf_op jit(solution)/shard_map/ppermute | solution.py:19
  10.6 3.1 %copy-start.2 = (f32[16,32,128]{2,1,0:T(8,128)S(1)}, f32[16,32,128]{2,1,0:T(8,128)}, u32[]{:S(2)}) copy-start(f32[16,32,128]{2,1,0:T(8,128)} %param.3) | copy-start | bytes 786436
  14.1 17.4 %copy-start.1 = (f32[16,32,128]{2,1,0:T(8,128)}, f32[16,32,128]{2,1,0:T(8,128)S(1)}, u32[]{:S(2)}) copy-start(f32[16,32,128]{2,1,0:T(8,128)S(1)} %get-tuple-element.19.h_ref) | copy-start | bytes 786436
  35.7 38.2 %copy-start.3 = (f32[3,128,4,128]{3,2,1,0:T(4,128)S(1)}, f32[3,128,4,128]{3,2,1,0:T(4,128)}, u32[]{:S(2)}) copy-start(f32[3,128,4,128]{3,2,1,0:T(4,128)} %get-tuple-element.12) | copy-start | bytes 2359300

commit v2 on v1

--- a/solution.py
+++ b/solution.py
@@ -148,9 +148,17 @@
     )(h_lines, d_lines)
 
 
-def distributed_solve(h_lines, d_lines, axis):
+def slot_gather(part, axis):
+    slots = jnp.zeros((lax.axis_size(axis),) + part.shape, part.dtype)
+    return lax.psum(lax.dynamic_update_index_in_dim(slots, part, lax.axis_index(axis), 0), axis)
+
+
+def distributed_solve(h_lines, d_lines, axis, by_sum):
     responses, reduced = partition_call(h_lines, d_lines)
-    gathered = lax.all_gather(reduced, axis)
+    if by_sum:
+        gathered = slot_gather(reduced, axis)
+    else:
+        gathered = lax.all_gather(reduced, axis)
     ends = reduced_call(gathered)
     head, tail = lax.dynamic_index_in_dim(ends, lax.axis_index(axis), 0, keepdims=False)
     interior = responses[0, 1:-1] + responses[1, 1:-1] * head + responses[2, 1:-1] * tail
@@ -187,13 +195,13 @@
         forward_euler_increment - implicit_weight * horizontal_implicit_solve, 1, 0
     )
     first_rate = jnp.moveaxis(half_rate, 1, 0)
-    first_pass = jnp.moveaxis(distributed_solve(first_rate, first_side, "gx"), 0, 1)
+    first_pass = jnp.moveaxis(distributed_solve(first_rate, first_side, "gx", False), 0, 1)
     second_side = first_pass - implicit_weight * vertical_implicit_solve
     lanes = 128
     groups = plane_count * row_count // lanes
     side_lines = jnp.transpose(second_side, (2, 0, 1)).reshape(column_count, groups, lanes)
     rate_lines = jnp.transpose(half_rate, (2, 0, 1)).reshape(column_count, groups, lanes)
-    column_lines = distributed_solve(rate_lines, side_lines, "gy")
+    column_lines = distributed_solve(rate_lines, side_lines, "gy", True)
     second = jnp.transpose(column_lines.reshape(column_count, plane_count, row_count), (1, 2, 0))
     plane_side = second - implicit_weight * depth_implicit_solve
     return sweep_call(half_rate, plane_side)

time: 78 us -> 128 us (1.64)
  waiting for transfers between devices: 2.78 us -> 72.5 us
  blocking collectives: 43.8 us -> 8.56 us
  between operations: 0.19 us -> 13.6 us
  local copies, waits for them, and re-layouts: 9.3 us -> 11.9 us
    psum x0 -> x1, waiting for transfers between devices: none -> 69.8 us  [slot_gather(): lax.psum(lax.dynamic_update_index_in_dim(slots, part, lax.axis_index(axis...]
    all_gather x2 -> x1, blocking collectives: 43.8 us -> 8.56 us  [distributed_solve(): gathered = lax.all_gather(reduced, axis)]
    unnamed x10 -> x12, local copies, waits for them, and re-layouts: 0.33 us -> 1.68 us
  transfers between devices with their start and end apart: 4 -> 5, of which waited for: 2 -> 3; matrix products, arithmetic and copies ran while one was open for 1% -> 2% of each run, Pallas kernels for 0% -> 0%
where the time goes in v2:
time: 128 us
  waiting for transfers between devices  72.5 us (57%)
  between operations  13.6 us (11%)
  local copies, waits for them, and re-layouts  11.9 us (9%)
  Pallas kernels  10.8 us (8%)
  starting transfers between devices  8.89 us (7%)
  blocking collectives  8.56 us (7%)
  other arithmetic  1.61 us (1%)
    psum x1, waiting for transfers between devices, slot_gather(): lax.psum(lax.dynamic_update_index_in_dim(slots, part, lax.axis_index(axis...  69.8 us
    all_gather x1, blocking collectives, distributed_solve(): gathered = lax.all_gather(reduced, axis)  8.56 us
    ppermute x2, starting transfers between devices, halos(): low = lax.ppermute(last, axis, forward)  6.3 us
    pallas_call x2, Pallas kernels, partition_call(): pl.pallas_call(partition_kernel, out_shape=(jax.ShapeDtypeStruct((3, n) +...  5.57 us
    pallas_call x2, Pallas kernels, reduced_call(): pl.pallas_call(reduced_kernel, out_shape=jax.ShapeDtypeStruct((count, 2)...  3.35 us
    ppermute x2, waiting for transfers between devices, halos(): high = lax.ppermute(first, axis, backward)  2.78 us
    ppermute x2, starting transfers between devices, halos(): high = lax.ppermute(first, axis, backward)  2.59 us
  transfers between devices with their start and end apart: 5, of which 3 were waited for; matrix products, arithmetic and copies ran while one was open for 2% of the time, Pallas kernels for 0%

profile of v2, /device:TPU:0, one launch (start us, length us, event | category | flops | bytes accessed | tf_op | source)
XLA Modules:
  0.0 127.9 jit_solution(2217021642470168525)
XLA Ops:
  6.5 1.2 fusion.16
  7.9 4.8 %collective-permute-start.2 = (f32[16,32]{1,0:T(8,128)S(1)}, f32[16,32]{1,0:T(8,128)S(1)}, u32[]{:S(2)}, u32[]{:S(2)}) collective-permute-start(f32[16,32]{1,0:T(8,128)S(1)} %bitcast.72), channel_id=1, source_target_pairs={{0,1},{1,2},{2,3},{3,4},{4,5},{5,6},{6,7},{8,9},{9,10},{10,11},{11... | collective-permute-start | bytes 6152 | tf_op jit(solution)/shard_map/ppermute | solution.py:18
  12.9 1.3 %collective-permute-start.3 = (f32[16,32]{1,0:T(8,128)S(1)}, f32[16,32]{1,0:T(8,128)S(1)}, u32[]{:S(2)}, u32[]{:S(2)}) collective-permute-start(f32[16,32]{1,0:T(8,128)S(1)} %bitcast.74), channel_id=1, source_target_pairs={{1,0},{2,1},{3,2},{4,3},{5,4},{6,5},{7,6},{9,8},{10,9},{11,10},{12... | collective-permute-start | bytes 6152 | tf_op jit(solution)/shard_map/ppermute | solution.py:19
  14.2 1.5 %collective-permute-start = (f32[16,128]{1,0:T(8,128)S(1)}, f32[16,128]{1,0:T(8,128)S(1)}, u32[]{:S(2)}, u32[]{:S(2)}) collective-permute-start(f32[16,128]{1,0:T(8,128)S(1)} %bitcast.77), channel_id=1, source_target_pairs={{0,8},{8,16},{16,24},{1,9},{9,17},{17,25},{2,10},{10,18},{18,26},{... | collective-permute-start | bytes 24584 | tf_op jit(solution)/shard_map/ppermute | solution.py:18
  15.7 1.3 %collective-permute-start.1 = (f32[16,128]{1,0:T(8,128)S(1)}, f32[16,128]{1,0:T(8,128)S(1)}, u32[]{:S(2)}, u32[]{:S(2)}) collective-permute-start(f32[16,128]{1,0:T(8,128)S(1)} %bitcast.76), channel_id=1, source_target_pairs={{8,0},{16,8},{24,16},{9,1},{17,9},{25,17},{10,2},{18,10},{26,18},{... | collective-permute-start | bytes 24584 | tf_op jit(solution)/shard_map/ppermute | solution.py:19
  17.4 1.0 collective-permute-done.3
  18.6 1.7 %collective-permute-done.1 = f32[16,128]{1,0:T(8,128)S(1)} collective-permute-done((f32[16,128]{1,0:T(8,128)S(1)}, f32[16,128]{1,0:T(8,128)S(1)}, u32[]{:S(2)}, u32[]{:S(2)}) %collective-permute-start.1) | collective-permute-done | bytes 8224 | tf_op jit(solution)/shard_map/ppermute | solution.py:19
  20.7 0.9 copy.43.h_ref
  21.5 0.9 copy.44.d_ref
  22.4 2.3 %shard_map.28 = (f32[3,32,16,128]{3,2,1,0:T(8,128)}, f32[4,2,16,128]{3,2,1,0:T(8,128)}) custom-call(f32[32,16,128]{2,1,0:T(8,128)} %copy.43.h_ref, f32[32,16,128]{2,1,0:T(8,128)} %copy.44.d_ref), custom_call_target="tpu_custom_call" | custom-call | tf_op jit(solution)/shard_map/pallas_call | solution.py:72
  24.7 8.6 %all-gather = f32[16,2,16,128]{3,2,1,0:T(8,128)} all-gather(f32[4,2,16,128]{3,2,1,0:T(8,128)} %get-tuple-element.9), channel_id=2, replica_groups=mesh['gx'=4,'gy'=8] {'gx'}, dimensions={0}, use_global_device_ids=true | all-gather | bytes 327680 | tf_op jit(solution)/shard_map/all_gather | solution.py:161
  33.2 1.7 %shard_map.29 = f32[4,2,16,128]{3,2,1,0:T(8,128)} custom-call(f32[4,4,2,16,128]{4,3,2,1,0:T(8,128)} %bitcast.62), custom_call_target="tpu_custom_call" | custom-call | tf_op jit(solution)/shard_map/pallas_call | solution.py:115
  34.9 1.4 %copy.45 = f32[3,32,16,128]{3,1,2,0:T(8,128)S(1)} copy(f32[3,32,16,128]{3,2,1,0:T(8,128)} %get-tuple-element.10) | data formatting | bytes 1572864 | tf_op jit(solution)/shard_map/pallas_call | solution.py:72
  36.3 0.7 constant_dynamic-slice_fusion.1
  37.2 0.9 copy.50.d_ref
  38.1 0.8 copy.49.h_ref
  38.9 3.3 %shard_map.30 = (f32[3,128,4,128]{3,2,1,0:T(4,128)}, f32[4,2,4,128]{3,2,1,0:T(4,128)}) custom-call(f32[128,4,128]{2,1,0:T(4,128)} %copy.49.h_ref, f32[128,4,128]{2,1,0:T(4,128)} %copy.50.d_ref), custom_call_target="tpu_custom_call" | custom-call | tf_op jit(solution)/shard_map/pallas_call | solution.py:72
  42.2 0.7 copy-done.4
  43.6 1.2 fusion.15
  45.3 69.8 %all-reduce.3.cloned.1.call-done.g_ref = f32[8,4,2,4,128]{4,3,2,1,0:T(4,128)} async-done(((f32[8,4,2,4,128]{4,3,2,1,0:T(4,128)}), f32[8,4,2,4,128]{4,3,2,1,0:T(4,128)}) %all-reduce.3.cloned.1.call-update) | async-done | bytes 131088 | tf_op jit(solution)/shard_map/psum | solution.py:153
  115.1 1.7 %shard_map.31 = f32[8,2,4,128]{3,2,1,0:T(4,128)} custom-call(f32[8,4,2,4,128]{4,3,2,1,0:T(4,128)} %all-reduce.3.cloned.1.call-done.g_ref), custom_call_target="tpu_custom_call" | custom-call | tf_op jit(solution)/shard_map/pallas_call | solution.py:115
  116.7 0.7 constant_dynamic-slice_fusion
  118.2 0.9 fusion.12.d_ref
  119.1 1.9 %shard_map.32 = f32[16,32,128]{2,1,0:T(8,128)} custom-call(f32[16,32,128]{2,1,0:T(8,128)} %copy-done.1, f32[16,32,128]{2,1,0:T(8,128)} %fusion.12.d_ref), custom_call_target="tpu_custom_call" | custom-call | tf_op jit(solution)/shard_map/pallas_call | solution.py:144
  (33 shorter events, 3.3 us)
Async XLA Ops:
  6.5 108.5 %all-reduce.3.cloned.1.call-start = ((), (), s32[]{:S(2)}) async-start(), calls=%async_computation | async-start | bytes 262144 | tf_op jit(solution)/shard_map/psum | solution.py:153
  7.7 6.5 %copy-start = (f32[16,32,128]{2,1,0:T(8,128)S(1)}, f32[16,32,128]{2,1,0:T(8,128)}, u32[]{:S(2)}) copy-start(f32[16,32,128]{2,1,0:T(8,128)} %param.2) | copy-start | bytes 786436
  7.9 9.3 %collective-permute-start.2 = (f32[16,32]{1,0:T(8,128)S(1)}, f32[16,32]{1,0:T(8,128)S(1)}, u32[]{:S(2)}, u32[]{:S(2)}) collective-permute-start(f32[16,32]{1,0:T(8,128)S(1)} %bitcast.72), channel_id=1, source_target_pairs={{0,1},{1,2},{2,3},{3,4},{4,5},{5,6},{6,7},{8,9},{9,10},{10,11},{11... | collective-permute-start | bytes 6152 | tf_op jit(solution)/shard_map/ppermute | solution.py:18
  12.9 5.5 %collective-permute-start.3 = (f32[16,32]{1,0:T(8,128)S(1)}, f32[16,32]{1,0:T(8,128)S(1)}, u32[]{:S(2)}, u32[]{:S(2)}) collective-permute-start(f32[16,32]{1,0:T(8,128)S(1)} %bitcast.74), channel_id=1, source_target_pairs={{1,0},{2,1},{3,2},{4,3},{5,4},{6,5},{7,6},{9,8},{10,9},{11,10},{12... | collective-permute-start | bytes 6152 | tf_op jit(solution)/shard_map/ppermute | solution.py:19
  14.2 4.4 %collective-permute-start = (f32[16,128]{1,0:T(8,128)S(1)}, f32[16,128]{1,0:T(8,128)S(1)}, u32[]{:S(2)}, u32[]{:S(2)}) collective-permute-start(f32[16,128]{1,0:T(8,128)S(1)} %bitcast.77), channel_id=1, source_target_pairs={{0,8},{8,16},{16,24},{1,9},{9,17},{17,25},{2,10},{10,18},{18,26},{... | collective-permute-start | bytes 24584 | tf_op jit(solution)/shard_map/ppermute | solution.py:18
  15.7 4.7 %collective-permute-start.1 = (f32[16,128]{1,0:T(8,128)S(1)}, f32[16,128]{1,0:T(8,128)S(1)}, u32[]{:S(2)}, u32[]{:S(2)}) collective-permute-start(f32[16,128]{1,0:T(8,128)S(1)} %bitcast.76), channel_id=1, source_target_pairs={{8,0},{16,8},{24,16},{9,1},{17,9},{25,17},{10,2},{18,10},{26,18},{... | collective-permute-start | bytes 24584 | tf_op jit(solution)/shard_map/ppermute | solution.py:19
  17.2 3.1 %copy-start.2 = (f32[16,32,128]{2,1,0:T(8,128)S(1)}, f32[16,32,128]{2,1,0:T(8,128)}, u32[]{:S(2)}) copy-start(f32[16,32,128]{2,1,0:T(8,128)} %param.3) | copy-start | bytes 786436
  20.7 17.4 %copy-start.1 = (f32[16,32,128]{2,1,0:T(8,128)}, f32[16,32,128]{2,1,0:T(8,128)S(1)}, u32[]{:S(2)}) copy-start(f32[16,32,128]{2,1,0:T(8,128)S(1)} %get-tuple-element.19.h_ref) | copy-start | bytes 786436
  42.2 0.7 copy-start.4
  42.9 0.7 copy-start.3
Sparse Core Ops, SparseCore 0:
  43.7 71.2 all-reduce.2

commit v3 on v2

--- a/solution.py
+++ b/solution.py
@@ -148,15 +148,27 @@
     )(h_lines, d_lines)
 
 
-def slot_gather(part, axis):
-    slots = jnp.zeros((lax.axis_size(axis),) + part.shape, part.dtype)
-    return lax.psum(lax.dynamic_update_index_in_dim(slots, part, lax.axis_index(axis), 0), axis)
-
-
-def distributed_solve(h_lines, d_lines, axis, by_sum):
+def doubling_gather(part, axis):
+    count = lax.axis_size(axis)
+    if count & (count - 1):
+        return lax.all_gather(part, axis)
+    mine = lax.axis_index(axis)
+    held = part[None]
+    step = 1
+    while step < count:
+        other = lax.ppermute(held, axis, [(i, i ^ step) for i in range(count)])
+        lower = (mine // step) % 2 == 0
+        held = jnp.where(
+            lower, jnp.concatenate([held, other], 0), jnp.concatenate([other, held], 0)
+        )
+        step *= 2
+    return held
+
+
+def distributed_solve(h_lines, d_lines, axis, doubling):
     responses, reduced = partition_call(h_lines, d_lines)
-    if by_sum:
-        gathered = slot_gather(reduced, axis)
+    if doubling:
+        gathered = doubling_gather(reduced, axis)
     else:
         gathered = lax.all_gather(reduced, axis)
     ends = reduced_call(gathered)

time: 128 us -> 57.7 us (0.45)
  waiting for transfers between devices: 72.5 us -> 7.22 us
  between operations: 13.6 us -> 0.19 us
  starting transfers between devices: 8.89 us -> 17.6 us
  local copies, waits for them, and re-layouts: 11.9 us -> 10.5 us
    psum x1 -> x0, waiting for transfers between devices: 69.8 us -> none  [slot_gather(): lax.psum(lax.dynamic_update_index_in_dim(slots, part, lax.axis_index(axis...]
    ppermute x0 -> x3, starting transfers between devices: none -> 8.75 us  [doubling_gather(): other = lax.ppermute(held, axis, [(i, i ^ step) for i in range(count)])]
    ppermute x0 -> x3, waiting for transfers between devices: none -> 4.44 us  [doubling_gather(): other = lax.ppermute(held, axis, [(i, i ^ step) for i in range(count)])]
    unnamed x12 -> x10, local copies, waits for them, and re-layouts: 1.68 us -> 0.33 us
  transfers between devices with their start and end apart: 5 -> 7, of which waited for: 3 -> 5; matrix products, arithmetic and copies ran while one was open for 2% -> 4% of each run, Pallas kernels for 0% -> 0%
where the time goes in v3:
time: 57.7 us; the launch traced here: 57.2 us
  starting transfers between devices  17.6 us (31%)
  Pallas kernels  10.8 us (19%)
  local copies, waits for them, and re-layouts  10.5 us (18%)
  blocking collectives  8.56 us (15%)
  waiting for transfers between devices  7.22 us (13%)
  other arithmetic  2.33 us (4%)
    ppermute x3, starting transfers between devices, doubling_gather(): other = lax.ppermute(held, axis, [(i, i ^ step) for i in range(count)])  8.75 us
    all_gather x1, blocking collectives, distributed_solve(): gathered = lax.all_gather(reduced, axis)  8.56 us
    ppermute x2, starting transfers between devices, halos(): low = lax.ppermute(last, axis, forward)  6.3 us
    pallas_call x2, Pallas kernels, partition_call(): pl.pallas_call(partition_kernel, out_shape=(jax.ShapeDtypeStruct((3, n) +...  5.56 us
    ppermute x3, waiting for transfers between devices, doubling_gather(): other = lax.ppermute(held, axis, [(i, i ^ step) for i in range(count)])  4.44 us
    pallas_call x2, Pallas kernels, reduced_call(): pl.pallas_call(reduced_kernel, out_shape=jax.ShapeDtypeStruct((count, 2)...  3.35 us
    ppermute x2, waiting for transfers between devices, halos(): high = lax.ppermute(first, axis, backward)  2.77 us
    ppermute x2, starting transfers between devices, halos(): high = lax.ppermute(first, axis, backward)  2.59 us
  transfers between devices with their start and end apart: 7, of which 5 were waited for; matrix products, arithmetic and copies ran while one was open for 4% of the time, Pallas kernels for 0%

profile of v3, /device:TPU:0, one launch (start us, length us, event | category | flops | bytes accessed | tf_op | source)
XLA Modules:
  0.0 57.2 jit_solution(1527163262770048129)
XLA Ops:
  0.0 1.2 %fusion.16 = (f32[16,32,1]{2,1,0:T(8,128)S(1)}, f32[16,32,1]{2,1,0:T(8,128)S(1)}) fusion(f32[16,32,128]{2,1,0:T(8,128)} %param.2), kind=kLoop, calls=%fused_computation.34 | loop fusion | bytes 8192 | tf_op jit(solution)/shard_map/slice | solution.py:16
  1.3 4.8 %collective-permute-start.2 = (f32[16,32]{1,0:T(8,128)S(1)}, f32[16,32]{1,0:T(8,128)S(1)}, u32[]{:S(2)}, u32[]{:S(2)}) collective-permute-start(f32[16,32]{1,0:T(8,128)S(1)} %bitcast.73), channel_id=1, source_target_pairs={{0,1},{1,2},{2,3},{3,4},{4,5},{5,6},{6,7},{8,9},{9,10},{10,11},{11... | collective-permute-start | bytes 6152 | tf_op jit(solution)/shard_map/ppermute | solution.py:18
  6.3 1.3 %collective-permute-start.3 = (f32[16,32]{1,0:T(8,128)S(1)}, f32[16,32]{1,0:T(8,128)S(1)}, u32[]{:S(2)}, u32[]{:S(2)}) collective-permute-start(f32[16,32]{1,0:T(8,128)S(1)} %bitcast.75), channel_id=1, source_target_pairs={{1,0},{2,1},{3,2},{4,3},{5,4},{6,5},{7,6},{9,8},{10,9},{11,10},{12... | collective-permute-start | bytes 6152 | tf_op jit(solution)/shard_map/ppermute | solution.py:19
  7.7 1.5 %collective-permute-start = (f32[16,128]{1,0:T(8,128)S(1)}, f32[16,128]{1,0:T(8,128)S(1)}, u32[]{:S(2)}, u32[]{:S(2)}) collective-permute-start(f32[16,128]{1,0:T(8,128)S(1)} %bitcast.78), channel_id=1, source_target_pairs={{0,8},{8,16},{16,24},{1,9},{9,17},{17,25},{2,10},{10,18},{18,26},{... | collective-permute-start | bytes 24584 | tf_op jit(solution)/shard_map/ppermute | solution.py:18
  9.1 1.3 %collective-permute-start.1 = (f32[16,128]{1,0:T(8,128)S(1)}, f32[16,128]{1,0:T(8,128)S(1)}, u32[]{:S(2)}, u32[]{:S(2)}) collective-permute-start(f32[16,128]{1,0:T(8,128)S(1)} %bitcast.77), channel_id=1, source_target_pairs={{8,0},{16,8},{24,16},{9,1},{17,9},{25,17},{10,2},{18,10},{26,18},{... | collective-permute-start | bytes 24584 | tf_op jit(solution)/shard_map/ppermute | solution.py:19
  10.8 1.0 %collective-permute-done.3 = f32[16,32]{1,0:T(8,128)S(1)} collective-permute-done((f32[16,32]{1,0:T(8,128)S(1)}, f32[16,32]{1,0:T(8,128)S(1)}, u32[]{:S(2)}, u32[]{:S(2)}) %collective-permute-start.3) | collective-permute-done | bytes 2080 | tf_op jit(solution)/shard_map/ppermute | solution.py:19
  12.1 1.7 %collective-permute-done.1 = f32[16,128]{1,0:T(8,128)S(1)} collective-permute-done((f32[16,128]{1,0:T(8,128)S(1)}, f32[16,128]{1,0:T(8,128)S(1)}, u32[]{:S(2)}, u32[]{:S(2)}) %collective-permute-start.1) | collective-permute-done | bytes 8224 | tf_op jit(solution)/shard_map/ppermute | solution.py:19
  14.1 0.9 %copy.43.h_ref = f32[32,16,128]{2,1,0:T(8,128)} copy(f32[32,16,128]{2,0,1:T(8,128)S(1)} %get-tuple-element.18) | data formatting | bytes 524288 | tf_op jit(solution)/shard_map/transpose | solution.py:209
  15.0 0.9 %copy.44.d_ref = f32[32,16,128]{2,1,0:T(8,128)} copy(f32[32,16,128]{2,0,1:T(8,128)S(1)} %get-tuple-element.13) | data formatting | bytes 524288 | tf_op jit(solution)/shard_map/transpose | solution.py:206
  15.9 2.3 %shard_map.28 = (f32[3,32,16,128]{3,2,1,0:T(8,128)}, f32[4,2,16,128]{3,2,1,0:T(8,128)}) custom-call(f32[32,16,128]{2,1,0:T(8,128)} %copy.43.h_ref, f32[32,16,128]{2,1,0:T(8,128)} %copy.44.d_ref), custom_call_target="tpu_custom_call" | custom-call | tf_op jit(solution)/shard_map/pallas_call | solution.py:72
  18.1 8.6 %all-gather = f32[16,2,16,128]{3,2,1,0:T(8,128)} all-gather(f32[4,2,16,128]{3,2,1,0:T(8,128)} %get-tuple-element.9), channel_id=2, replica_groups=mesh['gx'=4,'gy'=8] {'gx'}, dimensions={0}, use_global_device_ids=true | all-gather | bytes 327680 | tf_op jit(solution)/shard_map/all_gather | solution.py:173
  26.7 1.7 %shard_map.29 = f32[4,2,16,128]{3,2,1,0:T(8,128)} custom-call(f32[4,4,2,16,128]{4,3,2,1,0:T(8,128)} %bitcast.61), custom_call_target="tpu_custom_call" | custom-call | tf_op jit(solution)/shard_map/pallas_call | solution.py:115
  28.4 1.4 %copy.45 = f32[3,32,16,128]{3,1,2,0:T(8,128)S(1)} copy(f32[3,32,16,128]{3,2,1,0:T(8,128)} %get-tuple-element.10) | data formatting | bytes 1572864 | tf_op jit(solution)/shard_map/pallas_call | solution.py:72
  30.7 0.9 %copy.50.d_ref = f32[128,4,128]{2,1,0:T(4,128)} copy(f32[128,4,128]{0,2,1:T(8,128)S(1)} %bitcast.60) | data formatting | bytes 524288 | tf_op jit(solution)/shard_map/reshape | solution.py:214
  32.3 3.3 %shard_map.30 = (f32[3,128,4,128]{3,2,1,0:T(4,128)}, f32[4,2,4,128]{3,2,1,0:T(4,128)}) custom-call(f32[128,4,128]{2,1,0:T(4,128)} %copy.49.h_ref, f32[128,4,128]{2,1,0:T(4,128)} %copy.50.d_ref), custom_call_target="tpu_custom_call" | custom-call | tf_op jit(solution)/shard_map/pallas_call | solution.py:72
  35.7 2.6 %collective-permute-start.4 = (f32[1,4,2,4,128]{4,3,2,1,0:T(4,128)}, f32[1,4,2,4,128]{4,3,2,1,0:T(4,128)S(1)}, u32[]{:S(2)}, u32[]{:S(2)}) collective-permute-start(f32[1,4,2,4,128]{4,3,2,1,0:T(4,128)} %bitcast.69), channel_id=1, source_target_pairs={{0,1},{1,0},{2,3},{3,2},{4,5},{5,4},{6,7},{7,6},{8,9},{9,8},{10,11... | collective-permute-start | bytes 49160 | tf_op jit(solution)/shard_map/ppermute | solution.py:159
  38.3 2.0 %collective-permute-done.4 = f32[1,4,2,4,128]{4,3,2,1,0:T(4,128)S(1)} collective-permute-done((f32[1,4,2,4,128]{4,3,2,1,0:T(4,128)}, f32[1,4,2,4,128]{4,3,2,1,0:T(4,128)S(1)}, u32[]{:S(2)}, u32[]{:S(2)}) %collective-permute-start.4) | collective-permute-done | bytes 16416 | tf_op jit(solution)/shard_map/ppermute | solution.py:159
  40.3 3.0 %collective-permute-start.5 = (f32[2,4,2,4,128]{4,3,2,1,0:T(4,128)S(1)}, f32[2,4,2,4,128]{4,3,2,1,0:T(4,128)S(1)}, u32[]{:S(2)}, u32[]{:S(2)}) collective-permute-start(f32[2,4,2,4,128]{4,3,2,1,0:T(4,128)S(1)} %maximum_select_fusion.2), channel_id=1, source_target_pairs={{0,2},{1,3},{2,0},{3,1},{4,6},{5,7},{6,4},{7,5},{8,10},{9,11},{10,... | collective-permute-start | bytes 98312 | tf_op jit(solution)/shard_map/ppermute | solution.py:159
  43.3 1.9 %collective-permute-done.5 = f32[2,4,2,4,128]{4,3,2,1,0:T(4,128)S(1)} collective-permute-done((f32[2,4,2,4,128]{4,3,2,1,0:T(4,128)S(1)}, f32[2,4,2,4,128]{4,3,2,1,0:T(4,128)S(1)}, u32[]{:S(2)}, u32[]{:S(2)}) %collective-permute-start.5) | collective-permute-done | bytes 32800 | tf_op jit(solution)/shard_map/ppermute | solution.py:159
  45.2 3.1 %collective-permute-start.6 = (f32[4,4,2,4,128]{4,3,2,1,0:T(4,128)S(1)}, f32[4,4,2,4,128]{4,3,2,1,0:T(4,128)S(1)}, u32[]{:S(2)}, u32[]{:S(2)}) collective-permute-start(f32[4,4,2,4,128]{4,3,2,1,0:T(4,128)S(1)} %maximum_select_fusion.1), channel_id=1, source_target_pairs={{0,4},{1,5},{2,6},{3,7},{4,0},{5,1},{6,2},{7,3},{8,12},{9,13},{10,... | collective-permute-start | bytes 196616 | tf_op jit(solution)/shard_map/ppermute | solution.py:159
  48.3 1.2 %fusion.15 = (f32[1,126,4,128]{3,2,1,0:T(4,128)S(1)}, f32[1,126,4,128]{3,2,1,0:T(4,128)S(1)}, f32[1,126,4,128]{3,2,1,0:T(4,128)S(1)}) fusion(f32[3,128,4,128]{3,2,1,0:T(4,128)} %get-tuple-element.12), kind=kLoop, calls=%fused_computation.33 | loop fusion | bytes 1548288 | tf_op jit(solution)/shard_map/slice | solution.py:176
  51.3 1.7 %shard_map.31 = f32[8,2,4,128]{3,2,1,0:T(4,128)} custom-call(f32[8,4,2,4,128]{4,3,2,1,0:T(4,128)} %maximum_select_fusion.g_ref), custom_call_target="tpu_custom_call" | custom-call | tf_op jit(solution)/shard_map/pallas_call | solution.py:115
  54.4 0.9 %fusion.12.d_ref = f32[16,32,128]{2,1,0:T(8,128)} fusion(f32[1,16,32]{0,2,1:T(8,128)S(1)} %concatenate.56, f32[126,16,32]{0,2,1:T(8,128)S(1)} %multiply_add_fusion, f32[1,16,32]{0,2,1:T(8,128)S(1)} %concatenate.55, f32[16,32,128]{2,1,0:T(8,128)S(1)} %copy-done, f32[16,32,128]{2,1,0:T(8,128)S(1)} %copy-done.2), kind=kLoop, calls=%fused_computation.21 | loop fusion | flops 589824 | bytes 1048576 | tf_op jit(solution)/shard_map/sub | solution.py:218
  55.3 1.9 %shard_map.32 = f32[16,32,128]{2,1,0:T(8,128)} custom-call(f32[16,32,128]{2,1,0:T(8,128)} %copy-done.1, f32[16,32,128]{2,1,0:T(8,128)} %fusion.12.d_ref), custom_call_target="tpu_custom_call" | custom-call | tf_op jit(solution)/shard_map/pallas_call | solution.py:144
  (35 shorter events, 6.1 us)
Async XLA Ops:
  1.2 6.5 %copy-start = (f32[16,32,128]{2,1,0:T(8,128)S(1)}, f32[16,32,128]{2,1,0:T(8,128)}, u32[]{:S(2)}) copy-start(f32[16,32,128]{2,1,0:T(8,128)} %param.2) | copy-start | bytes 786436
  1.3 9.3 %collective-permute-start.2 = (f32[16,32]{1,0:T(8,128)S(1)}, f32[16,32]{1,0:T(8,128)S(1)}, u32[]{:S(2)}, u32[]{:S(2)}) collective-permute-start(f32[16,32]{1,0:T(8,128)S(1)} %bitcast.73), channel_id=1, source_target_pairs={{0,1},{1,2},{2,3},{3,4},{4,5},{5,6},{6,7},{8,9},{9,10},{10,11},{11... | collective-permute-start | bytes 6152 | tf_op jit(solution)/shard_map/ppermute | solution.py:18
  6.3 5.5 %collective-permute-start.3 = (f32[16,32]{1,0:T(8,128)S(1)}, f32[16,32]{1,0:T(8,128)S(1)}, u32[]{:S(2)}, u32[]{:S(2)}) collective-permute-start(f32[16,32]{1,0:T(8,128)S(1)} %bitcast.75), channel_id=1, source_target_pairs={{1,0},{2,1},{3,2},{4,3},{5,4},{6,5},{7,6},{9,8},{10,9},{11,10},{12... | collective-permute-start | bytes 6152 | tf_op jit(solution)/shard_map/ppermute | solution.py:19
  7.7 4.4 %collective-permute-start = (f32[16,128]{1,0:T(8,128)S(1)}, f32[16,128]{1,0:T(8,128)S(1)}, u32[]{:S(2)}, u32[]{:S(2)}) collective-permute-start(f32[16,128]{1,0:T(8,128)S(1)} %bitcast.78), channel_id=1, source_target_pairs={{0,8},{8,16},{16,24},{1,9},{9,17},{17,25},{2,10},{10,18},{18,26},{... | collective-permute-start | bytes 24584 | tf_op jit(solution)/shard_map/ppermute | solution.py:18
  9.1 4.7 %collective-permute-start.1 = (f32[16,128]{1,0:T(8,128)S(1)}, f32[16,128]{1,0:T(8,128)S(1)}, u32[]{:S(2)}, u32[]{:S(2)}) collective-permute-start(f32[16,128]{1,0:T(8,128)S(1)} %bitcast.77), channel_id=1, source_target_pairs={{8,0},{16,8},{24,16},{9,1},{17,9},{25,17},{10,2},{18,10},{26,18},{... | collective-permute-start | bytes 24584 | tf_op jit(solution)/shard_map/ppermute | solution.py:19
  10.6 3.1 %copy-start.2 = (f32[16,32,128]{2,1,0:T(8,128)S(1)}, f32[16,32,128]{2,1,0:T(8,128)}, u32[]{:S(2)}) copy-start(f32[16,32,128]{2,1,0:T(8,128)} %param.3) | copy-start | bytes 786436
  14.1 17.4 %copy-start.1 = (f32[16,32,128]{2,1,0:T(8,128)}, f32[16,32,128]{2,1,0:T(8,128)S(1)}, u32[]{:S(2)}) copy-start(f32[16,32,128]{2,1,0:T(8,128)S(1)} %get-tuple-element.19.h_ref) | copy-start | bytes 786436
  35.7 4.6 %copy-start.3 = (f32[4,2,4,128]{3,2,1,0:T(4,128)S(1)}, f32[4,2,4,128]{3,2,1,0:T(4,128)}, u32[]{:S(2)}) copy-start(f32[4,2,4,128]{3,2,1,0:T(4,128)} %get-tuple-element.11) | copy-start | bytes 49156
  35.7 4.6 %collective-permute-start.4 = (f32[1,4,2,4,128]{4,3,2,1,0:T(4,128)}, f32[1,4,2,4,128]{4,3,2,1,0:T(4,128)S(1)}, u32[]{:S(2)}, u32[]{:S(2)}) collective-permute-start(f32[1,4,2,4,128]{4,3,2,1,0:T(4,128)} %bitcast.69), channel_id=1, source_target_pairs={{0,1},{1,0},{2,3},{3,2},{4,5},{5,4},{6,7},{7,6},{8,9},{9,8},{10,11... | collective-permute-start | bytes 49160 | tf_op jit(solution)/shard_map/ppermute | solution.py:159
  40.3 4.9 %collective-permute-start.5 = (f32[2,4,2,4,128]{4,3,2,1,0:T(4,128)S(1)}, f32[2,4,2,4,128]{4,3,2,1,0:T(4,128)S(1)}, u32[]{:S(2)}, u32[]{:S(2)}) collective-permute-start(f32[2,4,2,4,128]{4,3,2,1,0:T(4,128)S(1)} %maximum_select_fusion.2), channel_id=1, source_target_pairs={{0,2},{1,3},{2,0},{3,1},{4,6},{5,7},{6,4},{7,5},{8,10},{9,11},{10,... | collective-permute-start | bytes 98312 | tf_op jit(solution)/shard_map/ppermute | solution.py:159
  45.2 5.3 %collective-permute-start.6 = (f32[4,4,2,4,128]{4,3,2,1,0:T(4,128)S(1)}, f32[4,4,2,4,128]{4,3,2,1,0:T(4,128)S(1)}, u32[]{:S(2)}, u32[]{:S(2)}) collective-permute-start(f32[4,4,2,4,128]{4,3,2,1,0:T(4,128)S(1)} %maximum_select_fusion.1), channel_id=1, source_target_pairs={{0,4},{1,5},{2,6},{3,7},{4,0},{5,1},{6,2},{7,3},{8,12},{9,13},{10,... | collective-permute-start | bytes 196616 | tf_op jit(solution)/shard_map/ppermute | solution.py:159

commit v4 on v3

--- a/solution.py
+++ b/solution.py
@@ -168,7 +168,8 @@
 def distributed_solve(h_lines, d_lines, axis, doubling):
     responses, reduced = partition_call(h_lines, d_lines)
     if doubling:
-        gathered = doubling_gather(reduced, axis)
+        copies = jnp.broadcast_to(reduced[None], (lax.axis_size(axis),) + reduced.shape)
+        gathered = lax.all_to_all(copies, axis, 0, 0)
     else:
         gathered = lax.all_gather(reduced, axis)
     ends = reduced_call(gathered)

time: 57.7 us -> 58.8 us (1.019)
  local copies, waits for them, and re-layouts: 10.5 us -> 12.5 us
  starting transfers between devices: 17.6 us -> 15.8 us
  waiting for transfers between devices: 7.22 us -> 8.58 us
  other arithmetic: 2.33 us -> 1.61 us
    ppermute x3 -> x0, starting transfers between devices: 8.75 us -> none  [doubling_gather(): other = lax.ppermute(held, axis, [(i, i ^ step) for i in range(count)])]
    all_to_all x0 -> x1, starting transfers between devices: none -> 6.96 us  [distributed_solve(): gathered = lax.all_to_all(copies, axis, 0, 0)]
    all_to_all x0 -> x1, waiting for transfers between devices: none -> 5.8 us  [distributed_solve(): gathered = lax.all_to_all(copies, axis, 0, 0)]
    ppermute x3 -> x0, waiting for transfers between devices: 4.44 us -> none  [doubling_gather(): other = lax.ppermute(held, axis, [(i, i ^ step) for i in range(count)])]
    broadcast_in_dim x0 -> x1, local copies, waits for them, and re-layouts: none -> 1.39 us  [distributed_solve(): jnp.broadcast_to(reduced[None], (lax.axis_size(axis),) + reduced.shape)]
    select_n x3 -> x0, other arithmetic: 0.71 us -> none  [doubling_gather(): jnp.where(lower, jnp.concatenate([held, other], 0), jnp.concatenate([othe...]
    unnamed x10, local copies, waits for them, and re-layouts: 0.33 us -> 0.98 us
  transfers between devices with their start and end apart: 7 -> 5, of which waited for: 5 -> 3; matrix products, arithmetic and copies ran while one was open for 4% -> 4% of each run, Pallas kernels for 0% -> 0%
where the time goes in v4:
time: 58.8 us; the launch traced here: 58.1 us
  starting transfers between devices  15.8 us (27%)
  local copies, waits for them, and re-layouts  12.5 us (21%)
  Pallas kernels  10.8 us (18%)
  waiting for transfers between devices  8.58 us (15%)
  blocking collectives  8.56 us (15%)
  other arithmetic  1.61 us (3%)
    all_gather x1, blocking collectives, distributed_solve(): gathered = lax.all_gather(reduced, axis)  8.56 us
    all_to_all x1, starting transfers between devices, distributed_solve(): gathered = lax.all_to_all(copies, axis, 0, 0)  6.96 us
    ppermute x2, starting transfers between devices, halos(): low = lax.ppermute(last, axis, forward)  6.3 us
    all_to_all x1, waiting for transfers between devices, distributed_solve(): gathered = lax.all_to_all(copies, axis, 0, 0)  5.8 us
    pallas_call x2, Pallas kernels, partition_call(): pl.pallas_call(partition_kernel, out_shape=(jax.ShapeDtypeStruct((3, n) +...  5.57 us
    pallas_call x2, Pallas kernels, reduced_call(): pl.pallas_call(reduced_kernel, out_shape=jax.ShapeDtypeStruct((count, 2)...  3.35 us
    ppermute x2, waiting for transfers between devices, halos(): high = lax.ppermute(first, axis, backward)  2.78 us
    ppermute x2, starting transfers between devices, halos(): high = lax.ppermute(first, axis, backward)  2.59 us
  transfers between devices with their start and end apart: 5, of which 3 were waited for; matrix products, arithmetic and copies ran while one was open for 4% of the time, Pallas kernels for 0%

profile of v4, /device:TPU:0, one launch (start us, length us, event | category | flops | bytes accessed | tf_op | source)
XLA Modules:
  0.0 58.1 jit_solution(11422009258088631378)
XLA Ops:
  0.0 1.2 %fusion.16 = (f32[16,32,1]{2,1,0:T(8,128)S(1)}, f32[16,32,1]{2,1,0:T(8,128)S(1)}) fusion(f32[16,32,128]{2,1,0:T(8,128)} %param.2), kind=kLoop, calls=%fused_computation.31 | loop fusion | bytes 8192 | tf_op jit(solution)/shard_map/slice | solution.py:16
  1.3 4.8 %collective-permute-start.2 = (f32[16,32]{1,0:T(8,128)S(1)}, f32[16,32]{1,0:T(8,128)S(1)}, u32[]{:S(2)}, u32[]{:S(2)}) collective-permute-start(f32[16,32]{1,0:T(8,128)S(1)} %bitcast.70), channel_id=1, source_target_pairs={{0,1},{1,2},{2,3},{3,4},{4,5},{5,6},{6,7},{8,9},{9,10},{10,11},{11... | collective-permute-start | bytes 6152 | tf_op jit(solution)/shard_map/ppermute | solution.py:18
  6.3 1.3 %collective-permute-start.3 = (f32[16,32]{1,0:T(8,128)S(1)}, f32[16,32]{1,0:T(8,128)S(1)}, u32[]{:S(2)}, u32[]{:S(2)}) collective-permute-start(f32[16,32]{1,0:T(8,128)S(1)} %bitcast.72), channel_id=1, source_target_pairs={{1,0},{2,1},{3,2},{4,3},{5,4},{6,5},{7,6},{9,8},{10,9},{11,10},{12... | collective-permute-start | bytes 6152 | tf_op jit(solution)/shard_map/ppermute | solution.py:19
  7.7 1.5 %collective-permute-start = (f32[16,128]{1,0:T(8,128)S(1)}, f32[16,128]{1,0:T(8,128)S(1)}, u32[]{:S(2)}, u32[]{:S(2)}) collective-permute-start(f32[16,128]{1,0:T(8,128)S(1)} %bitcast.75), channel_id=1, source_target_pairs={{0,8},{8,16},{16,24},{1,9},{9,17},{17,25},{2,10},{10,18},{18,26},{... | collective-permute-start | bytes 24584 | tf_op jit(solution)/shard_map/ppermute | solution.py:18
  9.1 1.3 %collective-permute-start.1 = (f32[16,128]{1,0:T(8,128)S(1)}, f32[16,128]{1,0:T(8,128)S(1)}, u32[]{:S(2)}, u32[]{:S(2)}) collective-permute-start(f32[16,128]{1,0:T(8,128)S(1)} %bitcast.74), channel_id=1, source_target_pairs={{8,0},{16,8},{24,16},{9,1},{17,9},{25,17},{10,2},{18,10},{26,18},{... | collective-permute-start | bytes 24584 | tf_op jit(solution)/shard_map/ppermute | solution.py:19
  10.8 1.0 %collective-permute-done.3 = f32[16,32]{1,0:T(8,128)S(1)} collective-permute-done((f32[16,32]{1,0:T(8,128)S(1)}, f32[16,32]{1,0:T(8,128)S(1)}, u32[]{:S(2)}, u32[]{:S(2)}) %collective-permute-start.3) | collective-permute-done | bytes 2080 | tf_op jit(solution)/shard_map/ppermute | solution.py:19
  12.1 1.7 %collective-permute-done.1 = f32[16,128]{1,0:T(8,128)S(1)} collective-permute-done((f32[16,128]{1,0:T(8,128)S(1)}, f32[16,128]{1,0:T(8,128)S(1)}, u32[]{:S(2)}, u32[]{:S(2)}) %collective-permute-start.1) | collective-permute-done | bytes 8224 | tf_op jit(solution)/shard_map/ppermute | solution.py:19
  14.1 0.9 %copy.43.h_ref = f32[32,16,128]{2,1,0:T(8,128)} copy(f32[32,16,128]{2,0,1:T(8,128)S(1)} %get-tuple-element.18) | data formatting | bytes 524288 | tf_op jit(solution)/shard_map/transpose | solution.py:210
  15.0 0.9 %copy.44.d_ref = f32[32,16,128]{2,1,0:T(8,128)} copy(f32[32,16,128]{2,0,1:T(8,128)S(1)} %get-tuple-element.13) | data formatting | bytes 524288 | tf_op jit(solution)/shard_map/transpose | solution.py:207
  15.9 2.3 %shard_map.28 = (f32[3,32,16,128]{3,2,1,0:T(8,128)}, f32[4,2,16,128]{3,2,1,0:T(8,128)}) custom-call(f32[32,16,128]{2,1,0:T(8,128)} %copy.43.h_ref, f32[32,16,128]{2,1,0:T(8,128)} %copy.44.d_ref), custom_call_target="tpu_custom_call" | custom-call | tf_op jit(solution)/shard_map/pallas_call | solution.py:72
  18.1 8.6 %all-gather = f32[16,2,16,128]{3,2,1,0:T(8,128)} all-gather(f32[4,2,16,128]{3,2,1,0:T(8,128)} %get-tuple-element.9), channel_id=2, replica_groups=mesh['gx'=4,'gy'=8] {'gx'}, dimensions={0}, use_global_device_ids=true | all-gather | bytes 327680 | tf_op jit(solution)/shard_map/all_gather | solution.py:174
  26.7 1.7 %shard_map.29 = f32[4,2,16,128]{3,2,1,0:T(8,128)} custom-call(f32[4,4,2,16,128]{4,3,2,1,0:T(8,128)} %bitcast.60), custom_call_target="tpu_custom_call" | custom-call | tf_op jit(solution)/shard_map/pallas_call | solution.py:115
  28.4 1.4 %copy.45 = f32[3,32,16,128]{3,1,2,0:T(8,128)S(1)} copy(f32[3,32,16,128]{3,2,1,0:T(8,128)} %get-tuple-element.10) | data formatting | bytes 1572864 | tf_op jit(solution)/shard_map/pallas_call | solution.py:72
  29.7 0.7 %constant_dynamic-slice_fusion.1 = (f32[1,1,16,128]{3,2,1,0:T(8,128)S(1)}, f32[1,1,16,128]{3,2,1,0:T(8,128)S(1)}) fusion(f32[4,2,16,128]{3,2,1,0:T(8,128)} %shard_map.29, s32[]{:T(128)S(6)} %select_n.8, s32[]{:T(128)S(6)} %add.54), kind=kLoop, calls=%fused_computation.26 | loop fusion | bytes 32776 | tf_op jit(solution)/shard_map/unstack | solution.py:176
  30.7 0.9 %copy.50.d_ref = f32[128,4,128]{2,1,0:T(4,128)} copy(f32[128,4,128]{0,2,1:T(8,128)S(1)} %bitcast.59) | data formatting | bytes 524288 | tf_op jit(solution)/shard_map/reshape | solution.py:215
  31.5 0.8 %copy.49.h_ref = f32[128,4,128]{2,1,0:T(4,128)} copy(f32[128,4,128]{0,2,1:T(8,128)S(1)} %bitcast.58) | data formatting | bytes 524288 | tf_op jit(solution)/shard_map/reshape | solution.py:216
  32.4 3.3 %shard_map.30 = (f32[3,128,4,128]{3,2,1,0:T(4,128)}, f32[4,2,4,128]{3,2,1,0:T(4,128)}) custom-call(f32[128,4,128]{2,1,0:T(4,128)} %copy.49.h_ref, f32[128,4,128]{2,1,0:T(4,128)} %copy.50.d_ref), custom_call_target="tpu_custom_call" | custom-call | tf_op jit(solution)/shard_map/pallas_call | solution.py:72
  35.7 1.4 %broadcast_in_dim.22 = f32[8,4,2,4,128]{4,3,2,1,0:T(4,128)} broadcast(f32[4,2,4,128]{3,2,1,0:T(4,128)} %get-tuple-element.11), dimensions={1,2,3,4} | broadcast | bytes 147456 | tf_op jit(solution)/shard_map/broadcast_in_dim | solution.py:171
  37.1 7.0 %all-to-all-start = ((f32[8,4,2,4,128]{4,3,2,1,0:T(4,128)}), f32[8,4,2,4,128]{4,3,2,1,0:T(4,128)S(1)}, u32[]{:S(2)}, u32[]{:S(2)}) async-start(f32[8,4,2,4,128]{4,3,2,1,0:T(4,128)} %broadcast_in_dim.22), calls=%async_computation | async-start | bytes 262144 | tf_op jit(solution)/shard_map/all_to_all | solution.py:172
  44.0 1.2 %fusion.15 = (f32[1,126,4,128]{3,2,1,0:T(4,128)S(1)}, f32[1,126,4,128]{3,2,1,0:T(4,128)S(1)}, f32[1,126,4,128]{3,2,1,0:T(4,128)S(1)}) fusion(f32[3,128,4,128]{3,2,1,0:T(4,128)} %get-tuple-element.12), kind=kLoop, calls=%fused_computation.30 | loop fusion | bytes 1548288 | tf_op jit(solution)/shard_map/slice | solution.py:177
  45.7 5.8 %all-to-all-done.g_ref = f32[8,4,2,4,128]{4,3,2,1,0:T(4,128)S(1)} async-done(((f32[8,4,2,4,128]{4,3,2,1,0:T(4,128)}), f32[8,4,2,4,128]{4,3,2,1,0:T(4,128)S(1)}, u32[]{:S(2)}, u32[]{:S(2)}) %all-to-all-start) | async-done | bytes 131104 | tf_op jit(solution)/shard_map/all_to_all | solution.py:172
  52.2 1.7 %shard_map.31 = f32[8,2,4,128]{3,2,1,0:T(4,128)} custom-call(f32[8,4,2,4,128]{4,3,2,1,0:T(4,128)} %copy-done.3), custom_call_target="tpu_custom_call" | custom-call | tf_op jit(solution)/shard_map/pallas_call | solution.py:115
  55.3 0.9 %fusion.12.d_ref = f32[16,32,128]{2,1,0:T(8,128)} fusion(f32[1,16,32]{0,2,1:T(8,128)S(1)} %concatenate.32, f32[126,16,32]{0,2,1:T(8,128)S(1)} %multiply_add_fusion, f32[1,16,32]{0,2,1:T(8,128)S(1)} %concatenate.31, f32[16,32,128]{2,1,0:T(8,128)S(1)} %copy-done, f32[16,32,128]{2,1,0:T(8,128)S(1)} %copy-done.2), kind=kLoop, calls=%fused_computation.21 | loop fusion | flops 589824 | bytes 1048576 | tf_op jit(solution)/shard_map/sub | solution.py:219
  56.2 1.9 %shard_map.32 = f32[16,32,128]{2,1,0:T(8,128)} custom-call(f32[16,32,128]{2,1,0:T(8,128)} %copy-done.1, f32[16,32,128]{2,1,0:T(8,128)} %fusion.12.d_ref), custom_call_target="tpu_custom_call" | custom-call | tf_op jit(solution)/shard_map/pallas_call | solution.py:144
  (29 shorter events, 3.9 us)
Async XLA Ops:
  1.2 6.5 %copy-start = (f32[16,32,128]{2,1,0:T(8,128)S(1)}, f32[16,32,128]{2,1,0:T(8,128)}, u32[]{:S(2)}) copy-start(f32[16,32,128]{2,1,0:T(8,128)} %param.2) | copy-start | bytes 786436
  1.3 9.3 %collective-permute-start.2 = (f32[16,32]{1,0:T(8,128)S(1)}, f32[16,32]{1,0:T(8,128)S(1)}, u32[]{:S(2)}, u32[]{:S(2)}) collective-permute-start(f32[16,32]{1,0:T(8,128)S(1)} %bitcast.70), channel_id=1, source_target_pairs={{0,1},{1,2},{2,3},{3,4},{4,5},{5,6},{6,7},{8,9},{9,10},{10,11},{11... | collective-permute-start | bytes 6152 | tf_op jit(solution)/shard_map/ppermute | solution.py:18
  6.3 5.5 %collective-permute-start.3 = (f32[16,32]{1,0:T(8,128)S(1)}, f32[16,32]{1,0:T(8,128)S(1)}, u32[]{:S(2)}, u32[]{:S(2)}) collective-permute-start(f32[16,32]{1,0:T(8,128)S(1)} %bitcast.72), channel_id=1, source_target_pairs={{1,0},{2,1},{3,2},{4,3},{5,4},{6,5},{7,6},{9,8},{10,9},{11,10},{12... | collective-permute-start | bytes 6152 | tf_op jit(solution)/shard_map/ppermute | solution.py:19
  7.7 4.4 %collective-permute-start = (f32[16,128]{1,0:T(8,128)S(1)}, f32[16,128]{1,0:T(8,128)S(1)}, u32[]{:S(2)}, u32[]{:S(2)}) collective-permute-start(f32[16,128]{1,0:T(8,128)S(1)} %bitcast.75), channel_id=1, source_target_pairs={{0,8},{8,16},{16,24},{1,9},{9,17},{17,25},{2,10},{10,18},{18,26},{... | collective-permute-start | bytes 24584 | tf_op jit(solution)/shard_map/ppermute | solution.py:18
  9.1 4.7 %collective-permute-start.1 = (f32[16,128]{1,0:T(8,128)S(1)}, f32[16,128]{1,0:T(8,128)S(1)}, u32[]{:S(2)}, u32[]{:S(2)}) collective-permute-start(f32[16,128]{1,0:T(8,128)S(1)} %bitcast.74), channel_id=1, source_target_pairs={{8,0},{16,8},{24,16},{9,1},{17,9},{25,17},{10,2},{18,10},{26,18},{... | collective-permute-start | bytes 24584 | tf_op jit(solution)/shard_map/ppermute | solution.py:19
  10.6 3.1 %copy-start.2 = (f32[16,32,128]{2,1,0:T(8,128)S(1)}, f32[16,32,128]{2,1,0:T(8,128)}, u32[]{:S(2)}) copy-start(f32[16,32,128]{2,1,0:T(8,128)} %param.3) | copy-start | bytes 786436
  14.1 17.4 %copy-start.1 = (f32[16,32,128]{2,1,0:T(8,128)}, f32[16,32,128]{2,1,0:T(8,128)S(1)}, u32[]{:S(2)}) copy-start(f32[16,32,128]{2,1,0:T(8,128)S(1)} %get-tuple-element.19.h_ref) | copy-start | bytes 786436
  37.1 14.4 %all-to-all-start = ((f32[8,4,2,4,128]{4,3,2,1,0:T(4,128)}), f32[8,4,2,4,128]{4,3,2,1,0:T(4,128)S(1)}, u32[]{:S(2)}, u32[]{:S(2)}) async-start(f32[8,4,2,4,128]{4,3,2,1,0:T(4,128)} %broadcast_in_dim.22), calls=%async_computation | async-start | bytes 262144 | tf_op jit(solution)/shard_map/all_to_all | solution.py:172
  51.5 0.7 %copy-start.3 = (f32[8,4,2,4,128]{4,3,2,1,0:T(4,128)}, f32[8,4,2,4,128]{4,3,2,1,0:T(4,128)S(1)}, u32[]{:S(2)}) copy-start(f32[8,4,2,4,128]{4,3,2,1,0:T(4,128)S(1)} %all-to-all-done.g_ref) | copy-start | bytes 393220

commit v5 on v3

--- a/solution.py
+++ b/solution.py
@@ -20,63 +20,91 @@
     return jnp.expand_dims(low, dim), jnp.expand_dims(high, dim)
 
 
-def partition_kernel(h_ref, d_ref, out_ref, red_ref, ratio_ref):
+def coefficient_kernel(h_ref, denom_ref, ratio_ref, resp_ref, red_ref):
     n = h_ref.shape[0]
     ratio = jnp.zeros(h_ref.shape[1:], jnp.float32)
-    vb = jnp.zeros_like(ratio)
     vf = jnp.zeros_like(ratio)
     for i in range(1, n - 1):
         hi = h_ref[i]
         denom = 1.0 + 2.0 * hi + hi * ratio
         ratio = -hi / denom
         if i == 1:
-            vb = d_ref[i] / denom
             vf = hi / denom
         else:
-            vb = (d_ref[i] + hi * vb) / denom
             vf = (hi * vf) / denom
         if i == n - 2:
             vl = hi / denom
+        denom_ref[i] = denom
         ratio_ref[i] = ratio
-        out_ref[0, i] = vb
-        out_ref[1, i] = vf
-    b, f, l = vb, vf, vl
-    out_ref[2, n - 2] = l
+        resp_ref[0, i] = vf
+    f, l = vf, vl
+    resp_ref[1, n - 2] = l
     for i in range(n - 3, 0, -1):
         r = ratio_ref[i]
-        b = out_ref[0, i] - r * b
-        f = out_ref[1, i] - r * f
+        f = resp_ref[0, i] - r * f
         l = -r * l
-        out_ref[0, i] = b
-        out_ref[1, i] = f
-        out_ref[2, i] = l
+        resp_ref[0, i] = f
+        resp_ref[1, i] = l
     zero = jnp.zeros_like(ratio)
-    for k in range(3):
-        out_ref[k, 0] = zero
-        out_ref[k, n - 1] = zero
+    for k in range(2):
+        resp_ref[k, 0] = zero
+        resp_ref[k, n - 1] = zero
     rh = h_ref[0]
     rt = h_ref[n - 1]
     red_ref[0, 0] = -rh
-    red_ref[0, 1] = -rt * out_ref[1, n - 2]
-    red_ref[1, 0] = 1.0 + 2.0 * rh - rh * out_ref[1, 1]
-    red_ref[1, 1] = 1.0 + 2.0 * rt - rt * out_ref[2, n - 2]
-    red_ref[2, 0] = -rh * out_ref[2, 1]
+    red_ref[0, 1] = -rt * resp_ref[0, n - 2]
+    red_ref[1, 0] = 1.0 + 2.0 * rh - rh * resp_ref[0, 1]
+    red_ref[1, 1] = 1.0 + 2.0 * rt - rt * resp_ref[1, n - 2]
+    red_ref[2, 0] = -rh * resp_ref[1, 1]
     red_ref[2, 1] = -rt
-    red_ref[3, 0] = d_ref[0] + rh * out_ref[0, 1]
-    red_ref[3, 1] = d_ref[n - 1] + rt * out_ref[0, n - 2]
-
-
-def partition_call(h_lines, d_lines):
+
+
+def coefficient_call(h_lines):
     n = h_lines.shape[0]
     rest = h_lines.shape[1:]
     return pl.pallas_call(
-        partition_kernel,
+        coefficient_kernel,
         out_shape=(
-            jax.ShapeDtypeStruct((3, n) + rest, jnp.float32),
+            jax.ShapeDtypeStruct((n,) + rest, jnp.float32),
+            jax.ShapeDtypeStruct((n,) + rest, jnp.float32),
+            jax.ShapeDtypeStruct((2, n) + rest, jnp.float32),
+            jax.ShapeDtypeStruct((3, 2) + rest, jnp.float32),
+        ),
+    )(h_lines)
+
+
+def side_kernel(h_ref, d_ref, denom_ref, ratio_ref, coef_ref, base_ref, red_ref):
+    n = h_ref.shape[0]
+    vb = d_ref[1] / denom_ref[1]
+    base_ref[1] = vb
+    for i in range(2, n - 1):
+        vb = (d_ref[i] + h_ref[i] * vb) / denom_ref[i]
+        base_ref[i] = vb
+    b = vb
+    for i in range(n - 3, 0, -1):
+        b = base_ref[i] - ratio_ref[i] * b
+        base_ref[i] = b
+    zero = jnp.zeros_like(b)
+    base_ref[0] = zero
+    base_ref[n - 1] = zero
+    for k in range(3):
+        for q in range(2):
+            red_ref[k, q] = coef_ref[k, q]
+    red_ref[3, 0] = d_ref[0] + h_ref[0] * base_ref[1]
+    red_ref[3, 1] = d_ref[n - 1] + h_ref[n - 1] * base_ref[n - 2]
+
+
+def side_call(h_lines, d_lines, coefficients):
+    denom, ratio, _, coef = coefficients
+    n = h_lines.shape[0]
+    rest = h_lines.shape[1:]
+    return pl.pallas_call(
+        side_kernel,
+        out_shape=(
+            jax.ShapeDtypeStruct((n,) + rest, jnp.float32),
             jax.ShapeDtypeStruct((4, 2) + rest, jnp.float32),
         ),
-        scratch_shapes=[pltpu_vmem((n,) + rest)],
-    )(h_lines, d_lines)
+    )(h_lines, d_lines, denom, ratio, coef)
 
 
 def pltpu_vmem(shape):
@@ -119,20 +147,26 @@
     )(gathered)
 
 
-def sweep_kernel(h_ref, d_ref, out_ref, ratio_ref):
+def sweep_coefficient_kernel(h_ref, denom_ref, ratio_ref):
     n = h_ref.shape[0]
     ratio = None
-    value = None
     for i in range(n):
         hi = h_ref[i]
         if i == 0:
             denom = 1.0 + 2.0 * hi
-            value = d_ref[i] / denom
         else:
             denom = 1.0 + 2.0 * hi + hi * ratio
-            value = (d_ref[i] + hi * value) / denom
         ratio = -hi / denom
+        denom_ref[i] = denom
         ratio_ref[i] = ratio
+
+
+def sweep_side_kernel(h_ref, d_ref, denom_ref, ratio_ref, out_ref):
+    n = h_ref.shape[0]
+    value = d_ref[0] / denom_ref[0]
+    out_ref[0] = value
+    for i in range(1, n):
+        value = (d_ref[i] + h_ref[i] * value) / denom_ref[i]
         out_ref[i] = value
     x = value
     for i in range(n - 2, -1, -1):
@@ -140,12 +174,16 @@
         out_ref[i] = x
 
 
-def sweep_call(h_lines, d_lines):
-    return pl.pallas_call(
-        sweep_kernel,
+def sweep_coefficient_call(h_lines):
+    shape = jax.ShapeDtypeStruct(h_lines.shape, jnp.float32)
+    return pl.pallas_call(sweep_coefficient_kernel, out_shape=(shape, shape))(h_lines)
+
+
+def sweep_side_call(h_lines, d_lines, coefficients):
+    return pl.pallas_call(
+        sweep_side_kernel,
         out_shape=jax.ShapeDtypeStruct(h_lines.shape, jnp.float32),
-        scratch_shapes=[pltpu_vmem(h_lines.shape)],
-    )(h_lines, d_lines)
+    )(h_lines, d_lines, *coefficients)
 
 
 def doubling_gather(part, axis):
@@ -165,15 +203,16 @@
     return held
 
 
-def distributed_solve(h_lines, d_lines, axis, doubling):
-    responses, reduced = partition_call(h_lines, d_lines)
+def distributed_solve(h_lines, d_lines, coefficients, axis, doubling):
+    base, reduced = side_call(h_lines, d_lines, coefficients)
+    responses = coefficients[2]
     if doubling:
         gathered = doubling_gather(reduced, axis)
     else:
         gathered = lax.all_gather(reduced, axis)
     ends = reduced_call(gathered)
     head, tail = lax.dynamic_index_in_dim(ends, lax.axis_index(axis), 0, keepdims=False)
-    interior = responses[0, 1:-1] + responses[1, 1:-1] * head + responses[2, 1:-1] * tail
+    interior = base[1:-1] + responses[0, 1:-1] * head + responses[1, 1:-1] * tail
     return jnp.concatenate([head[None], interior, tail[None]], 0)
 
 
@@ -183,6 +222,23 @@
     plane_count, row_count, column_count = initial_heat_values.shape
     x_low, x_high = halos(initial_heat_values, "gx", 1)
     y_low, y_high = halos(initial_heat_values, "gy", 2)
+    lanes = 128
+    groups = plane_count * row_count // lanes
+    first_rate = jnp.moveaxis(half_rate, 1, 0)
+    rate_lines = jnp.transpose(half_rate, (2, 0, 1)).reshape(column_count, groups, lanes)
+    first_coefficients = coefficient_call(first_rate)
+    column_coefficients = coefficient_call(rate_lines)
+    plane_coefficients = sweep_coefficient_call(half_rate)
+    (x_low, x_high, y_low, y_high), first_coefficients, column_coefficients, plane_coefficients = (
+        lax.optimization_barrier(
+            (
+                (x_low, x_high, y_low, y_high),
+                first_coefficients,
+                column_coefficients,
+                plane_coefficients,
+            )
+        )
+    )
     horizontal_implicit_solve = conductivity_map * (
         jnp.concatenate([x_low, initial_heat_values[:, :-1]], 1)
         - 2.0 * initial_heat_values
@@ -206,17 +262,15 @@
     first_side = jnp.moveaxis(
         forward_euler_increment - implicit_weight * horizontal_implicit_solve, 1, 0
     )
-    first_rate = jnp.moveaxis(half_rate, 1, 0)
-    first_pass = jnp.moveaxis(distributed_solve(first_rate, first_side, "gx", False), 0, 1)
+    first_pass = jnp.moveaxis(
+        distributed_solve(first_rate, first_side, first_coefficients, "gx", False), 0, 1
+    )
     second_side = first_pass - implicit_weight * vertical_implicit_solve
-    lanes = 128
-    groups = plane_count * row_count // lanes
     side_lines = jnp.transpose(second_side, (2, 0, 1)).reshape(column_count, groups, lanes)
-    rate_lines = jnp.transpose(half_rate, (2, 0, 1)).reshape(column_count, groups, lanes)
-    column_lines = distributed_solve(rate_lines, side_lines, "gy", True)
+    column_lines = distributed_solve(rate_lines, side_lines, column_coefficients, "gy", True)
     second = jnp.transpose(column_lines.reshape(column_count, plane_count, row_count), (1, 2, 0))
     plane_side = second - implicit_weight * depth_implicit_solve
-    return sweep_call(half_rate, plane_side)
+    return sweep_side_call(half_rate, plane_side, plane_coefficients)
 
 
 def solution(mesh):

time: 57.7 us -> 64.1 us (1.11)
  Pallas kernels: 10.8 us -> 17.3 us
  blocking collectives: 8.56 us -> 10.8 us
  local copies, waits for them, and re-layouts: 10.5 us -> 9.07 us
  starting transfers between devices: 17.6 us -> 16.2 us
  other arithmetic: 2.33 us -> 2.99 us
    pallas_call x3 -> x6, Pallas kernels: 7.47 us -> 13.9 us  [the longest x2 5.38 us: coefficient_call(): pl.pallas_call(coefficient_kernel, out_shape=(jax.ShapeDtypeStruct((n,) +...]
    ppermute x2, waiting for transfers between devices: 2.77 us -> 0.01 us  [halos(): high = lax.ppermute(first, axis, backward)]
    ppermute x3, waiting for transfers between devices: 4.44 us -> 6.91 us  [doubling_gather(): other = lax.ppermute(held, axis, [(i, i ^ step) for i in range(count)])]
    all_gather x1, blocking collectives: 8.56 us -> 10.8 us  [distributed_solve(): gathered = lax.all_gather(reduced, axis)]
    ppermute x3, starting transfers between devices: 8.75 us -> 6.69 us  [doubling_gather(): other = lax.ppermute(held, axis, [(i, i ^ step) for i in range(count)])]
    slice x6 -> x2, local copies, waits for them, and re-layouts: 2.84 us -> 1.17 us  [halos(): first = lax.index_in_dim(block, 0, dim, keepdims=False)]
    unnamed x10 -> x18, local copies, waits for them, and re-layouts: 0.33 us -> 1.75 us
    pallas_call x1, local copies, waits for them, and re-layouts: 1.39 us -> 0.09 us  [side_call(): pl.pallas_call(side_kernel, out_shape=(jax.ShapeDtypeStruct((n,) + rest,...]
  transfers between devices with their start and end apart: 7 -> 7, of which waited for: 5 -> 3; matrix products, arithmetic and copies ran while one was open for 4% -> 4% of each run, Pallas kernels for 0% -> 12%
where the time goes in v5:
time: 64.1 us; the launch traced here: 63.5 us
  Pallas kernels  17.3 us (27%)
  starting transfers between devices  16.2 us (25%)
  blocking collectives  10.8 us (17%)
  local copies, waits for them, and re-layouts  9.07 us (14%)
  waiting for transfers between devices  6.92 us (11%)
  other arithmetic  2.99 us (5%)
    all_gather x1, blocking collectives, distributed_solve(): gathered = lax.all_gather(reduced, axis)  10.8 us
    ppermute x2, starting transfers between devices, halos(): low = lax.ppermute(last, axis, forward)  6.93 us
    ppermute x3, waiting for transfers between devices, doubling_gather(): other = lax.ppermute(held, axis, [(i, i ^ step) for i in range(count)])  6.91 us
    ppermute x3, starting transfers between devices, doubling_gather(): other = lax.ppermute(held, axis, [(i, i ^ step) for i in range(count)])  6.69 us
    pallas_call x2, Pallas kernels, coefficient_call(): pl.pallas_call(coefficient_kernel, out_shape=(jax.ShapeDtypeStruct((n,) +...  5.38 us
    pallas_call x2, Pallas kernels, side_call(): pl.pallas_call(side_kernel, out_shape=(jax.ShapeDtypeStruct((n,) + rest,...  4.63 us
    pallas_call x2, Pallas kernels, reduced_call(): pl.pallas_call(reduced_kernel, out_shape=jax.ShapeDtypeStruct((count, 2)...  3.32 us
    ppermute x2, starting transfers between devices, halos(): high = lax.ppermute(first, axis, backward)  2.59 us
  transfers between devices with their start and end apart: 7, of which 3 were waited for; matrix products, arithmetic and copies ran while one was open for 4% of the time, Pallas kernels for 12%

profile of v5, /device:TPU:0, one launch (start us, length us, event | category | flops | bytes accessed | tf_op | source)
XLA Modules:
  0.0 63.5 jit_solution(17980828515119842044)
XLA Ops:
  0.0 1.2 %fusion.19 = (f32[16,32,1]{2,1,0:T(8,128)S(1)}, f32[16,32,1]{2,1,0:T(8,128)S(1)}) fusion(f32[16,32,128]{2,1,0:T(8,128)} %param.2), kind=kLoop, calls=%fused_computation.37 | loop fusion | bytes 8192 | tf_op jit(solution)/shard_map/slice | solution.py:17
  1.3 1.3 %collective-permute-start.3 = (f32[16,32]{1,0:T(8,128)S(1)}, f32[16,32]{1,0:T(8,128)S(1)}, u32[]{:S(2)}, u32[]{:S(2)}) collective-permute-start(f32[16,32]{1,0:T(8,128)S(1)} %bitcast.81), channel_id=1, source_target_pairs={{1,0},{2,1},{3,2},{4,3},{5,4},{6,5},{7,6},{9,8},{10,9},{11,10},{12... | collective-permute-start | bytes 6152 | tf_op jit(solution)/shard_map/ppermute | solution.py:19
  2.8 5.5 %collective-permute-start.2 = (f32[16,32]{1,0:T(8,128)S(1)}, f32[16,32]{1,0:T(8,128)S(1)}, u32[]{:S(2)}, u32[]{:S(2)}) collective-permute-start(f32[16,32]{1,0:T(8,128)S(1)} %bitcast.82), channel_id=1, source_target_pairs={{0,1},{1,2},{2,3},{3,4},{4,5},{5,6},{6,7},{8,9},{9,10},{10,11},{11... | collective-permute-start | bytes 6152 | tf_op jit(solution)/shard_map/ppermute | solution.py:18
  8.3 1.5 %collective-permute-start = (f32[16,128]{1,0:T(8,128)S(1)}, f32[16,128]{1,0:T(8,128)S(1)}, u32[]{:S(2)}, u32[]{:S(2)}) collective-permute-start(f32[16,128]{1,0:T(8,128)S(1)} %bitcast.84), channel_id=1, source_target_pairs={{0,8},{8,16},{16,24},{1,9},{9,17},{17,25},{2,10},{10,18},{18,26},{... | collective-permute-start | bytes 24584 | tf_op jit(solution)/shard_map/ppermute | solution.py:18
  9.8 1.3 %collective-permute-start.1 = (f32[16,128]{1,0:T(8,128)S(1)}, f32[16,128]{1,0:T(8,128)S(1)}, u32[]{:S(2)}, u32[]{:S(2)}) collective-permute-start(f32[16,128]{1,0:T(8,128)S(1)} %bitcast.83), channel_id=1, source_target_pairs={{8,0},{16,8},{24,16},{9,1},{17,9},{25,17},{10,2},{18,10},{26,18},{... | collective-permute-start | bytes 24584 | tf_op jit(solution)/shard_map/ppermute | solution.py:19
  11.3 0.9 %copy-done.2 = f32[16,32,128]{2,1,0:T(8,128)S(1)} copy-done((f32[16,32,128]{2,1,0:T(8,128)S(1)}, f32[16,32,128]{2,1,0:T(8,128)}, u32[]{:S(2)}) %copy-start.2) | copy-done | bytes 262168
  12.9 2.0 %shard_map.30 = (f32[16,32,128]{2,1,0:T(8,128)}, f32[16,32,128]{2,1,0:T(8,128)}) custom-call(f32[16,32,128]{2,1,0:T(8,128)} %get-tuple-element.72.h_ref), custom_call_target="tpu_custom_call" | custom-call | tf_op jit(solution)/shard_map/pallas_call | solution.py:179
  15.7 3.2 %shard_map.29 = (f32[128,4,128]{2,1,0:T(4,128)}, f32[128,4,128]{2,1,0:T(4,128)}, f32[2,128,4,128]{3,2,1,0:T(4,128)}, f32[3,2,4,128]{3,2,1,0:T(4,128)}) custom-call(f32[128,4,128]{2,1,0:T(4,128)} %copy.51.h_ref), custom_call_target="tpu_custom_call" | custom-call | tf_op jit(solution)/shard_map/pallas_call | solution.py:65
  18.9 0.9 %copy.45.h_ref = f32[32,16,128]{2,1,0:T(8,128)} copy(f32[32,16,128]{2,0,1:T(8,128)S(1)} %get-tuple-element.71) | data formatting | bytes 524288 | tf_op jit(solution)/shard_map/transpose | solution.py:227
  19.7 2.2 %shard_map.28 = (f32[32,16,128]{2,1,0:T(8,128)}, f32[32,16,128]{2,1,0:T(8,128)}, f32[2,32,16,128]{3,2,1,0:T(8,128)}, f32[3,2,16,128]{3,2,1,0:T(8,128)}) custom-call(f32[32,16,128]{2,1,0:T(8,128)} %copy.45.h_ref), custom_call_target="tpu_custom_call" | custom-call | tf_op jit(solution)/shard_map/pallas_call | solution.py:65
  22.7 0.9 %copy.46.d_ref = f32[32,16,128]{2,1,0:T(8,128)} copy(f32[32,16,128]{2,0,1:T(8,128)S(1)} %get-tuple-element.61) | data formatting | bytes 524288 | tf_op jit(solution)/shard_map/transpose | solution.py:262
  23.5 2.1 %shard_map.31 = (f32[32,16,128]{2,1,0:T(8,128)}, f32[4,2,16,128]{3,2,1,0:T(8,128)}) custom-call(f32[32,16,128]{2,1,0:T(8,128)} %copy.45.h_ref, f32[32,16,128]{2,1,0:T(8,128)} %copy.46.d_ref, f32[32,16,128]{2,1,0:T(8,128)} %get-tuple-element.47.denom_ref, f32[32,16,128]{2,1,0:T(8,128)} %get-tuple-element.48.ratio_ref, ...), custom_call_target="tpu_custom_call" | custom-call | tf_op jit(solution)/shard_map/pallas_call | solution.py:101
  25.6 10.8 %all-gather = f32[16,2,16,128]{3,2,1,0:T(8,128)} all-gather(f32[4,2,16,128]{3,2,1,0:T(8,128)} %get-tuple-element.50), channel_id=2, replica_groups=mesh['gx'=4,'gy'=8] {'gx'}, dimensions={0}, use_global_device_ids=true | all-gather | bytes 327680 | tf_op jit(solution)/shard_map/all_gather | solution.py:212
  36.4 1.6 %shard_map.32 = f32[4,2,16,128]{3,2,1,0:T(8,128)} custom-call(f32[4,4,2,16,128]{4,3,2,1,0:T(8,128)} %bitcast.67), custom_call_target="tpu_custom_call" | custom-call | tf_op jit(solution)/shard_map/pallas_call | solution.py:143
  40.1 2.6 %shard_map.33 = (f32[128,4,128]{2,1,0:T(4,128)}, f32[4,2,4,128]{3,2,1,0:T(4,128)}) custom-call(f32[128,4,128]{2,1,0:T(4,128)} %copy.51.h_ref, f32[128,4,128]{2,1,0:T(4,128)} %copy.52.d_ref, f32[128,4,128]{2,1,0:T(4,128)} %get-tuple-element.53.denom_ref, f32[128,4,128]{2,1,0:T(4,128)} %get-tuple-element.54.ratio_ref, f32[3,2,4,128]{3,2,1,0:T(4,128)} %get-tuple-element.55.coef_ref), custom_call_target="tpu_custom_call" | custom-call | tf_op jit(solution)/shard_map/pallas_call | solution.py:101
  42.7 2.4 %collective-permute-start.4 = (f32[1,4,2,4,128]{4,3,2,1,0:T(4,128)}, f32[1,4,2,4,128]{4,3,2,1,0:T(4,128)S(1)}, u32[]{:S(2)}, u32[]{:S(2)}) collective-permute-start(f32[1,4,2,4,128]{4,3,2,1,0:T(4,128)} %bitcast.75), channel_id=1, source_target_pairs={{0,1},{1,0},{2,3},{3,2},{4,5},{5,4},{6,7},{7,6},{8,9},{9,8},{10,11... | collective-permute-start | bytes 49160 | tf_op jit(solution)/shard_map/ppermute | solution.py:197
  45.1 2.0 %collective-permute-done.4 = f32[1,4,2,4,128]{4,3,2,1,0:T(4,128)S(1)} collective-permute-done((f32[1,4,2,4,128]{4,3,2,1,0:T(4,128)}, f32[1,4,2,4,128]{4,3,2,1,0:T(4,128)S(1)}, u32[]{:S(2)}, u32[]{:S(2)}) %collective-permute-start.4) | collective-permute-done | bytes 16416 | tf_op jit(solution)/shard_map/ppermute | solution.py:197
  47.1 1.6 %collective-permute-start.5 = (f32[2,4,2,4,128]{4,3,2,1,0:T(4,128)S(1)}, f32[2,4,2,4,128]{4,3,2,1,0:T(4,128)S(1)}, u32[]{:S(2)}, u32[]{:S(2)}) collective-permute-start(f32[2,4,2,4,128]{4,3,2,1,0:T(4,128)S(1)} %maximum_select_fusion.2), channel_id=1, source_target_pairs={{0,2},{1,3},{2,0},{3,1},{4,6},{5,7},{6,4},{7,5},{8,10},{9,11},{10,... | collective-permute-start | bytes 98312 | tf_op jit(solution)/shard_map/ppermute | solution.py:197
  48.7 2.3 %collective-permute-done.5 = f32[2,4,2,4,128]{4,3,2,1,0:T(4,128)S(1)} collective-permute-done((f32[2,4,2,4,128]{4,3,2,1,0:T(4,128)S(1)}, f32[2,4,2,4,128]{4,3,2,1,0:T(4,128)S(1)}, u32[]{:S(2)}, u32[]{:S(2)}) %collective-permute-start.5) | collective-permute-done | bytes 32800 | tf_op jit(solution)/shard_map/ppermute | solution.py:197
  51.1 2.7 %collective-permute-start.6 = (f32[4,4,2,4,128]{4,3,2,1,0:T(4,128)S(1)}, f32[4,4,2,4,128]{4,3,2,1,0:T(4,128)S(1)}, u32[]{:S(2)}, u32[]{:S(2)}) collective-permute-start(f32[4,4,2,4,128]{4,3,2,1,0:T(4,128)S(1)} %maximum_select_fusion.1), channel_id=1, source_target_pairs={{0,4},{1,5},{2,6},{3,7},{4,0},{5,1},{6,2},{7,3},{8,12},{9,13},{10,... | collective-permute-start | bytes 196616 | tf_op jit(solution)/shard_map/ppermute | solution.py:197
  53.8 2.6 %collective-permute-done.6 = f32[4,4,2,4,128]{4,3,2,1,0:T(4,128)S(1)} collective-permute-done((f32[4,4,2,4,128]{4,3,2,1,0:T(4,128)S(1)}, f32[4,4,2,4,128]{4,3,2,1,0:T(4,128)S(1)}, u32[]{:S(2)}, u32[]{:S(2)}) %collective-permute-start.6) | collective-permute-done | bytes 65568 | tf_op jit(solution)/shard_map/ppermute | solution.py:197
  57.0 1.7 %shard_map.34 = f32[8,2,4,128]{3,2,1,0:T(4,128)} custom-call(f32[8,4,2,4,128]{4,3,2,1,0:T(4,128)} %maximum_select_fusion.g_ref), custom_call_target="tpu_custom_call" | custom-call | tf_op jit(solution)/shard_map/pallas_call | solution.py:143
  60.6 0.9 %fusion.12.d_ref = f32[16,32,128]{2,1,0:T(8,128)} fusion(f32[1,16,32]{0,2,1:T(8,128)S(1)} %concatenate.59, f32[126,16,32]{0,2,1:T(8,128)S(1)} %bitcast.68, f32[1,16,32]{0,2,1:T(8,128)S(1)} %concatenate.58, f32[16,32,128]{2,1,0:T(8,128)S(1)} %copy-done, f32[16,32,128]{2,1,0:T(8,128)S(1)} %copy-done.2), kind=kLoop, calls=%fused_computation.20 | loop fusion | flops 589824 | bytes 1048576 | tf_op jit(solution)/shard_map/sub | solution.py:272
  61.5 2.0 %shard_map.35 = f32[16,32,128]{2,1,0:T(8,128)} custom-call(f32[16,32,128]{2,1,0:T(8,128)} %get-tuple-element.72.h_ref, f32[16,32,128]{2,1,0:T(8,128)} %fusion.12.d_ref, f32[16,32,128]{2,1,0:T(8,128)} %get-tuple-element.59.denom_ref, f32[16,32,128]{2,1,0:T(8,128)} %get-tuple-element.60.ratio_ref), custom_call_target="tpu_custom_call" | custom-call | tf_op jit(solution)/shard_map/pallas_call | solution.py:183
  (43 shorter events, 7.4 us)
Async XLA Ops:
  1.2 7.1 %copy-start = (f32[16,32,128]{2,1,0:T(8,128)S(1)}, f32[16,32,128]{2,1,0:T(8,128)}, u32[]{:S(2)}) copy-start(f32[16,32,128]{2,1,0:T(8,128)} %param.2) | copy-start | bytes 786436
  1.3 20.6 %collective-permute-start.3 = (f32[16,32]{1,0:T(8,128)S(1)}, f32[16,32]{1,0:T(8,128)S(1)}, u32[]{:S(2)}, u32[]{:S(2)}) collective-permute-start(f32[16,32]{1,0:T(8,128)S(1)} %bitcast.81), channel_id=1, source_target_pairs={{1,0},{2,1},{3,2},{4,3},{5,4},{6,5},{7,6},{9,8},{10,9},{11,10},{12... | collective-permute-start | bytes 6152 | tf_op jit(solution)/shard_map/ppermute | solution.py:19
  2.8 19.2 %collective-permute-start.2 = (f32[16,32]{1,0:T(8,128)S(1)}, f32[16,32]{1,0:T(8,128)S(1)}, u32[]{:S(2)}, u32[]{:S(2)}) collective-permute-start(f32[16,32]{1,0:T(8,128)S(1)} %bitcast.82), channel_id=1, source_target_pairs={{0,1},{1,2},{2,3},{3,4},{4,5},{5,6},{6,7},{8,9},{9,10},{10,11},{11... | collective-permute-start | bytes 6152 | tf_op jit(solution)/shard_map/ppermute | solution.py:18
  8.3 13.7 %collective-permute-start = (f32[16,128]{1,0:T(8,128)S(1)}, f32[16,128]{1,0:T(8,128)S(1)}, u32[]{:S(2)}, u32[]{:S(2)}) collective-permute-start(f32[16,128]{1,0:T(8,128)S(1)} %bitcast.84), channel_id=1, source_target_pairs={{0,8},{8,16},{16,24},{1,9},{9,17},{17,25},{2,10},{10,18},{18,26},{... | collective-permute-start | bytes 24584 | tf_op jit(solution)/shard_map/ppermute | solution.py:18
  9.8 12.2 %collective-permute-start.1 = (f32[16,128]{1,0:T(8,128)S(1)}, f32[16,128]{1,0:T(8,128)S(1)}, u32[]{:S(2)}, u32[]{:S(2)}) collective-permute-start(f32[16,128]{1,0:T(8,128)S(1)} %bitcast.83), channel_id=1, source_target_pairs={{8,0},{16,8},{24,16},{9,1},{17,9},{25,17},{10,2},{18,10},{26,18},{... | collective-permute-start | bytes 24584 | tf_op jit(solution)/shard_map/ppermute | solution.py:19
  11.2 1.0 %copy-start.2 = (f32[16,32,128]{2,1,0:T(8,128)S(1)}, f32[16,32,128]{2,1,0:T(8,128)}, u32[]{:S(2)}) copy-start(f32[16,32,128]{2,1,0:T(8,128)} %param.3) | copy-start | bytes 786436
  12.9 2.0 %copy-start.1 = (f32[16,32,128]{2,1,0:T(8,128)S(1)}, f32[16,32,128]{2,1,0:T(8,128)}, u32[]{:S(2)}) copy-start(f32[16,32,128]{2,1,0:T(8,128)} %get-tuple-element.72.h_ref) | copy-start | bytes 786436
  25.6 12.5 %copy-start.5 = (f32[32,16,128]{2,1,0:T(8,128)S(1)}, f32[32,16,128]{2,1,0:T(8,128)}, u32[]{:S(2)}) copy-start(f32[32,16,128]{2,1,0:T(8,128)} %get-tuple-element.51) | copy-start | bytes 786436
  25.6 12.6 %copy-start.3 = (f32[2,32,16,128]{3,2,1,0:T(8,128)S(1)}, f32[2,32,16,128]{3,2,1,0:T(8,128)}, u32[]{:S(2)}) copy-start(f32[2,32,16,128]{3,2,1,0:T(8,128)} %get-tuple-element.52) | copy-start | bytes 1572868
  42.7 4.4 %copy-start.7 = (f32[4,2,4,128]{3,2,1,0:T(4,128)S(1)}, f32[4,2,4,128]{3,2,1,0:T(4,128)}, u32[]{:S(2)}) copy-start(f32[4,2,4,128]{3,2,1,0:T(4,128)} %get-tuple-element.56) | copy-start | bytes 49156
  42.7 4.4 %collective-permute-start.4 = (f32[1,4,2,4,128]{4,3,2,1,0:T(4,128)}, f32[1,4,2,4,128]{4,3,2,1,0:T(4,128)S(1)}, u32[]{:S(2)}, u32[]{:S(2)}) collective-permute-start(f32[1,4,2,4,128]{4,3,2,1,0:T(4,128)} %bitcast.75), channel_id=1, source_target_pairs={{0,1},{1,0},{2,3},{3,2},{4,5},{5,4},{6,7},{7,6},{8,9},{9,8},{10,11... | collective-permute-start | bytes 49160 | tf_op jit(solution)/shard_map/ppermute | solution.py:197
  47.1 4.0 %collective-permute-start.5 = (f32[2,4,2,4,128]{4,3,2,1,0:T(4,128)S(1)}, f32[2,4,2,4,128]{4,3,2,1,0:T(4,128)S(1)}, u32[]{:S(2)}, u32[]{:S(2)}) collective-permute-start(f32[2,4,2,4,128]{4,3,2,1,0:T(4,128)S(1)} %maximum_select_fusion.2), channel_id=1, source_target_pairs={{0,2},{1,3},{2,0},{3,1},{4,6},{5,7},{6,4},{7,5},{8,10},{9,11},{10,... | collective-permute-start | bytes 98312 | tf_op jit(solution)/shard_map/ppermute | solution.py:197
  51.1 8.7 %copy-start.4 = (f32[2,128,4,128]{3,2,1,0:T(4,128)S(1)}, f32[2,128,4,128]{3,2,1,0:T(4,128)}, u32[]{:S(2)}) copy-start(f32[2,128,4,128]{3,2,1,0:T(4,128)} %get-tuple-element.58) | copy-start | bytes 1572868
  51.1 5.2 %collective-permute-start.6 = (f32[4,4,2,4,128]{4,3,2,1,0:T(4,128)S(1)}, f32[4,4,2,4,128]{4,3,2,1,0:T(4,128)S(1)}, u32[]{:S(2)}, u32[]{:S(2)}) collective-permute-start(f32[4,4,2,4,128]{4,3,2,1,0:T(4,128)S(1)} %maximum_select_fusion.1), channel_id=1, source_target_pairs={{0,4},{1,5},{2,6},{3,7},{4,0},{5,1},{6,2},{7,3},{8,12},{9,13},{10,... | collective-permute-start | bytes 196616 | tf_op jit(solution)/shard_map/ppermute | solution.py:197
  59.4 1.0 %copy-start.6 = (f32[128,4,128]{2,1,0:T(4,128)S(1)}, f32[128,4,128]{2,1,0:T(4,128)}, u32[]{:S(2)}) copy-start(f32[128,4,128]{2,1,0:T(4,128)} %get-tuple-element.57) | copy-start | bytes 786436

commit v6 on v3

--- a/solution.py
+++ b/solution.py
@@ -165,9 +165,21 @@
     return held
 
 
+def shifted_gather(part, axis):
+    count = lax.axis_size(axis)
+    received = [part]
+    for shift in range(1, count):
+        received.append(
+            lax.ppermute(part, axis, [(i, (i - shift) % count) for i in range(count)])
+        )
+    return jnp.roll(jnp.stack(received, 0), lax.axis_index(axis), 0)
+
+
 def distributed_solve(h_lines, d_lines, axis, doubling):
     responses, reduced = partition_call(h_lines, d_lines)
-    if doubling:
+    if doubling and lax.axis_size(axis) <= 8:
+        gathered = shifted_gather(reduced, axis)
+    elif doubling:
         gathered = doubling_gather(reduced, axis)
     else:
         gathered = lax.all_gather(reduced, axis)

time: 57.7 us -> 63 us (1.092)
  starting transfers between devices: 17.6 us -> 21.5 us
  local copies, waits for them, and re-layouts: 10.5 us -> 12 us
  other arithmetic: 2.33 us -> 1.63 us
    ppermute x3 -> x7, starting transfers between devices: 8.75 us -> 12.6 us  [shifted_gather(): lax.ppermute(part, axis, [(i, (i - shift) % count) for i in range(count)])]
    unnamed x10 -> x25, local copies, waits for them, and re-layouts: 0.33 us -> 1.24 us
    select_n x3 -> x0, other arithmetic: 0.71 us -> none  [doubling_gather(): jnp.where(lower, jnp.concatenate([held, other], 0), jnp.concatenate([othe...]
    dynamic_slice x0 -> x1, local copies, waits for them, and re-layouts: none -> 0.67 us  [shifted_gather(): return jnp.roll(jnp.stack(received, 0), lax.axis_index(axis), 0)]
    ppermute x3 -> x7, waiting for transfers between devices: 4.44 us -> 4.84 us  [shifted_gather(): lax.ppermute(part, axis, [(i, (i - shift) % count) for i in range(count)])]
  transfers between devices with their start and end apart: 7 -> 11, of which waited for: 5 -> 5; matrix products, arithmetic and copies ran while one was open for 4% -> 4% of each run, Pallas kernels for 0% -> 0%
where the time goes in v6:
time: 63 us; the launch traced here: 62.4 us
  starting transfers between devices  21.5 us (34%)
  local copies, waits for them, and re-layouts  12 us (19%)
  Pallas kernels  10.9 us (17%)
  blocking collectives  8.56 us (14%)
  waiting for transfers between devices  7.61 us (12%)
  other arithmetic  1.63 us (3%)
    ppermute x7, starting transfers between devices, shifted_gather(): lax.ppermute(part, axis, [(i, (i - shift) % count) for i in range(count)])  12.6 us
    all_gather x1, blocking collectives, distributed_solve(): gathered = lax.all_gather(reduced, axis)  8.56 us
    ppermute x2, starting transfers between devices, halos(): low = lax.ppermute(last, axis, forward)  6.3 us
    pallas_call x2, Pallas kernels, partition_call(): pl.pallas_call(partition_kernel, out_shape=(jax.ShapeDtypeStruct((3, n) +...  5.58 us
    ppermute x7, waiting for transfers between devices, shifted_gather(): lax.ppermute(part, axis, [(i, (i - shift) % count) for i in range(count)])  4.84 us
    pallas_call x2, Pallas kernels, reduced_call(): pl.pallas_call(reduced_kernel, out_shape=jax.ShapeDtypeStruct((count, 2)...  3.36 us
    ppermute x2, waiting for transfers between devices, halos(): high = lax.ppermute(first, axis, backward)  2.76 us
    ppermute x2, starting transfers between devices, halos(): high = lax.ppermute(first, axis, backward)  2.59 us
  transfers between devices with their start and end apart: 11, of which 5 were waited for; matrix products, arithmetic and copies ran while one was open for 4% of the time, Pallas kernels for 0%

profile of v6, /device:TPU:0, one launch (start us, length us, event | category | flops | bytes accessed | tf_op | source)
XLA Modules:
  0.0 62.4 jit_solution(695997608052687506)
XLA Ops:
  0.0 1.2 %fusion.16 = (f32[16,32,1]{2,1,0:T(8,128)S(1)}, f32[16,32,1]{2,1,0:T(8,128)S(1)}) fusion(f32[16,32,128]{2,1,0:T(8,128)} %param.2), kind=kLoop, calls=%fused_computation.48 | loop fusion | bytes 8192 | tf_op jit(solution)/shard_map/slice | solution.py:16
  1.3 4.8 %collective-permute-start.2 = (f32[16,32]{1,0:T(8,128)S(1)}, f32[16,32]{1,0:T(8,128)S(1)}, u32[]{:S(2)}, u32[]{:S(2)}) collective-permute-start(f32[16,32]{1,0:T(8,128)S(1)} %bitcast.94), channel_id=1, source_target_pairs={{0,1},{1,2},{2,3},{3,4},{4,5},{5,6},{6,7},{8,9},{9,10},{10,11},{11... | collective-permute-start | bytes 6152 | tf_op jit(solution)/shard_map/ppermute | solution.py:18
  6.3 1.3 %collective-permute-start.3 = (f32[16,32]{1,0:T(8,128)S(1)}, f32[16,32]{1,0:T(8,128)S(1)}, u32[]{:S(2)}, u32[]{:S(2)}) collective-permute-start(f32[16,32]{1,0:T(8,128)S(1)} %bitcast.96), channel_id=1, source_target_pairs={{1,0},{2,1},{3,2},{4,3},{5,4},{6,5},{7,6},{9,8},{10,9},{11,10},{12... | collective-permute-start | bytes 6152 | tf_op jit(solution)/shard_map/ppermute | solution.py:19
  7.7 1.5 %collective-permute-start = (f32[16,128]{1,0:T(8,128)S(1)}, f32[16,128]{1,0:T(8,128)S(1)}, u32[]{:S(2)}, u32[]{:S(2)}) collective-permute-start(f32[16,128]{1,0:T(8,128)S(1)} %bitcast.99), channel_id=1, source_target_pairs={{0,8},{8,16},{16,24},{1,9},{9,17},{17,25},{2,10},{10,18},{18,26},{... | collective-permute-start | bytes 24584 | tf_op jit(solution)/shard_map/ppermute | solution.py:18
  9.1 1.3 %collective-permute-start.1 = (f32[16,128]{1,0:T(8,128)S(1)}, f32[16,128]{1,0:T(8,128)S(1)}, u32[]{:S(2)}, u32[]{:S(2)}) collective-permute-start(f32[16,128]{1,0:T(8,128)S(1)} %bitcast.98), channel_id=1, source_target_pairs={{8,0},{16,8},{24,16},{9,1},{17,9},{25,17},{10,2},{18,10},{26,18},{... | collective-permute-start | bytes 24584 | tf_op jit(solution)/shard_map/ppermute | solution.py:19
  10.8 1.0 %collective-permute-done.3 = f32[16,32]{1,0:T(8,128)S(1)} collective-permute-done((f32[16,32]{1,0:T(8,128)S(1)}, f32[16,32]{1,0:T(8,128)S(1)}, u32[]{:S(2)}, u32[]{:S(2)}) %collective-permute-start.3) | collective-permute-done | bytes 2080 | tf_op jit(solution)/shard_map/ppermute | solution.py:19
  12.1 1.7 %collective-permute-done.1 = f32[16,128]{1,0:T(8,128)S(1)} collective-permute-done((f32[16,128]{1,0:T(8,128)S(1)}, f32[16,128]{1,0:T(8,128)S(1)}, u32[]{:S(2)}, u32[]{:S(2)}) %collective-permute-start.1) | collective-permute-done | bytes 8224 | tf_op jit(solution)/shard_map/ppermute | solution.py:19
  14.1 0.9 %copy.43.h_ref = f32[32,16,128]{2,1,0:T(8,128)} copy(f32[32,16,128]{2,0,1:T(8,128)S(1)} %get-tuple-element.18) | data formatting | bytes 524288 | tf_op jit(solution)/shard_map/transpose | solution.py:221
  15.9 2.3 %shard_map.28 = (f32[3,32,16,128]{3,2,1,0:T(8,128)}, f32[4,2,16,128]{3,2,1,0:T(8,128)}) custom-call(f32[32,16,128]{2,1,0:T(8,128)} %copy.43.h_ref, f32[32,16,128]{2,1,0:T(8,128)} %copy.44.d_ref), custom_call_target="tpu_custom_call" | custom-call | tf_op jit(solution)/shard_map/pallas_call | solution.py:72
  18.1 8.6 %all-gather = f32[16,2,16,128]{3,2,1,0:T(8,128)} all-gather(f32[4,2,16,128]{3,2,1,0:T(8,128)} %get-tuple-element.9), channel_id=2, replica_groups=mesh['gx'=4,'gy'=8] {'gx'}, dimensions={0}, use_global_device_ids=true | all-gather | bytes 327680 | tf_op jit(solution)/shard_map/all_gather | solution.py:185
  26.7 1.7 %shard_map.29 = f32[4,2,16,128]{3,2,1,0:T(8,128)} custom-call(f32[4,4,2,16,128]{4,3,2,1,0:T(8,128)} %bitcast.84), custom_call_target="tpu_custom_call" | custom-call | tf_op jit(solution)/shard_map/pallas_call | solution.py:115
  28.4 1.4 %copy.45 = f32[3,32,16,128]{3,1,2,0:T(8,128)S(1)} copy(f32[3,32,16,128]{3,2,1,0:T(8,128)} %get-tuple-element.10) | data formatting | bytes 1572864 | tf_op jit(solution)/shard_map/pallas_call | solution.py:72
  32.3 3.3 %shard_map.30 = (f32[3,128,4,128]{3,2,1,0:T(4,128)}, f32[4,2,4,128]{3,2,1,0:T(4,128)}) custom-call(f32[128,4,128]{2,1,0:T(4,128)} %copy.49.h_ref, f32[128,4,128]{2,1,0:T(4,128)} %copy.50.d_ref), custom_call_target="tpu_custom_call" | custom-call | tf_op jit(solution)/shard_map/pallas_call | solution.py:72
  36.4 5.7 %collective-permute-start.4 = (f32[4,2,4,128]{3,2,1,0:T(4,128)S(1)}, f32[4,2,4,128]{3,2,1,0:T(4,128)S(1)}, u32[]{:S(2)}, u32[]{:S(2)}) collective-permute-start(f32[4,2,4,128]{3,2,1,0:T(4,128)S(1)} %copy-done.3), channel_id=1, source_target_pairs={{0,7},{1,0},{2,1},{3,2},{4,3},{5,4},{6,5},{7,6},{8,15},{9,8},{10,9... | collective-permute-start | bytes 49160 | tf_op jit(solution)/shard_map/ppermute | solution.py:173
  43.0 3.5 %collective-permute-start.7 = (f32[4,2,4,128]{3,2,1,0:T(4,128)S(1)}, f32[4,2,4,128]{3,2,1,0:T(4,128)S(1)}, u32[]{:S(2)}, u32[]{:S(2)}) collective-permute-start(f32[4,2,4,128]{3,2,1,0:T(4,128)S(1)} %copy-done.3), channel_id=1, source_target_pairs={{0,4},{1,5},{2,6},{3,7},{4,0},{5,1},{6,2},{7,3},{8,12},{9,13},{10,... | collective-permute-start | bytes 49160 | tf_op jit(solution)/shard_map/ppermute | solution.py:173
  46.5 1.2 %fusion.15 = (f32[1,126,4,128]{3,2,1,0:T(4,128)S(1)}, f32[1,126,4,128]{3,2,1,0:T(4,128)S(1)}, f32[1,126,4,128]{3,2,1,0:T(4,128)S(1)}) fusion(f32[3,128,4,128]{3,2,1,0:T(4,128)} %get-tuple-element.12), kind=kLoop, calls=%fused_computation.47 | loop fusion | bytes 1548288 | tf_op jit(solution)/shard_map/slice | solution.py:188
  48.2 1.0 %collective-permute-start.9 = (f32[4,2,4,128]{3,2,1,0:T(4,128)S(1)}, f32[4,2,4,128]{3,2,1,0:T(4,128)S(1)}, u32[]{:S(2)}, u32[]{:S(2)}) collective-permute-start(f32[4,2,4,128]{3,2,1,0:T(4,128)S(1)} %copy-done.3), channel_id=1, source_target_pairs={{0,2},{1,3},{2,4},{3,5},{4,6},{5,7},{6,0},{7,1},{8,10},{9,11},{10,... | collective-permute-start | bytes 49160 | tf_op jit(solution)/shard_map/ppermute | solution.py:173
  49.2 1.5 %collective-permute-start.10 = (f32[4,2,4,128]{3,2,1,0:T(4,128)S(1)}, f32[4,2,4,128]{3,2,1,0:T(4,128)S(1)}, u32[]{:S(2)}, u32[]{:S(2)}) collective-permute-start(f32[4,2,4,128]{3,2,1,0:T(4,128)S(1)} %copy-done.3), channel_id=1, source_target_pairs={{0,1},{1,2},{2,3},{3,4},{4,5},{5,6},{6,7},{7,0},{8,9},{9,10},{10,1... | collective-permute-start | bytes 49160 | tf_op jit(solution)/shard_map/ppermute | solution.py:173
  50.8 1.3 %collective-permute-done.8 = f32[4,2,4,128]{3,2,1,0:T(4,128)S(1)} collective-permute-done((f32[4,2,4,128]{3,2,1,0:T(4,128)S(1)}, f32[4,2,4,128]{3,2,1,0:T(4,128)S(1)}, u32[]{:S(2)}, u32[]{:S(2)}) %collective-permute-start.8) | collective-permute-done | bytes 16416 | tf_op jit(solution)/shard_map/ppermute | solution.py:173
  52.0 1.8 %collective-permute-done.9 = f32[4,2,4,128]{3,2,1,0:T(4,128)S(1)} collective-permute-done((f32[4,2,4,128]{3,2,1,0:T(4,128)S(1)}, f32[4,2,4,128]{3,2,1,0:T(4,128)S(1)}, u32[]{:S(2)}, u32[]{:S(2)}) %collective-permute-start.9) | collective-permute-done | bytes 16416 | tf_op jit(solution)/shard_map/ppermute | solution.py:173
  53.8 1.8 %collective-permute-done.10 = f32[4,2,4,128]{3,2,1,0:T(4,128)S(1)} collective-permute-done((f32[4,2,4,128]{3,2,1,0:T(4,128)S(1)}, f32[4,2,4,128]{3,2,1,0:T(4,128)S(1)}, u32[]{:S(2)}, u32[]{:S(2)}) %collective-permute-start.10) | collective-permute-done | bytes 16416 | tf_op jit(solution)/shard_map/ppermute | solution.py:173
  56.4 1.7 %shard_map.31 = f32[8,2,4,128]{3,2,1,0:T(4,128)} custom-call(f32[8,4,2,4,128]{4,3,2,1,0:T(4,128)} %constant_dynamic-slice_fusion.3.g_ref), custom_call_target="tpu_custom_call" | custom-call | tf_op jit(solution)/shard_map/pallas_call | solution.py:115
  59.6 0.9 %fusion.12.d_ref = f32[16,32,128]{2,1,0:T(8,128)} fusion(f32[1,16,32]{0,2,1:T(8,128)S(1)} %concatenate.38, f32[126,16,32]{0,2,1:T(8,128)S(1)} %multiply_add_fusion, f32[1,16,32]{0,2,1:T(8,128)S(1)} %concatenate.37, f32[16,32,128]{2,1,0:T(8,128)S(1)} %copy-done, f32[16,32,128]{2,1,0:T(8,128)S(1)} %copy-done.2), kind=kLoop, calls=%fused_computation.21 | loop fusion | flops 589824 | bytes 1048576 | tf_op jit(solution)/shard_map/sub | solution.py:230
  60.5 1.9 %shard_map.32 = f32[16,32,128]{2,1,0:T(8,128)} custom-call(f32[16,32,128]{2,1,0:T(8,128)} %copy-done.1, f32[16,32,128]{2,1,0:T(8,128)} %fusion.12.d_ref), custom_call_target="tpu_custom_call" | custom-call | tf_op jit(solution)/shard_map/pallas_call | solution.py:144
  (57 shorter events, 9.0 us)
Async XLA Ops:
  1.2 6.5 %copy-start = (f32[16,32,128]{2,1,0:T(8,128)S(1)}, f32[16,32,128]{2,1,0:T(8,128)}, u32[]{:S(2)}) copy-start(f32[16,32,128]{2,1,0:T(8,128)} %param.2) | copy-start | bytes 786436
  1.3 9.3 %collective-permute-start.2 = (f32[16,32]{1,0:T(8,128)S(1)}, f32[16,32]{1,0:T(8,128)S(1)}, u32[]{:S(2)}, u32[]{:S(2)}) collective-permute-start(f32[16,32]{1,0:T(8,128)S(1)} %bitcast.94), channel_id=1, source_target_pairs={{0,1},{1,2},{2,3},{3,4},{4,5},{5,6},{6,7},{8,9},{9,10},{10,11},{11... | collective-permute-start | bytes 6152 | tf_op jit(solution)/shard_map/ppermute | solution.py:18
  6.3 5.5 %collective-permute-start.3 = (f32[16,32]{1,0:T(8,128)S(1)}, f32[16,32]{1,0:T(8,128)S(1)}, u32[]{:S(2)}, u32[]{:S(2)}) collective-permute-start(f32[16,32]{1,0:T(8,128)S(1)} %bitcast.96), channel_id=1, source_target_pairs={{1,0},{2,1},{3,2},{4,3},{5,4},{6,5},{7,6},{9,8},{10,9},{11,10},{12... | collective-permute-start | bytes 6152 | tf_op jit(solution)/shard_map/ppermute | solution.py:19
  7.7 4.4 %collective-permute-start = (f32[16,128]{1,0:T(8,128)S(1)}, f32[16,128]{1,0:T(8,128)S(1)}, u32[]{:S(2)}, u32[]{:S(2)}) collective-permute-start(f32[16,128]{1,0:T(8,128)S(1)} %bitcast.99), channel_id=1, source_target_pairs={{0,8},{8,16},{16,24},{1,9},{9,17},{17,25},{2,10},{10,18},{18,26},{... | collective-permute-start | bytes 24584 | tf_op jit(solution)/shard_map/ppermute | solution.py:18
  9.1 4.7 %collective-permute-start.1 = (f32[16,128]{1,0:T(8,128)S(1)}, f32[16,128]{1,0:T(8,128)S(1)}, u32[]{:S(2)}, u32[]{:S(2)}) collective-permute-start(f32[16,128]{1,0:T(8,128)S(1)} %bitcast.98), channel_id=1, source_target_pairs={{8,0},{16,8},{24,16},{9,1},{17,9},{25,17},{10,2},{18,10},{26,18},{... | collective-permute-start | bytes 24584 | tf_op jit(solution)/shard_map/ppermute | solution.py:19
  10.7 3.1 %copy-start.2 = (f32[16,32,128]{2,1,0:T(8,128)S(1)}, f32[16,32,128]{2,1,0:T(8,128)}, u32[]{:S(2)}) copy-start(f32[16,32,128]{2,1,0:T(8,128)} %param.3) | copy-start | bytes 786436
  14.1 17.4 %copy-start.1 = (f32[16,32,128]{2,1,0:T(8,128)}, f32[16,32,128]{2,1,0:T(8,128)S(1)}, u32[]{:S(2)}) copy-start(f32[16,32,128]{2,1,0:T(8,128)S(1)} %get-tuple-element.19.h_ref) | copy-start | bytes 786436
  35.6 0.8 %copy-start.3 = (f32[4,2,4,128]{3,2,1,0:T(4,128)S(1)}, f32[4,2,4,128]{3,2,1,0:T(4,128)}, u32[]{:S(2)}) copy-start(f32[4,2,4,128]{3,2,1,0:T(4,128)} %get-tuple-element.11) | copy-start | bytes 49156
  36.4 11.7 %collective-permute-start.4 = (f32[4,2,4,128]{3,2,1,0:T(4,128)S(1)}, f32[4,2,4,128]{3,2,1,0:T(4,128)S(1)}, u32[]{:S(2)}, u32[]{:S(2)}) collective-permute-start(f32[4,2,4,128]{3,2,1,0:T(4,128)S(1)} %copy-done.3), channel_id=1, source_target_pairs={{0,7},{1,0},{2,1},{3,2},{4,3},{5,4},{6,5},{7,6},{8,15},{9,8},{10,9... | collective-permute-start | bytes 49160 | tf_op jit(solution)/shard_map/ppermute | solution.py:173
  42.1 7.1 %collective-permute-start.5 = (f32[4,2,4,128]{3,2,1,0:T(4,128)S(1)}, f32[4,2,4,128]{3,2,1,0:T(4,128)S(1)}, u32[]{:S(2)}, u32[]{:S(2)}) collective-permute-start(f32[4,2,4,128]{3,2,1,0:T(4,128)S(1)} %copy-done.3), channel_id=1, source_target_pairs={{0,6},{1,7},{2,0},{3,1},{4,2},{5,3},{6,4},{7,5},{8,14},{9,15},{10,... | collective-permute-start | bytes 49160 | tf_op jit(solution)/shard_map/ppermute | solution.py:173
  42.6 8.2 %collective-permute-start.6 = (f32[4,2,4,128]{3,2,1,0:T(4,128)S(1)}, f32[4,2,4,128]{3,2,1,0:T(4,128)S(1)}, u32[]{:S(2)}, u32[]{:S(2)}) collective-permute-start(f32[4,2,4,128]{3,2,1,0:T(4,128)S(1)} %copy-done.3), channel_id=1, source_target_pairs={{0,5},{1,6},{2,7},{3,0},{4,1},{5,2},{6,3},{7,4},{8,13},{9,14},{10,... | collective-permute-start | bytes 49160 | tf_op jit(solution)/shard_map/ppermute | solution.py:173
  43.0 7.8 %collective-permute-start.7 = (f32[4,2,4,128]{3,2,1,0:T(4,128)S(1)}, f32[4,2,4,128]{3,2,1,0:T(4,128)S(1)}, u32[]{:S(2)}, u32[]{:S(2)}) collective-permute-start(f32[4,2,4,128]{3,2,1,0:T(4,128)S(1)} %copy-done.3), channel_id=1, source_target_pairs={{0,4},{1,5},{2,6},{3,7},{4,0},{5,1},{6,2},{7,3},{8,12},{9,13},{10,... | collective-permute-start | bytes 49160 | tf_op jit(solution)/shard_map/ppermute | solution.py:173
  46.5 5.5 %collective-permute-start.8 = (f32[4,2,4,128]{3,2,1,0:T(4,128)S(1)}, f32[4,2,4,128]{3,2,1,0:T(4,128)S(1)}, u32[]{:S(2)}, u32[]{:S(2)}) collective-permute-start(f32[4,2,4,128]{3,2,1,0:T(4,128)S(1)} %copy-done.3), channel_id=1, source_target_pairs={{0,3},{1,4},{2,5},{3,6},{4,7},{5,0},{6,1},{7,2},{8,11},{9,12},{10,... | collective-permute-start | bytes 49160 | tf_op jit(solution)/shard_map/ppermute | solution.py:173
  48.2 5.6 %collective-permute-start.9 = (f32[4,2,4,128]{3,2,1,0:T(4,128)S(1)}, f32[4,2,4,128]{3,2,1,0:T(4,128)S(1)}, u32[]{:S(2)}, u32[]{:S(2)}) collective-permute-start(f32[4,2,4,128]{3,2,1,0:T(4,128)S(1)} %copy-done.3), channel_id=1, source_target_pairs={{0,2},{1,3},{2,4},{3,5},{4,6},{5,7},{6,0},{7,1},{8,10},{9,11},{10,... | collective-permute-start | bytes 49160 | tf_op jit(solution)/shard_map/ppermute | solution.py:173
  49.2 6.4 %collective-permute-start.10 = (f32[4,2,4,128]{3,2,1,0:T(4,128)S(1)}, f32[4,2,4,128]{3,2,1,0:T(4,128)S(1)}, u32[]{:S(2)}, u32[]{:S(2)}) collective-permute-start(f32[4,2,4,128]{3,2,1,0:T(4,128)S(1)} %copy-done.3), channel_id=1, source_target_pairs={{0,1},{1,2},{2,3},{3,4},{4,5},{5,6},{6,7},{7,0},{8,9},{9,10},{10,1... | collective-permute-start | bytes 49160 | tf_op jit(solution)/shard_map/ppermute | solution.py:173

commit v7 on v3

--- a/solution.py
+++ b/solution.py
@@ -83,8 +83,9 @@
     return pltpu.VMEM(shape, jnp.float32)
 
 
-def reduced_kernel(g_ref, out_ref, ratio_ref):
+def finish_kernel(position_ref, g_ref, responses_ref, out_ref, ratio_ref, ends_ref):
     count = g_ref.shape[0]
+    n = responses_ref.shape[1]
     ratio = None
     value = None
     for j in range(2 * count):
@@ -101,22 +102,34 @@
             value = (side - lower * value) / denom
         ratio = upper / denom
         ratio_ref[j] = ratio
-        out_ref[k, q] = value
+        ends_ref[j] = value
     x = value
     for j in range(2 * count - 2, -1, -1):
-        k, q = divmod(j, 2)
-        x = out_ref[k, q] - ratio_ref[j] * x
-        out_ref[k, q] = x
-
-
-def reduced_call(gathered):
+        x = ends_ref[j] - ratio_ref[j] * x
+        ends_ref[j] = x
+    mine = position_ref[0]
+    head = ends_ref[2 * mine]
+    tail = ends_ref[2 * mine + 1]
+    out_ref[0] = head
+    out_ref[n - 1] = tail
+    for i in range(1, n - 1):
+        out_ref[i] = responses_ref[0, i] + responses_ref[1, i] * head + responses_ref[2, i] * tail
+
+
+def finish_call(gathered, responses, position):
     count = gathered.shape[0]
     rest = gathered.shape[3:]
+    n = responses.shape[1]
     return pl.pallas_call(
-        reduced_kernel,
-        out_shape=jax.ShapeDtypeStruct((count, 2) + rest, jnp.float32),
-        scratch_shapes=[pltpu_vmem((2 * count,) + rest)],
-    )(gathered)
+        finish_kernel,
+        out_shape=jax.ShapeDtypeStruct((n,) + rest, jnp.float32),
+        in_specs=[
+            pl.BlockSpec(memory_space=pltpu.SMEM),
+            pl.BlockSpec(memory_space=pltpu.VMEM),
+            pl.BlockSpec(memory_space=pltpu.VMEM),
+        ],
+        scratch_shapes=[pltpu_vmem((2 * count,) + rest), pltpu_vmem((2 * count,) + rest)],
+    )(position, gathered, responses)
 
 
 def sweep_kernel(h_ref, d_ref, out_ref, ratio_ref):
@@ -171,10 +184,8 @@
         gathered = doubling_gather(reduced, axis)
     else:
         gathered = lax.all_gather(reduced, axis)
-    ends = reduced_call(gathered)
-    head, tail = lax.dynamic_index_in_dim(ends, lax.axis_index(axis), 0, keepdims=False)
-    interior = responses[0, 1:-1] + responses[1, 1:-1] * head + responses[2, 1:-1] * tail
-    return jnp.concatenate([head[None], interior, tail[None]], 0)
+    position = jnp.reshape(lax.axis_index(axis), (1,)).astype(jnp.int32)
+    return finish_call(gathered, responses, position)
 
 
 def per_device(initial_heat_values, spreading_coefficients):

time: 57.7 us -> 57.9 us (level)
  local copies, waits for them, and re-layouts: 10.5 us -> 7.39 us
  starting transfers between devices: 17.6 us -> 20.3 us
  Pallas kernels: 10.8 us -> 11.7 us
  blocking collectives: 8.56 us -> 7.89 us
    ppermute x2, waiting for transfers between devices: 2.77 us -> 0.01 us  [halos(): high = lax.ppermute(first, axis, backward)]
    ppermute x2, starting transfers between devices: 6.3 us -> 8.5 us  [halos(): low = lax.ppermute(last, axis, forward)]
    ppermute x3, waiting for transfers between devices: 4.44 us -> 6.14 us  [doubling_gather(): other = lax.ppermute(held, axis, [(i, i ^ step) for i in range(count)])]
    slice x4 -> x0, local copies, waits for them, and re-layouts: 1.67 us -> none  [the longest x2 1.39 us: distributed_solve(): responses[1, 1:-1] * head]
    another operation x2 -> x0, local copies, waits for them, and re-layouts: 1.4 us -> none  [distributed_solve(): head, tail = lax.dynamic_index_in_dim(ends, lax.axis_index(axis), 0, keep...]
    sub x1, other arithmetic: 0.07 us -> 1.05 us  [per_device(): second_side = first_pass - implicit_weight * vertical_implicit_solve]
    ppermute x2, waiting for transfers between devices: 0.01 us -> 0.95 us  [halos(): low = lax.ppermute(last, axis, forward)]
    slice x2, local copies, waits for them, and re-layouts: 1.17 us -> 2.04 us  [halos(): last = lax.index_in_dim(block, block.shape[dim] - 1, dim, keepdims=False)]
  transfers between devices with their start and end apart: 7 -> 7, of which waited for: 5 -> 4; matrix products, arithmetic and copies ran while one was open for 4% -> 3% of each run, Pallas kernels for 0% -> 0%
where the time goes in v7:
time: 57.9 us; the launch traced here: 57.4 us
  starting transfers between devices  20.3 us (35%)
  Pallas kernels  11.7 us (20%)
  blocking collectives  7.89 us (14%)
  local copies, waits for them, and re-layouts  7.39 us (13%)
  waiting for transfers between devices  7.09 us (12%)
  other arithmetic  2.86 us (5%)
    ppermute x3, starting transfers between devices, doubling_gather(): other = lax.ppermute(held, axis, [(i, i ^ step) for i in range(count)])  9.23 us
    ppermute x2, starting transfers between devices, halos(): low = lax.ppermute(last, axis, forward)  8.5 us
    all_gather x1, blocking collectives, distributed_solve(): gathered = lax.all_gather(reduced, axis)  7.89 us
    ppermute x3, waiting for transfers between devices, doubling_gather(): other = lax.ppermute(held, axis, [(i, i ^ step) for i in range(count)])  6.14 us
    pallas_call x2, Pallas kernels, partition_call(): pl.pallas_call(partition_kernel, out_shape=(jax.ShapeDtypeStruct((3, n) +...  5.62 us
    pallas_call x2, Pallas kernels, finish_call(): pl.pallas_call(finish_kernel, out_shape=jax.ShapeDtypeStruct((n,) + rest,...  4.22 us
    ppermute x2, starting transfers between devices, halos(): high = lax.ppermute(first, axis, backward)  2.59 us
    slice x2, local copies, waits for them, and re-layouts, halos(): last = lax.index_in_dim(block, block.shape[dim] - 1, dim, keepdims=False)  2.04 us
  transfers between devices with their start and end apart: 7, of which 4 were waited for; matrix products, arithmetic and copies ran while one was open for 3% of the time, Pallas kernels for 0%

profile of v7, /device:TPU:0, one launch (start us, length us, event | category | flops | bytes accessed | tf_op | source)
XLA Modules:
  0.0 57.4 jit_solution(11416754285312157642)
XLA Ops:
  0.0 0.9 %fusion.11 = (f32[16,1,128]{2,1,0:T(1,128)S(1)}, f32[16,1,128]{2,1,0:T(1,128)S(1)}) fusion(f32[16,32,128]{2,1,0:T(8,128)} %param.2), kind=kLoop, calls=%fused_computation.21 | loop fusion | bytes 32768 | tf_op jit(solution)/shard_map/slice | solution.py:16
  0.9 1.3 %collective-permute-start.1 = (f32[16,128]{1,0:T(8,128)S(1)}, f32[16,128]{1,0:T(8,128)S(1)}, u32[]{:S(2)}, u32[]{:S(2)}) collective-permute-start(f32[16,128]{1,0:T(8,128)S(1)} %bitcast.44), channel_id=1, source_target_pairs={{8,0},{16,8},{24,16},{9,1},{17,9},{25,17},{10,2},{18,10},{26,18},{... | collective-permute-start | bytes 24584 | tf_op jit(solution)/shard_map/ppermute | solution.py:19
  2.2 3.0 %collective-permute-start = (f32[16,128]{1,0:T(8,128)S(1)}, f32[16,128]{1,0:T(8,128)S(1)}, u32[]{:S(2)}, u32[]{:S(2)}) collective-permute-start(f32[16,128]{1,0:T(8,128)S(1)} %bitcast.43), channel_id=1, source_target_pairs={{0,8},{8,16},{16,24},{1,9},{9,17},{17,25},{2,10},{10,18},{18,26},{... | collective-permute-start | bytes 24584 | tf_op jit(solution)/shard_map/ppermute | solution.py:18
  5.2 1.2 %fusion.9 = (f32[16,32,1]{2,1,0:T(8,128)S(1)}, f32[16,32,1]{2,1,0:T(8,128)S(1)}) fusion(f32[16,32,128]{2,1,0:T(8,128)} %param.2), kind=kLoop, calls=%fused_computation.19 | loop fusion | bytes 8192 | tf_op jit(solution)/shard_map/slice | solution.py:16
  6.6 1.3 %collective-permute-start.3 = (f32[16,32]{1,0:T(8,128)S(1)}, f32[16,32]{1,0:T(8,128)S(1)}, u32[]{:S(2)}, u32[]{:S(2)}) collective-permute-start(f32[16,32]{1,0:T(8,128)S(1)} %bitcast.39), channel_id=1, source_target_pairs={{1,0},{2,1},{3,2},{4,3},{5,4},{6,5},{7,6},{9,8},{10,9},{11,10},{12... | collective-permute-start | bytes 6152 | tf_op jit(solution)/shard_map/ppermute | solution.py:19
  8.0 5.5 %collective-permute-start.2 = (f32[16,32]{1,0:T(8,128)S(1)}, f32[16,32]{1,0:T(8,128)S(1)}, u32[]{:S(2)}, u32[]{:S(2)}) collective-permute-start(f32[16,32]{1,0:T(8,128)S(1)} %bitcast.41), channel_id=1, source_target_pairs={{0,1},{1,2},{2,3},{3,4},{4,5},{5,6},{6,7},{8,9},{9,10},{10,11},{11... | collective-permute-start | bytes 6152 | tf_op jit(solution)/shard_map/ppermute | solution.py:18
  13.9 0.9 %collective-permute-done.2 = f32[16,32]{1,0:T(8,128)S(1)} collective-permute-done((f32[16,32]{1,0:T(8,128)S(1)}, f32[16,32]{1,0:T(8,128)S(1)}, u32[]{:S(2)}, u32[]{:S(2)}) %collective-permute-start.2) | collective-permute-done | bytes 2080 | tf_op jit(solution)/shard_map/ppermute | solution.py:18
  16.2 0.9 %copy.31.h_ref = f32[32,16,128]{2,1,0:T(8,128)} copy(f32[32,16,128]{2,0,1:T(8,128)S(1)} %get-tuple-element.15) | data formatting | bytes 524288 | tf_op jit(solution)/shard_map/transpose | solution.py:220
  17.1 0.9 %copy.32.d_ref = f32[32,16,128]{2,1,0:T(8,128)} copy(f32[32,16,128]{2,0,1:T(8,128)S(1)} %get-tuple-element.13) | data formatting | bytes 524288 | tf_op jit(solution)/shard_map/transpose | solution.py:217
  18.0 2.3 %shard_map.28 = (f32[3,32,16,128]{3,2,1,0:T(8,128)}, f32[4,2,16,128]{3,2,1,0:T(8,128)}) custom-call(f32[32,16,128]{2,1,0:T(8,128)} %copy.31.h_ref, f32[32,16,128]{2,1,0:T(8,128)} %copy.32.d_ref), custom_call_target="tpu_custom_call" | custom-call | tf_op jit(solution)/shard_map/pallas_call | solution.py:72
  20.2 7.9 %all-gather = f32[16,2,16,128]{3,2,1,0:T(8,128)} all-gather(f32[4,2,16,128]{3,2,1,0:T(8,128)} %get-tuple-element.9), channel_id=2, replica_groups=mesh['gx'=4,'gy'=8] {'gx'}, dimensions={0}, use_global_device_ids=true | all-gather | bytes 327680 | tf_op jit(solution)/shard_map/all_gather | solution.py:186
  28.1 2.0 %shard_map.29 = f32[32,16,128]{2,1,0:T(8,128)} custom-call(s32[1]{0:T(128)} %bitcast.3.position_ref, f32[4,4,2,16,128]{4,3,2,1,0:T(8,128)} %bitcast.32, f32[3,32,16,128]{3,2,1,0:T(8,128)} %get-tuple-element.10.responses_ref), custom_call_target="tpu_custom_call" | custom-call | tf_op jit(solution)/shard_map/pallas_call | solution.py:123
  30.2 1.0 %bitcast_subtract_fusion = f32[16,32,128]{2,1,0:T(8,128)S(1)} fusion(f32[32,16,128]{2,1,0:T(8,128)} %shard_map.29, f32[16,32,128]{2,1,0:T(8,128)S(1)} %get-tuple-element.14), kind=kLoop, calls=%fused_computation.11 | loop fusion | flops 131072 | bytes 786432 | tf_op jit(solution)/shard_map/sub | solution.py:222
  31.2 0.9 %copy.35.d_ref = f32[128,4,128]{2,1,0:T(4,128)} copy(f32[128,4,128]{0,2,1:T(8,128)S(1)} %bitcast.33) | data formatting | bytes 524288 | tf_op jit(solution)/shard_map/reshape | solution.py:225
  32.1 3.3 %shard_map.30 = (f32[3,128,4,128]{3,2,1,0:T(4,128)}, f32[4,2,4,128]{3,2,1,0:T(4,128)}) custom-call(f32[128,4,128]{2,1,0:T(4,128)} %copy.34.h_ref, f32[128,4,128]{2,1,0:T(4,128)} %copy.35.d_ref), custom_call_target="tpu_custom_call" | custom-call | tf_op jit(solution)/shard_map/pallas_call | solution.py:72
  35.4 2.4 %collective-permute-start.4 = (f32[1,4,2,4,128]{4,3,2,1,0:T(4,128)}, f32[1,4,2,4,128]{4,3,2,1,0:T(4,128)S(1)}, u32[]{:S(2)}, u32[]{:S(2)}) collective-permute-start(f32[1,4,2,4,128]{4,3,2,1,0:T(4,128)} %bitcast.35), channel_id=1, source_target_pairs={{0,1},{1,0},{2,3},{3,2},{4,5},{5,4},{6,7},{7,6},{8,9},{9,8},{10,11... | collective-permute-start | bytes 49160 | tf_op jit(solution)/shard_map/ppermute | solution.py:172
  37.8 2.0 %collective-permute-done.4 = f32[1,4,2,4,128]{4,3,2,1,0:T(4,128)S(1)} collective-permute-done((f32[1,4,2,4,128]{4,3,2,1,0:T(4,128)}, f32[1,4,2,4,128]{4,3,2,1,0:T(4,128)S(1)}, u32[]{:S(2)}, u32[]{:S(2)}) %collective-permute-start.4) | collective-permute-done | bytes 16416 | tf_op jit(solution)/shard_map/ppermute | solution.py:172
  39.8 3.7 %collective-permute-start.5 = (f32[2,4,2,4,128]{4,3,2,1,0:T(4,128)S(1)}, f32[2,4,2,4,128]{4,3,2,1,0:T(4,128)S(1)}, u32[]{:S(2)}, u32[]{:S(2)}) collective-permute-start(f32[2,4,2,4,128]{4,3,2,1,0:T(4,128)S(1)} %maximum_select_fusion.2), channel_id=1, source_target_pairs={{0,2},{1,3},{2,0},{3,1},{4,6},{5,7},{6,4},{7,5},{8,10},{9,11},{10,... | collective-permute-start | bytes 98312 | tf_op jit(solution)/shard_map/ppermute | solution.py:172
  43.6 1.9 %collective-permute-done.5 = f32[2,4,2,4,128]{4,3,2,1,0:T(4,128)S(1)} collective-permute-done((f32[2,4,2,4,128]{4,3,2,1,0:T(4,128)S(1)}, f32[2,4,2,4,128]{4,3,2,1,0:T(4,128)S(1)}, u32[]{:S(2)}, u32[]{:S(2)}) %collective-permute-start.5) | collective-permute-done | bytes 32800 | tf_op jit(solution)/shard_map/ppermute | solution.py:172
  45.5 3.1 %collective-permute-start.6 = (f32[4,4,2,4,128]{4,3,2,1,0:T(4,128)S(1)}, f32[4,4,2,4,128]{4,3,2,1,0:T(4,128)S(1)}, u32[]{:S(2)}, u32[]{:S(2)}) collective-permute-start(f32[4,4,2,4,128]{4,3,2,1,0:T(4,128)S(1)} %maximum_select_fusion.1), channel_id=1, source_target_pairs={{0,4},{1,5},{2,6},{3,7},{4,0},{5,1},{6,2},{7,3},{8,12},{9,13},{10,... | collective-permute-start | bytes 196616 | tf_op jit(solution)/shard_map/ppermute | solution.py:172
  48.6 2.2 %collective-permute-done.6 = f32[4,4,2,4,128]{4,3,2,1,0:T(4,128)S(1)} collective-permute-done((f32[4,4,2,4,128]{4,3,2,1,0:T(4,128)S(1)}, f32[4,4,2,4,128]{4,3,2,1,0:T(4,128)S(1)}, u32[]{:S(2)}, u32[]{:S(2)}) %collective-permute-start.6) | collective-permute-done | bytes 65568 | tf_op jit(solution)/shard_map/ppermute | solution.py:172
  51.5 2.2 %shard_map.31 = f32[128,4,128]{2,1,0:T(4,128)} custom-call(s32[1]{0:T(128)} %bitcast.position_ref, f32[8,4,2,4,128]{4,3,2,1,0:T(4,128)} %maximum_select_fusion.g_ref, f32[3,128,4,128]{3,2,1,0:T(4,128)} %get-tuple-element.12.responses_ref), custom_call_target="tpu_custom_call" | custom-call | tf_op jit(solution)/shard_map/pallas_call | solution.py:123
  53.7 1.1 %copy.36 = f32[128,4,128]{0,2,1:T(8,128)S(1)} copy(f32[128,4,128]{2,1,0:T(4,128)} %shard_map.31) | data formatting | bytes 524288 | tf_op jit(solution)/shard_map/pallas_call | solution.py:123
  55.5 1.9 %shard_map.32 = f32[16,32,128]{2,1,0:T(8,128)} custom-call(f32[16,32,128]{2,1,0:T(8,128)} %copy-done.1, f32[16,32,128]{2,1,0:T(8,128)} %multiply_subtract_fusion.d_ref), custom_call_target="tpu_custom_call" | custom-call | tf_op jit(solution)/shard_map/pallas_call | solution.py:157
  (23 shorter events, 3.5 us)
Async XLA Ops:
  0.9 14.1 %collective-permute-start.1 = (f32[16,128]{1,0:T(8,128)S(1)}, f32[16,128]{1,0:T(8,128)S(1)}, u32[]{:S(2)}, u32[]{:S(2)}) collective-permute-start(f32[16,128]{1,0:T(8,128)S(1)} %bitcast.44), channel_id=1, source_target_pairs={{8,0},{16,8},{24,16},{9,1},{17,9},{25,17},{10,2},{18,10},{26,18},{... | collective-permute-start | bytes 24584 | tf_op jit(solution)/shard_map/ppermute | solution.py:19
  2.2 12.8 %collective-permute-start = (f32[16,128]{1,0:T(8,128)S(1)}, f32[16,128]{1,0:T(8,128)S(1)}, u32[]{:S(2)}, u32[]{:S(2)}) collective-permute-start(f32[16,128]{1,0:T(8,128)S(1)} %bitcast.43), channel_id=1, source_target_pairs={{0,8},{8,16},{16,24},{1,9},{9,17},{17,25},{2,10},{10,18},{18,26},{... | collective-permute-start | bytes 24584 | tf_op jit(solution)/shard_map/ppermute | solution.py:18
  6.4 7.1 %copy-start = (f32[16,32,128]{2,1,0:T(8,128)S(1)}, f32[16,32,128]{2,1,0:T(8,128)}, u32[]{:S(2)}) copy-start(f32[16,32,128]{2,1,0:T(8,128)} %param.2) | copy-start | bytes 786436
  6.6 7.1 %collective-permute-start.3 = (f32[16,32]{1,0:T(8,128)S(1)}, f32[16,32]{1,0:T(8,128)S(1)}, u32[]{:S(2)}, u32[]{:S(2)}) collective-permute-start(f32[16,32]{1,0:T(8,128)S(1)} %bitcast.39), channel_id=1, source_target_pairs={{1,0},{2,1},{3,2},{4,3},{5,4},{6,5},{7,6},{9,8},{10,9},{11,10},{12... | collective-permute-start | bytes 6152 | tf_op jit(solution)/shard_map/ppermute | solution.py:19
  8.0 6.8 %collective-permute-start.2 = (f32[16,32]{1,0:T(8,128)S(1)}, f32[16,32]{1,0:T(8,128)S(1)}, u32[]{:S(2)}, u32[]{:S(2)}) collective-permute-start(f32[16,32]{1,0:T(8,128)S(1)} %bitcast.41), channel_id=1, source_target_pairs={{0,1},{1,2},{2,3},{3,4},{4,5},{5,6},{6,7},{8,9},{9,10},{10,11},{11... | collective-permute-start | bytes 6152 | tf_op jit(solution)/shard_map/ppermute | solution.py:18
  13.7 1.3 %copy-start.2 = (f32[16,32,128]{2,1,0:T(8,128)S(1)}, f32[16,32,128]{2,1,0:T(8,128)}, u32[]{:S(2)}) copy-start(f32[16,32,128]{2,1,0:T(8,128)} %param.3) | copy-start | bytes 786436
  15.4 0.8 %copy-start.1 = (f32[16,32,128]{2,1,0:T(8,128)}, f32[16,32,128]{2,1,0:T(8,128)S(1)}, u32[]{:S(2)}) copy-start(f32[16,32,128]{2,1,0:T(8,128)S(1)} %get-tuple-element.16.h_ref) | copy-start | bytes 786436
  35.4 4.4 %copy-start.3 = (f32[4,2,4,128]{3,2,1,0:T(4,128)S(1)}, f32[4,2,4,128]{3,2,1,0:T(4,128)}, u32[]{:S(2)}) copy-start(f32[4,2,4,128]{3,2,1,0:T(4,128)} %get-tuple-element.11) | copy-start | bytes 49156
  35.4 4.4 %collective-permute-start.4 = (f32[1,4,2,4,128]{4,3,2,1,0:T(4,128)}, f32[1,4,2,4,128]{4,3,2,1,0:T(4,128)S(1)}, u32[]{:S(2)}, u32[]{:S(2)}) collective-permute-start(f32[1,4,2,4,128]{4,3,2,1,0:T(4,128)} %bitcast.35), channel_id=1, source_target_pairs={{0,1},{1,0},{2,3},{3,2},{4,5},{5,4},{6,7},{7,6},{8,9},{9,8},{10,11... | collective-permute-start | bytes 49160 | tf_op jit(solution)/shard_map/ppermute | solution.py:172
  39.8 5.6 %collective-permute-start.5 = (f32[2,4,2,4,128]{4,3,2,1,0:T(4,128)S(1)}, f32[2,4,2,4,128]{4,3,2,1,0:T(4,128)S(1)}, u32[]{:S(2)}, u32[]{:S(2)}) collective-permute-start(f32[2,4,2,4,128]{4,3,2,1,0:T(4,128)S(1)} %maximum_select_fusion.2), channel_id=1, source_target_pairs={{0,2},{1,3},{2,0},{3,1},{4,6},{5,7},{6,4},{7,5},{8,10},{9,11},{10,... | collective-permute-start | bytes 98312 | tf_op jit(solution)/shard_map/ppermute | solution.py:172
  45.5 5.3 %collective-permute-start.6 = (f32[4,4,2,4,128]{4,3,2,1,0:T(4,128)S(1)}, f32[4,4,2,4,128]{4,3,2,1,0:T(4,128)S(1)}, u32[]{:S(2)}, u32[]{:S(2)}) collective-permute-start(f32[4,4,2,4,128]{4,3,2,1,0:T(4,128)S(1)} %maximum_select_fusion.1), channel_id=1, source_target_pairs={{0,4},{1,5},{2,6},{3,7},{4,0},{5,1},{6,2},{7,3},{8,12},{9,13},{10,... | collective-permute-start | bytes 196616 | tf_op jit(solution)/shard_map/ppermute | solution.py:172

commit v8 on v7

--- a/solution.py
+++ b/solution.py
@@ -20,7 +20,12 @@
     return jnp.expand_dims(low, dim), jnp.expand_dims(high, dim)
 
 
-def partition_kernel(h_ref, d_ref, out_ref, red_ref, ratio_ref):
+def partition_kernel(h_ref, d_ref, *refs):
+    if len(refs) == 4:
+        edges_ref, out_ref, red_ref, ratio_ref = refs
+    else:
+        edges_ref = None
+        out_ref, red_ref, ratio_ref = refs
     n = h_ref.shape[0]
     ratio = jnp.zeros(h_ref.shape[1:], jnp.float32)
     vb = jnp.zeros_like(ratio)
@@ -64,19 +69,24 @@
     red_ref[2, 1] = -rt
     red_ref[3, 0] = d_ref[0] + rh * out_ref[0, 1]
     red_ref[3, 1] = d_ref[n - 1] + rt * out_ref[0, n - 2]
-
-
-def partition_call(h_lines, d_lines):
+    if edges_ref is not None:
+        red_ref[4, 0] = edges_ref[0]
+        red_ref[4, 1] = edges_ref[1]
+
+
+def partition_call(h_lines, d_lines, edges):
     n = h_lines.shape[0]
     rest = h_lines.shape[1:]
+    operands = (h_lines, d_lines) if edges is None else (h_lines, d_lines, edges)
+    rows = 4 if edges is None else 5
     return pl.pallas_call(
         partition_kernel,
         out_shape=(
             jax.ShapeDtypeStruct((3, n) + rest, jnp.float32),
-            jax.ShapeDtypeStruct((4, 2) + rest, jnp.float32),
+            jax.ShapeDtypeStruct((rows, 2) + rest, jnp.float32),
         ),
         scratch_shapes=[pltpu_vmem((n,) + rest)],
-    )(h_lines, d_lines)
+    )(*operands)
 
 
 def pltpu_vmem(shape):
@@ -94,6 +104,10 @@
         centre = g_ref[k, 1, q]
         upper = g_ref[k, 2, q]
         side = g_ref[k, 3, q]
+        if g_ref.shape[1] == 5 and q == 0 and k > 0:
+            side = side - lower * g_ref[k - 1, 4, 1]
+        if g_ref.shape[1] == 5 and q == 1 and k < count - 1:
+            side = side - upper * g_ref[k + 1, 4, 0]
         if j == 0:
             denom = centre
             value = side / denom
@@ -178,8 +192,8 @@
     return held
 
 
-def distributed_solve(h_lines, d_lines, axis, doubling):
-    responses, reduced = partition_call(h_lines, d_lines)
+def distributed_solve(h_lines, d_lines, axis, doubling, edges=None):
+    responses, reduced = partition_call(h_lines, d_lines, edges)
     if doubling:
         gathered = doubling_gather(reduced, axis)
     else:
@@ -192,7 +206,8 @@
     conductivity_map = diffusion_number * spreading_coefficients
     half_rate = implicit_weight * conductivity_map
     plane_count, row_count, column_count = initial_heat_values.shape
-    x_low, x_high = halos(initial_heat_values, "gx", 1)
+    x_low = jnp.zeros_like(initial_heat_values[:, :1])
+    x_high = x_low
     y_low, y_high = halos(initial_heat_values, "gy", 2)
     horizontal_implicit_solve = conductivity_map * (
         jnp.concatenate([x_low, initial_heat_values[:, :-1]], 1)
@@ -218,7 +233,13 @@
         forward_euler_increment - implicit_weight * horizontal_implicit_solve, 1, 0
     )
     first_rate = jnp.moveaxis(half_rate, 1, 0)
-    first_pass = jnp.moveaxis(distributed_solve(first_rate, first_side, "gx", False), 0, 1)
+    first_pass = jnp.moveaxis(distributed_solve(
+            first_rate,
+            first_side,
+            "gx",
+            False,
+            jnp.stack([initial_heat_values[:, 0], initial_heat_values[:, row_count - 1]], 0),
+        ), 0, 1)
     second_side = first_pass - implicit_weight * vertical_implicit_solve
     lanes = 128
     groups = plane_count * row_count // lanes

time: 57.9 us -> 52.8 us (0.912)
  starting transfers between devices: 20.3 us -> 15.7 us
  local copies, waits for them, and re-layouts: 7.39 us -> 6.77 us
  waiting for transfers between devices: 7.09 us -> 6.49 us
  other arithmetic: 2.86 us -> 3.45 us
    ppermute x2 -> x1, starting transfers between devices: 8.5 us -> 5.47 us  [halos(): low = lax.ppermute(last, axis, forward)]
    ppermute x2 -> x1, starting transfers between devices: 2.59 us -> 1.29 us  [halos(): high = lax.ppermute(first, axis, backward)]
    slice x2 -> x1, local copies, waits for them, and re-layouts: 2.04 us -> 1.16 us  [halos(): last = lax.index_in_dim(block, block.shape[dim] - 1, dim, keepdims=False)]
    ppermute x2 -> x1, waiting for transfers between devices: 0.95 us -> 0.35 us  [halos(): low = lax.ppermute(last, axis, forward)]
    another operation x0 -> x1, other arithmetic: none -> 0.6 us  [per_device(): jnp.stack([initial_heat_values[:, 0], initial_heat_values[:, row_count -...]
  transfers between devices with their start and end apart: 7 -> 5, of which waited for: 4 -> 4; matrix products, arithmetic and copies ran while one was open for 3% -> 2% of each run, Pallas kernels for 0% -> 0%
where the time goes in v8:
time: 52.8 us; the launch traced here: 52.4 us
  starting transfers between devices  15.7 us (30%)
  Pallas kernels  11.8 us (22%)
  blocking collectives  8.1 us (15%)
  local copies, waits for them, and re-layouts  6.77 us (13%)
  waiting for transfers between devices  6.49 us (12%)
  other arithmetic  3.45 us (7%)
    ppermute x3, starting transfers between devices, doubling_gather(): other = lax.ppermute(held, axis, [(i, i ^ step) for i in range(count)])  8.98 us
    all_gather x1, blocking collectives, distributed_solve(): gathered = lax.all_gather(reduced, axis)  8.1 us
    ppermute x3, waiting for transfers between devices, doubling_gather(): other = lax.ppermute(held, axis, [(i, i ^ step) for i in range(count)])  6.14 us
    pallas_call x2, Pallas kernels, partition_call(): pl.pallas_call(partition_kernel, out_shape=(jax.ShapeDtypeStruct((3, n) +...  5.61 us
    ppermute x1, starting transfers between devices, halos(): low = lax.ppermute(last, axis, forward)  5.47 us
    pallas_call x2, Pallas kernels, finish_call(): pl.pallas_call(finish_kernel, out_shape=jax.ShapeDtypeStruct((n,) + rest,...  4.24 us
    pallas_call x1, Pallas kernels, sweep_call(): pl.pallas_call(sweep_kernel, out_shape=jax.ShapeDtypeStruct(h_lines.shape...  1.91 us
    ppermute x1, starting transfers between devices, halos(): high = lax.ppermute(first, axis, backward)  1.29 us
  transfers between devices with their start and end apart: 5, of which 4 were waited for; matrix products, arithmetic and copies ran while one was open for 2% of the time, Pallas kernels for 0%

profile of v8, /device:TPU:0, one launch (start us, length us, event | category | flops | bytes accessed | tf_op | source)
XLA Modules:
  0.0 52.4 jit_solution(11832539603675460268)
XLA Ops:
  0.0 1.2 %fusion.8 = (f32[16,32,1]{2,1,0:T(8,128)S(1)}, f32[16,32,1]{2,1,0:T(8,128)S(1)}) fusion(f32[16,32,128]{2,1,0:T(8,128)} %param.2), kind=kLoop, calls=%fused_computation.18 | loop fusion | bytes 8192 | tf_op jit(solution)/shard_map/slice | solution.py:16
  1.3 1.3 %collective-permute-start.1 = (f32[16,32]{1,0:T(8,128)S(1)}, f32[16,32]{1,0:T(8,128)S(1)}, u32[]{:S(2)}, u32[]{:S(2)}) collective-permute-start(f32[16,32]{1,0:T(8,128)S(1)} %bitcast.37), channel_id=1, source_target_pairs={{1,0},{2,1},{3,2},{4,3},{5,4},{6,5},{7,6},{9,8},{10,9},{11,10},{12... | collective-permute-start | bytes 6152 | tf_op jit(solution)/shard_map/ppermute | solution.py:19
  2.8 5.5 %collective-permute-start = (f32[16,32]{1,0:T(8,128)S(1)}, f32[16,32]{1,0:T(8,128)S(1)}, u32[]{:S(2)}, u32[]{:S(2)}) collective-permute-start(f32[16,32]{1,0:T(8,128)S(1)} %bitcast.39), channel_id=1, source_target_pairs={{0,1},{1,2},{2,3},{3,4},{4,5},{5,6},{6,7},{8,9},{9,10},{10,11},{11... | collective-permute-start | bytes 6152 | tf_op jit(solution)/shard_map/ppermute | solution.py:18
  8.5 0.6 %pad_maximum_fusion.refs_0_ = f32[2,16,128]{2,1,0:T(8,128)} fusion(f32[1,16,128]{2,1,0:T(8,128)S(1)} %bitcast.34, f32[1,16,128]{2,1,0:T(8,128)S(1)} %bitcast.33), kind=kLoop, calls=%fused_computation.15 | loop fusion | flops 4096 | bytes 32768 | tf_op jit(solution)/shard_map/stack | solution.py:241
  10.4 0.8 %copy.34.h_ref = f32[128,4,128]{2,1,0:T(4,128)} copy(f32[128,4,128]{0,2,1:T(8,128)S(1)} %bitcast.29) | data formatting | bytes 524288 | tf_op jit(solution)/shard_map/reshape | solution.py:247
  11.2 0.9 %copy.31.h_ref = f32[32,16,128]{2,1,0:T(8,128)} copy(f32[32,16,128]{2,0,1:T(8,128)S(1)} %get-tuple-element.17) | data formatting | bytes 524288 | tf_op jit(solution)/shard_map/transpose | solution.py:235
  12.1 0.9 %copy.32.d_ref = f32[32,16,128]{2,1,0:T(8,128)} copy(f32[32,16,128]{2,0,1:T(8,128)S(1)} %get-tuple-element.13) | data formatting | bytes 524288 | tf_op jit(solution)/shard_map/transpose | solution.py:232
  13.0 2.3 %shard_map.28 = (f32[3,32,16,128]{3,2,1,0:T(8,128)}, f32[5,2,16,128]{3,2,1,0:T(8,128)}) custom-call(f32[32,16,128]{2,1,0:T(8,128)} %copy.31.h_ref, f32[32,16,128]{2,1,0:T(8,128)} %copy.32.d_ref, f32[2,16,128]{2,1,0:T(8,128)} %pad_maximum_fusion.refs_0_), custom_call_target="tpu_custom_call" | custom-call | tf_op jit(solution)/shard_map/pallas_call | solution.py:82
  15.2 8.1 %all-gather = f32[20,2,16,128]{3,2,1,0:T(8,128)} all-gather(f32[5,2,16,128]{3,2,1,0:T(8,128)} %get-tuple-element.9), channel_id=2, replica_groups=mesh['gx'=4,'gy'=8] {'gx'}, dimensions={0}, use_global_device_ids=true | all-gather | bytes 409600 | tf_op jit(solution)/shard_map/all_gather | solution.py:200
  23.3 2.1 %shard_map.29 = f32[32,16,128]{2,1,0:T(8,128)} custom-call(s32[1]{0:T(128)} %bitcast.3.position_ref, f32[4,5,2,16,128]{4,3,2,1,0:T(8,128)} %bitcast.30, f32[3,32,16,128]{3,2,1,0:T(8,128)} %get-tuple-element.10.responses_ref), custom_call_target="tpu_custom_call" | custom-call | tf_op jit(solution)/shard_map/pallas_call | solution.py:137
  25.4 1.0 %bitcast_subtract_fusion = f32[16,32,128]{2,1,0:T(8,128)S(1)} fusion(f32[32,16,128]{2,1,0:T(8,128)} %shard_map.29, f32[16,32,128]{2,1,0:T(8,128)S(1)} %get-tuple-element.14), kind=kLoop, calls=%fused_computation.8 | loop fusion | flops 131072 | bytes 786432 | tf_op jit(solution)/shard_map/sub | solution.py:243
  26.5 0.9 %copy.35.d_ref = f32[128,4,128]{2,1,0:T(4,128)} copy(f32[128,4,128]{0,2,1:T(8,128)S(1)} %bitcast.31) | data formatting | bytes 524288 | tf_op jit(solution)/shard_map/reshape | solution.py:246
  27.3 3.3 %shard_map.30 = (f32[3,128,4,128]{3,2,1,0:T(4,128)}, f32[4,2,4,128]{3,2,1,0:T(4,128)}) custom-call(f32[128,4,128]{2,1,0:T(4,128)} %copy.34.h_ref, f32[128,4,128]{2,1,0:T(4,128)} %copy.35.d_ref), custom_call_target="tpu_custom_call" | custom-call | tf_op jit(solution)/shard_map/pallas_call | solution.py:82
  30.6 2.4 %collective-permute-start.2 = (f32[1,4,2,4,128]{4,3,2,1,0:T(4,128)}, f32[1,4,2,4,128]{4,3,2,1,0:T(4,128)S(1)}, u32[]{:S(2)}, u32[]{:S(2)}) collective-permute-start(f32[1,4,2,4,128]{4,3,2,1,0:T(4,128)} %bitcast.35), channel_id=1, source_target_pairs={{0,1},{1,0},{2,3},{3,2},{4,5},{5,4},{6,7},{7,6},{8,9},{9,8},{10,11... | collective-permute-start | bytes 49160 | tf_op jit(solution)/shard_map/ppermute | solution.py:186
  33.0 2.0 %collective-permute-done.2 = f32[1,4,2,4,128]{4,3,2,1,0:T(4,128)S(1)} collective-permute-done((f32[1,4,2,4,128]{4,3,2,1,0:T(4,128)}, f32[1,4,2,4,128]{4,3,2,1,0:T(4,128)S(1)}, u32[]{:S(2)}, u32[]{:S(2)}) %collective-permute-start.2) | collective-permute-done | bytes 16416 | tf_op jit(solution)/shard_map/ppermute | solution.py:186
  35.0 3.5 %collective-permute-start.3 = (f32[2,4,2,4,128]{4,3,2,1,0:T(4,128)S(1)}, f32[2,4,2,4,128]{4,3,2,1,0:T(4,128)S(1)}, u32[]{:S(2)}, u32[]{:S(2)}) collective-permute-start(f32[2,4,2,4,128]{4,3,2,1,0:T(4,128)S(1)} %maximum_select_fusion.2), channel_id=1, source_target_pairs={{0,2},{1,3},{2,0},{3,1},{4,6},{5,7},{6,4},{7,5},{8,10},{9,11},{10,... | collective-permute-start | bytes 98312 | tf_op jit(solution)/shard_map/ppermute | solution.py:186
  38.5 1.9 %collective-permute-done.3 = f32[2,4,2,4,128]{4,3,2,1,0:T(4,128)S(1)} collective-permute-done((f32[2,4,2,4,128]{4,3,2,1,0:T(4,128)S(1)}, f32[2,4,2,4,128]{4,3,2,1,0:T(4,128)S(1)}, u32[]{:S(2)}, u32[]{:S(2)}) %collective-permute-start.3) | collective-permute-done | bytes 32800 | tf_op jit(solution)/shard_map/ppermute | solution.py:186
  40.5 3.1 %collective-permute-start.4 = (f32[4,4,2,4,128]{4,3,2,1,0:T(4,128)S(1)}, f32[4,4,2,4,128]{4,3,2,1,0:T(4,128)S(1)}, u32[]{:S(2)}, u32[]{:S(2)}) collective-permute-start(f32[4,4,2,4,128]{4,3,2,1,0:T(4,128)S(1)} %maximum_select_fusion.1), channel_id=1, source_target_pairs={{0,4},{1,5},{2,6},{3,7},{4,0},{5,1},{6,2},{7,3},{8,12},{9,13},{10,... | collective-permute-start | bytes 196616 | tf_op jit(solution)/shard_map/ppermute | solution.py:186
  43.6 2.2 %collective-permute-done.4 = f32[4,4,2,4,128]{4,3,2,1,0:T(4,128)S(1)} collective-permute-done((f32[4,4,2,4,128]{4,3,2,1,0:T(4,128)S(1)}, f32[4,4,2,4,128]{4,3,2,1,0:T(4,128)S(1)}, u32[]{:S(2)}, u32[]{:S(2)}) %collective-permute-start.4) | collective-permute-done | bytes 65568 | tf_op jit(solution)/shard_map/ppermute | solution.py:186
  45.8 0.7 %maximum_select_fusion.g_ref = f32[8,4,2,4,128]{4,3,2,1,0:T(4,128)} fusion(f32[4,4,2,4,128]{4,3,2,1,0:T(4,128)S(1)} %collective-permute-done.4, f32[4,4,2,4,128]{4,3,2,1,0:T(4,128)S(1)} %maximum_select_fusion.1, pred[]{:T(512)S(6)} %eq.13), kind=kLoop, calls=%fused_computation.11 | loop fusion | flops 98304 | bytes 262145 | tf_op jit(solution)/shard_map/jit(_where)/select_n | solution.py:188
  46.5 2.2 %shard_map.31 = f32[128,4,128]{2,1,0:T(4,128)} custom-call(s32[1]{0:T(128)} %bitcast.position_ref, f32[8,4,2,4,128]{4,3,2,1,0:T(4,128)} %maximum_select_fusion.g_ref, f32[3,128,4,128]{3,2,1,0:T(4,128)} %get-tuple-element.12.responses_ref), custom_call_target="tpu_custom_call" | custom-call | tf_op jit(solution)/shard_map/pallas_call | solution.py:137
  48.7 1.1 %copy.36 = f32[128,4,128]{0,2,1:T(8,128)S(1)} copy(f32[128,4,128]{2,1,0:T(4,128)} %shard_map.31) | data formatting | bytes 524288 | tf_op jit(solution)/shard_map/pallas_call | solution.py:137
  49.7 0.8 %multiply_subtract_fusion.d_ref = f32[16,32,128]{2,1,0:T(8,128)} fusion(f32[16,32,128]{2,1,0:T(8,128)S(1)} %bitcast.32, f32[16,32,128]{2,1,0:T(8,128)S(1)} %copy-done, f32[16,32,128]{2,1,0:T(8,128)S(1)} %copy-done.2), kind=kLoop, calls=%fused_computation.9 | loop fusion | flops 458752 | bytes 1048576 | tf_op jit(solution)/shard_map/sub | solution.py:250
  50.5 1.9 %shard_map.32 = f32[16,32,128]{2,1,0:T(8,128)} custom-call(f32[16,32,128]{2,1,0:T(8,128)} %copy-done.1, f32[16,32,128]{2,1,0:T(8,128)} %multiply_subtract_fusion.d_ref), custom_call_target="tpu_custom_call" | custom-call | tf_op jit(solution)/shard_map/pallas_call | solution.py:171
  (20 shorter events, 1.8 us)
Async XLA Ops:
  1.2 7.1 %copy-start = (f32[16,32,128]{2,1,0:T(8,128)S(1)}, f32[16,32,128]{2,1,0:T(8,128)}, u32[]{:S(2)}) copy-start(f32[16,32,128]{2,1,0:T(8,128)} %param.2) | copy-start | bytes 786436
  1.3 7.8 %collective-permute-start.1 = (f32[16,32]{1,0:T(8,128)S(1)}, f32[16,32]{1,0:T(8,128)S(1)}, u32[]{:S(2)}, u32[]{:S(2)}) collective-permute-start(f32[16,32]{1,0:T(8,128)S(1)} %bitcast.37), channel_id=1, source_target_pairs={{1,0},{2,1},{3,2},{4,3},{5,4},{6,5},{7,6},{9,8},{10,9},{11,10},{12... | collective-permute-start | bytes 6152 | tf_op jit(solution)/shard_map/ppermute | solution.py:19
  2.8 6.8 %collective-permute-start = (f32[16,32]{1,0:T(8,128)S(1)}, f32[16,32]{1,0:T(8,128)S(1)}, u32[]{:S(2)}, u32[]{:S(2)}) collective-permute-start(f32[16,32]{1,0:T(8,128)S(1)} %bitcast.39), channel_id=1, source_target_pairs={{0,1},{1,2},{2,3},{3,4},{4,5},{5,6},{6,7},{8,9},{9,10},{10,11},{11... | collective-permute-start | bytes 6152 | tf_op jit(solution)/shard_map/ppermute | solution.py:18
  9.1 1.0 %copy-start.2 = (f32[16,32,128]{2,1,0:T(8,128)S(1)}, f32[16,32,128]{2,1,0:T(8,128)}, u32[]{:S(2)}) copy-start(f32[16,32,128]{2,1,0:T(8,128)} %param.3) | copy-start | bytes 786436
  10.4 0.8 %copy-start.1 = (f32[16,32,128]{2,1,0:T(8,128)}, f32[16,32,128]{2,1,0:T(8,128)S(1)}, u32[]{:S(2)}) copy-start(f32[16,32,128]{2,1,0:T(8,128)S(1)} %get-tuple-element.18.h_ref) | copy-start | bytes 786436
  30.6 4.4 %copy-start.3 = (f32[4,2,4,128]{3,2,1,0:T(4,128)S(1)}, f32[4,2,4,128]{3,2,1,0:T(4,128)}, u32[]{:S(2)}) copy-start(f32[4,2,4,128]{3,2,1,0:T(4,128)} %get-tuple-element.11) | copy-start | bytes 49156
  30.6 4.4 %collective-permute-start.2 = (f32[1,4,2,4,128]{4,3,2,1,0:T(4,128)}, f32[1,4,2,4,128]{4,3,2,1,0:T(4,128)S(1)}, u32[]{:S(2)}, u32[]{:S(2)}) collective-permute-start(f32[1,4,2,4,128]{4,3,2,1,0:T(4,128)} %bitcast.35), channel_id=1, source_target_pairs={{0,1},{1,0},{2,3},{3,2},{4,5},{5,4},{6,7},{7,6},{8,9},{9,8},{10,11... | collective-permute-start | bytes 49160 | tf_op jit(solution)/shard_map/ppermute | solution.py:186
  35.0 5.4 %collective-permute-start.3 = (f32[2,4,2,4,128]{4,3,2,1,0:T(4,128)S(1)}, f32[2,4,2,4,128]{4,3,2,1,0:T(4,128)S(1)}, u32[]{:S(2)}, u32[]{:S(2)}) collective-permute-start(f32[2,4,2,4,128]{4,3,2,1,0:T(4,128)S(1)} %maximum_select_fusion.2), channel_id=1, source_target_pairs={{0,2},{1,3},{2,0},{3,1},{4,6},{5,7},{6,4},{7,5},{8,10},{9,11},{10,... | collective-permute-start | bytes 98312 | tf_op jit(solution)/shard_map/ppermute | solution.py:186
  40.5 5.3 %collective-permute-start.4 = (f32[4,4,2,4,128]{4,3,2,1,0:T(4,128)S(1)}, f32[4,4,2,4,128]{4,3,2,1,0:T(4,128)S(1)}, u32[]{:S(2)}, u32[]{:S(2)}) collective-permute-start(f32[4,4,2,4,128]{4,3,2,1,0:T(4,128)S(1)} %maximum_select_fusion.1), channel_id=1, source_target_pairs={{0,4},{1,5},{2,6},{3,7},{4,0},{5,1},{6,2},{7,3},{8,12},{9,13},{10,... | collective-permute-start | bytes 196616 | tf_op jit(solution)/shard_map/ppermute | solution.py:186

commit v9 on v8

--- a/solution.py
+++ b/solution.py
@@ -32,16 +32,17 @@
     vf = jnp.zeros_like(ratio)
     for i in range(1, n - 1):
         hi = h_ref[i]
-        denom = 1.0 + 2.0 * hi + hi * ratio
-        ratio = -hi / denom
+        pivot = 1.0 / (1.0 + 2.0 * hi + hi * ratio)
+        scaled = hi * pivot
+        ratio = -scaled
         if i == 1:
-            vb = d_ref[i] / denom
-            vf = hi / denom
+            vb = d_ref[i] * pivot
+            vf = scaled
         else:
-            vb = (d_ref[i] + hi * vb) / denom
-            vf = (hi * vf) / denom
+            vb = (d_ref[i] + hi * vb) * pivot
+            vf = scaled * vf
         if i == n - 2:
-            vl = hi / denom
+            vl = scaled
         ratio_ref[i] = ratio
         out_ref[0, i] = vb
         out_ref[1, i] = vf
@@ -109,12 +110,12 @@
         if g_ref.shape[1] == 5 and q == 1 and k < count - 1:
             side = side - upper * g_ref[k + 1, 4, 0]
         if j == 0:
-            denom = centre
-            value = side / denom
+            pivot = 1.0 / centre
+            value = side * pivot
         else:
-            denom = centre - lower * ratio
-            value = (side - lower * value) / denom
-        ratio = upper / denom
+            pivot = 1.0 / (centre - lower * ratio)
+            value = (side - lower * value) * pivot
+        ratio = upper * pivot
         ratio_ref[j] = ratio
         ends_ref[j] = value
     x = value
@@ -153,12 +154,12 @@
     for i in range(n):
         hi = h_ref[i]
         if i == 0:
-            denom = 1.0 + 2.0 * hi
-            value = d_ref[i] / denom
+            pivot = 1.0 / (1.0 + 2.0 * hi)
+            value = d_ref[i] * pivot
         else:
-            denom = 1.0 + 2.0 * hi + hi * ratio
-            value = (d_ref[i] + hi * value) / denom
-        ratio = -hi / denom
+            pivot = 1.0 / (1.0 + 2.0 * hi + hi * ratio)
+            value = (d_ref[i] + hi * value) * pivot
+        ratio = -hi * pivot
         ratio_ref[i] = ratio
         out_ref[i] = value
     x = value

time: 52.8 us -> 53 us (level)
  no operation moved by 1% of the time
where the time goes in v9:
time: 53 us; the launch traced here: 52.6 us
  starting transfers between devices  15.7 us (30%)
  Pallas kernels  11.9 us (22%)
  blocking collectives  8.1 us (15%)
  local copies, waits for them, and re-layouts  6.77 us (13%)
  waiting for transfers between devices  6.49 us (12%)
  other arithmetic  3.45 us (7%)
    ppermute x3, starting transfers between devices, doubling_gather(): other = lax.ppermute(held, axis, [(i, i ^ step) for i in range(count)])  8.98 us
    all_gather x1, blocking collectives, distributed_solve(): gathered = lax.all_gather(reduced, axis)  8.1 us
    ppermute x3, waiting for transfers between devices, doubling_gather(): other = lax.ppermute(held, axis, [(i, i ^ step) for i in range(count)])  6.14 us
    pallas_call x2, Pallas kernels, partition_call(): pl.pallas_call(partition_kernel, out_shape=(jax.ShapeDtypeStruct((3, n) +...  5.77 us
    ppermute x1, starting transfers between devices, halos(): low = lax.ppermute(last, axis, forward)  5.47 us
    pallas_call x2, Pallas kernels, finish_call(): pl.pallas_call(finish_kernel, out_shape=jax.ShapeDtypeStruct((n,) + rest,...  4.24 us
    pallas_call x1, Pallas kernels, sweep_call(): pl.pallas_call(sweep_kernel, out_shape=jax.ShapeDtypeStruct(h_lines.shape...  1.91 us
    ppermute x1, starting transfers between devices, halos(): high = lax.ppermute(first, axis, backward)  1.29 us
  transfers between devices with their start and end apart: 5, of which 4 were waited for; matrix products, arithmetic and copies ran while one was open for 2% of the time, Pallas kernels for 0%

profile of v9, /device:TPU:0, one launch (start us, length us, event | category | flops | bytes accessed | tf_op | source)
XLA Modules:
  0.0 52.6 jit_solution(16190865193753595151)
XLA Ops:
  0.0 1.2 %fusion.8 = (f32[16,32,1]{2,1,0:T(8,128)S(1)}, f32[16,32,1]{2,1,0:T(8,128)S(1)}) fusion(f32[16,32,128]{2,1,0:T(8,128)} %param.2), kind=kLoop, calls=%fused_computation.18 | loop fusion | bytes 8192 | tf_op jit(solution)/shard_map/slice | solution.py:16
  1.3 1.3 %collective-permute-start.1 = (f32[16,32]{1,0:T(8,128)S(1)}, f32[16,32]{1,0:T(8,128)S(1)}, u32[]{:S(2)}, u32[]{:S(2)}) collective-permute-start(f32[16,32]{1,0:T(8,128)S(1)} %bitcast.37), channel_id=1, source_target_pairs={{1,0},{2,1},{3,2},{4,3},{5,4},{6,5},{7,6},{9,8},{10,9},{11,10},{12... | collective-permute-start | bytes 6152 | tf_op jit(solution)/shard_map/ppermute | solution.py:19
  2.8 5.5 %collective-permute-start = (f32[16,32]{1,0:T(8,128)S(1)}, f32[16,32]{1,0:T(8,128)S(1)}, u32[]{:S(2)}, u32[]{:S(2)}) collective-permute-start(f32[16,32]{1,0:T(8,128)S(1)} %bitcast.39), channel_id=1, source_target_pairs={{0,1},{1,2},{2,3},{3,4},{4,5},{5,6},{6,7},{8,9},{9,10},{10,11},{11... | collective-permute-start | bytes 6152 | tf_op jit(solution)/shard_map/ppermute | solution.py:18
  8.5 0.6 %pad_maximum_fusion.refs_0_ = f32[2,16,128]{2,1,0:T(8,128)} fusion(f32[1,16,128]{2,1,0:T(8,128)S(1)} %bitcast.34, f32[1,16,128]{2,1,0:T(8,128)S(1)} %bitcast.33), kind=kLoop, calls=%fused_computation.15 | loop fusion | flops 4096 | bytes 32768 | tf_op jit(solution)/shard_map/stack | solution.py:242
  10.4 0.8 %copy.34.h_ref = f32[128,4,128]{2,1,0:T(4,128)} copy(f32[128,4,128]{0,2,1:T(8,128)S(1)} %bitcast.29) | data formatting | bytes 524288 | tf_op jit(solution)/shard_map/reshape | solution.py:248
  11.2 0.9 %copy.31.h_ref = f32[32,16,128]{2,1,0:T(8,128)} copy(f32[32,16,128]{2,0,1:T(8,128)S(1)} %get-tuple-element.17) | data formatting | bytes 524288 | tf_op jit(solution)/shard_map/transpose | solution.py:236
  12.1 0.9 %copy.32.d_ref = f32[32,16,128]{2,1,0:T(8,128)} copy(f32[32,16,128]{2,0,1:T(8,128)S(1)} %get-tuple-element.13) | data formatting | bytes 524288 | tf_op jit(solution)/shard_map/transpose | solution.py:233
  13.0 2.3 %shard_map.28 = (f32[3,32,16,128]{3,2,1,0:T(8,128)}, f32[5,2,16,128]{3,2,1,0:T(8,128)}) custom-call(f32[32,16,128]{2,1,0:T(8,128)} %copy.31.h_ref, f32[32,16,128]{2,1,0:T(8,128)} %copy.32.d_ref, f32[2,16,128]{2,1,0:T(8,128)} %pad_maximum_fusion.refs_0_), custom_call_target="tpu_custom_call" | custom-call | tf_op jit(solution)/shard_map/pallas_call | solution.py:83
  15.3 8.1 %all-gather = f32[20,2,16,128]{3,2,1,0:T(8,128)} all-gather(f32[5,2,16,128]{3,2,1,0:T(8,128)} %get-tuple-element.9), channel_id=2, replica_groups=mesh['gx'=4,'gy'=8] {'gx'}, dimensions={0}, use_global_device_ids=true | all-gather | bytes 409600 | tf_op jit(solution)/shard_map/all_gather | solution.py:201
  23.4 2.1 %shard_map.29 = f32[32,16,128]{2,1,0:T(8,128)} custom-call(s32[1]{0:T(128)} %bitcast.3.position_ref, f32[4,5,2,16,128]{4,3,2,1,0:T(8,128)} %bitcast.30, f32[3,32,16,128]{3,2,1,0:T(8,128)} %get-tuple-element.10.responses_ref), custom_call_target="tpu_custom_call" | custom-call | tf_op jit(solution)/shard_map/pallas_call | solution.py:138
  25.4 1.0 %bitcast_subtract_fusion = f32[16,32,128]{2,1,0:T(8,128)S(1)} fusion(f32[32,16,128]{2,1,0:T(8,128)} %shard_map.29, f32[16,32,128]{2,1,0:T(8,128)S(1)} %get-tuple-element.14), kind=kLoop, calls=%fused_computation.8 | loop fusion | flops 131072 | bytes 786432 | tf_op jit(solution)/shard_map/sub | solution.py:244
  26.5 0.9 %copy.35.d_ref = f32[128,4,128]{2,1,0:T(4,128)} copy(f32[128,4,128]{0,2,1:T(8,128)S(1)} %bitcast.31) | data formatting | bytes 524288 | tf_op jit(solution)/shard_map/reshape | solution.py:247
  27.3 3.5 %shard_map.30 = (f32[3,128,4,128]{3,2,1,0:T(4,128)}, f32[4,2,4,128]{3,2,1,0:T(4,128)}) custom-call(f32[128,4,128]{2,1,0:T(4,128)} %copy.34.h_ref, f32[128,4,128]{2,1,0:T(4,128)} %copy.35.d_ref), custom_call_target="tpu_custom_call" | custom-call | tf_op jit(solution)/shard_map/pallas_call | solution.py:83
  30.8 2.4 %collective-permute-start.2 = (f32[1,4,2,4,128]{4,3,2,1,0:T(4,128)}, f32[1,4,2,4,128]{4,3,2,1,0:T(4,128)S(1)}, u32[]{:S(2)}, u32[]{:S(2)}) collective-permute-start(f32[1,4,2,4,128]{4,3,2,1,0:T(4,128)} %bitcast.35), channel_id=1, source_target_pairs={{0,1},{1,0},{2,3},{3,2},{4,5},{5,4},{6,7},{7,6},{8,9},{9,8},{10,11... | collective-permute-start | bytes 49160 | tf_op jit(solution)/shard_map/ppermute | solution.py:187
  33.2 2.0 %collective-permute-done.2 = f32[1,4,2,4,128]{4,3,2,1,0:T(4,128)S(1)} collective-permute-done((f32[1,4,2,4,128]{4,3,2,1,0:T(4,128)}, f32[1,4,2,4,128]{4,3,2,1,0:T(4,128)S(1)}, u32[]{:S(2)}, u32[]{:S(2)}) %collective-permute-start.2) | collective-permute-done | bytes 16416 | tf_op jit(solution)/shard_map/ppermute | solution.py:187
  35.2 3.5 %collective-permute-start.3 = (f32[2,4,2,4,128]{4,3,2,1,0:T(4,128)S(1)}, f32[2,4,2,4,128]{4,3,2,1,0:T(4,128)S(1)}, u32[]{:S(2)}, u32[]{:S(2)}) collective-permute-start(f32[2,4,2,4,128]{4,3,2,1,0:T(4,128)S(1)} %maximum_select_fusion.2), channel_id=1, source_target_pairs={{0,2},{1,3},{2,0},{3,1},{4,6},{5,7},{6,4},{7,5},{8,10},{9,11},{10,... | collective-permute-start | bytes 98312 | tf_op jit(solution)/shard_map/ppermute | solution.py:187
  38.7 1.9 %collective-permute-done.3 = f32[2,4,2,4,128]{4,3,2,1,0:T(4,128)S(1)} collective-permute-done((f32[2,4,2,4,128]{4,3,2,1,0:T(4,128)S(1)}, f32[2,4,2,4,128]{4,3,2,1,0:T(4,128)S(1)}, u32[]{:S(2)}, u32[]{:S(2)}) %collective-permute-start.3) | collective-permute-done | bytes 32800 | tf_op jit(solution)/shard_map/ppermute | solution.py:187
  40.6 3.1 %collective-permute-start.4 = (f32[4,4,2,4,128]{4,3,2,1,0:T(4,128)S(1)}, f32[4,4,2,4,128]{4,3,2,1,0:T(4,128)S(1)}, u32[]{:S(2)}, u32[]{:S(2)}) collective-permute-start(f32[4,4,2,4,128]{4,3,2,1,0:T(4,128)S(1)} %maximum_select_fusion.1), channel_id=1, source_target_pairs={{0,4},{1,5},{2,6},{3,7},{4,0},{5,1},{6,2},{7,3},{8,12},{9,13},{10,... | collective-permute-start | bytes 196616 | tf_op jit(solution)/shard_map/ppermute | solution.py:187
  43.7 2.2 %collective-permute-done.4 = f32[4,4,2,4,128]{4,3,2,1,0:T(4,128)S(1)} collective-permute-done((f32[4,4,2,4,128]{4,3,2,1,0:T(4,128)S(1)}, f32[4,4,2,4,128]{4,3,2,1,0:T(4,128)S(1)}, u32[]{:S(2)}, u32[]{:S(2)}) %collective-permute-start.4) | collective-permute-done | bytes 65568 | tf_op jit(solution)/shard_map/ppermute | solution.py:187
  46.0 0.7 %maximum_select_fusion.g_ref = f32[8,4,2,4,128]{4,3,2,1,0:T(4,128)} fusion(f32[4,4,2,4,128]{4,3,2,1,0:T(4,128)S(1)} %collective-permute-done.4, f32[4,4,2,4,128]{4,3,2,1,0:T(4,128)S(1)} %maximum_select_fusion.1, pred[]{:T(512)S(6)} %eq.13), kind=kLoop, calls=%fused_computation.11 | loop fusion | flops 98304 | bytes 262145 | tf_op jit(solution)/shard_map/jit(_where)/select_n | solution.py:189
  46.6 2.2 %shard_map.31 = f32[128,4,128]{2,1,0:T(4,128)} custom-call(s32[1]{0:T(128)} %bitcast.position_ref, f32[8,4,2,4,128]{4,3,2,1,0:T(4,128)} %maximum_select_fusion.g_ref, f32[3,128,4,128]{3,2,1,0:T(4,128)} %get-tuple-element.12.responses_ref), custom_call_target="tpu_custom_call" | custom-call | tf_op jit(solution)/shard_map/pallas_call | solution.py:138
  48.8 1.1 %copy.36 = f32[128,4,128]{0,2,1:T(8,128)S(1)} copy(f32[128,4,128]{2,1,0:T(4,128)} %shard_map.31) | data formatting | bytes 524288 | tf_op jit(solution)/shard_map/pallas_call | solution.py:138
  49.9 0.8 %multiply_subtract_fusion.d_ref = f32[16,32,128]{2,1,0:T(8,128)} fusion(f32[16,32,128]{2,1,0:T(8,128)S(1)} %bitcast.32, f32[16,32,128]{2,1,0:T(8,128)S(1)} %copy-done, f32[16,32,128]{2,1,0:T(8,128)S(1)} %copy-done.2), kind=kLoop, calls=%fused_computation.9 | loop fusion | flops 458752 | bytes 1048576 | tf_op jit(solution)/shard_map/sub | solution.py:251
  50.7 1.9 %shard_map.32 = f32[16,32,128]{2,1,0:T(8,128)} custom-call(f32[16,32,128]{2,1,0:T(8,128)} %copy-done.1, f32[16,32,128]{2,1,0:T(8,128)} %multiply_subtract_fusion.d_ref), custom_call_target="tpu_custom_call" | custom-call | tf_op jit(solution)/shard_map/pallas_call | solution.py:172
  (20 shorter events, 1.8 us)
Async XLA Ops:
  1.2 7.1 %copy-start = (f32[16,32,128]{2,1,0:T(8,128)S(1)}, f32[16,32,128]{2,1,0:T(8,128)}, u32[]{:S(2)}) copy-start(f32[16,32,128]{2,1,0:T(8,128)} %param.2) | copy-start | bytes 786436
  1.3 7.8 %collective-permute-start.1 = (f32[16,32]{1,0:T(8,128)S(1)}, f32[16,32]{1,0:T(8,128)S(1)}, u32[]{:S(2)}, u32[]{:S(2)}) collective-permute-start(f32[16,32]{1,0:T(8,128)S(1)} %bitcast.37), channel_id=1, source_target_pairs={{1,0},{2,1},{3,2},{4,3},{5,4},{6,5},{7,6},{9,8},{10,9},{11,10},{12... | collective-permute-start | bytes 6152 | tf_op jit(solution)/shard_map/ppermute | solution.py:19
  2.8 6.8 %collective-permute-start = (f32[16,32]{1,0:T(8,128)S(1)}, f32[16,32]{1,0:T(8,128)S(1)}, u32[]{:S(2)}, u32[]{:S(2)}) collective-permute-start(f32[16,32]{1,0:T(8,128)S(1)} %bitcast.39), channel_id=1, source_target_pairs={{0,1},{1,2},{2,3},{3,4},{4,5},{5,6},{6,7},{8,9},{9,10},{10,11},{11... | collective-permute-start | bytes 6152 | tf_op jit(solution)/shard_map/ppermute | solution.py:18
  9.1 1.0 %copy-start.2 = (f32[16,32,128]{2,1,0:T(8,128)S(1)}, f32[16,32,128]{2,1,0:T(8,128)}, u32[]{:S(2)}) copy-start(f32[16,32,128]{2,1,0:T(8,128)} %param.3) | copy-start | bytes 786436
  10.4 0.8 %copy-start.1 = (f32[16,32,128]{2,1,0:T(8,128)}, f32[16,32,128]{2,1,0:T(8,128)S(1)}, u32[]{:S(2)}) copy-start(f32[16,32,128]{2,1,0:T(8,128)S(1)} %get-tuple-element.18.h_ref) | copy-start | bytes 786436
  30.8 4.4 %copy-start.3 = (f32[4,2,4,128]{3,2,1,0:T(4,128)S(1)}, f32[4,2,4,128]{3,2,1,0:T(4,128)}, u32[]{:S(2)}) copy-start(f32[4,2,4,128]{3,2,1,0:T(4,128)} %get-tuple-element.11) | copy-start | bytes 49156
  30.8 4.4 %collective-permute-start.2 = (f32[1,4,2,4,128]{4,3,2,1,0:T(4,128)}, f32[1,4,2,4,128]{4,3,2,1,0:T(4,128)S(1)}, u32[]{:S(2)}, u32[]{:S(2)}) collective-permute-start(f32[1,4,2,4,128]{4,3,2,1,0:T(4,128)} %bitcast.35), channel_id=1, source_target_pairs={{0,1},{1,0},{2,3},{3,2},{4,5},{5,4},{6,7},{7,6},{8,9},{9,8},{10,11... | collective-permute-start | bytes 49160 | tf_op jit(solution)/shard_map/ppermute | solution.py:187
  35.2 5.4 %collective-permute-start.3 = (f32[2,4,2,4,128]{4,3,2,1,0:T(4,128)S(1)}, f32[2,4,2,4,128]{4,3,2,1,0:T(4,128)S(1)}, u32[]{:S(2)}, u32[]{:S(2)}) collective-permute-start(f32[2,4,2,4,128]{4,3,2,1,0:T(4,128)S(1)} %maximum_select_fusion.2), channel_id=1, source_target_pairs={{0,2},{1,3},{2,0},{3,1},{4,6},{5,7},{6,4},{7,5},{8,10},{9,11},{10,... | collective-permute-start | bytes 98312 | tf_op jit(solution)/shard_map/ppermute | solution.py:187
  40.6 5.3 %collective-permute-start.4 = (f32[4,4,2,4,128]{4,3,2,1,0:T(4,128)S(1)}, f32[4,4,2,4,128]{4,3,2,1,0:T(4,128)S(1)}, u32[]{:S(2)}, u32[]{:S(2)}) collective-permute-start(f32[4,4,2,4,128]{4,3,2,1,0:T(4,128)S(1)} %maximum_select_fusion.1), channel_id=1, source_target_pairs={{0,4},{1,5},{2,6},{3,7},{4,0},{5,1},{6,2},{7,3},{8,12},{9,13},{10,... | collective-permute-start | bytes 196616 | tf_op jit(solution)/shard_map/ppermute | solution.py:187

commit v10 on v8

--- a/solution.py
+++ b/solution.py
@@ -1,3 +1,5 @@
+import functools
+
 import jax
 import jax.numpy as jnp
 from jax import lax
@@ -20,69 +22,82 @@
     return jnp.expand_dims(low, dim), jnp.expand_dims(high, dim)
 
 
-def partition_kernel(h_ref, d_ref, *refs):
+def line(ref, lead, i, axis):
+    if axis == 0:
+        return ref[lead + (i,)]
+    return ref[lead + (slice(None), i)]
+
+
+def put(ref, lead, i, value, axis):
+    if axis == 0:
+        ref[lead + (i,)] = value
+    else:
+        ref[lead + (slice(None), i)] = value
+
+
+def partition_kernel(axis, h_ref, d_ref, *refs):
     if len(refs) == 4:
         edges_ref, out_ref, red_ref, ratio_ref = refs
     else:
         edges_ref = None
         out_ref, red_ref, ratio_ref = refs
-    n = h_ref.shape[0]
-    ratio = jnp.zeros(h_ref.shape[1:], jnp.float32)
+    n = h_ref.shape[axis]
+    ratio = jnp.zeros(ratio_ref.shape[1:], jnp.float32)
     vb = jnp.zeros_like(ratio)
     vf = jnp.zeros_like(ratio)
     for i in range(1, n - 1):
-        hi = h_ref[i]
+        hi = line(h_ref, (), i, axis)
         denom = 1.0 + 2.0 * hi + hi * ratio
         ratio = -hi / denom
         if i == 1:
-            vb = d_ref[i] / denom
+            vb = line(d_ref, (), i, axis) / denom
             vf = hi / denom
         else:
-            vb = (d_ref[i] + hi * vb) / denom
+            vb = (line(d_ref, (), i, axis) + hi * vb) / denom
             vf = (hi * vf) / denom
         if i == n - 2:
             vl = hi / denom
         ratio_ref[i] = ratio
-        out_ref[0, i] = vb
-        out_ref[1, i] = vf
+        put(out_ref, (0,), i, vb, axis)
+        put(out_ref, (1,), i, vf, axis)
     b, f, l = vb, vf, vl
-    out_ref[2, n - 2] = l
+    put(out_ref, (2,), n - 2, l, axis)
     for i in range(n - 3, 0, -1):
         r = ratio_ref[i]
-        b = out_ref[0, i] - r * b
-        f = out_ref[1, i] - r * f
+        b = line(out_ref, (0,), i, axis) - r * b
+        f = line(out_ref, (1,), i, axis) - r * f
         l = -r * l
-        out_ref[0, i] = b
-        out_ref[1, i] = f
-        out_ref[2, i] = l
+        put(out_ref, (0,), i, b, axis)
+        put(out_ref, (1,), i, f, axis)
+        put(out_ref, (2,), i, l, axis)
     zero = jnp.zeros_like(ratio)
     for k in range(3):
-        out_ref[k, 0] = zero
-        out_ref[k, n - 1] = zero
-    rh = h_ref[0]
-    rt = h_ref[n - 1]
+        put(out_ref, (k,), 0, zero, axis)
+        put(out_ref, (k,), n - 1, zero, axis)
+    rh = line(h_ref, (), 0, axis)
+    rt = line(h_ref, (), n - 1, axis)
     red_ref[0, 0] = -rh
-    red_ref[0, 1] = -rt * out_ref[1, n - 2]
-    red_ref[1, 0] = 1.0 + 2.0 * rh - rh * out_ref[1, 1]
-    red_ref[1, 1] = 1.0 + 2.0 * rt - rt * out_ref[2, n - 2]
-    red_ref[2, 0] = -rh * out_ref[2, 1]
+    red_ref[0, 1] = -rt * line(out_ref, (1,), n - 2, axis)
+    red_ref[1, 0] = 1.0 + 2.0 * rh - rh * line(out_ref, (1,), 1, axis)
+    red_ref[1, 1] = 1.0 + 2.0 * rt - rt * line(out_ref, (2,), n - 2, axis)
+    red_ref[2, 0] = -rh * line(out_ref, (2,), 1, axis)
     red_ref[2, 1] = -rt
-    red_ref[3, 0] = d_ref[0] + rh * out_ref[0, 1]
-    red_ref[3, 1] = d_ref[n - 1] + rt * out_ref[0, n - 2]
+    red_ref[3, 0] = line(d_ref, (), 0, axis) + rh * line(out_ref, (0,), 1, axis)
+    red_ref[3, 1] = line(d_ref, (), n - 1, axis) + rt * line(out_ref, (0,), n - 2, axis)
     if edges_ref is not None:
         red_ref[4, 0] = edges_ref[0]
         red_ref[4, 1] = edges_ref[1]
 
 
-def partition_call(h_lines, d_lines, edges):
-    n = h_lines.shape[0]
-    rest = h_lines.shape[1:]
+def partition_call(h_lines, d_lines, edges, axis):
+    n = h_lines.shape[axis]
+    rest = h_lines.shape[:axis] + h_lines.shape[axis + 1 :]
     operands = (h_lines, d_lines) if edges is None else (h_lines, d_lines, edges)
     rows = 4 if edges is None else 5
     return pl.pallas_call(
-        partition_kernel,
+        functools.partial(partition_kernel, axis),
         out_shape=(
-            jax.ShapeDtypeStruct((3, n) + rest, jnp.float32),
+            jax.ShapeDtypeStruct((3,) + h_lines.shape, jnp.float32),
             jax.ShapeDtypeStruct((rows, 2) + rest, jnp.float32),
         ),
         scratch_shapes=[pltpu_vmem((n,) + rest)],
@@ -93,9 +108,9 @@
     return pltpu.VMEM(shape, jnp.float32)
 
 
-def finish_kernel(position_ref, g_ref, responses_ref, out_ref, ratio_ref, ends_ref):
+def finish_kernel(axis, position_ref, g_ref, responses_ref, out_ref, ratio_ref, ends_ref):
     count = g_ref.shape[0]
-    n = responses_ref.shape[1]
+    n = responses_ref.shape[axis + 1]
     ratio = None
     value = None
     for j in range(2 * count):
@@ -124,19 +139,18 @@
     mine = position_ref[0]
     head = ends_ref[2 * mine]
     tail = ends_ref[2 * mine + 1]
-    out_ref[0] = head
-    out_ref[n - 1] = tail
+    put(out_ref, (), 0, head, axis)
+    put(out_ref, (), n - 1, tail, axis)
     for i in range(1, n - 1):
-        out_ref[i] = responses_ref[0, i] + responses_ref[1, i] * head + responses_ref[2, i] * tail
-
-
-def finish_call(gathered, responses, position):
+        put(out_ref, (), i, line(responses_ref, (0,), i, axis) + line(responses_ref, (1,), i, axis) * head + line(responses_ref, (2,), i, axis) * tail, axis)
+
+
+def finish_call(gathered, responses, position, axis):
     count = gathered.shape[0]
     rest = gathered.shape[3:]
-    n = responses.shape[1]
     return pl.pallas_call(
-        finish_kernel,
-        out_shape=jax.ShapeDtypeStruct((n,) + rest, jnp.float32),
+        functools.partial(finish_kernel, axis),
+        out_shape=jax.ShapeDtypeStruct(responses.shape[1:], jnp.float32),
         in_specs=[
             pl.BlockSpec(memory_space=pltpu.SMEM),
             pl.BlockSpec(memory_space=pltpu.VMEM),
@@ -192,14 +206,14 @@
     return held
 
 
-def distributed_solve(h_lines, d_lines, axis, doubling, edges=None):
-    responses, reduced = partition_call(h_lines, d_lines, edges)
+def distributed_solve(h_lines, d_lines, axis, doubling, edges=None, line_axis=0):
+    responses, reduced = partition_call(h_lines, d_lines, edges, line_axis)
     if doubling:
         gathered = doubling_gather(reduced, axis)
     else:
         gathered = lax.all_gather(reduced, axis)
     position = jnp.reshape(lax.axis_index(axis), (1,)).astype(jnp.int32)
-    return finish_call(gathered, responses, position)
+    return finish_call(gathered, responses, position, line_axis)
 
 
 def per_device(initial_heat_values, spreading_coefficients):
@@ -229,17 +243,15 @@
         + vertical_implicit_solve
         + depth_implicit_solve
     )
-    first_side = jnp.moveaxis(
-        forward_euler_increment - implicit_weight * horizontal_implicit_solve, 1, 0
-    )
-    first_rate = jnp.moveaxis(half_rate, 1, 0)
-    first_pass = jnp.moveaxis(distributed_solve(
-            first_rate,
-            first_side,
-            "gx",
-            False,
-            jnp.stack([initial_heat_values[:, 0], initial_heat_values[:, row_count - 1]], 0),
-        ), 0, 1)
+    first_side = forward_euler_increment - implicit_weight * horizontal_implicit_solve
+    first_pass = distributed_solve(
+        half_rate,
+        first_side,
+        "gx",
+        False,
+        jnp.stack([initial_heat_values[:, 0], initial_heat_values[:, row_count - 1]], 0),
+        1,
+    )
     second_side = first_pass - implicit_weight * vertical_implicit_solve
     lanes = 128
     groups = plane_count * row_count // lanes

time: 52.8 us -> 54.1 us (1.025)
  Pallas kernels: 11.8 us -> 14.1 us
  local copies, waits for them, and re-layouts: 6.77 us -> 5.02 us
  other arithmetic: 3.45 us -> 4.09 us
    pallas_call x4, Pallas kernels: 9.85 us -> 12.2 us  [the longest x2 7.47 us: partition_call(): pl.pallas_call(functools.partial(partition_kernel, axis), out_shape=(jax....]
    transpose x2 -> x0, local copies, waits for them, and re-layouts: 1.74 us -> none  [the longest x1 0.87 us: per_device(): first_rate = jnp.moveaxis(half_rate, 1, 0)]
    sub x0 -> x1, other arithmetic: none -> 1.03 us  [per_device(): forward_euler_increment - implicit_weight * horizontal_implicit_solve]
where the time goes in v10:
time: 54.1 us; the launch traced here: 53.7 us
  starting transfers between devices  15.7 us (29%)
  Pallas kernels  14.1 us (26%)
  blocking collectives  8.1 us (15%)
  waiting for transfers between devices  6.48 us (12%)
  local copies, waits for them, and re-layouts  5.02 us (9%)
  other arithmetic  4.09 us (8%)
    ppermute x3, starting transfers between devices, doubling_gather(): other = lax.ppermute(held, axis, [(i, i ^ step) for i in range(count)])  8.98 us
    all_gather x1, blocking collectives, distributed_solve(): gathered = lax.all_gather(reduced, axis)  8.1 us
    pallas_call x2, Pallas kernels, partition_call(): pl.pallas_call(functools.partial(partition_kernel, axis), out_shape=(jax....  7.47 us
    ppermute x3, waiting for transfers between devices, doubling_gather(): other = lax.ppermute(held, axis, [(i, i ^ step) for i in range(count)])  6.14 us
    ppermute x1, starting transfers between devices, halos(): low = lax.ppermute(last, axis, forward)  5.47 us
    pallas_call x2, Pallas kernels, finish_call(): pl.pallas_call(functools.partial(finish_kernel, axis), out_shape=jax.Shap...  4.76 us
    pallas_call x1, Pallas kernels, sweep_call(): pl.pallas_call(sweep_kernel, out_shape=jax.ShapeDtypeStruct(h_lines.shape...  1.91 us
    ppermute x1, starting transfers between devices, halos(): high = lax.ppermute(first, axis, backward)  1.29 us
  transfers between devices with their start and end apart: 5, of which 4 were waited for; matrix products, arithmetic and copies ran while one was open for 2% of the time, Pallas kernels for 0%

profile of v10, /device:TPU:0, one launch (start us, length us, event | category | flops | bytes accessed | tf_op | source)
XLA Modules:
  0.0 53.7 jit_solution(14283758092049467260)
XLA Ops:
  0.0 1.2 %fusion.7 = (f32[16,32,1]{2,1,0:T(8,128)S(1)}, f32[16,32,1]{2,1,0:T(8,128)S(1)}) fusion(f32[16,32,128]{2,1,0:T(8,128)} %param.2), kind=kLoop, calls=%fused_computation.17 | loop fusion | bytes 8192 | tf_op jit(solution)/shard_map/slice | solution.py:18
  1.3 1.3 %collective-permute-start.1 = (f32[16,32]{1,0:T(8,128)S(1)}, f32[16,32]{1,0:T(8,128)S(1)}, u32[]{:S(2)}, u32[]{:S(2)}) collective-permute-start(f32[16,32]{1,0:T(8,128)S(1)} %bitcast.31), channel_id=1, source_target_pairs={{1,0},{2,1},{3,2},{4,3},{5,4},{6,5},{7,6},{9,8},{10,9},{11,10},{12... | collective-permute-start | bytes 6152 | tf_op jit(solution)/shard_map/ppermute | solution.py:21
  2.8 5.5 %collective-permute-start = (f32[16,32]{1,0:T(8,128)S(1)}, f32[16,32]{1,0:T(8,128)S(1)}, u32[]{:S(2)}, u32[]{:S(2)}) collective-permute-start(f32[16,32]{1,0:T(8,128)S(1)} %bitcast.33), channel_id=1, source_target_pairs={{0,1},{1,2},{2,3},{3,4},{4,5},{5,6},{6,7},{8,9},{9,10},{10,11},{11... | collective-permute-start | bytes 6152 | tf_op jit(solution)/shard_map/ppermute | solution.py:20
  8.5 0.6 %pad_maximum_fusion.refs_0_ = f32[2,16,128]{2,1,0:T(8,128)} fusion(f32[1,16,128]{2,1,0:T(8,128)S(1)} %bitcast.28, f32[1,16,128]{2,1,0:T(8,128)S(1)} %bitcast.27), kind=kLoop, calls=%fused_computation.15 | loop fusion | flops 4096 | bytes 32768 | tf_op jit(solution)/shard_map/stack | solution.py:252
  9.3 0.3 collective-permute-done
  10.0 1.0 %multiply_subtract_fusion.2 = (f32[16,32,128]{2,1,0:T(8,128)}, f32[16,32,128]{2,1,0:T(8,128)S(1)}, f32[16,32,128]{2,1,0:T(8,128)S(1)}) fusion(f32[16,32,128]{2,1,0:T(8,128)S(1)} %copy-done, f32[16,31,128]{2,1,0:T(8,128)S(1)} %get-tuple-element.23, f32[16,31,128]{2,1,0:T(8,128)S(1)} %get-tuple-element.22, f32[16,32,128]{2,1,0:T(8,128)S(1)} %copy-done.2, ...), kind=kLoop, calls=%fused_computation.10 | loop fusion | flops 1245184 | bytes 2342912 | tf_op jit(solution)/shard_map/sub | solution.py:246
  11.1 0.8 %copy.25.h_ref = f32[128,4,128]{2,1,0:T(4,128)} copy(f32[128,4,128]{0,2,1:T(8,128)S(1)} %bitcast.23) | data formatting | bytes 524288 | tf_op jit(solution)/shard_map/reshape | solution.py:259
  11.9 4.1 %shard_map.28 = (f32[3,16,32,128]{3,2,1,0:T(8,128)}, f32[5,2,16,128]{3,2,1,0:T(8,128)}) custom-call(f32[16,32,128]{2,1,0:T(8,128)} %copy-done.1, f32[16,32,128]{2,1,0:T(8,128)} %get-tuple-element.13.d_ref, f32[2,16,128]{2,1,0:T(8,128)} %pad_maximum_fusion.refs_0_), custom_call_target="tpu_custom_call" | custom-call | tf_op jit(solution)/shard_map/pallas_call | solution.py:97
  16.0 8.1 %all-gather = f32[20,2,16,128]{3,2,1,0:T(8,128)} all-gather(f32[5,2,16,128]{3,2,1,0:T(8,128)} %get-tuple-element.9), channel_id=2, replica_groups=mesh['gx'=4,'gy'=8] {'gx'}, dimensions={0}, use_global_device_ids=true | all-gather | bytes 409600 | tf_op jit(solution)/shard_map/all_gather | solution.py:214
  24.1 2.6 %shard_map.29 = f32[16,32,128]{2,1,0:T(8,128)} custom-call(s32[1]{0:T(128)} %bitcast.3.position_ref, f32[4,5,2,16,128]{4,3,2,1,0:T(8,128)} %bitcast.24, f32[3,16,32,128]{3,2,1,0:T(8,128)} %get-tuple-element.10.responses_ref), custom_call_target="tpu_custom_call" | custom-call | tf_op jit(solution)/shard_map/pallas_call | solution.py:151
  26.7 1.0 %multiply_subtract_fusion.1 = f32[16,32,128]{2,1,0:T(8,128)S(1)} fusion(f32[16,32,128]{2,1,0:T(8,128)} %shard_map.29, f32[16,32,128]{2,1,0:T(8,128)S(1)} %get-tuple-element.14), kind=kLoop, calls=%fused_computation.9 | loop fusion | flops 131072 | bytes 786432 | tf_op jit(solution)/shard_map/sub | solution.py:255
  27.7 0.8 %copy.26.d_ref = f32[128,4,128]{2,1,0:T(4,128)} copy(f32[128,4,128]{0,2,1:T(8,128)S(1)} %bitcast.25) | data formatting | bytes 524288 | tf_op jit(solution)/shard_map/reshape | solution.py:258
  28.6 3.3 %shard_map.30 = (f32[3,128,4,128]{3,2,1,0:T(4,128)}, f32[4,2,4,128]{3,2,1,0:T(4,128)}) custom-call(f32[128,4,128]{2,1,0:T(4,128)} %copy.25.h_ref, f32[128,4,128]{2,1,0:T(4,128)} %copy.26.d_ref), custom_call_target="tpu_custom_call" | custom-call | tf_op jit(solution)/shard_map/pallas_call | solution.py:97
  31.9 2.4 %collective-permute-start.2 = (f32[1,4,2,4,128]{4,3,2,1,0:T(4,128)}, f32[1,4,2,4,128]{4,3,2,1,0:T(4,128)S(1)}, u32[]{:S(2)}, u32[]{:S(2)}) collective-permute-start(f32[1,4,2,4,128]{4,3,2,1,0:T(4,128)} %bitcast.29), channel_id=1, source_target_pairs={{0,1},{1,0},{2,3},{3,2},{4,5},{5,4},{6,7},{7,6},{8,9},{9,8},{10,11... | collective-permute-start | bytes 49160 | tf_op jit(solution)/shard_map/ppermute | solution.py:200
  34.3 2.0 %collective-permute-done.2 = f32[1,4,2,4,128]{4,3,2,1,0:T(4,128)S(1)} collective-permute-done((f32[1,4,2,4,128]{4,3,2,1,0:T(4,128)}, f32[1,4,2,4,128]{4,3,2,1,0:T(4,128)S(1)}, u32[]{:S(2)}, u32[]{:S(2)}) %collective-permute-start.2) | collective-permute-done | bytes 16416 | tf_op jit(solution)/shard_map/ppermute | solution.py:200
  36.3 3.5 %collective-permute-start.3 = (f32[2,4,2,4,128]{4,3,2,1,0:T(4,128)S(1)}, f32[2,4,2,4,128]{4,3,2,1,0:T(4,128)S(1)}, u32[]{:S(2)}, u32[]{:S(2)}) collective-permute-start(f32[2,4,2,4,128]{4,3,2,1,0:T(4,128)S(1)} %maximum_select_fusion.2), channel_id=1, source_target_pairs={{0,2},{1,3},{2,0},{3,1},{4,6},{5,7},{6,4},{7,5},{8,10},{9,11},{10,... | collective-permute-start | bytes 98312 | tf_op jit(solution)/shard_map/ppermute | solution.py:200
  39.8 1.9 %collective-permute-done.3 = f32[2,4,2,4,128]{4,3,2,1,0:T(4,128)S(1)} collective-permute-done((f32[2,4,2,4,128]{4,3,2,1,0:T(4,128)S(1)}, f32[2,4,2,4,128]{4,3,2,1,0:T(4,128)S(1)}, u32[]{:S(2)}, u32[]{:S(2)}) %collective-permute-start.3) | collective-permute-done | bytes 32800 | tf_op jit(solution)/shard_map/ppermute | solution.py:200
  41.7 3.1 %collective-permute-start.4 = (f32[4,4,2,4,128]{4,3,2,1,0:T(4,128)S(1)}, f32[4,4,2,4,128]{4,3,2,1,0:T(4,128)S(1)}, u32[]{:S(2)}, u32[]{:S(2)}) collective-permute-start(f32[4,4,2,4,128]{4,3,2,1,0:T(4,128)S(1)} %maximum_select_fusion.1), channel_id=1, source_target_pairs={{0,4},{1,5},{2,6},{3,7},{4,0},{5,1},{6,2},{7,3},{8,12},{9,13},{10,... | collective-permute-start | bytes 196616 | tf_op jit(solution)/shard_map/ppermute | solution.py:200
  44.8 2.2 %collective-permute-done.4 = f32[4,4,2,4,128]{4,3,2,1,0:T(4,128)S(1)} collective-permute-done((f32[4,4,2,4,128]{4,3,2,1,0:T(4,128)S(1)}, f32[4,4,2,4,128]{4,3,2,1,0:T(4,128)S(1)}, u32[]{:S(2)}, u32[]{:S(2)}) %collective-permute-start.4) | collective-permute-done | bytes 65568 | tf_op jit(solution)/shard_map/ppermute | solution.py:200
  47.1 0.7 %maximum_select_fusion.g_ref = f32[8,4,2,4,128]{4,3,2,1,0:T(4,128)} fusion(f32[4,4,2,4,128]{4,3,2,1,0:T(4,128)S(1)} %collective-permute-done.4, f32[4,4,2,4,128]{4,3,2,1,0:T(4,128)S(1)} %maximum_select_fusion.1, pred[]{:T(512)S(6)} %eq.13), kind=kLoop, calls=%fused_computation.11 | loop fusion | flops 98304 | bytes 262145 | tf_op jit(solution)/shard_map/jit(_where)/select_n | solution.py:202
  47.7 2.2 %shard_map.31 = f32[128,4,128]{2,1,0:T(4,128)} custom-call(s32[1]{0:T(128)} %bitcast.position_ref, f32[8,4,2,4,128]{4,3,2,1,0:T(4,128)} %maximum_select_fusion.g_ref, f32[3,128,4,128]{3,2,1,0:T(4,128)} %get-tuple-element.12.responses_ref), custom_call_target="tpu_custom_call" | custom-call | tf_op jit(solution)/shard_map/pallas_call | solution.py:151
  49.9 1.1 %copy.27 = f32[128,4,128]{0,2,1:T(8,128)S(1)} copy(f32[128,4,128]{2,1,0:T(4,128)} %shard_map.31) | data formatting | bytes 524288 | tf_op jit(solution)/shard_map/pallas_call | solution.py:151
  51.0 0.8 %multiply_subtract_fusion.d_ref = f32[16,32,128]{2,1,0:T(8,128)} fusion(f32[16,32,128]{2,1,0:T(8,128)S(1)} %bitcast.26, f32[16,32,128]{2,1,0:T(8,128)S(1)} %copy-done, f32[16,32,128]{2,1,0:T(8,128)S(1)} %copy-done.2), kind=kLoop, calls=%fused_computation.8 | loop fusion | flops 458752 | bytes 1048576 | tf_op jit(solution)/shard_map/sub | solution.py:262
  51.8 1.9 %shard_map.32 = f32[16,32,128]{2,1,0:T(8,128)} custom-call(f32[16,32,128]{2,1,0:T(8,128)} %copy-done.1, f32[16,32,128]{2,1,0:T(8,128)} %multiply_subtract_fusion.d_ref), custom_call_target="tpu_custom_call" | custom-call | tf_op jit(solution)/shard_map/pallas_call | solution.py:185
  (18 shorter events, 1.1 us)
Async XLA Ops:
  1.2 7.1 %copy-start = (f32[16,32,128]{2,1,0:T(8,128)S(1)}, f32[16,32,128]{2,1,0:T(8,128)}, u32[]{:S(2)}) copy-start(f32[16,32,128]{2,1,0:T(8,128)} %param.2) | copy-start | bytes 786436
  1.3 7.8 %collective-permute-start.1 = (f32[16,32]{1,0:T(8,128)S(1)}, f32[16,32]{1,0:T(8,128)S(1)}, u32[]{:S(2)}, u32[]{:S(2)}) collective-permute-start(f32[16,32]{1,0:T(8,128)S(1)} %bitcast.31), channel_id=1, source_target_pairs={{1,0},{2,1},{3,2},{4,3},{5,4},{6,5},{7,6},{9,8},{10,9},{11,10},{12... | collective-permute-start | bytes 6152 | tf_op jit(solution)/shard_map/ppermute | solution.py:21
  2.8 6.8 %collective-permute-start = (f32[16,32]{1,0:T(8,128)S(1)}, f32[16,32]{1,0:T(8,128)S(1)}, u32[]{:S(2)}, u32[]{:S(2)}) collective-permute-start(f32[16,32]{1,0:T(8,128)S(1)} %bitcast.33), channel_id=1, source_target_pairs={{0,1},{1,2},{2,3},{3,4},{4,5},{5,6},{6,7},{8,9},{9,10},{10,11},{11... | collective-permute-start | bytes 6152 | tf_op jit(solution)/shard_map/ppermute | solution.py:20
  9.1 1.0 %copy-start.2 = (f32[16,32,128]{2,1,0:T(8,128)S(1)}, f32[16,32,128]{2,1,0:T(8,128)}, u32[]{:S(2)}) copy-start(f32[16,32,128]{2,1,0:T(8,128)} %param.3) | copy-start | bytes 786436
  11.1 0.8 %copy-start.1 = (f32[16,32,128]{2,1,0:T(8,128)}, f32[16,32,128]{2,1,0:T(8,128)S(1)}, u32[]{:S(2)}) copy-start(f32[16,32,128]{2,1,0:T(8,128)S(1)} %get-tuple-element.17.h_ref) | copy-start | bytes 786436
  31.9 4.4 %copy-start.3 = (f32[4,2,4,128]{3,2,1,0:T(4,128)S(1)}, f32[4,2,4,128]{3,2,1,0:T(4,128)}, u32[]{:S(2)}) copy-start(f32[4,2,4,128]{3,2,1,0:T(4,128)} %get-tuple-element.11) | copy-start | bytes 49156
  31.9 4.4 %collective-permute-start.2 = (f32[1,4,2,4,128]{4,3,2,1,0:T(4,128)}, f32[1,4,2,4,128]{4,3,2,1,0:T(4,128)S(1)}, u32[]{:S(2)}, u32[]{:S(2)}) collective-permute-start(f32[1,4,2,4,128]{4,3,2,1,0:T(4,128)} %bitcast.29), channel_id=1, source_target_pairs={{0,1},{1,0},{2,3},{3,2},{4,5},{5,4},{6,7},{7,6},{8,9},{9,8},{10,11... | collective-permute-start | bytes 49160 | tf_op jit(solution)/shard_map/ppermute | solution.py:200
  36.3 5.4 %collective-permute-start.3 = (f32[2,4,2,4,128]{4,3,2,1,0:T(4,128)S(1)}, f32[2,4,2,4,128]{4,3,2,1,0:T(4,128)S(1)}, u32[]{:S(2)}, u32[]{:S(2)}) collective-permute-start(f32[2,4,2,4,128]{4,3,2,1,0:T(4,128)S(1)} %maximum_select_fusion.2), channel_id=1, source_target_pairs={{0,2},{1,3},{2,0},{3,1},{4,6},{5,7},{6,4},{7,5},{8,10},{9,11},{10,... | collective-permute-start | bytes 98312 | tf_op jit(solution)/shard_map/ppermute | solution.py:200
  41.7 5.3 %collective-permute-start.4 = (f32[4,4,2,4,128]{4,3,2,1,0:T(4,128)S(1)}, f32[4,4,2,4,128]{4,3,2,1,0:T(4,128)S(1)}, u32[]{:S(2)}, u32[]{:S(2)}) collective-permute-start(f32[4,4,2,4,128]{4,3,2,1,0:T(4,128)S(1)} %maximum_select_fusion.1), channel_id=1, source_target_pairs={{0,4},{1,5},{2,6},{3,7},{4,0},{5,1},{6,2},{7,3},{8,12},{9,13},{10,... | collective-permute-start | bytes 196616 | tf_op jit(solution)/shard_map/ppermute | solution.py:200

commit v11 on v8

--- a/solution.py
+++ b/solution.py
@@ -74,18 +74,33 @@
         red_ref[4, 1] = edges_ref[1]
 
 
+def line_block(size):
+    return 8 if size % 8 == 0 and size > 8 else size
+
+
 def partition_call(h_lines, d_lines, edges):
-    n = h_lines.shape[0]
-    rest = h_lines.shape[1:]
-    operands = (h_lines, d_lines) if edges is None else (h_lines, d_lines, edges)
+    n, size, lanes = h_lines.shape
+    block = line_block(size)
     rows = 4 if edges is None else 5
+    lines = pl.BlockSpec((n, block, lanes), lambda i: (0, i, 0))
+    in_specs = [lines, lines]
+    operands = (h_lines, d_lines)
+    if edges is not None:
+        in_specs.append(pl.BlockSpec((2, block, lanes), lambda i: (0, i, 0)))
+        operands = operands + (edges,)
     return pl.pallas_call(
         partition_kernel,
+        grid=(size // block,),
+        in_specs=in_specs,
+        out_specs=(
+            pl.BlockSpec((3, n, block, lanes), lambda i: (0, 0, i, 0)),
+            pl.BlockSpec((rows, 2, block, lanes), lambda i: (0, 0, i, 0)),
+        ),
         out_shape=(
-            jax.ShapeDtypeStruct((3, n) + rest, jnp.float32),
-            jax.ShapeDtypeStruct((rows, 2) + rest, jnp.float32),
+            jax.ShapeDtypeStruct((3, n, size, lanes), jnp.float32),
+            jax.ShapeDtypeStruct((rows, 2, size, lanes), jnp.float32),
         ),
-        scratch_shapes=[pltpu_vmem((n,) + rest)],
+        scratch_shapes=[pltpu_vmem((n, block, lanes))],
     )(*operands)
 
 
@@ -131,18 +146,24 @@
 
 
 def finish_call(gathered, responses, position):
-    count = gathered.shape[0]
-    rest = gathered.shape[3:]
+    count, rows = gathered.shape[:2]
+    size, lanes = gathered.shape[3:]
     n = responses.shape[1]
+    block = line_block(size)
     return pl.pallas_call(
         finish_kernel,
-        out_shape=jax.ShapeDtypeStruct((n,) + rest, jnp.float32),
+        grid=(size // block,),
+        out_shape=jax.ShapeDtypeStruct((n, size, lanes), jnp.float32),
         in_specs=[
             pl.BlockSpec(memory_space=pltpu.SMEM),
-            pl.BlockSpec(memory_space=pltpu.VMEM),
-            pl.BlockSpec(memory_space=pltpu.VMEM),
+            pl.BlockSpec((count, rows, 2, block, lanes), lambda i: (0, 0, 0, i, 0)),
+            pl.BlockSpec((3, n, block, lanes), lambda i: (0, 0, i, 0)),
         ],
-        scratch_shapes=[pltpu_vmem((2 * count,) + rest), pltpu_vmem((2 * count,) + rest)],
+        out_specs=pl.BlockSpec((n, block, lanes), lambda i: (0, i, 0)),
+        scratch_shapes=[
+            pltpu_vmem((2 * count, block, lanes)),
+            pltpu_vmem((2 * count, block, lanes)),
+        ],
     )(position, gathered, responses)
 
 
@@ -168,10 +189,16 @@
 
 
 def sweep_call(h_lines, d_lines):
+    n, size, lanes = h_lines.shape
+    block = line_block(size)
+    lines = pl.BlockSpec((n, block, lanes), lambda i: (0, i, 0))
     return pl.pallas_call(
         sweep_kernel,
+        grid=(size // block,),
+        in_specs=[lines, lines],
+        out_specs=lines,
         out_shape=jax.ShapeDtypeStruct(h_lines.shape, jnp.float32),
-        scratch_shapes=[pltpu_vmem(h_lines.shape)],
+        scratch_shapes=[pltpu_vmem((n, block, lanes))],
     )(h_lines, d_lines)
 
 

time: 52.8 us -> 54.6 us (1.034)
  Pallas kernels: 11.8 us -> 13.4 us
    pallas_call x5, Pallas kernels: 11.8 us -> 13.4 us  [the longest x2 5.8 us: partition_call(): pl.pallas_call(partition_kernel, grid=(size // block,), in_specs=in_specs...]
where the time goes in v11:
time: 54.6 us; the launch traced here: 54 us
  starting transfers between devices  15.7 us (29%)
  Pallas kernels  13.4 us (25%)
  blocking collectives  8.1 us (15%)
  local copies, waits for them, and re-layouts  6.77 us (12%)
  waiting for transfers between devices  6.49 us (12%)
  other arithmetic  3.45 us (6%)
    ppermute x3, starting transfers between devices, doubling_gather(): other = lax.ppermute(held, axis, [(i, i ^ step) for i in range(count)])  8.98 us
    all_gather x1, blocking collectives, distributed_solve(): gathered = lax.all_gather(reduced, axis)  8.1 us
    ppermute x3, waiting for transfers between devices, doubling_gather(): other = lax.ppermute(held, axis, [(i, i ^ step) for i in range(count)])  6.14 us
    pallas_call x2, Pallas kernels, partition_call(): pl.pallas_call(partition_kernel, grid=(size // block,), in_specs=in_specs...  5.8 us
    ppermute x1, starting transfers between devices, halos(): low = lax.ppermute(last, axis, forward)  5.47 us
    pallas_call x2, Pallas kernels, finish_call(): pl.pallas_call(finish_kernel, grid=(size // block,), out_shape=jax.ShapeD...  4.2 us
    pallas_call x1, Pallas kernels, sweep_call(): pl.pallas_call(sweep_kernel, grid=(size // block,), in_specs=[lines, line...  3.37 us
    ppermute x1, starting transfers between devices, halos(): high = lax.ppermute(first, axis, backward)  1.29 us
  transfers between devices with their start and end apart: 5, of which 4 were waited for; matrix products, arithmetic and copies ran while one was open for 2% of the time, Pallas kernels for 0%

profile of v11, /device:TPU:0, one launch (start us, length us, event | category | flops | bytes accessed | tf_op | source)
XLA Modules:
  0.0 54.0 jit_solution(17358665103186083764)
XLA Ops:
  0.0 1.2 %fusion.8 = (f32[16,32,1]{2,1,0:T(8,128)S(1)}, f32[16,32,1]{2,1,0:T(8,128)S(1)}) fusion(f32[16,32,128]{2,1,0:T(8,128)} %param.2), kind=kLoop, calls=%fused_computation.18 | loop fusion | bytes 8192 | tf_op jit(solution)/shard_map/slice | solution.py:16
  1.3 1.3 %collective-permute-start.1 = (f32[16,32]{1,0:T(8,128)S(1)}, f32[16,32]{1,0:T(8,128)S(1)}, u32[]{:S(2)}, u32[]{:S(2)}) collective-permute-start(f32[16,32]{1,0:T(8,128)S(1)} %bitcast.37), channel_id=1, source_target_pairs={{1,0},{2,1},{3,2},{4,3},{5,4},{6,5},{7,6},{9,8},{10,9},{11,10},{12... | collective-permute-start | bytes 6152 | tf_op jit(solution)/shard_map/ppermute | solution.py:19
  2.8 5.5 %collective-permute-start = (f32[16,32]{1,0:T(8,128)S(1)}, f32[16,32]{1,0:T(8,128)S(1)}, u32[]{:S(2)}, u32[]{:S(2)}) collective-permute-start(f32[16,32]{1,0:T(8,128)S(1)} %bitcast.39), channel_id=1, source_target_pairs={{0,1},{1,2},{2,3},{3,4},{4,5},{5,6},{6,7},{8,9},{9,10},{10,11},{11... | collective-permute-start | bytes 6152 | tf_op jit(solution)/shard_map/ppermute | solution.py:18
  8.5 0.6 %pad_maximum_fusion.refs_0_ = f32[2,16,128]{2,1,0:T(8,128)} fusion(f32[1,16,128]{2,1,0:T(8,128)S(1)} %bitcast.34, f32[1,16,128]{2,1,0:T(8,128)S(1)} %bitcast.33), kind=kLoop, calls=%fused_computation.15 | loop fusion | flops 4096 | bytes 32768 | tf_op jit(solution)/shard_map/stack | solution.py:268
  10.4 0.8 %copy.34.h_ref = f32[128,4,128]{2,1,0:T(4,128)} copy(f32[128,4,128]{0,2,1:T(8,128)S(1)} %bitcast.29) | data formatting | bytes 524288 | tf_op jit(solution)/shard_map/reshape | solution.py:274
  11.2 0.9 %copy.31.h_ref = f32[32,16,128]{2,1,0:T(8,128)} copy(f32[32,16,128]{2,0,1:T(8,128)S(1)} %get-tuple-element.17) | data formatting | bytes 524288 | tf_op jit(solution)/shard_map/transpose | solution.py:262
  12.1 0.9 %copy.32.d_ref = f32[32,16,128]{2,1,0:T(8,128)} copy(f32[32,16,128]{2,0,1:T(8,128)S(1)} %get-tuple-element.13) | data formatting | bytes 524288 | tf_op jit(solution)/shard_map/transpose | solution.py:259
  13.0 2.5 %shard_map.28 = (f32[3,32,16,128]{3,2,1,0:T(8,128)}, f32[5,2,16,128]{3,2,1,0:T(8,128)}) custom-call(f32[32,16,128]{2,1,0:T(8,128)} %copy.31.h_ref, f32[32,16,128]{2,1,0:T(8,128)} %copy.32.d_ref, f32[2,16,128]{2,1,0:T(8,128)} %pad_maximum_fusion.refs_0_), custom_call_target="tpu_custom_call" | custom-call | tf_op jit(solution)/shard_map/pallas_call | solution.py:91
  15.4 8.1 %all-gather = f32[20,2,16,128]{3,2,1,0:T(8,128)} all-gather(f32[5,2,16,128]{3,2,1,0:T(8,128)} %get-tuple-element.9), channel_id=2, replica_groups=mesh['gx'=4,'gy'=8] {'gx'}, dimensions={0}, use_global_device_ids=true | all-gather | bytes 409600 | tf_op jit(solution)/shard_map/all_gather | solution.py:227
  23.5 2.0 %shard_map.29 = f32[32,16,128]{2,1,0:T(8,128)} custom-call(s32[1]{0:T(128)} %bitcast.3.position_ref, f32[4,5,2,16,128]{4,3,2,1,0:T(8,128)} %bitcast.30, f32[3,32,16,128]{3,2,1,0:T(8,128)} %get-tuple-element.10.responses_ref), custom_call_target="tpu_custom_call" | custom-call | tf_op jit(solution)/shard_map/pallas_call | solution.py:153
  25.6 1.0 %bitcast_subtract_fusion = f32[16,32,128]{2,1,0:T(8,128)S(1)} fusion(f32[32,16,128]{2,1,0:T(8,128)} %shard_map.29, f32[16,32,128]{2,1,0:T(8,128)S(1)} %get-tuple-element.14), kind=kLoop, calls=%fused_computation.8 | loop fusion | flops 131072 | bytes 786432 | tf_op jit(solution)/shard_map/sub | solution.py:270
  26.6 0.9 %copy.35.d_ref = f32[128,4,128]{2,1,0:T(4,128)} copy(f32[128,4,128]{0,2,1:T(8,128)S(1)} %bitcast.31) | data formatting | bytes 524288 | tf_op jit(solution)/shard_map/reshape | solution.py:273
  27.5 3.3 %shard_map.30 = (f32[3,128,4,128]{3,2,1,0:T(4,128)}, f32[4,2,4,128]{3,2,1,0:T(4,128)}) custom-call(f32[128,4,128]{2,1,0:T(4,128)} %copy.34.h_ref, f32[128,4,128]{2,1,0:T(4,128)} %copy.35.d_ref), custom_call_target="tpu_custom_call" | custom-call | tf_op jit(solution)/shard_map/pallas_call | solution.py:91
  30.8 2.4 %collective-permute-start.2 = (f32[1,4,2,4,128]{4,3,2,1,0:T(4,128)}, f32[1,4,2,4,128]{4,3,2,1,0:T(4,128)S(1)}, u32[]{:S(2)}, u32[]{:S(2)}) collective-permute-start(f32[1,4,2,4,128]{4,3,2,1,0:T(4,128)} %bitcast.35), channel_id=1, source_target_pairs={{0,1},{1,0},{2,3},{3,2},{4,5},{5,4},{6,7},{7,6},{8,9},{9,8},{10,11... | collective-permute-start | bytes 49160 | tf_op jit(solution)/shard_map/ppermute | solution.py:213
  33.2 2.0 %collective-permute-done.2 = f32[1,4,2,4,128]{4,3,2,1,0:T(4,128)S(1)} collective-permute-done((f32[1,4,2,4,128]{4,3,2,1,0:T(4,128)}, f32[1,4,2,4,128]{4,3,2,1,0:T(4,128)S(1)}, u32[]{:S(2)}, u32[]{:S(2)}) %collective-permute-start.2) | collective-permute-done | bytes 16416 | tf_op jit(solution)/shard_map/ppermute | solution.py:213
  35.2 3.5 %collective-permute-start.3 = (f32[2,4,2,4,128]{4,3,2,1,0:T(4,128)S(1)}, f32[2,4,2,4,128]{4,3,2,1,0:T(4,128)S(1)}, u32[]{:S(2)}, u32[]{:S(2)}) collective-permute-start(f32[2,4,2,4,128]{4,3,2,1,0:T(4,128)S(1)} %maximum_select_fusion.2), channel_id=1, source_target_pairs={{0,2},{1,3},{2,0},{3,1},{4,6},{5,7},{6,4},{7,5},{8,10},{9,11},{10,... | collective-permute-start | bytes 98312 | tf_op jit(solution)/shard_map/ppermute | solution.py:213
  38.7 1.9 %collective-permute-done.3 = f32[2,4,2,4,128]{4,3,2,1,0:T(4,128)S(1)} collective-permute-done((f32[2,4,2,4,128]{4,3,2,1,0:T(4,128)S(1)}, f32[2,4,2,4,128]{4,3,2,1,0:T(4,128)S(1)}, u32[]{:S(2)}, u32[]{:S(2)}) %collective-permute-start.3) | collective-permute-done | bytes 32800 | tf_op jit(solution)/shard_map/ppermute | solution.py:213
  40.6 3.1 %collective-permute-start.4 = (f32[4,4,2,4,128]{4,3,2,1,0:T(4,128)S(1)}, f32[4,4,2,4,128]{4,3,2,1,0:T(4,128)S(1)}, u32[]{:S(2)}, u32[]{:S(2)}) collective-permute-start(f32[4,4,2,4,128]{4,3,2,1,0:T(4,128)S(1)} %maximum_select_fusion.1), channel_id=1, source_target_pairs={{0,4},{1,5},{2,6},{3,7},{4,0},{5,1},{6,2},{7,3},{8,12},{9,13},{10,... | collective-permute-start | bytes 196616 | tf_op jit(solution)/shard_map/ppermute | solution.py:213
  43.7 2.2 %collective-permute-done.4 = f32[4,4,2,4,128]{4,3,2,1,0:T(4,128)S(1)} collective-permute-done((f32[4,4,2,4,128]{4,3,2,1,0:T(4,128)S(1)}, f32[4,4,2,4,128]{4,3,2,1,0:T(4,128)S(1)}, u32[]{:S(2)}, u32[]{:S(2)}) %collective-permute-start.4) | collective-permute-done | bytes 65568 | tf_op jit(solution)/shard_map/ppermute | solution.py:213
  46.0 0.7 %maximum_select_fusion.g_ref = f32[8,4,2,4,128]{4,3,2,1,0:T(4,128)} fusion(f32[4,4,2,4,128]{4,3,2,1,0:T(4,128)S(1)} %collective-permute-done.4, f32[4,4,2,4,128]{4,3,2,1,0:T(4,128)S(1)} %maximum_select_fusion.1, pred[]{:T(512)S(6)} %eq.13), kind=kLoop, calls=%fused_computation.11 | loop fusion | flops 98304 | bytes 262145 | tf_op jit(solution)/shard_map/jit(_where)/select_n | solution.py:215
  46.6 2.2 %shard_map.31 = f32[128,4,128]{2,1,0:T(4,128)} custom-call(s32[1]{0:T(128)} %bitcast.position_ref, f32[8,4,2,4,128]{4,3,2,1,0:T(4,128)} %maximum_select_fusion.g_ref, f32[3,128,4,128]{3,2,1,0:T(4,128)} %get-tuple-element.12.responses_ref), custom_call_target="tpu_custom_call" | custom-call | tf_op jit(solution)/shard_map/pallas_call | solution.py:153
  48.8 1.1 %copy.36 = f32[128,4,128]{0,2,1:T(8,128)S(1)} copy(f32[128,4,128]{2,1,0:T(4,128)} %shard_map.31) | data formatting | bytes 524288 | tf_op jit(solution)/shard_map/pallas_call | solution.py:153
  49.9 0.8 %multiply_subtract_fusion.d_ref = f32[16,32,128]{2,1,0:T(8,128)} fusion(f32[16,32,128]{2,1,0:T(8,128)S(1)} %bitcast.32, f32[16,32,128]{2,1,0:T(8,128)S(1)} %copy-done, f32[16,32,128]{2,1,0:T(8,128)S(1)} %copy-done.2), kind=kLoop, calls=%fused_computation.9 | loop fusion | flops 458752 | bytes 1048576 | tf_op jit(solution)/shard_map/sub | solution.py:277
  50.7 3.4 %shard_map.32 = f32[16,32,128]{2,1,0:T(8,128)} custom-call(f32[16,32,128]{2,1,0:T(8,128)} %copy-done.1, f32[16,32,128]{2,1,0:T(8,128)} %multiply_subtract_fusion.d_ref), custom_call_target="tpu_custom_call" | custom-call | tf_op jit(solution)/shard_map/pallas_call | solution.py:195
  (20 shorter events, 1.8 us)
Async XLA Ops:
  1.2 7.1 %copy-start = (f32[16,32,128]{2,1,0:T(8,128)S(1)}, f32[16,32,128]{2,1,0:T(8,128)}, u32[]{:S(2)}) copy-start(f32[16,32,128]{2,1,0:T(8,128)} %param.2) | copy-start | bytes 786436
  1.3 7.8 %collective-permute-start.1 = (f32[16,32]{1,0:T(8,128)S(1)}, f32[16,32]{1,0:T(8,128)S(1)}, u32[]{:S(2)}, u32[]{:S(2)}) collective-permute-start(f32[16,32]{1,0:T(8,128)S(1)} %bitcast.37), channel_id=1, source_target_pairs={{1,0},{2,1},{3,2},{4,3},{5,4},{6,5},{7,6},{9,8},{10,9},{11,10},{12... | collective-permute-start | bytes 6152 | tf_op jit(solution)/shard_map/ppermute | solution.py:19
  2.8 6.8 %collective-permute-start = (f32[16,32]{1,0:T(8,128)S(1)}, f32[16,32]{1,0:T(8,128)S(1)}, u32[]{:S(2)}, u32[]{:S(2)}) collective-permute-start(f32[16,32]{1,0:T(8,128)S(1)} %bitcast.39), channel_id=1, source_target_pairs={{0,1},{1,2},{2,3},{3,4},{4,5},{5,6},{6,7},{8,9},{9,10},{10,11},{11... | collective-permute-start | bytes 6152 | tf_op jit(solution)/shard_map/ppermute | solution.py:18
  9.1 1.0 %copy-start.2 = (f32[16,32,128]{2,1,0:T(8,128)S(1)}, f32[16,32,128]{2,1,0:T(8,128)}, u32[]{:S(2)}) copy-start(f32[16,32,128]{2,1,0:T(8,128)} %param.3) | copy-start | bytes 786436
  10.4 0.8 %copy-start.1 = (f32[16,32,128]{2,1,0:T(8,128)}, f32[16,32,128]{2,1,0:T(8,128)S(1)}, u32[]{:S(2)}) copy-start(f32[16,32,128]{2,1,0:T(8,128)S(1)} %get-tuple-element.18.h_ref) | copy-start | bytes 786436
  30.8 4.4 %copy-start.3 = (f32[4,2,4,128]{3,2,1,0:T(4,128)S(1)}, f32[4,2,4,128]{3,2,1,0:T(4,128)}, u32[]{:S(2)}) copy-start(f32[4,2,4,128]{3,2,1,0:T(4,128)} %get-tuple-element.11) | copy-start | bytes 49156
  30.8 4.4 %collective-permute-start.2 = (f32[1,4,2,4,128]{4,3,2,1,0:T(4,128)}, f32[1,4,2,4,128]{4,3,2,1,0:T(4,128)S(1)}, u32[]{:S(2)}, u32[]{:S(2)}) collective-permute-start(f32[1,4,2,4,128]{4,3,2,1,0:T(4,128)} %bitcast.35), channel_id=1, source_target_pairs={{0,1},{1,0},{2,3},{3,2},{4,5},{5,4},{6,7},{7,6},{8,9},{9,8},{10,11... | collective-permute-start | bytes 49160 | tf_op jit(solution)/shard_map/ppermute | solution.py:213
  35.2 5.4 %collective-permute-start.3 = (f32[2,4,2,4,128]{4,3,2,1,0:T(4,128)S(1)}, f32[2,4,2,4,128]{4,3,2,1,0:T(4,128)S(1)}, u32[]{:S(2)}, u32[]{:S(2)}) collective-permute-start(f32[2,4,2,4,128]{4,3,2,1,0:T(4,128)S(1)} %maximum_select_fusion.2), channel_id=1, source_target_pairs={{0,2},{1,3},{2,0},{3,1},{4,6},{5,7},{6,4},{7,5},{8,10},{9,11},{10,... | collective-permute-start | bytes 98312 | tf_op jit(solution)/shard_map/ppermute | solution.py:213
  40.6 5.3 %collective-permute-start.4 = (f32[4,4,2,4,128]{4,3,2,1,0:T(4,128)S(1)}, f32[4,4,2,4,128]{4,3,2,1,0:T(4,128)S(1)}, u32[]{:S(2)}, u32[]{:S(2)}) collective-permute-start(f32[4,4,2,4,128]{4,3,2,1,0:T(4,128)S(1)} %maximum_select_fusion.1), channel_id=1, source_target_pairs={{0,4},{1,5},{2,6},{3,7},{4,0},{5,1},{6,2},{7,3},{8,12},{9,13},{10,... | collective-permute-start | bytes 196616 | tf_op jit(solution)/shard_map/ppermute | solution.py:213

commit v12 on v8

--- a/solution.py
+++ b/solution.py
@@ -237,7 +237,7 @@
             first_rate,
             first_side,
             "gx",
-            False,
+            True,
             jnp.stack([initial_heat_values[:, 0], initial_heat_values[:, row_count - 1]], 0),
         ), 0, 1)
     second_side = first_pass - implicit_weight * vertical_implicit_solve

time: 52.8 us -> 54.3 us (1.028)
  blocking collectives: 8.1 us -> 0 us
  waiting for transfers between devices: 6.49 us -> 11.6 us
  starting transfers between devices: 15.7 us -> 18.4 us
  other arithmetic: 3.45 us -> 5.17 us
    all_gather x1 -> x0, blocking collectives: 8.1 us -> none  [distributed_solve(): gathered = lax.all_gather(reduced, axis)]
    ppermute x3 -> x5, waiting for transfers between devices: 6.14 us -> 11.3 us  [doubling_gather(): other = lax.ppermute(held, axis, [(i, i ^ step) for i in range(count)])]
    ppermute x3 -> x5, starting transfers between devices: 8.98 us -> 11.7 us  [doubling_gather(): other = lax.ppermute(held, axis, [(i, i ^ step) for i in range(count)])]
    select_n x3 -> x5, other arithmetic: 0.7 us -> 2.44 us  [doubling_gather(): jnp.where(lower, jnp.concatenate([held, other], 0), jnp.concatenate([othe...]
  transfers between devices with their start and end apart: 5 -> 7, of which waited for: 4 -> 6; matrix products, arithmetic and copies ran while one was open for 2% -> 4% of each run, Pallas kernels for 0% -> 0%
where the time goes in v12:
time: 54.3 us; the launch traced here: 53.9 us
  starting transfers between devices  18.4 us (34%)
  Pallas kernels  11.7 us (22%)
  waiting for transfers between devices  11.6 us (21%)
  local copies, waits for them, and re-layouts  6.77 us (12%)
  other arithmetic  5.17 us (10%)
    ppermute x5, starting transfers between devices, doubling_gather(): other = lax.ppermute(held, axis, [(i, i ^ step) for i in range(count)])  11.7 us
    ppermute x5, waiting for transfers between devices, doubling_gather(): other = lax.ppermute(held, axis, [(i, i ^ step) for i in range(count)])  11.3 us
    pallas_call x2, Pallas kernels, partition_call(): pl.pallas_call(partition_kernel, out_shape=(jax.ShapeDtypeStruct((3, n) +...  5.6 us
    ppermute x1, starting transfers between devices, halos(): low = lax.ppermute(last, axis, forward)  5.47 us
    pallas_call x2, Pallas kernels, finish_call(): pl.pallas_call(finish_kernel, out_shape=jax.ShapeDtypeStruct((n,) + rest,...  4.24 us
    select_n x5, other arithmetic, doubling_gather(): jnp.where(lower, jnp.concatenate([held, other], 0), jnp.concatenate([othe...  2.44 us
    pallas_call x1, Pallas kernels, sweep_call(): pl.pallas_call(sweep_kernel, out_shape=jax.ShapeDtypeStruct(h_lines.shape...  1.91 us
    ppermute x1, starting transfers between devices, halos(): high = lax.ppermute(first, axis, backward)  1.29 us
  transfers between devices with their start and end apart: 7, of which 6 were waited for; matrix products, arithmetic and copies ran while one was open for 4% of the time, Pallas kernels for 0%

profile of v12, /device:TPU:0, one launch (start us, length us, event | category | flops | bytes accessed | tf_op | source)
XLA Modules:
  0.0 53.9 jit_solution(5421432713361403538)
XLA Ops:
  0.0 1.2 %fusion.8 = (f32[16,32,1]{2,1,0:T(8,128)S(1)}, f32[16,32,1]{2,1,0:T(8,128)S(1)}) fusion(f32[16,32,128]{2,1,0:T(8,128)} %param.2), kind=kLoop, calls=%fused_computation.20 | loop fusion | bytes 8192 | tf_op jit(solution)/shard_map/slice | solution.py:16
  1.3 1.3 %collective-permute-start.1 = (f32[16,32]{1,0:T(8,128)S(1)}, f32[16,32]{1,0:T(8,128)S(1)}, u32[]{:S(2)}, u32[]{:S(2)}) collective-permute-start(f32[16,32]{1,0:T(8,128)S(1)} %bitcast.38), channel_id=1, source_target_pairs={{1,0},{2,1},{3,2},{4,3},{5,4},{6,5},{7,6},{9,8},{10,9},{11,10},{12... | collective-permute-start | bytes 6152 | tf_op jit(solution)/shard_map/ppermute | solution.py:19
  2.8 5.5 %collective-permute-start = (f32[16,32]{1,0:T(8,128)S(1)}, f32[16,32]{1,0:T(8,128)S(1)}, u32[]{:S(2)}, u32[]{:S(2)}) collective-permute-start(f32[16,32]{1,0:T(8,128)S(1)} %bitcast.40), channel_id=1, source_target_pairs={{0,1},{1,2},{2,3},{3,4},{4,5},{5,6},{6,7},{8,9},{9,10},{10,11},{11... | collective-permute-start | bytes 6152 | tf_op jit(solution)/shard_map/ppermute | solution.py:18
  10.4 0.9 %copy.19.h_ref = f32[32,16,128]{2,1,0:T(8,128)} copy(f32[32,16,128]{2,0,1:T(8,128)S(1)} %get-tuple-element.17) | data formatting | bytes 524288 | tf_op jit(solution)/shard_map/transpose | solution.py:235
  11.2 0.9 %copy.20.d_ref = f32[32,16,128]{2,1,0:T(8,128)} copy(f32[32,16,128]{2,0,1:T(8,128)S(1)} %get-tuple-element.13) | data formatting | bytes 524288 | tf_op jit(solution)/shard_map/transpose | solution.py:232
  12.1 2.3 %shard_map.28 = (f32[3,32,16,128]{3,2,1,0:T(8,128)}, f32[5,2,16,128]{3,2,1,0:T(8,128)}) custom-call(f32[32,16,128]{2,1,0:T(8,128)} %copy.19.h_ref, f32[32,16,128]{2,1,0:T(8,128)} %copy.20.d_ref, f32[2,16,128]{2,1,0:T(8,128)} %pad_maximum_fusion.refs_0_), custom_call_target="tpu_custom_call" | custom-call | tf_op jit(solution)/shard_map/pallas_call | solution.py:82
  14.4 1.5 %collective-permute-done.2 = f32[1,5,2,16,128]{4,3,2,1,0:T(8,128)S(1)} collective-permute-done((f32[1,5,2,16,128]{4,3,2,1,0:T(8,128)}, f32[1,5,2,16,128]{4,3,2,1,0:T(8,128)S(1)}, u32[]{:S(2)}, u32[]{:S(2)}) %collective-permute-start.2) | collective-permute-done | bytes 81952 | tf_op jit(solution)/shard_map/ppermute | solution.py:186
  15.9 1.0 %maximum_select_fusion.1 = f32[2,5,2,16,128]{4,3,2,1,0:T(8,128)S(1)} fusion(f32[1,5,2,16,128]{4,3,2,1,0:T(8,128)S(1)} %collective-permute-done.2, f32[1,5,2,16,128]{4,3,2,1,0:T(8,128)} %bitcast.33, pred[]{:T(512)S(6)} %eq.25), kind=kLoop, calls=%fused_computation.12 | loop fusion | flops 122880 | bytes 327681 | tf_op jit(solution)/shard_map/jit(_where)/select_n | solution.py:188
  16.9 2.1 %collective-permute-start.3 = (f32[2,5,2,16,128]{4,3,2,1,0:T(8,128)S(1)}, f32[2,5,2,16,128]{4,3,2,1,0:T(8,128)S(1)}, u32[]{:S(2)}, u32[]{:S(2)}) collective-permute-start(f32[2,5,2,16,128]{4,3,2,1,0:T(8,128)S(1)} %maximum_select_fusion.1), channel_id=1, source_target_pairs={{0,16},{8,24},{16,0},{24,8},{1,17},{9,25},{17,1},{25,9},{2,18},{10... | collective-permute-start | bytes 491528 | tf_op jit(solution)/shard_map/ppermute | solution.py:186
  19.0 0.8 %copy.22.h_ref = f32[128,4,128]{2,1,0:T(4,128)} copy(f32[128,4,128]{0,2,1:T(8,128)S(1)} %bitcast.29) | data formatting | bytes 524288 | tf_op jit(solution)/shard_map/reshape | solution.py:247
  19.8 3.7 %collective-permute-done.3 = f32[2,5,2,16,128]{4,3,2,1,0:T(8,128)S(1)} collective-permute-done((f32[2,5,2,16,128]{4,3,2,1,0:T(8,128)S(1)}, f32[2,5,2,16,128]{4,3,2,1,0:T(8,128)S(1)}, u32[]{:S(2)}, u32[]{:S(2)}) %collective-permute-start.3) | collective-permute-done | bytes 163872 | tf_op jit(solution)/shard_map/ppermute | solution.py:186
  24.2 2.1 %shard_map.29 = f32[32,16,128]{2,1,0:T(8,128)} custom-call(s32[1]{0:T(128)} %bitcast.3.position_ref, f32[4,5,2,16,128]{4,3,2,1,0:T(8,128)} %maximum_select_fusion.g_ref, f32[3,32,16,128]{3,2,1,0:T(8,128)} %get-tuple-element.10.responses_ref), custom_call_target="tpu_custom_call" | custom-call | tf_op jit(solution)/shard_map/pallas_call | solution.py:137
  26.3 1.0 %bitcast_subtract_fusion = f32[16,32,128]{2,1,0:T(8,128)S(1)} fusion(f32[32,16,128]{2,1,0:T(8,128)} %shard_map.29, f32[16,32,128]{2,1,0:T(8,128)S(1)} %get-tuple-element.14), kind=kLoop, calls=%fused_computation.9 | loop fusion | flops 131072 | bytes 786432 | tf_op jit(solution)/shard_map/sub | solution.py:243
  27.4 0.9 %copy.23.d_ref = f32[128,4,128]{2,1,0:T(4,128)} copy(f32[128,4,128]{0,2,1:T(8,128)S(1)} %bitcast.30) | data formatting | bytes 524288 | tf_op jit(solution)/shard_map/reshape | solution.py:246
  28.2 3.3 %shard_map.30 = (f32[3,128,4,128]{3,2,1,0:T(4,128)}, f32[4,2,4,128]{3,2,1,0:T(4,128)}) custom-call(f32[128,4,128]{2,1,0:T(4,128)} %copy.22.h_ref, f32[128,4,128]{2,1,0:T(4,128)} %copy.23.d_ref), custom_call_target="tpu_custom_call" | custom-call | tf_op jit(solution)/shard_map/pallas_call | solution.py:82
  31.5 2.6 %collective-permute-start.4 = (f32[1,4,2,4,128]{4,3,2,1,0:T(4,128)}, f32[1,4,2,4,128]{4,3,2,1,0:T(4,128)S(1)}, u32[]{:S(2)}, u32[]{:S(2)}) collective-permute-start(f32[1,4,2,4,128]{4,3,2,1,0:T(4,128)} %bitcast.36), channel_id=1, source_target_pairs={{0,1},{1,0},{2,3},{3,2},{4,5},{5,4},{6,7},{7,6},{8,9},{9,8},{10,11... | collective-permute-start | bytes 49160 | tf_op jit(solution)/shard_map/ppermute | solution.py:186
  34.1 2.0 %collective-permute-done.4 = f32[1,4,2,4,128]{4,3,2,1,0:T(4,128)S(1)} collective-permute-done((f32[1,4,2,4,128]{4,3,2,1,0:T(4,128)}, f32[1,4,2,4,128]{4,3,2,1,0:T(4,128)S(1)}, u32[]{:S(2)}, u32[]{:S(2)}) %collective-permute-start.4) | collective-permute-done | bytes 16416 | tf_op jit(solution)/shard_map/ppermute | solution.py:186
  36.2 3.5 %collective-permute-start.5 = (f32[2,4,2,4,128]{4,3,2,1,0:T(4,128)S(1)}, f32[2,4,2,4,128]{4,3,2,1,0:T(4,128)S(1)}, u32[]{:S(2)}, u32[]{:S(2)}) collective-permute-start(f32[2,4,2,4,128]{4,3,2,1,0:T(4,128)S(1)} %maximum_select_fusion.4), channel_id=1, source_target_pairs={{0,2},{1,3},{2,0},{3,1},{4,6},{5,7},{6,4},{7,5},{8,10},{9,11},{10,... | collective-permute-start | bytes 98312 | tf_op jit(solution)/shard_map/ppermute | solution.py:186
  39.6 1.9 %collective-permute-done.5 = f32[2,4,2,4,128]{4,3,2,1,0:T(4,128)S(1)} collective-permute-done((f32[2,4,2,4,128]{4,3,2,1,0:T(4,128)S(1)}, f32[2,4,2,4,128]{4,3,2,1,0:T(4,128)S(1)}, u32[]{:S(2)}, u32[]{:S(2)}) %collective-permute-start.5) | collective-permute-done | bytes 32800 | tf_op jit(solution)/shard_map/ppermute | solution.py:186
  41.6 3.4 %collective-permute-start.6 = (f32[4,4,2,4,128]{4,3,2,1,0:T(4,128)S(1)}, f32[4,4,2,4,128]{4,3,2,1,0:T(4,128)S(1)}, u32[]{:S(2)}, u32[]{:S(2)}) collective-permute-start(f32[4,4,2,4,128]{4,3,2,1,0:T(4,128)S(1)} %maximum_select_fusion.3), channel_id=1, source_target_pairs={{0,4},{1,5},{2,6},{3,7},{4,0},{5,1},{6,2},{7,3},{8,12},{9,13},{10,... | collective-permute-start | bytes 196616 | tf_op jit(solution)/shard_map/ppermute | solution.py:186
  45.0 2.2 %collective-permute-done.6 = f32[4,4,2,4,128]{4,3,2,1,0:T(4,128)S(1)} collective-permute-done((f32[4,4,2,4,128]{4,3,2,1,0:T(4,128)S(1)}, f32[4,4,2,4,128]{4,3,2,1,0:T(4,128)S(1)}, u32[]{:S(2)}, u32[]{:S(2)}) %collective-permute-start.6) | collective-permute-done | bytes 65568 | tf_op jit(solution)/shard_map/ppermute | solution.py:186
  47.9 2.2 %shard_map.31 = f32[128,4,128]{2,1,0:T(4,128)} custom-call(s32[1]{0:T(128)} %bitcast.position_ref, f32[8,4,2,4,128]{4,3,2,1,0:T(4,128)} %maximum_select_fusion.2.g_ref, f32[3,128,4,128]{3,2,1,0:T(4,128)} %get-tuple-element.12.responses_ref), custom_call_target="tpu_custom_call" | custom-call | tf_op jit(solution)/shard_map/pallas_call | solution.py:137
  50.1 1.1 %copy.24 = f32[128,4,128]{0,2,1:T(8,128)S(1)} copy(f32[128,4,128]{2,1,0:T(4,128)} %shard_map.31) | data formatting | bytes 524288 | tf_op jit(solution)/shard_map/pallas_call | solution.py:137
  52.0 1.9 %shard_map.32 = f32[16,32,128]{2,1,0:T(8,128)} custom-call(f32[16,32,128]{2,1,0:T(8,128)} %copy-done.1, f32[16,32,128]{2,1,0:T(8,128)} %multiply_subtract_fusion.d_ref), custom_call_target="tpu_custom_call" | custom-call | tf_op jit(solution)/shard_map/pallas_call | solution.py:171
  (25 shorter events, 4.6 us)
Async XLA Ops:
  1.2 7.1 %copy-start = (f32[16,32,128]{2,1,0:T(8,128)S(1)}, f32[16,32,128]{2,1,0:T(8,128)}, u32[]{:S(2)}) copy-start(f32[16,32,128]{2,1,0:T(8,128)} %param.2) | copy-start | bytes 786436
  1.3 7.8 %collective-permute-start.1 = (f32[16,32]{1,0:T(8,128)S(1)}, f32[16,32]{1,0:T(8,128)S(1)}, u32[]{:S(2)}, u32[]{:S(2)}) collective-permute-start(f32[16,32]{1,0:T(8,128)S(1)} %bitcast.38), channel_id=1, source_target_pairs={{1,0},{2,1},{3,2},{4,3},{5,4},{6,5},{7,6},{9,8},{10,9},{11,10},{12... | collective-permute-start | bytes 6152 | tf_op jit(solution)/shard_map/ppermute | solution.py:19
  2.8 6.8 %collective-permute-start = (f32[16,32]{1,0:T(8,128)S(1)}, f32[16,32]{1,0:T(8,128)S(1)}, u32[]{:S(2)}, u32[]{:S(2)}) collective-permute-start(f32[16,32]{1,0:T(8,128)S(1)} %bitcast.40), channel_id=1, source_target_pairs={{0,1},{1,2},{2,3},{3,4},{4,5},{5,6},{6,7},{8,9},{9,10},{10,11},{11... | collective-permute-start | bytes 6152 | tf_op jit(solution)/shard_map/ppermute | solution.py:18
  9.1 1.0 %copy-start.2 = (f32[16,32,128]{2,1,0:T(8,128)S(1)}, f32[16,32,128]{2,1,0:T(8,128)}, u32[]{:S(2)}) copy-start(f32[16,32,128]{2,1,0:T(8,128)} %param.3) | copy-start | bytes 786436
  10.4 8.6 %copy-start.1 = (f32[16,32,128]{2,1,0:T(8,128)}, f32[16,32,128]{2,1,0:T(8,128)S(1)}, u32[]{:S(2)}) copy-start(f32[16,32,128]{2,1,0:T(8,128)S(1)} %get-tuple-element.18.h_ref) | copy-start | bytes 786436
  14.4 1.5 %collective-permute-start.2 = (f32[1,5,2,16,128]{4,3,2,1,0:T(8,128)}, f32[1,5,2,16,128]{4,3,2,1,0:T(8,128)S(1)}, u32[]{:S(2)}, u32[]{:S(2)}) collective-permute-start(f32[1,5,2,16,128]{4,3,2,1,0:T(8,128)} %bitcast.32), channel_id=1, source_target_pairs={{0,8},{8,0},{16,24},{24,16},{1,9},{9,1},{17,25},{25,17},{2,10},{10... | collective-permute-start | bytes 245768 | tf_op jit(solution)/shard_map/ppermute | solution.py:186
  16.9 6.6 %collective-permute-start.3 = (f32[2,5,2,16,128]{4,3,2,1,0:T(8,128)S(1)}, f32[2,5,2,16,128]{4,3,2,1,0:T(8,128)S(1)}, u32[]{:S(2)}, u32[]{:S(2)}) collective-permute-start(f32[2,5,2,16,128]{4,3,2,1,0:T(8,128)S(1)} %maximum_select_fusion.1), channel_id=1, source_target_pairs={{0,16},{8,24},{16,0},{24,8},{1,17},{9,25},{17,1},{25,9},{2,18},{10... | collective-permute-start | bytes 491528 | tf_op jit(solution)/shard_map/ppermute | solution.py:186
  31.5 4.6 %copy-start.3 = (f32[4,2,4,128]{3,2,1,0:T(4,128)S(1)}, f32[4,2,4,128]{3,2,1,0:T(4,128)}, u32[]{:S(2)}) copy-start(f32[4,2,4,128]{3,2,1,0:T(4,128)} %get-tuple-element.11) | copy-start | bytes 49156
  31.5 4.6 %collective-permute-start.4 = (f32[1,4,2,4,128]{4,3,2,1,0:T(4,128)}, f32[1,4,2,4,128]{4,3,2,1,0:T(4,128)S(1)}, u32[]{:S(2)}, u32[]{:S(2)}) collective-permute-start(f32[1,4,2,4,128]{4,3,2,1,0:T(4,128)} %bitcast.36), channel_id=1, source_target_pairs={{0,1},{1,0},{2,3},{3,2},{4,5},{5,4},{6,7},{7,6},{8,9},{9,8},{10,11... | collective-permute-start | bytes 49160 | tf_op jit(solution)/shard_map/ppermute | solution.py:186
  36.2 5.4 %collective-permute-start.5 = (f32[2,4,2,4,128]{4,3,2,1,0:T(4,128)S(1)}, f32[2,4,2,4,128]{4,3,2,1,0:T(4,128)S(1)}, u32[]{:S(2)}, u32[]{:S(2)}) collective-permute-start(f32[2,4,2,4,128]{4,3,2,1,0:T(4,128)S(1)} %maximum_select_fusion.4), channel_id=1, source_target_pairs={{0,2},{1,3},{2,0},{3,1},{4,6},{5,7},{6,4},{7,5},{8,10},{9,11},{10,... | collective-permute-start | bytes 98312 | tf_op jit(solution)/shard_map/ppermute | solution.py:186
  41.6 5.7 %collective-permute-start.6 = (f32[4,4,2,4,128]{4,3,2,1,0:T(4,128)S(1)}, f32[4,4,2,4,128]{4,3,2,1,0:T(4,128)S(1)}, u32[]{:S(2)}, u32[]{:S(2)}) collective-permute-start(f32[4,4,2,4,128]{4,3,2,1,0:T(4,128)S(1)} %maximum_select_fusion.3), channel_id=1, source_target_pairs={{0,4},{1,5},{2,6},{3,7},{4,0},{5,1},{6,2},{7,3},{8,12},{9,13},{10,... | collective-permute-start | bytes 196616 | tf_op jit(solution)/shard_map/ppermute | solution.py:186

commit v13 on v8

--- a/solution.py
+++ b/solution.py
@@ -146,18 +146,28 @@
     )(position, gathered, responses)
 
 
-def sweep_kernel(h_ref, d_ref, out_ref, ratio_ref):
+def sweep_kernel(h_ref, s_ref, u_ref, out_ref, ratio_ref):
     n = h_ref.shape[0]
+
+    def side(i):
+        centre = u_ref[i]
+        curve = -2.0 * centre
+        if i > 0:
+            curve = u_ref[i - 1] + curve
+        if i < n - 1:
+            curve = curve + u_ref[i + 1]
+        return s_ref[i] - h_ref[i] * curve
+
     ratio = None
     value = None
     for i in range(n):
         hi = h_ref[i]
         if i == 0:
             denom = 1.0 + 2.0 * hi
-            value = d_ref[i] / denom
+            value = side(i) / denom
         else:
             denom = 1.0 + 2.0 * hi + hi * ratio
-            value = (d_ref[i] + hi * value) / denom
+            value = (side(i) + hi * value) / denom
         ratio = -hi / denom
         ratio_ref[i] = ratio
         out_ref[i] = value
@@ -167,12 +177,12 @@
         out_ref[i] = x
 
 
-def sweep_call(h_lines, d_lines):
+def sweep_call(h_lines, d_lines, u_lines):
     return pl.pallas_call(
         sweep_kernel,
         out_shape=jax.ShapeDtypeStruct(h_lines.shape, jnp.float32),
         scratch_shapes=[pltpu_vmem(h_lines.shape)],
-    )(h_lines, d_lines)
+    )(h_lines, d_lines, u_lines)
 
 
 def doubling_gather(part, axis):
@@ -247,8 +257,7 @@
     rate_lines = jnp.transpose(half_rate, (2, 0, 1)).reshape(column_count, groups, lanes)
     column_lines = distributed_solve(rate_lines, side_lines, "gy", True)
     second = jnp.transpose(column_lines.reshape(column_count, plane_count, row_count), (1, 2, 0))
-    plane_side = second - implicit_weight * depth_implicit_solve
-    return sweep_call(half_rate, plane_side)
+    return sweep_call(half_rate, second, initial_heat_values)
 
 
 def solution(mesh):

time: 52.8 us -> 52.1 us (0.987)
  starting transfers between devices: 15.7 us -> 14.5 us
  local copies, waits for them, and re-layouts: 6.77 us -> 7.5 us
  blocking collectives: 8.1 us -> 7.57 us
    sub x2 -> x0, other arithmetic: 1.82 us -> none  [the longest x1 1.05 us: per_device(): second_side = first_pass - implicit_weight * vertical_implicit_solve]
    transpose x0 -> x2, other arithmetic: none -> 1.02 us  [the longest x1 0.98 us: per_device(): jnp.transpose(second_side, (2, 0, 1)).reshape(column_count, groups, lanes)]
    transpose x1, other arithmetic: 0.33 us -> 1.18 us  [per_device(): jnp.moveaxis(forward_euler_increment - implicit_weight * horizontal_impli...]
    unnamed x10 -> x11, local copies, waits for them, and re-layouts: 0.57 us -> 1.38 us
    transpose x1, local copies, waits for them, and re-layouts: 0.86 us -> 0.09 us  [per_device(): jnp.transpose(second_side, (2, 0, 1)).reshape(column_count, groups, lanes)]
    pallas_call x1, local copies, waits for them, and re-layouts: 1.07 us -> 1.78 us  [finish_call(): pl.pallas_call(finish_kernel, out_shape=jax.ShapeDtypeStruct((n,) + rest,...]
    ppermute x1, starting transfers between devices: 5.47 us -> 4.84 us  [halos(): low = lax.ppermute(last, axis, forward)]
    ppermute x3, starting transfers between devices: 8.98 us -> 8.39 us  [doubling_gather(): other = lax.ppermute(held, axis, [(i, i ^ step) for i in range(count)])]
  transfers between devices with their start and end apart: 5 -> 5, of which waited for: 4 -> 4; matrix products, arithmetic and copies ran while one was open for 2% -> 6% of each run, Pallas kernels for 0% -> 0%
where the time goes in v13:
time: 52.1 us; the launch traced here: 51.6 us
  starting transfers between devices  14.5 us (28%)
  Pallas kernels  11.8 us (23%)
  blocking collectives  7.57 us (15%)
  local copies, waits for them, and re-layouts  7.5 us (14%)
  waiting for transfers between devices  6.51 us (12%)
  other arithmetic  3.56 us (7%)
    ppermute x3, starting transfers between devices, doubling_gather(): other = lax.ppermute(held, axis, [(i, i ^ step) for i in range(count)])  8.39 us
    all_gather x1, blocking collectives, distributed_solve(): gathered = lax.all_gather(reduced, axis)  7.57 us
    ppermute x3, waiting for transfers between devices, doubling_gather(): other = lax.ppermute(held, axis, [(i, i ^ step) for i in range(count)])  6.14 us
    pallas_call x2, Pallas kernels, partition_call(): pl.pallas_call(partition_kernel, out_shape=(jax.ShapeDtypeStruct((3, n) +...  5.6 us
    ppermute x1, starting transfers between devices, halos(): low = lax.ppermute(last, axis, forward)  4.84 us
    pallas_call x2, Pallas kernels, finish_call(): pl.pallas_call(finish_kernel, out_shape=jax.ShapeDtypeStruct((n,) + rest,...  4.24 us
    pallas_call x1, Pallas kernels, sweep_call(): pl.pallas_call(sweep_kernel, out_shape=jax.ShapeDtypeStruct(h_lines.shape...  1.99 us
    pallas_call x1, local copies, waits for them, and re-layouts, finish_call(): pl.pallas_call(finish_kernel, out_shape=jax.ShapeDtypeStruct((n,) + rest,...  1.78 us
  transfers between devices with their start and end apart: 5, of which 4 were waited for; matrix products, arithmetic and copies ran while one was open for 6% of the time, Pallas kernels for 0%

profile of v13, /device:TPU:0, one launch (start us, length us, event | category | flops | bytes accessed | tf_op | source)
XLA Modules:
  0.0 51.6 jit_solution(12653278982736073773)
XLA Ops:
  0.0 1.2 %fusion.11 = (f32[16,32,1]{2,1,0:T(8,128)S(1)}, f32[16,32,1]{2,1,0:T(8,128)S(1)}) fusion(f32[16,32,128]{2,1,0:T(8,128)} %u_ref.1), kind=kLoop, calls=%fused_computation.22 | loop fusion | bytes 8192 | tf_op jit(solution)/shard_map/slice | solution.py:16
  1.3 4.8 %collective-permute-start = (f32[16,32]{1,0:T(8,128)S(1)}, f32[16,32]{1,0:T(8,128)S(1)}, u32[]{:S(2)}, u32[]{:S(2)}) collective-permute-start(f32[16,32]{1,0:T(8,128)S(1)} %bitcast.35), channel_id=1, source_target_pairs={{0,1},{1,2},{2,3},{3,4},{4,5},{5,6},{6,7},{8,9},{9,10},{10,11},{11... | collective-permute-start | bytes 6152 | tf_op jit(solution)/shard_map/ppermute | solution.py:18
  6.3 1.3 %collective-permute-start.1 = (f32[16,32]{1,0:T(8,128)S(1)}, f32[16,32]{1,0:T(8,128)S(1)}, u32[]{:S(2)}, u32[]{:S(2)}) collective-permute-start(f32[16,32]{1,0:T(8,128)S(1)} %bitcast.37), channel_id=1, source_target_pairs={{1,0},{2,1},{3,2},{4,3},{5,4},{6,5},{7,6},{9,8},{10,9},{11,10},{12... | collective-permute-start | bytes 6152 | tf_op jit(solution)/shard_map/ppermute | solution.py:19
  8.0 0.9 %copy-done.2 = f32[16,32,128]{2,1,0:T(8,128)S(1)} copy-done((f32[16,32,128]{2,1,0:T(8,128)S(1)}, f32[16,32,128]{2,1,0:T(8,128)}, u32[]{:S(2)}) %copy-start.2) | copy-done | bytes 262168
  9.0 0.6 %pad_maximum_fusion.refs_0_ = f32[2,16,128]{2,1,0:T(8,128)} fusion(f32[1,16,128]{2,1,0:T(8,128)S(1)} %get-tuple-element.16, f32[1,16,128]{2,1,0:T(8,128)S(1)} %get-tuple-element.15), kind=kLoop, calls=%fused_computation.18 | loop fusion | flops 4096 | bytes 32768 | tf_op jit(solution)/shard_map/stack | solution.py:251
  9.6 0.9 %copy.52.h_ref = f32[32,16,128]{2,1,0:T(8,128)} copy(f32[32,16,128]{2,0,1:T(8,128)S(1)} %get-tuple-element.23) | data formatting | bytes 524288 | tf_op jit(solution)/shard_map/transpose | solution.py:245
  10.5 0.8 %copy.54.h_ref = f32[128,4,128]{2,1,0:T(4,128)} copy(f32[128,4,128]{0,2,1:T(8,128)S(1)} %bitcast.29) | data formatting | bytes 524288 | tf_op jit(solution)/shard_map/reshape | solution.py:257
  12.1 1.2 %fusion.5 = (f32[32,16,128]{2,1,0:T(8,128)}, f32[16,32,128]{2,0,1:T(8,128)S(1)}) fusion(f32[16,32,128]{2,0,1:T(8,128)S(1)} %copy.42, f32[16,31,128]{2,0,1:T(8,128)S(1)} %get-tuple-element.22, f32[16,31,128]{2,0,1:T(8,128)S(1)} %get-tuple-element.21, f32[16,32,128]{2,1,0:T(8,128)S(1)} %copy-done.2, f32[16,32,1]{2,0,1:T(8,128)S(1)} %copy.48, ...), kind=kLoop, calls=%fused_computation.7 | loop fusion | flops 1245184 | bytes 2342912 | tf_op jit(solution)/shard_map/transpose | solution.py:242
  13.3 2.3 %shard_map.28 = (f32[3,32,16,128]{3,2,1,0:T(8,128)}, f32[5,2,16,128]{3,2,1,0:T(8,128)}) custom-call(f32[32,16,128]{2,1,0:T(8,128)} %copy.52.h_ref, f32[32,16,128]{2,1,0:T(8,128)} %get-tuple-element.13.d_ref, f32[2,16,128]{2,1,0:T(8,128)} %pad_maximum_fusion.refs_0_), custom_call_target="tpu_custom_call" | custom-call | tf_op jit(solution)/shard_map/pallas_call | solution.py:82
  15.5 7.6 %all-gather = f32[20,2,16,128]{3,2,1,0:T(8,128)} all-gather(f32[5,2,16,128]{3,2,1,0:T(8,128)} %get-tuple-element.9), channel_id=2, replica_groups=mesh['gx'=4,'gy'=8] {'gx'}, dimensions={0}, use_global_device_ids=true | all-gather | bytes 409600 | tf_op jit(solution)/shard_map/all_gather | solution.py:210
  23.1 2.1 %shard_map.29 = f32[32,16,128]{2,1,0:T(8,128)} custom-call(s32[1]{0:T(128)} %bitcast.3.position_ref, f32[4,5,2,16,128]{4,3,2,1,0:T(8,128)} %bitcast.30, f32[3,32,16,128]{3,2,1,0:T(8,128)} %get-tuple-element.10.responses_ref), custom_call_target="tpu_custom_call" | custom-call | tf_op jit(solution)/shard_map/pallas_call | solution.py:137
  25.2 1.0 %fusion.8 = f32[128,16,32]{0,1,2:T(8,128)S(1)} fusion(f32[32,16,128]{2,1,0:T(8,128)} %shard_map.29, f32[16,32,128]{2,0,1:T(8,128)S(1)} %get-tuple-element.14), kind=kLoop, calls=%fused_computation.12 | loop fusion | flops 131072 | bytes 786432 | tf_op jit(solution)/shard_map/transpose | solution.py:256
  26.3 0.8 %copy.55.d_ref = f32[128,4,128]{2,1,0:T(4,128)} copy(f32[128,4,128]{0,2,1:T(8,128)S(1)} %bitcast.31) | data formatting | bytes 524288 | tf_op jit(solution)/shard_map/reshape | solution.py:256
  27.1 3.3 %shard_map.30 = (f32[3,128,4,128]{3,2,1,0:T(4,128)}, f32[4,2,4,128]{3,2,1,0:T(4,128)}) custom-call(f32[128,4,128]{2,1,0:T(4,128)} %copy.54.h_ref, f32[128,4,128]{2,1,0:T(4,128)} %copy.55.d_ref), custom_call_target="tpu_custom_call" | custom-call | tf_op jit(solution)/shard_map/pallas_call | solution.py:82
  30.4 2.5 %collective-permute-start.2 = (f32[1,4,2,4,128]{4,3,2,1,0:T(4,128)}, f32[1,4,2,4,128]{4,3,2,1,0:T(4,128)S(1)}, u32[]{:S(2)}, u32[]{:S(2)}) collective-permute-start(f32[1,4,2,4,128]{4,3,2,1,0:T(4,128)} %bitcast.33), channel_id=1, source_target_pairs={{0,1},{1,0},{2,3},{3,2},{4,5},{5,4},{6,7},{7,6},{8,9},{9,8},{10,11... | collective-permute-start | bytes 49160 | tf_op jit(solution)/shard_map/ppermute | solution.py:196
  32.9 2.0 %collective-permute-done.2 = f32[1,4,2,4,128]{4,3,2,1,0:T(4,128)S(1)} collective-permute-done((f32[1,4,2,4,128]{4,3,2,1,0:T(4,128)}, f32[1,4,2,4,128]{4,3,2,1,0:T(4,128)S(1)}, u32[]{:S(2)}, u32[]{:S(2)}) %collective-permute-start.2) | collective-permute-done | bytes 16416 | tf_op jit(solution)/shard_map/ppermute | solution.py:196
  34.9 2.8 %collective-permute-start.3 = (f32[2,4,2,4,128]{4,3,2,1,0:T(4,128)S(1)}, f32[2,4,2,4,128]{4,3,2,1,0:T(4,128)S(1)}, u32[]{:S(2)}, u32[]{:S(2)}) collective-permute-start(f32[2,4,2,4,128]{4,3,2,1,0:T(4,128)S(1)} %maximum_select_fusion.2), channel_id=1, source_target_pairs={{0,2},{1,3},{2,0},{3,1},{4,6},{5,7},{6,4},{7,5},{8,10},{9,11},{10,... | collective-permute-start | bytes 98312 | tf_op jit(solution)/shard_map/ppermute | solution.py:196
  37.7 1.9 %collective-permute-done.3 = f32[2,4,2,4,128]{4,3,2,1,0:T(4,128)S(1)} collective-permute-done((f32[2,4,2,4,128]{4,3,2,1,0:T(4,128)S(1)}, f32[2,4,2,4,128]{4,3,2,1,0:T(4,128)S(1)}, u32[]{:S(2)}, u32[]{:S(2)}) %collective-permute-start.3) | collective-permute-done | bytes 32800 | tf_op jit(solution)/shard_map/ppermute | solution.py:196
  39.7 3.1 %collective-permute-start.4 = (f32[4,4,2,4,128]{4,3,2,1,0:T(4,128)S(1)}, f32[4,4,2,4,128]{4,3,2,1,0:T(4,128)S(1)}, u32[]{:S(2)}, u32[]{:S(2)}) collective-permute-start(f32[4,4,2,4,128]{4,3,2,1,0:T(4,128)S(1)} %maximum_select_fusion.1), channel_id=1, source_target_pairs={{0,4},{1,5},{2,6},{3,7},{4,0},{5,1},{6,2},{7,3},{8,12},{9,13},{10,... | collective-permute-start | bytes 196616 | tf_op jit(solution)/shard_map/ppermute | solution.py:196
  42.8 2.2 %collective-permute-done.4 = f32[4,4,2,4,128]{4,3,2,1,0:T(4,128)S(1)} collective-permute-done((f32[4,4,2,4,128]{4,3,2,1,0:T(4,128)S(1)}, f32[4,4,2,4,128]{4,3,2,1,0:T(4,128)S(1)}, u32[]{:S(2)}, u32[]{:S(2)}) %collective-permute-start.4) | collective-permute-done | bytes 65568 | tf_op jit(solution)/shard_map/ppermute | solution.py:196
  45.0 0.7 %maximum_select_fusion.g_ref = f32[8,4,2,4,128]{4,3,2,1,0:T(4,128)} fusion(f32[4,4,2,4,128]{4,3,2,1,0:T(4,128)S(1)} %collective-permute-done.4, f32[4,4,2,4,128]{4,3,2,1,0:T(4,128)S(1)} %maximum_select_fusion.1, pred[]{:T(512)S(6)} %eq.13), kind=kLoop, calls=%fused_computation.14 | loop fusion | flops 98304 | bytes 262145 | tf_op jit(solution)/shard_map/jit(_where)/select_n | solution.py:198
  45.7 2.2 %shard_map.31 = f32[128,4,128]{2,1,0:T(4,128)} custom-call(s32[1]{0:T(128)} %bitcast.position_ref, f32[8,4,2,4,128]{4,3,2,1,0:T(4,128)} %maximum_select_fusion.g_ref, f32[3,128,4,128]{3,2,1,0:T(4,128)} %get-tuple-element.12.responses_ref), custom_call_target="tpu_custom_call" | custom-call | tf_op jit(solution)/shard_map/pallas_call | solution.py:137
  47.9 1.8 %copy.56 = f32[128,4,128]{0,2,1:T(8,128)} copy(f32[128,4,128]{2,1,0:T(4,128)} %shard_map.31) | data formatting | bytes 524288 | tf_op jit(solution)/shard_map/pallas_call | solution.py:137
  49.6 2.0 %shard_map.32 = f32[16,32,128]{2,1,0:T(8,128)} custom-call(f32[16,32,128]{2,1,0:T(8,128)} %copy-done.1, f32[16,32,128]{2,1,0:T(8,128)} %bitcast.32, f32[16,32,128]{2,1,0:T(8,128)} %u_ref.1), custom_call_target="tpu_custom_call" | custom-call | tf_op jit(solution)/shard_map/pallas_call | solution.py:181
  (21 shorter events, 1.6 us)
Async XLA Ops:
  1.2 6.5 %copy-start = (f32[16,32,128]{2,1,0:T(8,128)S(1)}, f32[16,32,128]{2,1,0:T(8,128)}, u32[]{:S(2)}) copy-start(f32[16,32,128]{2,1,0:T(8,128)} %u_ref.1) | copy-start | bytes 786436
  1.3 10.0 %collective-permute-start = (f32[16,32]{1,0:T(8,128)S(1)}, f32[16,32]{1,0:T(8,128)S(1)}, u32[]{:S(2)}, u32[]{:S(2)}) collective-permute-start(f32[16,32]{1,0:T(8,128)S(1)} %bitcast.35), channel_id=1, source_target_pairs={{0,1},{1,2},{2,3},{3,4},{4,5},{5,6},{6,7},{8,9},{9,10},{10,11},{11... | collective-permute-start | bytes 6152 | tf_op jit(solution)/shard_map/ppermute | solution.py:18
  6.3 5.5 %collective-permute-start.1 = (f32[16,32]{1,0:T(8,128)S(1)}, f32[16,32]{1,0:T(8,128)S(1)}, u32[]{:S(2)}, u32[]{:S(2)}) collective-permute-start(f32[16,32]{1,0:T(8,128)S(1)} %bitcast.37), channel_id=1, source_target_pairs={{1,0},{2,1},{3,2},{4,3},{5,4},{6,5},{7,6},{9,8},{10,9},{11,10},{12... | collective-permute-start | bytes 6152 | tf_op jit(solution)/shard_map/ppermute | solution.py:19
  7.9 1.0 %copy-start.2 = (f32[16,32,128]{2,1,0:T(8,128)S(1)}, f32[16,32,128]{2,1,0:T(8,128)}, u32[]{:S(2)}) copy-start(f32[16,32,128]{2,1,0:T(8,128)} %param.3) | copy-start | bytes 786436
  8.9 1.5 %copy-start.1 = (f32[16,32,128]{2,1,0:T(8,128)}, f32[16,32,128]{2,1,0:T(8,128)S(1)}, u32[]{:S(2)}) copy-start(f32[16,32,128]{2,1,0:T(8,128)S(1)} %get-tuple-element.24.h_ref) | copy-start | bytes 786436
  30.4 4.5 %copy-start.3 = (f32[4,2,4,128]{3,2,1,0:T(4,128)S(1)}, f32[4,2,4,128]{3,2,1,0:T(4,128)}, u32[]{:S(2)}) copy-start(f32[4,2,4,128]{3,2,1,0:T(4,128)} %get-tuple-element.11) | copy-start | bytes 49156
  30.4 4.4 %collective-permute-start.2 = (f32[1,4,2,4,128]{4,3,2,1,0:T(4,128)}, f32[1,4,2,4,128]{4,3,2,1,0:T(4,128)S(1)}, u32[]{:S(2)}, u32[]{:S(2)}) collective-permute-start(f32[1,4,2,4,128]{4,3,2,1,0:T(4,128)} %bitcast.33), channel_id=1, source_target_pairs={{0,1},{1,0},{2,3},{3,2},{4,5},{5,4},{6,7},{7,6},{8,9},{9,8},{10,11... | collective-permute-start | bytes 49160 | tf_op jit(solution)/shard_map/ppermute | solution.py:196
  34.9 4.7 %collective-permute-start.3 = (f32[2,4,2,4,128]{4,3,2,1,0:T(4,128)S(1)}, f32[2,4,2,4,128]{4,3,2,1,0:T(4,128)S(1)}, u32[]{:S(2)}, u32[]{:S(2)}) collective-permute-start(f32[2,4,2,4,128]{4,3,2,1,0:T(4,128)S(1)} %maximum_select_fusion.2), channel_id=1, source_target_pairs={{0,2},{1,3},{2,0},{3,1},{4,6},{5,7},{6,4},{7,5},{8,10},{9,11},{10,... | collective-permute-start | bytes 98312 | tf_op jit(solution)/shard_map/ppermute | solution.py:196
  39.7 5.3 %collective-permute-start.4 = (f32[4,4,2,4,128]{4,3,2,1,0:T(4,128)S(1)}, f32[4,4,2,4,128]{4,3,2,1,0:T(4,128)S(1)}, u32[]{:S(2)}, u32[]{:S(2)}) collective-permute-start(f32[4,4,2,4,128]{4,3,2,1,0:T(4,128)S(1)} %maximum_select_fusion.1), channel_id=1, source_target_pairs={{0,4},{1,5},{2,6},{3,7},{4,0},{5,1},{6,2},{7,3},{8,12},{9,13},{10,... | collective-permute-start | bytes 196616 | tf_op jit(solution)/shard_map/ppermute | solution.py:196

commit v14 on v13

--- a/solution.py
+++ b/solution.py
@@ -1,3 +1,5 @@
+import functools
+
 import jax
 import jax.numpy as jnp
 from jax import lax
@@ -20,12 +22,22 @@
     return jnp.expand_dims(low, dim), jnp.expand_dims(high, dim)
 
 
-def partition_kernel(h_ref, d_ref, *refs):
-    if len(refs) == 4:
-        edges_ref, out_ref, red_ref, ratio_ref = refs
-    else:
-        edges_ref = None
-        out_ref, red_ref, ratio_ref = refs
+def partition_kernel(has_edges, has_curve, h_ref, d_ref, *refs):
+    refs = list(refs)
+    edges_ref = refs.pop(0) if has_edges else None
+    if has_curve:
+        u_ref, low_ref, high_ref = refs[:3]
+        refs = refs[3:]
+    out_ref, red_ref, ratio_ref = refs
+
+    def side(i):
+        if not has_curve:
+            return d_ref[i]
+        previous = u_ref[i - 1] if i > 0 else low_ref[...]
+        following = u_ref[i + 1] if i < u_ref.shape[0] - 1 else high_ref[...]
+        curve = previous - 2.0 * u_ref[i] + following
+        return d_ref[i] - h_ref[i] * curve
+
     n = h_ref.shape[0]
     ratio = jnp.zeros(h_ref.shape[1:], jnp.float32)
     vb = jnp.zeros_like(ratio)
@@ -35,10 +47,10 @@
         denom = 1.0 + 2.0 * hi + hi * ratio
         ratio = -hi / denom
         if i == 1:
-            vb = d_ref[i] / denom
+            vb = side(i) / denom
             vf = hi / denom
         else:
-            vb = (d_ref[i] + hi * vb) / denom
+            vb = (side(i) + hi * vb) / denom
             vf = (hi * vf) / denom
         if i == n - 2:
             vl = hi / denom
@@ -67,20 +79,24 @@
     red_ref[1, 1] = 1.0 + 2.0 * rt - rt * out_ref[2, n - 2]
     red_ref[2, 0] = -rh * out_ref[2, 1]
     red_ref[2, 1] = -rt
-    red_ref[3, 0] = d_ref[0] + rh * out_ref[0, 1]
-    red_ref[3, 1] = d_ref[n - 1] + rt * out_ref[0, n - 2]
+    red_ref[3, 0] = side(0) + rh * out_ref[0, 1]
+    red_ref[3, 1] = side(n - 1) + rt * out_ref[0, n - 2]
     if edges_ref is not None:
         red_ref[4, 0] = edges_ref[0]
         red_ref[4, 1] = edges_ref[1]
 
 
-def partition_call(h_lines, d_lines, edges):
+def partition_call(h_lines, d_lines, edges, curve):
     n = h_lines.shape[0]
     rest = h_lines.shape[1:]
-    operands = (h_lines, d_lines) if edges is None else (h_lines, d_lines, edges)
+    operands = (h_lines, d_lines)
+    if edges is not None:
+        operands = operands + (edges,)
+    if curve is not None:
+        operands = operands + tuple(curve)
     rows = 4 if edges is None else 5
     return pl.pallas_call(
-        partition_kernel,
+        functools.partial(partition_kernel, edges is not None, curve is not None),
         out_shape=(
             jax.ShapeDtypeStruct((3, n) + rest, jnp.float32),
             jax.ShapeDtypeStruct((rows, 2) + rest, jnp.float32),
@@ -202,8 +218,8 @@
     return held
 
 
-def distributed_solve(h_lines, d_lines, axis, doubling, edges=None):
-    responses, reduced = partition_call(h_lines, d_lines, edges)
+def distributed_solve(h_lines, d_lines, axis, doubling, edges=None, curve=None):
+    responses, reduced = partition_call(h_lines, d_lines, edges, curve)
     if doubling:
         gathered = doubling_gather(reduced, axis)
     else:
@@ -218,7 +234,14 @@
     plane_count, row_count, column_count = initial_heat_values.shape
     x_low = jnp.zeros_like(initial_heat_values[:, :1])
     x_high = x_low
-    y_low, y_high = halos(initial_heat_values, "gy", 2)
+    lanes = 128
+    groups = plane_count * row_count // lanes
+    field_lines = jnp.transpose(initial_heat_values, (2, 0, 1)).reshape(
+        column_count, groups, lanes
+    )
+    low_row, high_row = halos(field_lines, "gy", 0)
+    y_low = low_row.reshape(plane_count, row_count, 1)
+    y_high = high_row.reshape(plane_count, row_count, 1)
     horizontal_implicit_solve = conductivity_map * (
         jnp.concatenate([x_low, initial_heat_values[:, :-1]], 1)
         - 2.0 * initial_heat_values
@@ -250,12 +273,15 @@
             False,
             jnp.stack([initial_heat_values[:, 0], initial_heat_values[:, row_count - 1]], 0),
         ), 0, 1)
-    second_side = first_pass - implicit_weight * vertical_implicit_solve
-    lanes = 128
-    groups = plane_count * row_count // lanes
-    side_lines = jnp.transpose(second_side, (2, 0, 1)).reshape(column_count, groups, lanes)
+    side_lines = jnp.transpose(first_pass, (2, 0, 1)).reshape(column_count, groups, lanes)
     rate_lines = jnp.transpose(half_rate, (2, 0, 1)).reshape(column_count, groups, lanes)
-    column_lines = distributed_solve(rate_lines, side_lines, "gy", True)
+    column_lines = distributed_solve(
+        rate_lines,
+        side_lines,
+        "gy",
+        True,
+        curve=(field_lines, low_row[0], high_row[0]),
+    )
     second = jnp.transpose(column_lines.reshape(column_count, plane_count, row_count), (1, 2, 0))
     return sweep_call(half_rate, second, initial_heat_values)
 

time: 52.1 us -> 54.1 us (1.038)
  local copies, waits for them, and re-layouts: 7.5 us -> 10.5 us
  other arithmetic: 3.56 us -> 2.46 us
    another operation x0 -> x5, local copies, waits for them, and re-layouts: none -> 1.58 us  [the longest x1 1.04 us: per_device(): jnp.transpose(first_pass, (2, 0, 1)).reshape(column_count, groups, lanes)]
    transpose x1 -> x0, other arithmetic: 0.98 us -> none  [per_device(): jnp.transpose(second_side, (2, 0, 1)).reshape(column_count, groups, lanes)]
    reshape x1 -> x2, local copies, waits for them, and re-layouts: 0.84 us -> 1.69 us  [the longest x1 0.85 us: per_device(): jnp.transpose(first_pass, (2, 0, 1)).reshape(column_count, groups, lanes)]
    unnamed x11 -> x13, local copies, waits for them, and re-layouts: 1.38 us -> 2.08 us
  transfers between devices with their start and end apart: 5 -> 5, of which waited for: 4 -> 3; matrix products, arithmetic and copies ran while one was open for 6% -> 7% of each run, Pallas kernels for 0% -> 0%
where the time goes in v14:
time: 54.1 us; the launch traced here: 53.6 us
  starting transfers between devices  14.9 us (28%)
  Pallas kernels  11.9 us (22%)
  local copies, waits for them, and re-layouts  10.5 us (19%)
  blocking collectives  7.57 us (14%)
  waiting for transfers between devices  6.14 us (11%)
  other arithmetic  2.46 us (5%)
    ppermute x3, starting transfers between devices, doubling_gather(): other = lax.ppermute(held, axis, [(i, i ^ step) for i in range(count)])  8.75 us
    all_gather x1, blocking collectives, distributed_solve(): gathered = lax.all_gather(reduced, axis)  7.57 us
    ppermute x3, waiting for transfers between devices, doubling_gather(): other = lax.ppermute(held, axis, [(i, i ^ step) for i in range(count)])  6.14 us
    pallas_call x2, Pallas kernels, partition_call(): pl.pallas_call(functools.partial(partition_kernel, edges is not None, cur...  5.69 us
    ppermute x1, starting transfers between devices, halos(): low = lax.ppermute(last, axis, forward)  4.83 us
    pallas_call x2, Pallas kernels, finish_call(): pl.pallas_call(finish_kernel, out_shape=jax.ShapeDtypeStruct((n,) + rest,...  4.24 us
    unnamed x13, local copies, waits for them, and re-layouts  2.08 us
    pallas_call x1, Pallas kernels, sweep_call(): pl.pallas_call(sweep_kernel, out_shape=jax.ShapeDtypeStruct(h_lines.shape...  1.99 us
  transfers between devices with their start and end apart: 5, of which 3 were waited for; matrix products, arithmetic and copies ran while one was open for 7% of the time, Pallas kernels for 0%

profile of v14, /device:TPU:0, one launch (start us, length us, event | category | flops | bytes accessed | tf_op | source)
XLA Modules:
  0.0 53.6 jit_solution(9242728454436156944)
XLA Ops:
  0.0 1.4 %slice_reduce_fusion = (f32[16,32]{1,0:T(8,128)S(1)}, f32[16,32]{1,0:T(8,128)S(1)}) fusion(f32[128,16,32]{0,2,1:T(8,128)} %bitcast.23), kind=kLoop, calls=%fused_computation.8 | loop fusion | bytes 8192 | tf_op jit(solution)/shard_map/slice | solution.py:19
  1.5 4.8 %collective-permute-start = (f32[4,128]{1,0:T(4,128)S(1)}, f32[4,128]{1,0:T(4,128)S(1)}, u32[]{:S(2)}, u32[]{:S(2)}) collective-permute-start(f32[4,128]{1,0:T(4,128)S(1)} %squeeze.6), channel_id=1, source_target_pairs={{0,1},{1,2},{2,3},{3,4},{4,5},{5,6},{6,7},{8,9},{9,10},{10,11},{11... | collective-permute-start | bytes 6152 | tf_op jit(solution)/shard_map/ppermute | solution.py:20
  6.4 1.3 %collective-permute-start.1 = (f32[4,128]{1,0:T(4,128)S(1)}, f32[4,128]{1,0:T(4,128)S(1)}, u32[]{:S(2)}, u32[]{:S(2)}) collective-permute-start(f32[4,128]{1,0:T(4,128)S(1)} %squeeze.7), channel_id=1, source_target_pairs={{1,0},{2,1},{3,2},{4,3},{5,4},{6,5},{7,6},{9,8},{10,9},{11,10},{12... | collective-permute-start | bytes 6152 | tf_op jit(solution)/shard_map/ppermute | solution.py:21
  8.1 0.9 %copy-done.2 = f32[16,32,128]{2,1,0:T(8,128)S(1)} copy-done((f32[16,32,128]{2,1,0:T(8,128)S(1)}, f32[16,32,128]{2,1,0:T(8,128)}, u32[]{:S(2)}) %copy-start.2) | copy-done | bytes 262168
  9.6 0.9 %copy.50.h_ref = f32[32,16,128]{2,1,0:T(8,128)} copy(f32[32,16,128]{2,0,1:T(8,128)S(1)} %get-tuple-element.21) | data formatting | bytes 524288 | tf_op jit(solution)/shard_map/transpose | solution.py:268
  10.5 0.8 %copy.52.h_ref = f32[128,4,128]{2,1,0:T(4,128)} copy(f32[128,4,128]{0,2,1:T(8,128)S(1)} %bitcast.25) | data formatting | bytes 524288 | tf_op jit(solution)/shard_map/reshape | solution.py:277
  11.4 0.8 %copy.54.refs_0_ = f32[128,4,128]{2,1,0:T(4,128)} copy(f32[128,4,128]{0,2,1:T(8,128)S(1)} %bitcast.24) | data formatting | bytes 524288 | tf_op jit(solution)/shard_map/reshape | solution.py:239
  13.8 1.1 %fusion.5.d_ref = f32[32,16,128]{2,1,0:T(8,128)} fusion(f32[16,32,128]{2,0,1:T(8,128)S(1)} %copy.42, f32[16,32,127]{2,0,1:T(8,128)S(1)} %get-tuple-element.20, f32[16,32,1]{2,0,1:T(8,128)S(1)} %copy.44, f32[16,32,1]{2,0,1:T(8,128)S(1)} %copy.46, f32[16,32,127]{2,0,1:T(8,128)S(1)} %get-tuple-element.19, f32[16,32,128]{2,1,0:T(8,128)S(1)} %copy-done.2, ...), kind=kLoop, calls=%fused_computation.7 | loop fusion | flops 1179648 | bytes 1818624 | tf_op jit(solution)/shard_map/transpose | solution.py:265
  14.9 2.3 %shard_map.28 = (f32[3,32,16,128]{3,2,1,0:T(8,128)}, f32[5,2,16,128]{3,2,1,0:T(8,128)}) custom-call(f32[32,16,128]{2,1,0:T(8,128)} %copy.50.h_ref, f32[32,16,128]{2,1,0:T(8,128)} %fusion.5.d_ref, f32[2,16,128]{2,1,0:T(8,128)} %pad_maximum_fusion.refs_0_), custom_call_target="tpu_custom_call" | custom-call | tf_op jit(solution)/shard_map/pallas_call | solution.py:98
  17.1 7.6 %all-gather = f32[20,2,16,128]{3,2,1,0:T(8,128)} all-gather(f32[5,2,16,128]{3,2,1,0:T(8,128)} %get-tuple-element.9), channel_id=2, replica_groups=mesh['gx'=4,'gy'=8] {'gx'}, dimensions={0}, use_global_device_ids=true | all-gather | bytes 409600 | tf_op jit(solution)/shard_map/all_gather | solution.py:226
  24.7 2.1 %shard_map.29 = f32[32,16,128]{2,1,0:T(8,128)} custom-call(s32[1]{0:T(128)} %bitcast.3.position_ref, f32[4,5,2,16,128]{4,3,2,1,0:T(8,128)} %bitcast.26, f32[3,32,16,128]{3,2,1,0:T(8,128)} %get-tuple-element.10.responses_ref), custom_call_target="tpu_custom_call" | custom-call | tf_op jit(solution)/shard_map/pallas_call | solution.py:153
  26.8 1.0 %copy.51 = f32[128,16,32]{0,2,1:T(8,128)S(1)} copy(f32[128,16,32]{0,1,2:T(8,128)} %bitcast.27) | data formatting | bytes 524288 | tf_op jit(solution)/shard_map/transpose;transpose | solution.py:276
  27.8 0.8 %copy.53.d_ref = f32[128,4,128]{2,1,0:T(4,128)} copy(f32[128,4,128]{0,2,1:T(8,128)S(1)} %bitcast.28) | data formatting | bytes 524288 | tf_op jit(solution)/shard_map/reshape | solution.py:276
  28.7 3.4 %shard_map.30 = (f32[3,128,4,128]{3,2,1,0:T(4,128)}, f32[4,2,4,128]{3,2,1,0:T(4,128)}) custom-call(f32[128,4,128]{2,1,0:T(4,128)} %copy.52.h_ref, f32[128,4,128]{2,1,0:T(4,128)} %copy.53.d_ref, f32[128,4,128]{2,1,0:T(4,128)} %copy.54.refs_0_, f32[4,128]{1,0:T(4,128)} %copy-done.4, f32[4,128]{1,0:T(4,128)} %copy-done.5), custom_call_target="tpu_custom_call" | custom-call | tf_op jit(solution)/shard_map/pallas_call | solution.py:98
  32.1 2.6 %collective-permute-start.2 = (f32[1,4,2,4,128]{4,3,2,1,0:T(4,128)}, f32[1,4,2,4,128]{4,3,2,1,0:T(4,128)S(1)}, u32[]{:S(2)}, u32[]{:S(2)}) collective-permute-start(f32[1,4,2,4,128]{4,3,2,1,0:T(4,128)} %bitcast.30), channel_id=1, source_target_pairs={{0,1},{1,0},{2,3},{3,2},{4,5},{5,4},{6,7},{7,6},{8,9},{9,8},{10,11... | collective-permute-start | bytes 49160 | tf_op jit(solution)/shard_map/ppermute | solution.py:212
  34.7 2.0 %collective-permute-done.2 = f32[1,4,2,4,128]{4,3,2,1,0:T(4,128)S(1)} collective-permute-done((f32[1,4,2,4,128]{4,3,2,1,0:T(4,128)}, f32[1,4,2,4,128]{4,3,2,1,0:T(4,128)S(1)}, u32[]{:S(2)}, u32[]{:S(2)}) %collective-permute-start.2) | collective-permute-done | bytes 16416 | tf_op jit(solution)/shard_map/ppermute | solution.py:212
  36.7 3.0 %collective-permute-start.3 = (f32[2,4,2,4,128]{4,3,2,1,0:T(4,128)S(1)}, f32[2,4,2,4,128]{4,3,2,1,0:T(4,128)S(1)}, u32[]{:S(2)}, u32[]{:S(2)}) collective-permute-start(f32[2,4,2,4,128]{4,3,2,1,0:T(4,128)S(1)} %maximum_select_fusion.2), channel_id=1, source_target_pairs={{0,2},{1,3},{2,0},{3,1},{4,6},{5,7},{6,4},{7,5},{8,10},{9,11},{10,... | collective-permute-start | bytes 98312 | tf_op jit(solution)/shard_map/ppermute | solution.py:212
  39.7 1.9 %collective-permute-done.3 = f32[2,4,2,4,128]{4,3,2,1,0:T(4,128)S(1)} collective-permute-done((f32[2,4,2,4,128]{4,3,2,1,0:T(4,128)S(1)}, f32[2,4,2,4,128]{4,3,2,1,0:T(4,128)S(1)}, u32[]{:S(2)}, u32[]{:S(2)}) %collective-permute-start.3) | collective-permute-done | bytes 32800 | tf_op jit(solution)/shard_map/ppermute | solution.py:212
  41.7 3.1 %collective-permute-start.4 = (f32[4,4,2,4,128]{4,3,2,1,0:T(4,128)S(1)}, f32[4,4,2,4,128]{4,3,2,1,0:T(4,128)S(1)}, u32[]{:S(2)}, u32[]{:S(2)}) collective-permute-start(f32[4,4,2,4,128]{4,3,2,1,0:T(4,128)S(1)} %maximum_select_fusion.1), channel_id=1, source_target_pairs={{0,4},{1,5},{2,6},{3,7},{4,0},{5,1},{6,2},{7,3},{8,12},{9,13},{10,... | collective-permute-start | bytes 196616 | tf_op jit(solution)/shard_map/ppermute | solution.py:212
  44.8 2.2 %collective-permute-done.4 = f32[4,4,2,4,128]{4,3,2,1,0:T(4,128)S(1)} collective-permute-done((f32[4,4,2,4,128]{4,3,2,1,0:T(4,128)S(1)}, f32[4,4,2,4,128]{4,3,2,1,0:T(4,128)S(1)}, u32[]{:S(2)}, u32[]{:S(2)}) %collective-permute-start.4) | collective-permute-done | bytes 65568 | tf_op jit(solution)/shard_map/ppermute | solution.py:212
  47.0 0.7 %maximum_select_fusion.g_ref = f32[8,4,2,4,128]{4,3,2,1,0:T(4,128)} fusion(f32[4,4,2,4,128]{4,3,2,1,0:T(4,128)S(1)} %collective-permute-done.4, f32[4,4,2,4,128]{4,3,2,1,0:T(4,128)S(1)} %maximum_select_fusion.1, pred[]{:T(512)S(6)} %eq.13), kind=kLoop, calls=%fused_computation.15 | loop fusion | flops 98304 | bytes 262145 | tf_op jit(solution)/shard_map/jit(_where)/select_n | solution.py:214
  47.7 2.2 %shard_map.31 = f32[128,4,128]{2,1,0:T(4,128)} custom-call(s32[1]{0:T(128)} %bitcast.position_ref, f32[8,4,2,4,128]{4,3,2,1,0:T(4,128)} %maximum_select_fusion.g_ref, f32[3,128,4,128]{3,2,1,0:T(4,128)} %get-tuple-element.12.responses_ref), custom_call_target="tpu_custom_call" | custom-call | tf_op jit(solution)/shard_map/pallas_call | solution.py:153
  49.9 1.8 %copy.55 = f32[128,4,128]{0,2,1:T(8,128)} copy(f32[128,4,128]{2,1,0:T(4,128)} %shard_map.31) | data formatting | bytes 524288 | tf_op jit(solution)/shard_map/pallas_call | solution.py:153
  51.7 2.0 %shard_map.32 = f32[16,32,128]{2,1,0:T(8,128)} custom-call(f32[16,32,128]{2,1,0:T(8,128)} %copy-done.1, f32[16,32,128]{2,1,0:T(8,128)} %bitcast.29, f32[16,32,128]{2,1,0:T(8,128)} %u_ref.1), custom_call_target="tpu_custom_call" | custom-call | tf_op jit(solution)/shard_map/pallas_call | solution.py:197
  (27 shorter events, 2.8 us)
Async XLA Ops:
  0.0 7.7 %copy-start = (f32[16,32,128]{2,1,0:T(8,128)S(1)}, f32[16,32,128]{2,1,0:T(8,128)}, u32[]{:S(2)}) copy-start(f32[16,32,128]{2,1,0:T(8,128)} %u_ref.1) | copy-start | bytes 786436
  1.5 10.7 %collective-permute-start = (f32[4,128]{1,0:T(4,128)S(1)}, f32[4,128]{1,0:T(4,128)S(1)}, u32[]{:S(2)}, u32[]{:S(2)}) collective-permute-start(f32[4,128]{1,0:T(4,128)S(1)} %squeeze.6), channel_id=1, source_target_pairs={{0,1},{1,2},{2,3},{3,4},{4,5},{5,6},{6,7},{8,9},{9,10},{10,11},{11... | collective-permute-start | bytes 6152 | tf_op jit(solution)/shard_map/ppermute | solution.py:20
  6.4 6.6 %collective-permute-start.1 = (f32[4,128]{1,0:T(4,128)S(1)}, f32[4,128]{1,0:T(4,128)S(1)}, u32[]{:S(2)}, u32[]{:S(2)}) collective-permute-start(f32[4,128]{1,0:T(4,128)S(1)} %squeeze.7), channel_id=1, source_target_pairs={{1,0},{2,1},{3,2},{4,3},{5,4},{6,5},{7,6},{9,8},{10,9},{11,10},{12... | collective-permute-start | bytes 6152 | tf_op jit(solution)/shard_map/ppermute | solution.py:21
  8.0 1.0 %copy-start.2 = (f32[16,32,128]{2,1,0:T(8,128)S(1)}, f32[16,32,128]{2,1,0:T(8,128)}, u32[]{:S(2)}) copy-start(f32[16,32,128]{2,1,0:T(8,128)} %param.3) | copy-start | bytes 786436
  9.0 1.5 %copy-start.1 = (f32[16,32,128]{2,1,0:T(8,128)}, f32[16,32,128]{2,1,0:T(8,128)S(1)}, u32[]{:S(2)}) copy-start(f32[16,32,128]{2,1,0:T(8,128)S(1)} %get-tuple-element.22.h_ref) | copy-start | bytes 786436
  12.2 0.6 %copy-start.4 = (f32[4,128]{1,0:T(4,128)}, f32[4,128]{1,0:T(4,128)S(1)}, u32[]{:S(2)}) copy-start(f32[4,128]{1,0:T(4,128)S(1)} %collective-permute-done.refs_1_) | copy-start | bytes 6148
  13.0 0.6 %copy-start.5 = (f32[4,128]{1,0:T(4,128)}, f32[4,128]{1,0:T(4,128)S(1)}, u32[]{:S(2)}) copy-start(f32[4,128]{1,0:T(4,128)S(1)} %collective-permute-done.1.refs_2_) | copy-start | bytes 6148
  32.1 4.6 %copy-start.3 = (f32[4,2,4,128]{3,2,1,0:T(4,128)S(1)}, f32[4,2,4,128]{3,2,1,0:T(4,128)}, u32[]{:S(2)}) copy-start(f32[4,2,4,128]{3,2,1,0:T(4,128)} %get-tuple-element.11) | copy-start | bytes 49156
  32.1 4.6 %collective-permute-start.2 = (f32[1,4,2,4,128]{4,3,2,1,0:T(4,128)}, f32[1,4,2,4,128]{4,3,2,1,0:T(4,128)S(1)}, u32[]{:S(2)}, u32[]{:S(2)}) collective-permute-start(f32[1,4,2,4,128]{4,3,2,1,0:T(4,128)} %bitcast.30), channel_id=1, source_target_pairs={{0,1},{1,0},{2,3},{3,2},{4,5},{5,4},{6,7},{7,6},{8,9},{9,8},{10,11... | collective-permute-start | bytes 49160 | tf_op jit(solution)/shard_map/ppermute | solution.py:212
  36.7 4.9 %collective-permute-start.3 = (f32[2,4,2,4,128]{4,3,2,1,0:T(4,128)S(1)}, f32[2,4,2,4,128]{4,3,2,1,0:T(4,128)S(1)}, u32[]{:S(2)}, u32[]{:S(2)}) collective-permute-start(f32[2,4,2,4,128]{4,3,2,1,0:T(4,128)S(1)} %maximum_select_fusion.2), channel_id=1, source_target_pairs={{0,2},{1,3},{2,0},{3,1},{4,6},{5,7},{6,4},{7,5},{8,10},{9,11},{10,... | collective-permute-start | bytes 98312 | tf_op jit(solution)/shard_map/ppermute | solution.py:212
  41.7 5.3 %collective-permute-start.4 = (f32[4,4,2,4,128]{4,3,2,1,0:T(4,128)S(1)}, f32[4,4,2,4,128]{4,3,2,1,0:T(4,128)S(1)}, u32[]{:S(2)}, u32[]{:S(2)}) collective-permute-start(f32[4,4,2,4,128]{4,3,2,1,0:T(4,128)S(1)} %maximum_select_fusion.1), channel_id=1, source_target_pairs={{0,4},{1,5},{2,6},{3,7},{4,0},{5,1},{6,2},{7,3},{8,12},{9,13},{10,... | collective-permute-start | bytes 196616 | tf_op jit(solution)/shard_map/ppermute | solution.py:212

commit v15 on v13

--- a/solution.py
+++ b/solution.py
@@ -146,8 +146,13 @@
     )(position, gathered, responses)
 
 
-def sweep_kernel(h_ref, s_ref, u_ref, out_ref, ratio_ref):
+def sweep_kernel(h_ref, y_ref, u_ref, out_ref, ratio_ref, s_ref):
     n = h_ref.shape[0]
+    groups = y_ref.shape[1]
+    per = n // groups
+    for g in range(groups):
+        block = jnp.transpose(y_ref[:, g, :])
+        s_ref[g * per : (g + 1) * per] = block.reshape(per, s_ref.shape[1], s_ref.shape[2])
 
     def side(i):
         centre = u_ref[i]
@@ -181,7 +186,7 @@
     return pl.pallas_call(
         sweep_kernel,
         out_shape=jax.ShapeDtypeStruct(h_lines.shape, jnp.float32),
-        scratch_shapes=[pltpu_vmem(h_lines.shape)],
+        scratch_shapes=[pltpu_vmem(h_lines.shape), pltpu_vmem(h_lines.shape)],
     )(h_lines, d_lines, u_lines)
 
 
@@ -256,8 +261,7 @@
     side_lines = jnp.transpose(second_side, (2, 0, 1)).reshape(column_count, groups, lanes)
     rate_lines = jnp.transpose(half_rate, (2, 0, 1)).reshape(column_count, groups, lanes)
     column_lines = distributed_solve(rate_lines, side_lines, "gy", True)
-    second = jnp.transpose(column_lines.reshape(column_count, plane_count, row_count), (1, 2, 0))
-    return sweep_call(half_rate, second, initial_heat_values)
+    return sweep_call(half_rate, column_lines, initial_heat_values)
 
 
 def solution(mesh):

time: 52.1 us -> 50.4 us (0.967)
  local copies, waits for them, and re-layouts: 7.5 us -> 5.72 us
    pallas_call x1 -> x0, local copies, waits for them, and re-layouts: 1.78 us -> none  [finish_call(): pl.pallas_call(finish_kernel, out_shape=jax.ShapeDtypeStruct((n,) + rest,...]
where the time goes in v15:
time: 50.4 us; the launch traced here: 50 us
  starting transfers between devices  14.5 us (29%)
  Pallas kernels  12 us (24%)
  blocking collectives  7.57 us (15%)
  waiting for transfers between devices  6.51 us (13%)
  local copies, waits for them, and re-layouts  5.72 us (11%)
  other arithmetic  3.57 us (7%)
    ppermute x3, starting transfers between devices, doubling_gather(): other = lax.ppermute(held, axis, [(i, i ^ step) for i in range(count)])  8.39 us
    all_gather x1, blocking collectives, distributed_solve(): gathered = lax.all_gather(reduced, axis)  7.57 us
    ppermute x3, waiting for transfers between devices, doubling_gather(): other = lax.ppermute(held, axis, [(i, i ^ step) for i in range(count)])  6.14 us
    pallas_call x2, Pallas kernels, partition_call(): pl.pallas_call(partition_kernel, out_shape=(jax.ShapeDtypeStruct((3, n) +...  5.6 us
    ppermute x1, starting transfers between devices, halos(): low = lax.ppermute(last, axis, forward)  4.84 us
    pallas_call x2, Pallas kernels, finish_call(): pl.pallas_call(finish_kernel, out_shape=jax.ShapeDtypeStruct((n,) + rest,...  4.24 us
    pallas_call x1, Pallas kernels, sweep_call(): pl.pallas_call(sweep_kernel, out_shape=jax.ShapeDtypeStruct(h_lines.shape...  2.12 us
    unnamed x11, local copies, waits for them, and re-layouts  1.38 us
  transfers between devices with their start and end apart: 5, of which 4 were waited for; matrix products, arithmetic and copies ran while one was open for 6% of the time, Pallas kernels for 0%

profile of v15, /device:TPU:0, one launch (start us, length us, event | category | flops | bytes accessed | tf_op | source)
XLA Modules:
  0.0 50.0 jit_solution(4431016109967540002)
XLA Ops:
  0.0 1.2 %fusion.11 = (f32[16,32,1]{2,1,0:T(8,128)S(1)}, f32[16,32,1]{2,1,0:T(8,128)S(1)}) fusion(f32[16,32,128]{2,1,0:T(8,128)} %u_ref.1), kind=kLoop, calls=%fused_computation.22 | loop fusion | bytes 8192 | tf_op jit(solution)/shard_map/slice | solution.py:16
  1.3 4.8 %collective-permute-start = (f32[16,32]{1,0:T(8,128)S(1)}, f32[16,32]{1,0:T(8,128)S(1)}, u32[]{:S(2)}, u32[]{:S(2)}) collective-permute-start(f32[16,32]{1,0:T(8,128)S(1)} %bitcast.31), channel_id=1, source_target_pairs={{0,1},{1,2},{2,3},{3,4},{4,5},{5,6},{6,7},{8,9},{9,10},{10,11},{11... | collective-permute-start | bytes 6152 | tf_op jit(solution)/shard_map/ppermute | solution.py:18
  6.3 1.3 %collective-permute-start.1 = (f32[16,32]{1,0:T(8,128)S(1)}, f32[16,32]{1,0:T(8,128)S(1)}, u32[]{:S(2)}, u32[]{:S(2)}) collective-permute-start(f32[16,32]{1,0:T(8,128)S(1)} %bitcast.33), channel_id=1, source_target_pairs={{1,0},{2,1},{3,2},{4,3},{5,4},{6,5},{7,6},{9,8},{10,9},{11,10},{12... | collective-permute-start | bytes 6152 | tf_op jit(solution)/shard_map/ppermute | solution.py:19
  8.0 0.9 %copy-done.2 = f32[16,32,128]{2,1,0:T(8,128)S(1)} copy-done((f32[16,32,128]{2,1,0:T(8,128)S(1)}, f32[16,32,128]{2,1,0:T(8,128)}, u32[]{:S(2)}) %copy-start.2) | copy-done | bytes 262168
  9.0 0.6 %pad_maximum_fusion.refs_0_ = f32[2,16,128]{2,1,0:T(8,128)} fusion(f32[1,16,128]{2,1,0:T(8,128)S(1)} %get-tuple-element.16, f32[1,16,128]{2,1,0:T(8,128)S(1)} %get-tuple-element.15), kind=kLoop, calls=%fused_computation.18 | loop fusion | flops 4096 | bytes 32768 | tf_op jit(solution)/shard_map/stack | solution.py:256
  9.6 0.9 %copy.50.h_ref = f32[32,16,128]{2,1,0:T(8,128)} copy(f32[32,16,128]{2,0,1:T(8,128)S(1)} %get-tuple-element.23) | data formatting | bytes 524288 | tf_op jit(solution)/shard_map/transpose | solution.py:250
  10.5 0.8 %copy.52.h_ref = f32[128,4,128]{2,1,0:T(4,128)} copy(f32[128,4,128]{0,2,1:T(8,128)S(1)} %bitcast.26) | data formatting | bytes 524288 | tf_op jit(solution)/shard_map/reshape | solution.py:262
  11.5 0.4 collective-permute-done.1
  12.1 1.2 %fusion.5 = (f32[32,16,128]{2,1,0:T(8,128)}, f32[16,32,128]{2,0,1:T(8,128)S(1)}) fusion(f32[16,32,128]{2,0,1:T(8,128)S(1)} %copy.40, f32[16,31,128]{2,0,1:T(8,128)S(1)} %get-tuple-element.22, f32[16,31,128]{2,0,1:T(8,128)S(1)} %get-tuple-element.21, f32[16,32,128]{2,1,0:T(8,128)S(1)} %copy-done.2, f32[16,32,1]{2,0,1:T(8,128)S(1)} %copy.46, ...), kind=kLoop, calls=%fused_computation.7 | loop fusion | flops 1245184 | bytes 2342912 | tf_op jit(solution)/shard_map/transpose | solution.py:247
  13.3 2.3 %shard_map.28 = (f32[3,32,16,128]{3,2,1,0:T(8,128)}, f32[5,2,16,128]{3,2,1,0:T(8,128)}) custom-call(f32[32,16,128]{2,1,0:T(8,128)} %copy.50.h_ref, f32[32,16,128]{2,1,0:T(8,128)} %get-tuple-element.13.d_ref, f32[2,16,128]{2,1,0:T(8,128)} %pad_maximum_fusion.refs_0_), custom_call_target="tpu_custom_call" | custom-call | tf_op jit(solution)/shard_map/pallas_call | solution.py:82
  15.5 7.6 %all-gather = f32[20,2,16,128]{3,2,1,0:T(8,128)} all-gather(f32[5,2,16,128]{3,2,1,0:T(8,128)} %get-tuple-element.9), channel_id=2, replica_groups=mesh['gx'=4,'gy'=8] {'gx'}, dimensions={0}, use_global_device_ids=true | all-gather | bytes 409600 | tf_op jit(solution)/shard_map/all_gather | solution.py:215
  23.1 2.1 %shard_map.29 = f32[32,16,128]{2,1,0:T(8,128)} custom-call(s32[1]{0:T(128)} %bitcast.3.position_ref, f32[4,5,2,16,128]{4,3,2,1,0:T(8,128)} %bitcast.27, f32[3,32,16,128]{3,2,1,0:T(8,128)} %get-tuple-element.10.responses_ref), custom_call_target="tpu_custom_call" | custom-call | tf_op jit(solution)/shard_map/pallas_call | solution.py:137
  25.2 1.0 %fusion.8 = f32[128,16,32]{0,1,2:T(8,128)S(1)} fusion(f32[32,16,128]{2,1,0:T(8,128)} %shard_map.29, f32[16,32,128]{2,0,1:T(8,128)S(1)} %get-tuple-element.14), kind=kLoop, calls=%fused_computation.12 | loop fusion | flops 131072 | bytes 786432 | tf_op jit(solution)/shard_map/transpose | solution.py:261
  26.3 0.8 %copy.53.d_ref = f32[128,4,128]{2,1,0:T(4,128)} copy(f32[128,4,128]{0,2,1:T(8,128)S(1)} %bitcast.28) | data formatting | bytes 524288 | tf_op jit(solution)/shard_map/reshape | solution.py:261
  27.1 3.3 %shard_map.30 = (f32[3,128,4,128]{3,2,1,0:T(4,128)}, f32[4,2,4,128]{3,2,1,0:T(4,128)}) custom-call(f32[128,4,128]{2,1,0:T(4,128)} %copy.52.h_ref, f32[128,4,128]{2,1,0:T(4,128)} %copy.53.d_ref), custom_call_target="tpu_custom_call" | custom-call | tf_op jit(solution)/shard_map/pallas_call | solution.py:82
  30.4 2.5 %collective-permute-start.2 = (f32[1,4,2,4,128]{4,3,2,1,0:T(4,128)}, f32[1,4,2,4,128]{4,3,2,1,0:T(4,128)S(1)}, u32[]{:S(2)}, u32[]{:S(2)}) collective-permute-start(f32[1,4,2,4,128]{4,3,2,1,0:T(4,128)} %bitcast.29), channel_id=1, source_target_pairs={{0,1},{1,0},{2,3},{3,2},{4,5},{5,4},{6,7},{7,6},{8,9},{9,8},{10,11... | collective-permute-start | bytes 49160 | tf_op jit(solution)/shard_map/ppermute | solution.py:201
  32.9 2.0 %collective-permute-done.2 = f32[1,4,2,4,128]{4,3,2,1,0:T(4,128)S(1)} collective-permute-done((f32[1,4,2,4,128]{4,3,2,1,0:T(4,128)}, f32[1,4,2,4,128]{4,3,2,1,0:T(4,128)S(1)}, u32[]{:S(2)}, u32[]{:S(2)}) %collective-permute-start.2) | collective-permute-done | bytes 16416 | tf_op jit(solution)/shard_map/ppermute | solution.py:201
  34.9 2.8 %collective-permute-start.3 = (f32[2,4,2,4,128]{4,3,2,1,0:T(4,128)S(1)}, f32[2,4,2,4,128]{4,3,2,1,0:T(4,128)S(1)}, u32[]{:S(2)}, u32[]{:S(2)}) collective-permute-start(f32[2,4,2,4,128]{4,3,2,1,0:T(4,128)S(1)} %maximum_select_fusion.2), channel_id=1, source_target_pairs={{0,2},{1,3},{2,0},{3,1},{4,6},{5,7},{6,4},{7,5},{8,10},{9,11},{10,... | collective-permute-start | bytes 98312 | tf_op jit(solution)/shard_map/ppermute | solution.py:201
  37.7 1.9 %collective-permute-done.3 = f32[2,4,2,4,128]{4,3,2,1,0:T(4,128)S(1)} collective-permute-done((f32[2,4,2,4,128]{4,3,2,1,0:T(4,128)S(1)}, f32[2,4,2,4,128]{4,3,2,1,0:T(4,128)S(1)}, u32[]{:S(2)}, u32[]{:S(2)}) %collective-permute-start.3) | collective-permute-done | bytes 32800 | tf_op jit(solution)/shard_map/ppermute | solution.py:201
  39.7 3.1 %collective-permute-start.4 = (f32[4,4,2,4,128]{4,3,2,1,0:T(4,128)S(1)}, f32[4,4,2,4,128]{4,3,2,1,0:T(4,128)S(1)}, u32[]{:S(2)}, u32[]{:S(2)}) collective-permute-start(f32[4,4,2,4,128]{4,3,2,1,0:T(4,128)S(1)} %maximum_select_fusion.1), channel_id=1, source_target_pairs={{0,4},{1,5},{2,6},{3,7},{4,0},{5,1},{6,2},{7,3},{8,12},{9,13},{10,... | collective-permute-start | bytes 196616 | tf_op jit(solution)/shard_map/ppermute | solution.py:201
  42.8 2.2 %collective-permute-done.4 = f32[4,4,2,4,128]{4,3,2,1,0:T(4,128)S(1)} collective-permute-done((f32[4,4,2,4,128]{4,3,2,1,0:T(4,128)S(1)}, f32[4,4,2,4,128]{4,3,2,1,0:T(4,128)S(1)}, u32[]{:S(2)}, u32[]{:S(2)}) %collective-permute-start.4) | collective-permute-done | bytes 65568 | tf_op jit(solution)/shard_map/ppermute | solution.py:201
  45.0 0.7 %maximum_select_fusion.g_ref = f32[8,4,2,4,128]{4,3,2,1,0:T(4,128)} fusion(f32[4,4,2,4,128]{4,3,2,1,0:T(4,128)S(1)} %collective-permute-done.4, f32[4,4,2,4,128]{4,3,2,1,0:T(4,128)S(1)} %maximum_select_fusion.1, pred[]{:T(512)S(6)} %eq.13), kind=kLoop, calls=%fused_computation.14 | loop fusion | flops 98304 | bytes 262145 | tf_op jit(solution)/shard_map/jit(_where)/select_n | solution.py:203
  45.7 2.2 %shard_map.31.y_ref = f32[128,4,128]{2,1,0:T(4,128)} custom-call(s32[1]{0:T(128)} %bitcast.position_ref, f32[8,4,2,4,128]{4,3,2,1,0:T(4,128)} %maximum_select_fusion.g_ref, f32[3,128,4,128]{3,2,1,0:T(4,128)} %get-tuple-element.12.responses_ref), custom_call_target="tpu_custom_call" | custom-call | tf_op jit(solution)/shard_map/pallas_call | solution.py:137
  47.9 2.1 %shard_map.32 = f32[16,32,128]{2,1,0:T(8,128)} custom-call(f32[16,32,128]{2,1,0:T(8,128)} %copy-done.1, f32[128,4,128]{2,1,0:T(4,128)} %shard_map.31.y_ref, f32[16,32,128]{2,1,0:T(8,128)} %u_ref.1), custom_call_target="tpu_custom_call" | custom-call | tf_op jit(solution)/shard_map/pallas_call | solution.py:186
  (20 shorter events, 1.2 us)
Async XLA Ops:
  1.2 6.5 %copy-start = (f32[16,32,128]{2,1,0:T(8,128)S(1)}, f32[16,32,128]{2,1,0:T(8,128)}, u32[]{:S(2)}) copy-start(f32[16,32,128]{2,1,0:T(8,128)} %u_ref.1) | copy-start | bytes 786436
  1.3 10.0 %collective-permute-start = (f32[16,32]{1,0:T(8,128)S(1)}, f32[16,32]{1,0:T(8,128)S(1)}, u32[]{:S(2)}, u32[]{:S(2)}) collective-permute-start(f32[16,32]{1,0:T(8,128)S(1)} %bitcast.31), channel_id=1, source_target_pairs={{0,1},{1,2},{2,3},{3,4},{4,5},{5,6},{6,7},{8,9},{9,10},{10,11},{11... | collective-permute-start | bytes 6152 | tf_op jit(solution)/shard_map/ppermute | solution.py:18
  6.3 5.5 %collective-permute-start.1 = (f32[16,32]{1,0:T(8,128)S(1)}, f32[16,32]{1,0:T(8,128)S(1)}, u32[]{:S(2)}, u32[]{:S(2)}) collective-permute-start(f32[16,32]{1,0:T(8,128)S(1)} %bitcast.33), channel_id=1, source_target_pairs={{1,0},{2,1},{3,2},{4,3},{5,4},{6,5},{7,6},{9,8},{10,9},{11,10},{12... | collective-permute-start | bytes 6152 | tf_op jit(solution)/shard_map/ppermute | solution.py:19
  7.9 1.0 %copy-start.2 = (f32[16,32,128]{2,1,0:T(8,128)S(1)}, f32[16,32,128]{2,1,0:T(8,128)}, u32[]{:S(2)}) copy-start(f32[16,32,128]{2,1,0:T(8,128)} %param.3) | copy-start | bytes 786436
  8.9 1.5 %copy-start.1 = (f32[16,32,128]{2,1,0:T(8,128)}, f32[16,32,128]{2,1,0:T(8,128)S(1)}, u32[]{:S(2)}) copy-start(f32[16,32,128]{2,1,0:T(8,128)S(1)} %get-tuple-element.24.h_ref) | copy-start | bytes 786436
  30.4 4.5 %copy-start.3 = (f32[4,2,4,128]{3,2,1,0:T(4,128)S(1)}, f32[4,2,4,128]{3,2,1,0:T(4,128)}, u32[]{:S(2)}) copy-start(f32[4,2,4,128]{3,2,1,0:T(4,128)} %get-tuple-element.11) | copy-start | bytes 49156
  30.4 4.4 %collective-permute-start.2 = (f32[1,4,2,4,128]{4,3,2,1,0:T(4,128)}, f32[1,4,2,4,128]{4,3,2,1,0:T(4,128)S(1)}, u32[]{:S(2)}, u32[]{:S(2)}) collective-permute-start(f32[1,4,2,4,128]{4,3,2,1,0:T(4,128)} %bitcast.29), channel_id=1, source_target_pairs={{0,1},{1,0},{2,3},{3,2},{4,5},{5,4},{6,7},{7,6},{8,9},{9,8},{10,11... | collective-permute-start | bytes 49160 | tf_op jit(solution)/shard_map/ppermute | solution.py:201
  34.9 4.7 %collective-permute-start.3 = (f32[2,4,2,4,128]{4,3,2,1,0:T(4,128)S(1)}, f32[2,4,2,4,128]{4,3,2,1,0:T(4,128)S(1)}, u32[]{:S(2)}, u32[]{:S(2)}) collective-permute-start(f32[2,4,2,4,128]{4,3,2,1,0:T(4,128)S(1)} %maximum_select_fusion.2), channel_id=1, source_target_pairs={{0,2},{1,3},{2,0},{3,1},{4,6},{5,7},{6,4},{7,5},{8,10},{9,11},{10,... | collective-permute-start | bytes 98312 | tf_op jit(solution)/shard_map/ppermute | solution.py:201
  39.7 5.3 %collective-permute-start.4 = (f32[4,4,2,4,128]{4,3,2,1,0:T(4,128)S(1)}, f32[4,4,2,4,128]{4,3,2,1,0:T(4,128)S(1)}, u32[]{:S(2)}, u32[]{:S(2)}) collective-permute-start(f32[4,4,2,4,128]{4,3,2,1,0:T(4,128)S(1)} %maximum_select_fusion.1), channel_id=1, source_target_pairs={{0,4},{1,5},{2,6},{3,7},{4,0},{5,1},{6,2},{7,3},{8,12},{9,13},{10,... | collective-permute-start | bytes 196616 | tf_op jit(solution)/shard_map/ppermute | solution.py:201

commit v16 on v15

--- a/solution.py
+++ b/solution.py
@@ -23,6 +23,16 @@
 def partition_kernel(h_ref, d_ref, *refs):
     if len(refs) == 4:
         edges_ref, out_ref, red_ref, ratio_ref = refs
+    elif len(refs) == 5:
+        edges_ref = None
+        out_ref, red_ref, ratio_ref, hy_ref, dy_ref = refs
+        groups = hy_ref.shape[1]
+        per = h_ref.shape[0] // groups
+        for source, target in ((h_ref, hy_ref), (d_ref, dy_ref)):
+            for g in range(groups):
+                block = source[g * per : (g + 1) * per].reshape(target.shape[2], target.shape[0])
+                target[:, g, :] = jnp.transpose(block)
+        h_ref, d_ref = hy_ref, dy_ref
     else:
         edges_ref = None
         out_ref, red_ref, ratio_ref = refs
@@ -74,18 +84,22 @@
         red_ref[4, 1] = edges_ref[1]
 
 
-def partition_call(h_lines, d_lines, edges):
-    n = h_lines.shape[0]
-    rest = h_lines.shape[1:]
+def partition_call(h_lines, d_lines, edges, y_major=None):
     operands = (h_lines, d_lines) if edges is None else (h_lines, d_lines, edges)
     rows = 4 if edges is None else 5
+    shape = h_lines.shape if y_major is None else y_major
+    n = shape[0]
+    rest = shape[1:]
+    scratch = [pltpu_vmem((n,) + rest)]
+    if y_major is not None:
+        scratch = scratch + [pltpu_vmem(y_major), pltpu_vmem(y_major)]
     return pl.pallas_call(
         partition_kernel,
         out_shape=(
             jax.ShapeDtypeStruct((3, n) + rest, jnp.float32),
             jax.ShapeDtypeStruct((rows, 2) + rest, jnp.float32),
         ),
-        scratch_shapes=[pltpu_vmem((n,) + rest)],
+        scratch_shapes=scratch,
     )(*operands)
 
 
@@ -207,8 +221,8 @@
     return held
 
 
-def distributed_solve(h_lines, d_lines, axis, doubling, edges=None):
-    responses, reduced = partition_call(h_lines, d_lines, edges)
+def distributed_solve(h_lines, d_lines, axis, doubling, edges=None, y_major=None):
+    responses, reduced = partition_call(h_lines, d_lines, edges, y_major)
     if doubling:
         gathered = doubling_gather(reduced, axis)
     else:
@@ -258,9 +272,9 @@
     second_side = first_pass - implicit_weight * vertical_implicit_solve
     lanes = 128
     groups = plane_count * row_count // lanes
-    side_lines = jnp.transpose(second_side, (2, 0, 1)).reshape(column_count, groups, lanes)
-    rate_lines = jnp.transpose(half_rate, (2, 0, 1)).reshape(column_count, groups, lanes)
-    column_lines = distributed_solve(rate_lines, side_lines, "gy", True)
+    column_lines = distributed_solve(
+        half_rate, second_side, "gy", True, y_major=(column_count, groups, lanes)
+    )
     return sweep_call(half_rate, column_lines, initial_heat_values)
 
 

time: 50.4 us -> 50.6 us (level)
  local copies, waits for them, and re-layouts: 5.72 us -> 4 us
  starting transfers between devices: 14.5 us -> 15.7 us
  blocking collectives: 7.57 us -> 8.1 us
    sub x0 -> x1, other arithmetic: none -> 1.97 us  [per_device(): second_side = first_pass - implicit_weight * vertical_implicit_solve]
    reshape x2 -> x0, local copies, waits for them, and re-layouts: 1.68 us -> none  [the longest x1 0.84 us: per_device(): jnp.transpose(second_side, (2, 0, 1)).reshape(column_count, groups, lanes)]
    transpose x2 -> x0, other arithmetic: 1.02 us -> none  [the longest x1 0.98 us: per_device(): jnp.transpose(second_side, (2, 0, 1)).reshape(column_count, groups, lanes)]
    transpose x1, other arithmetic: 1.18 us -> 0.32 us  [per_device(): jnp.moveaxis(forward_euler_increment - implicit_weight * horizontal_impli...]
    unnamed x11 -> x8, local copies, waits for them, and re-layouts: 1.38 us -> 0.57 us
    transpose x1, local copies, waits for them, and re-layouts: 0.09 us -> 0.87 us  [per_device(): jnp.moveaxis(forward_euler_increment - implicit_weight * horizontal_impli...]
    ppermute x1, starting transfers between devices: 4.84 us -> 5.47 us  [halos(): low = lax.ppermute(last, axis, forward)]
    ppermute x3, starting transfers between devices: 8.39 us -> 8.98 us  [doubling_gather(): other = lax.ppermute(held, axis, [(i, i ^ step) for i in range(count)])]
  transfers between devices with their start and end apart: 5 -> 5, of which waited for: 4 -> 4; matrix products, arithmetic and copies ran while one was open for 6% -> 2% of each run, Pallas kernels for 0% -> 0%
where the time goes in v16:
time: 50.6 us; the launch traced here: 50.2 us
  starting transfers between devices  15.7 us (31%)
  Pallas kernels  12.2 us (24%)
  blocking collectives  8.1 us (16%)
  waiting for transfers between devices  6.49 us (13%)
  local copies, waits for them, and re-layouts  4 us (8%)
  other arithmetic  3.6 us (7%)
    ppermute x3, starting transfers between devices, doubling_gather(): other = lax.ppermute(held, axis, [(i, i ^ step) for i in range(count)])  8.98 us
    all_gather x1, blocking collectives, distributed_solve(): gathered = lax.all_gather(reduced, axis)  8.1 us
    ppermute x3, waiting for transfers between devices, doubling_gather(): other = lax.ppermute(held, axis, [(i, i ^ step) for i in range(count)])  6.14 us
    pallas_call x2, Pallas kernels, partition_call(): pl.pallas_call(partition_kernel, out_shape=(jax.ShapeDtypeStruct((3, n) +...  5.84 us
    ppermute x1, starting transfers between devices, halos(): low = lax.ppermute(last, axis, forward)  5.47 us
    pallas_call x2, Pallas kernels, finish_call(): pl.pallas_call(finish_kernel, out_shape=jax.ShapeDtypeStruct((n,) + rest,...  4.26 us
    pallas_call x1, Pallas kernels, sweep_call(): pl.pallas_call(sweep_kernel, out_shape=jax.ShapeDtypeStruct(h_lines.shape...  2.12 us
    sub x1, other arithmetic, per_device(): second_side = first_pass - implicit_weight * vertical_implicit_solve  1.97 us
  transfers between devices with their start and end apart: 5, of which 4 were waited for; matrix products, arithmetic and copies ran while one was open for 2% of the time, Pallas kernels for 0%

profile of v16, /device:TPU:0, one launch (start us, length us, event | category | flops | bytes accessed | tf_op | source)
XLA Modules:
  0.0 50.2 jit_solution(8652076810044202567)
XLA Ops:
  0.0 1.2 %fusion.10 = (f32[16,32,1]{2,1,0:T(8,128)S(1)}, f32[16,32,1]{2,1,0:T(8,128)S(1)}) fusion(f32[16,32,128]{2,1,0:T(8,128)} %u_ref.1), kind=kLoop, calls=%fused_computation.19 | loop fusion | bytes 8192 | tf_op jit(solution)/shard_map/slice | solution.py:16
  1.3 1.3 %collective-permute-start.1 = (f32[16,32]{1,0:T(8,128)S(1)}, f32[16,32]{1,0:T(8,128)S(1)}, u32[]{:S(2)}, u32[]{:S(2)}) collective-permute-start(f32[16,32]{1,0:T(8,128)S(1)} %bitcast.25), channel_id=1, source_target_pairs={{1,0},{2,1},{3,2},{4,3},{5,4},{6,5},{7,6},{9,8},{10,9},{11,10},{12... | collective-permute-start | bytes 6152 | tf_op jit(solution)/shard_map/ppermute | solution.py:19
  2.8 5.5 %collective-permute-start = (f32[16,32]{1,0:T(8,128)S(1)}, f32[16,32]{1,0:T(8,128)S(1)}, u32[]{:S(2)}, u32[]{:S(2)}) collective-permute-start(f32[16,32]{1,0:T(8,128)S(1)} %bitcast.27), channel_id=1, source_target_pairs={{0,1},{1,2},{2,3},{3,4},{4,5},{5,6},{6,7},{8,9},{9,10},{10,11},{11... | collective-permute-start | bytes 6152 | tf_op jit(solution)/shard_map/ppermute | solution.py:18
  8.5 0.6 %pad_maximum_fusion.refs_0_ = f32[2,16,128]{2,1,0:T(8,128)} fusion(f32[1,16,128]{2,1,0:T(8,128)S(1)} %bitcast.22, f32[1,16,128]{2,1,0:T(8,128)S(1)} %bitcast.21), kind=kLoop, calls=%fused_computation.16 | loop fusion | flops 4096 | bytes 32768 | tf_op jit(solution)/shard_map/stack | solution.py:270
  9.1 0.2 copy.22
  9.3 0.3 collective-permute-done
  9.8 0.2 copy-done.1
  10.0 0.3 fusion.5
  10.4 0.9 %copy.25.h_ref = f32[32,16,128]{2,1,0:T(8,128)} copy(f32[32,16,128]{2,0,1:T(8,128)S(1)} %get-tuple-element.18) | data formatting | bytes 524288 | tf_op jit(solution)/shard_map/transpose | solution.py:264
  11.2 0.9 %copy.26.d_ref = f32[32,16,128]{2,1,0:T(8,128)} copy(f32[32,16,128]{2,0,1:T(8,128)S(1)} %get-tuple-element.17) | data formatting | bytes 524288 | tf_op jit(solution)/shard_map/transpose | solution.py:261
  12.1 2.3 %shard_map.28 = (f32[3,32,16,128]{3,2,1,0:T(8,128)}, f32[5,2,16,128]{3,2,1,0:T(8,128)}) custom-call(f32[32,16,128]{2,1,0:T(8,128)} %copy.25.h_ref, f32[32,16,128]{2,1,0:T(8,128)} %copy.26.d_ref, f32[2,16,128]{2,1,0:T(8,128)} %pad_maximum_fusion.refs_0_), custom_call_target="tpu_custom_call" | custom-call | tf_op jit(solution)/shard_map/pallas_call | solution.py:96
  14.4 8.1 %all-gather = f32[20,2,16,128]{3,2,1,0:T(8,128)} all-gather(f32[5,2,16,128]{3,2,1,0:T(8,128)} %get-tuple-element.9), channel_id=2, replica_groups=mesh['gx'=4,'gy'=8] {'gx'}, dimensions={0}, use_global_device_ids=true | all-gather | bytes 409600 | tf_op jit(solution)/shard_map/all_gather | solution.py:229
  22.5 2.1 %shard_map.29 = f32[32,16,128]{2,1,0:T(8,128)} custom-call(s32[1]{0:T(128)} %bitcast.1.position_ref, f32[4,5,2,16,128]{4,3,2,1,0:T(8,128)} %bitcast.20, f32[3,32,16,128]{3,2,1,0:T(8,128)} %get-tuple-element.10.responses_ref), custom_call_target="tpu_custom_call" | custom-call | tf_op jit(solution)/shard_map/pallas_call | solution.py:151
  24.6 2.0 %bitcast_subtract_fusion = (f32[16,32,128]{2,1,0:T(8,128)}, f32[16,32,128]{2,1,0:T(8,128)}) fusion(f32[32,16,128]{2,1,0:T(8,128)} %shard_map.29, f32[16,32,1]{2,1,0:T(8,128)S(1)} %copy.22, f32[16,32,127]{2,1,0:T(8,128)S(1)} %get-tuple-element.22, f32[16,32,128]{2,1,0:T(8,128)S(1)} %copy-done, f32[16,32,127]{2,1,0:T(8,128)S(1)} %get-tuple-element.21, ...), kind=kLoop, calls=%fused_computation.11 | loop fusion | flops 655360 | bytes 1835008 | tf_op jit(solution)/shard_map/sub | solution.py:272
  26.5 3.5 %shard_map.30 = (f32[3,128,4,128]{3,2,1,0:T(4,128)}, f32[4,2,4,128]{3,2,1,0:T(4,128)}) custom-call(f32[16,32,128]{2,1,0:T(8,128)} %get-tuple-element.14.h_ref, f32[16,32,128]{2,1,0:T(8,128)} %get-tuple-element.13.d_ref), custom_call_target="tpu_custom_call" | custom-call | tf_op jit(solution)/shard_map/pallas_call | solution.py:96
  30.1 2.4 %collective-permute-start.2 = (f32[1,4,2,4,128]{4,3,2,1,0:T(4,128)}, f32[1,4,2,4,128]{4,3,2,1,0:T(4,128)S(1)}, u32[]{:S(2)}, u32[]{:S(2)}) collective-permute-start(f32[1,4,2,4,128]{4,3,2,1,0:T(4,128)} %bitcast.23), channel_id=1, source_target_pairs={{0,1},{1,0},{2,3},{3,2},{4,5},{5,4},{6,7},{7,6},{8,9},{9,8},{10,11... | collective-permute-start | bytes 49160 | tf_op jit(solution)/shard_map/ppermute | solution.py:215
  32.5 2.0 %collective-permute-done.2 = f32[1,4,2,4,128]{4,3,2,1,0:T(4,128)S(1)} collective-permute-done((f32[1,4,2,4,128]{4,3,2,1,0:T(4,128)}, f32[1,4,2,4,128]{4,3,2,1,0:T(4,128)S(1)}, u32[]{:S(2)}, u32[]{:S(2)}) %collective-permute-start.2) | collective-permute-done | bytes 16416 | tf_op jit(solution)/shard_map/ppermute | solution.py:215
  34.5 3.5 %collective-permute-start.3 = (f32[2,4,2,4,128]{4,3,2,1,0:T(4,128)S(1)}, f32[2,4,2,4,128]{4,3,2,1,0:T(4,128)S(1)}, u32[]{:S(2)}, u32[]{:S(2)}) collective-permute-start(f32[2,4,2,4,128]{4,3,2,1,0:T(4,128)S(1)} %maximum_select_fusion.2), channel_id=1, source_target_pairs={{0,2},{1,3},{2,0},{3,1},{4,6},{5,7},{6,4},{7,5},{8,10},{9,11},{10,... | collective-permute-start | bytes 98312 | tf_op jit(solution)/shard_map/ppermute | solution.py:215
  38.0 1.9 %collective-permute-done.3 = f32[2,4,2,4,128]{4,3,2,1,0:T(4,128)S(1)} collective-permute-done((f32[2,4,2,4,128]{4,3,2,1,0:T(4,128)S(1)}, f32[2,4,2,4,128]{4,3,2,1,0:T(4,128)S(1)}, u32[]{:S(2)}, u32[]{:S(2)}) %collective-permute-start.3) | collective-permute-done | bytes 32800 | tf_op jit(solution)/shard_map/ppermute | solution.py:215
  39.9 3.1 %collective-permute-start.4 = (f32[4,4,2,4,128]{4,3,2,1,0:T(4,128)S(1)}, f32[4,4,2,4,128]{4,3,2,1,0:T(4,128)S(1)}, u32[]{:S(2)}, u32[]{:S(2)}) collective-permute-start(f32[4,4,2,4,128]{4,3,2,1,0:T(4,128)S(1)} %maximum_select_fusion.1), channel_id=1, source_target_pairs={{0,4},{1,5},{2,6},{3,7},{4,0},{5,1},{6,2},{7,3},{8,12},{9,13},{10,... | collective-permute-start | bytes 196616 | tf_op jit(solution)/shard_map/ppermute | solution.py:215
  43.0 2.2 %collective-permute-done.4 = f32[4,4,2,4,128]{4,3,2,1,0:T(4,128)S(1)} collective-permute-done((f32[4,4,2,4,128]{4,3,2,1,0:T(4,128)S(1)}, f32[4,4,2,4,128]{4,3,2,1,0:T(4,128)S(1)}, u32[]{:S(2)}, u32[]{:S(2)}) %collective-permute-start.4) | collective-permute-done | bytes 65568 | tf_op jit(solution)/shard_map/ppermute | solution.py:215
  45.2 0.7 %maximum_select_fusion.g_ref = f32[8,4,2,4,128]{4,3,2,1,0:T(4,128)} fusion(f32[4,4,2,4,128]{4,3,2,1,0:T(4,128)S(1)} %collective-permute-done.4, f32[4,4,2,4,128]{4,3,2,1,0:T(4,128)S(1)} %maximum_select_fusion.1, pred[]{:T(512)S(6)} %eq.13), kind=kLoop, calls=%fused_computation.12 | loop fusion | flops 98304 | bytes 262145 | tf_op jit(solution)/shard_map/jit(_where)/select_n | solution.py:217
  45.9 2.2 %shard_map.31.y_ref = f32[128,4,128]{2,1,0:T(4,128)} custom-call(s32[1]{0:T(128)} %bitcast.position_ref, f32[8,4,2,4,128]{4,3,2,1,0:T(4,128)} %maximum_select_fusion.g_ref, f32[3,128,4,128]{3,2,1,0:T(4,128)} %get-tuple-element.12.responses_ref), custom_call_target="tpu_custom_call" | custom-call | tf_op jit(solution)/shard_map/pallas_call | solution.py:151
  48.1 2.1 %shard_map.32 = f32[16,32,128]{2,1,0:T(8,128)} custom-call(f32[16,32,128]{2,1,0:T(8,128)} %get-tuple-element.14.h_ref, f32[128,4,128]{2,1,0:T(4,128)} %shard_map.31.y_ref, f32[16,32,128]{2,1,0:T(8,128)} %u_ref.1), custom_call_target="tpu_custom_call" | custom-call | tf_op jit(solution)/shard_map/pallas_call | solution.py:200
  (14 shorter events, 0.7 us)
Async XLA Ops:
  1.2 7.1 %copy-start = (f32[16,32,128]{2,1,0:T(8,128)S(1)}, f32[16,32,128]{2,1,0:T(8,128)}, u32[]{:S(2)}) copy-start(f32[16,32,128]{2,1,0:T(8,128)} %u_ref.1) | copy-start | bytes 786436
  1.3 7.8 %collective-permute-start.1 = (f32[16,32]{1,0:T(8,128)S(1)}, f32[16,32]{1,0:T(8,128)S(1)}, u32[]{:S(2)}, u32[]{:S(2)}) collective-permute-start(f32[16,32]{1,0:T(8,128)S(1)} %bitcast.25), channel_id=1, source_target_pairs={{1,0},{2,1},{3,2},{4,3},{5,4},{6,5},{7,6},{9,8},{10,9},{11,10},{12... | collective-permute-start | bytes 6152 | tf_op jit(solution)/shard_map/ppermute | solution.py:19
  2.8 6.8 %collective-permute-start = (f32[16,32]{1,0:T(8,128)S(1)}, f32[16,32]{1,0:T(8,128)S(1)}, u32[]{:S(2)}, u32[]{:S(2)}) collective-permute-start(f32[16,32]{1,0:T(8,128)S(1)} %bitcast.27), channel_id=1, source_target_pairs={{0,1},{1,2},{2,3},{3,4},{4,5},{5,6},{6,7},{8,9},{9,10},{10,11},{11... | collective-permute-start | bytes 6152 | tf_op jit(solution)/shard_map/ppermute | solution.py:18
  9.1 1.0 %copy-start.1 = (f32[16,32,128]{2,1,0:T(8,128)S(1)}, f32[16,32,128]{2,1,0:T(8,128)}, u32[]{:S(2)}) copy-start(f32[16,32,128]{2,1,0:T(8,128)} %param.3) | copy-start | bytes 786436
  30.1 4.4 %copy-start.2 = (f32[4,2,4,128]{3,2,1,0:T(4,128)S(1)}, f32[4,2,4,128]{3,2,1,0:T(4,128)}, u32[]{:S(2)}) copy-start(f32[4,2,4,128]{3,2,1,0:T(4,128)} %get-tuple-element.11) | copy-start | bytes 49156
  30.1 4.4 %collective-permute-start.2 = (f32[1,4,2,4,128]{4,3,2,1,0:T(4,128)}, f32[1,4,2,4,128]{4,3,2,1,0:T(4,128)S(1)}, u32[]{:S(2)}, u32[]{:S(2)}) collective-permute-start(f32[1,4,2,4,128]{4,3,2,1,0:T(4,128)} %bitcast.23), channel_id=1, source_target_pairs={{0,1},{1,0},{2,3},{3,2},{4,5},{5,4},{6,7},{7,6},{8,9},{9,8},{10,11... | collective-permute-start | bytes 49160 | tf_op jit(solution)/shard_map/ppermute | solution.py:215
  34.5 5.4 %collective-permute-start.3 = (f32[2,4,2,4,128]{4,3,2,1,0:T(4,128)S(1)}, f32[2,4,2,4,128]{4,3,2,1,0:T(4,128)S(1)}, u32[]{:S(2)}, u32[]{:S(2)}) collective-permute-start(f32[2,4,2,4,128]{4,3,2,1,0:T(4,128)S(1)} %maximum_select_fusion.2), channel_id=1, source_target_pairs={{0,2},{1,3},{2,0},{3,1},{4,6},{5,7},{6,4},{7,5},{8,10},{9,11},{10,... | collective-permute-start | bytes 98312 | tf_op jit(solution)/shard_map/ppermute | solution.py:215
  39.9 5.3 %collective-permute-start.4 = (f32[4,4,2,4,128]{4,3,2,1,0:T(4,128)S(1)}, f32[4,4,2,4,128]{4,3,2,1,0:T(4,128)S(1)}, u32[]{:S(2)}, u32[]{:S(2)}) collective-permute-start(f32[4,4,2,4,128]{4,3,2,1,0:T(4,128)S(1)} %maximum_select_fusion.1), channel_id=1, source_target_pairs={{0,4},{1,5},{2,6},{3,7},{4,0},{5,1},{6,2},{7,3},{8,12},{9,13},{10,... | collective-permute-start | bytes 196616 | tf_op jit(solution)/shard_map/ppermute | solution.py:215

commit v17 on v16

--- a/solution.py
+++ b/solution.py
@@ -26,13 +26,12 @@
     elif len(refs) == 5:
         edges_ref = None
         out_ref, red_ref, ratio_ref, hy_ref, dy_ref = refs
-        groups = hy_ref.shape[1]
-        per = h_ref.shape[0] // groups
-        for source, target in ((h_ref, hy_ref), (d_ref, dy_ref)):
-            for g in range(groups):
-                block = source[g * per : (g + 1) * per].reshape(target.shape[2], target.shape[0])
-                target[:, g, :] = jnp.transpose(block)
-        h_ref, d_ref = hy_ref, dy_ref
+        groups = dy_ref.shape[1]
+        per = d_ref.shape[0] // groups
+        for g in range(groups):
+            block = d_ref[g * per : (g + 1) * per].reshape(dy_ref.shape[2], dy_ref.shape[0])
+            dy_ref[:, g, :] = jnp.transpose(block)
+        d_ref = dy_ref
     else:
         edges_ref = None
         out_ref, red_ref, ratio_ref = refs
@@ -272,8 +271,9 @@
     second_side = first_pass - implicit_weight * vertical_implicit_solve
     lanes = 128
     groups = plane_count * row_count // lanes
+    rate_lines = jnp.transpose(half_rate, (2, 0, 1)).reshape(column_count, groups, lanes)
     column_lines = distributed_solve(
-        half_rate, second_side, "gy", True, y_major=(column_count, groups, lanes)
+        rate_lines, second_side, "gy", True, y_major=(column_count, groups, lanes)
     )
     return sweep_call(half_rate, column_lines, initial_heat_values)
 

time: 50.6 us -> 51.3 us (1.014)
  local copies, waits for them, and re-layouts: 4 us -> 4.83 us
    reshape x0 -> x1, local copies, waits for them, and re-layouts: none -> 0.84 us  [per_device(): jnp.transpose(half_rate, (2, 0, 1)).reshape(column_count, groups, lanes)]
where the time goes in v17:
time: 51.3 us; the launch traced here: 50.9 us
  starting transfers between devices  15.8 us (31%)
  Pallas kernels  12.1 us (24%)
  blocking collectives  8.1 us (16%)
  waiting for transfers between devices  6.49 us (13%)
  local copies, waits for them, and re-layouts  4.83 us (9%)
  other arithmetic  3.56 us (7%)
    ppermute x3, starting transfers between devices, doubling_gather(): other = lax.ppermute(held, axis, [(i, i ^ step) for i in range(count)])  8.98 us
    all_gather x1, blocking collectives, distributed_solve(): gathered = lax.all_gather(reduced, axis)  8.1 us
    ppermute x3, waiting for transfers between devices, doubling_gather(): other = lax.ppermute(held, axis, [(i, i ^ step) for i in range(count)])  6.14 us
    pallas_call x2, Pallas kernels, partition_call(): pl.pallas_call(partition_kernel, out_shape=(jax.ShapeDtypeStruct((3, n) +...  5.74 us
    ppermute x1, starting transfers between devices, halos(): low = lax.ppermute(last, axis, forward)  5.47 us
    pallas_call x2, Pallas kernels, finish_call(): pl.pallas_call(finish_kernel, out_shape=jax.ShapeDtypeStruct((n,) + rest,...  4.26 us
    pallas_call x1, Pallas kernels, sweep_call(): pl.pallas_call(sweep_kernel, out_shape=jax.ShapeDtypeStruct(h_lines.shape...  2.12 us
    sub x1, other arithmetic, per_device(): second_side = first_pass - implicit_weight * vertical_implicit_solve  1.93 us
  transfers between devices with their start and end apart: 5, of which 4 were waited for; matrix products, arithmetic and copies ran while one was open for 2% of the time, Pallas kernels for 0%

profile of v17, /device:TPU:0, one launch (start us, length us, event | category | flops | bytes accessed | tf_op | source)
XLA Modules:
  0.0 50.9 jit_solution(944809977767080114)
XLA Ops:
  0.0 1.2 %fusion.10 = (f32[16,32,1]{2,1,0:T(8,128)S(1)}, f32[16,32,1]{2,1,0:T(8,128)S(1)}) fusion(f32[16,32,128]{2,1,0:T(8,128)} %u_ref.1), kind=kLoop, calls=%fused_computation.19 | loop fusion | bytes 8192 | tf_op jit(solution)/shard_map/slice | solution.py:16
  1.3 1.3 %collective-permute-start.1 = (f32[16,32]{1,0:T(8,128)S(1)}, f32[16,32]{1,0:T(8,128)S(1)}, u32[]{:S(2)}, u32[]{:S(2)}) collective-permute-start(f32[16,32]{1,0:T(8,128)S(1)} %bitcast.29), channel_id=1, source_target_pairs={{1,0},{2,1},{3,2},{4,3},{5,4},{6,5},{7,6},{9,8},{10,9},{11,10},{12... | collective-permute-start | bytes 6152 | tf_op jit(solution)/shard_map/ppermute | solution.py:19
  2.8 5.5 %collective-permute-start = (f32[16,32]{1,0:T(8,128)S(1)}, f32[16,32]{1,0:T(8,128)S(1)}, u32[]{:S(2)}, u32[]{:S(2)}) collective-permute-start(f32[16,32]{1,0:T(8,128)S(1)} %bitcast.31), channel_id=1, source_target_pairs={{0,1},{1,2},{2,3},{3,4},{4,5},{5,6},{6,7},{8,9},{9,10},{10,11},{11... | collective-permute-start | bytes 6152 | tf_op jit(solution)/shard_map/ppermute | solution.py:18
  8.5 0.6 %pad_maximum_fusion.refs_0_ = f32[2,16,128]{2,1,0:T(8,128)} fusion(f32[1,16,128]{2,1,0:T(8,128)S(1)} %bitcast.26, f32[1,16,128]{2,1,0:T(8,128)S(1)} %bitcast.25), kind=kLoop, calls=%fused_computation.16 | loop fusion | flops 4096 | bytes 32768 | tf_op jit(solution)/shard_map/stack | solution.py:269
  9.3 0.3 collective-permute-done
  9.8 0.2 copy-done.2
  10.0 0.3 fusion.5
  10.4 0.9 %copy.27.h_ref = f32[32,16,128]{2,1,0:T(8,128)} copy(f32[32,16,128]{2,0,1:T(8,128)S(1)} %get-tuple-element.18) | data formatting | bytes 524288 | tf_op jit(solution)/shard_map/transpose | solution.py:263
  11.2 0.9 %copy.28.d_ref = f32[32,16,128]{2,1,0:T(8,128)} copy(f32[32,16,128]{2,0,1:T(8,128)S(1)} %get-tuple-element.17) | data formatting | bytes 524288 | tf_op jit(solution)/shard_map/transpose | solution.py:260
  12.1 2.3 %shard_map.28 = (f32[3,32,16,128]{3,2,1,0:T(8,128)}, f32[5,2,16,128]{3,2,1,0:T(8,128)}) custom-call(f32[32,16,128]{2,1,0:T(8,128)} %copy.27.h_ref, f32[32,16,128]{2,1,0:T(8,128)} %copy.28.d_ref, f32[2,16,128]{2,1,0:T(8,128)} %pad_maximum_fusion.refs_0_), custom_call_target="tpu_custom_call" | custom-call | tf_op jit(solution)/shard_map/pallas_call | solution.py:95
  14.4 8.1 %all-gather = f32[20,2,16,128]{3,2,1,0:T(8,128)} all-gather(f32[5,2,16,128]{3,2,1,0:T(8,128)} %get-tuple-element.9), channel_id=2, replica_groups=mesh['gx'=4,'gy'=8] {'gx'}, dimensions={0}, use_global_device_ids=true | all-gather | bytes 409600 | tf_op jit(solution)/shard_map/all_gather | solution.py:228
  22.5 2.1 %shard_map.29 = f32[32,16,128]{2,1,0:T(8,128)} custom-call(s32[1]{0:T(128)} %bitcast.3.position_ref, f32[4,5,2,16,128]{4,3,2,1,0:T(8,128)} %bitcast.24, f32[3,32,16,128]{3,2,1,0:T(8,128)} %get-tuple-element.10.responses_ref), custom_call_target="tpu_custom_call" | custom-call | tf_op jit(solution)/shard_map/pallas_call | solution.py:150
  24.6 1.9 %bitcast_subtract_fusion = (f32[16,32,128]{2,1,0:T(8,128)}, f32[16,32,128]{2,1,0:T(8,128)S(1)}) fusion(f32[32,16,128]{2,1,0:T(8,128)} %shard_map.29, f32[16,32,1]{2,1,0:T(8,128)S(1)} %copy.24, f32[16,32,127]{2,1,0:T(8,128)S(1)} %get-tuple-element.22, f32[16,32,128]{2,1,0:T(8,128)S(1)} %copy-done, f32[16,32,127]{2,1,0:T(8,128)S(1)} %get-tuple-element.21, ...), kind=kLoop, calls=%fused_computation.11 | loop fusion | flops 655360 | bytes 1835008 | tf_op jit(solution)/shard_map/sub | solution.py:271
  26.5 0.8 %copy.30.h_ref = f32[128,4,128]{2,1,0:T(4,128)} copy(f32[128,4,128]{0,2,1:T(8,128)S(1)} %bitcast.23) | data formatting | bytes 524288 | tf_op jit(solution)/shard_map/reshape | solution.py:274
  27.3 3.4 %shard_map.30 = (f32[3,128,4,128]{3,2,1,0:T(4,128)}, f32[4,2,4,128]{3,2,1,0:T(4,128)}) custom-call(f32[128,4,128]{2,1,0:T(4,128)} %copy.30.h_ref, f32[16,32,128]{2,1,0:T(8,128)} %get-tuple-element.13.d_ref), custom_call_target="tpu_custom_call" | custom-call | tf_op jit(solution)/shard_map/pallas_call | solution.py:95
  30.8 2.4 %collective-permute-start.2 = (f32[1,4,2,4,128]{4,3,2,1,0:T(4,128)}, f32[1,4,2,4,128]{4,3,2,1,0:T(4,128)S(1)}, u32[]{:S(2)}, u32[]{:S(2)}) collective-permute-start(f32[1,4,2,4,128]{4,3,2,1,0:T(4,128)} %bitcast.27), channel_id=1, source_target_pairs={{0,1},{1,0},{2,3},{3,2},{4,5},{5,4},{6,7},{7,6},{8,9},{9,8},{10,11... | collective-permute-start | bytes 49160 | tf_op jit(solution)/shard_map/ppermute | solution.py:214
  33.1 2.0 %collective-permute-done.2 = f32[1,4,2,4,128]{4,3,2,1,0:T(4,128)S(1)} collective-permute-done((f32[1,4,2,4,128]{4,3,2,1,0:T(4,128)}, f32[1,4,2,4,128]{4,3,2,1,0:T(4,128)S(1)}, u32[]{:S(2)}, u32[]{:S(2)}) %collective-permute-start.2) | collective-permute-done | bytes 16416 | tf_op jit(solution)/shard_map/ppermute | solution.py:214
  35.2 3.5 %collective-permute-start.3 = (f32[2,4,2,4,128]{4,3,2,1,0:T(4,128)S(1)}, f32[2,4,2,4,128]{4,3,2,1,0:T(4,128)S(1)}, u32[]{:S(2)}, u32[]{:S(2)}) collective-permute-start(f32[2,4,2,4,128]{4,3,2,1,0:T(4,128)S(1)} %maximum_select_fusion.2), channel_id=1, source_target_pairs={{0,2},{1,3},{2,0},{3,1},{4,6},{5,7},{6,4},{7,5},{8,10},{9,11},{10,... | collective-permute-start | bytes 98312 | tf_op jit(solution)/shard_map/ppermute | solution.py:214
  38.7 1.9 %collective-permute-done.3 = f32[2,4,2,4,128]{4,3,2,1,0:T(4,128)S(1)} collective-permute-done((f32[2,4,2,4,128]{4,3,2,1,0:T(4,128)S(1)}, f32[2,4,2,4,128]{4,3,2,1,0:T(4,128)S(1)}, u32[]{:S(2)}, u32[]{:S(2)}) %collective-permute-start.3) | collective-permute-done | bytes 32800 | tf_op jit(solution)/shard_map/ppermute | solution.py:214
  40.6 3.1 %collective-permute-start.4 = (f32[4,4,2,4,128]{4,3,2,1,0:T(4,128)S(1)}, f32[4,4,2,4,128]{4,3,2,1,0:T(4,128)S(1)}, u32[]{:S(2)}, u32[]{:S(2)}) collective-permute-start(f32[4,4,2,4,128]{4,3,2,1,0:T(4,128)S(1)} %maximum_select_fusion.1), channel_id=1, source_target_pairs={{0,4},{1,5},{2,6},{3,7},{4,0},{5,1},{6,2},{7,3},{8,12},{9,13},{10,... | collective-permute-start | bytes 196616 | tf_op jit(solution)/shard_map/ppermute | solution.py:214
  43.7 2.2 %collective-permute-done.4 = f32[4,4,2,4,128]{4,3,2,1,0:T(4,128)S(1)} collective-permute-done((f32[4,4,2,4,128]{4,3,2,1,0:T(4,128)S(1)}, f32[4,4,2,4,128]{4,3,2,1,0:T(4,128)S(1)}, u32[]{:S(2)}, u32[]{:S(2)}) %collective-permute-start.4) | collective-permute-done | bytes 65568 | tf_op jit(solution)/shard_map/ppermute | solution.py:214
  45.9 0.7 %maximum_select_fusion.g_ref = f32[8,4,2,4,128]{4,3,2,1,0:T(4,128)} fusion(f32[4,4,2,4,128]{4,3,2,1,0:T(4,128)S(1)} %collective-permute-done.4, f32[4,4,2,4,128]{4,3,2,1,0:T(4,128)S(1)} %maximum_select_fusion.1, pred[]{:T(512)S(6)} %eq.13), kind=kLoop, calls=%fused_computation.12 | loop fusion | flops 98304 | bytes 262145 | tf_op jit(solution)/shard_map/jit(_where)/select_n | solution.py:216
  46.6 2.2 %shard_map.31.y_ref = f32[128,4,128]{2,1,0:T(4,128)} custom-call(s32[1]{0:T(128)} %bitcast.position_ref, f32[8,4,2,4,128]{4,3,2,1,0:T(4,128)} %maximum_select_fusion.g_ref, f32[3,128,4,128]{3,2,1,0:T(4,128)} %get-tuple-element.12.responses_ref), custom_call_target="tpu_custom_call" | custom-call | tf_op jit(solution)/shard_map/pallas_call | solution.py:150
  48.8 2.1 %shard_map.32 = f32[16,32,128]{2,1,0:T(8,128)} custom-call(f32[16,32,128]{2,1,0:T(8,128)} %copy-done.1, f32[128,4,128]{2,1,0:T(4,128)} %shard_map.31.y_ref, f32[16,32,128]{2,1,0:T(8,128)} %u_ref.1), custom_call_target="tpu_custom_call" | custom-call | tf_op jit(solution)/shard_map/pallas_call | solution.py:199
  (17 shorter events, 0.9 us)
Async XLA Ops:
  1.2 7.1 %copy-start = (f32[16,32,128]{2,1,0:T(8,128)S(1)}, f32[16,32,128]{2,1,0:T(8,128)}, u32[]{:S(2)}) copy-start(f32[16,32,128]{2,1,0:T(8,128)} %u_ref.1) | copy-start | bytes 786436
  1.3 7.8 %collective-permute-start.1 = (f32[16,32]{1,0:T(8,128)S(1)}, f32[16,32]{1,0:T(8,128)S(1)}, u32[]{:S(2)}, u32[]{:S(2)}) collective-permute-start(f32[16,32]{1,0:T(8,128)S(1)} %bitcast.29), channel_id=1, source_target_pairs={{1,0},{2,1},{3,2},{4,3},{5,4},{6,5},{7,6},{9,8},{10,9},{11,10},{12... | collective-permute-start | bytes 6152 | tf_op jit(solution)/shard_map/ppermute | solution.py:19
  2.8 6.8 %collective-permute-start = (f32[16,32]{1,0:T(8,128)S(1)}, f32[16,32]{1,0:T(8,128)S(1)}, u32[]{:S(2)}, u32[]{:S(2)}) collective-permute-start(f32[16,32]{1,0:T(8,128)S(1)} %bitcast.31), channel_id=1, source_target_pairs={{0,1},{1,2},{2,3},{3,4},{4,5},{5,6},{6,7},{8,9},{9,10},{10,11},{11... | collective-permute-start | bytes 6152 | tf_op jit(solution)/shard_map/ppermute | solution.py:18
  9.1 1.0 %copy-start.2 = (f32[16,32,128]{2,1,0:T(8,128)S(1)}, f32[16,32,128]{2,1,0:T(8,128)}, u32[]{:S(2)}) copy-start(f32[16,32,128]{2,1,0:T(8,128)} %param.3) | copy-start | bytes 786436
  26.5 0.8 %copy-start.1 = (f32[16,32,128]{2,1,0:T(8,128)}, f32[16,32,128]{2,1,0:T(8,128)S(1)}, u32[]{:S(2)}) copy-start(f32[16,32,128]{2,1,0:T(8,128)S(1)} %get-tuple-element.14.h_ref) | copy-start | bytes 786436
  30.8 4.4 %copy-start.3 = (f32[4,2,4,128]{3,2,1,0:T(4,128)S(1)}, f32[4,2,4,128]{3,2,1,0:T(4,128)}, u32[]{:S(2)}) copy-start(f32[4,2,4,128]{3,2,1,0:T(4,128)} %get-tuple-element.11) | copy-start | bytes 49156
  30.8 4.4 %collective-permute-start.2 = (f32[1,4,2,4,128]{4,3,2,1,0:T(4,128)}, f32[1,4,2,4,128]{4,3,2,1,0:T(4,128)S(1)}, u32[]{:S(2)}, u32[]{:S(2)}) collective-permute-start(f32[1,4,2,4,128]{4,3,2,1,0:T(4,128)} %bitcast.27), channel_id=1, source_target_pairs={{0,1},{1,0},{2,3},{3,2},{4,5},{5,4},{6,7},{7,6},{8,9},{9,8},{10,11... | collective-permute-start | bytes 49160 | tf_op jit(solution)/shard_map/ppermute | solution.py:214
  35.2 5.4 %collective-permute-start.3 = (f32[2,4,2,4,128]{4,3,2,1,0:T(4,128)S(1)}, f32[2,4,2,4,128]{4,3,2,1,0:T(4,128)S(1)}, u32[]{:S(2)}, u32[]{:S(2)}) collective-permute-start(f32[2,4,2,4,128]{4,3,2,1,0:T(4,128)S(1)} %maximum_select_fusion.2), channel_id=1, source_target_pairs={{0,2},{1,3},{2,0},{3,1},{4,6},{5,7},{6,4},{7,5},{8,10},{9,11},{10,... | collective-permute-start | bytes 98312 | tf_op jit(solution)/shard_map/ppermute | solution.py:214
  40.6 5.3 %collective-permute-start.4 = (f32[4,4,2,4,128]{4,3,2,1,0:T(4,128)S(1)}, f32[4,4,2,4,128]{4,3,2,1,0:T(4,128)S(1)}, u32[]{:S(2)}, u32[]{:S(2)}) collective-permute-start(f32[4,4,2,4,128]{4,3,2,1,0:T(4,128)S(1)} %maximum_select_fusion.1), channel_id=1, source_target_pairs={{0,4},{1,5},{2,6},{3,7},{4,0},{5,1},{6,2},{7,3},{8,12},{9,13},{10,... | collective-permute-start | bytes 196616 | tf_op jit(solution)/shard_map/ppermute | solution.py:214

commit v18 on v15

--- a/solution.py
+++ b/solution.py
@@ -93,17 +93,34 @@
     return pltpu.VMEM(shape, jnp.float32)
 
 
-def finish_kernel(position_ref, g_ref, responses_ref, out_ref, ratio_ref, ends_ref):
-    count = g_ref.shape[0]
+def finish_kernel(position_ref, g_ref, *refs):
+    if len(refs) == 5:
+        other_ref, responses_ref, out_ref, ratio_ref, ends_ref = refs
+        half = g_ref.shape[0]
+        count = 2 * half
+        first_held = (position_ref[0] // half) % 2 == 0
+
+        def entry(k, f, q):
+            if k < half:
+                return jnp.where(first_held, g_ref[k, f, q], other_ref[k, f, q])
+            return jnp.where(first_held, other_ref[k - half, f, q], g_ref[k - half, f, q])
+
+    else:
+        responses_ref, out_ref, ratio_ref, ends_ref = refs
+        count = g_ref.shape[0]
+
+        def entry(k, f, q):
+            return g_ref[k, f, q]
+
     n = responses_ref.shape[1]
     ratio = None
     value = None
     for j in range(2 * count):
         k, q = divmod(j, 2)
-        lower = g_ref[k, 0, q]
-        centre = g_ref[k, 1, q]
-        upper = g_ref[k, 2, q]
-        side = g_ref[k, 3, q]
+        lower = entry(k, 0, q)
+        centre = entry(k, 1, q)
+        upper = entry(k, 2, q)
+        side = entry(k, 3, q)
         if g_ref.shape[1] == 5 and q == 0 and k > 0:
             side = side - lower * g_ref[k - 1, 4, 1]
         if g_ref.shape[1] == 5 and q == 1 and k < count - 1:
@@ -131,19 +148,17 @@
 
 
 def finish_call(gathered, responses, position):
-    count = gathered.shape[0]
-    rest = gathered.shape[3:]
+    parts = gathered if isinstance(gathered, tuple) else (gathered,)
+    count = sum(part.shape[0] for part in parts)
+    rest = parts[0].shape[3:]
     n = responses.shape[1]
     return pl.pallas_call(
         finish_kernel,
         out_shape=jax.ShapeDtypeStruct((n,) + rest, jnp.float32),
-        in_specs=[
-            pl.BlockSpec(memory_space=pltpu.SMEM),
-            pl.BlockSpec(memory_space=pltpu.VMEM),
-            pl.BlockSpec(memory_space=pltpu.VMEM),
-        ],
+        in_specs=[pl.BlockSpec(memory_space=pltpu.SMEM)]
+        + [pl.BlockSpec(memory_space=pltpu.VMEM)] * (len(parts) + 1),
         scratch_shapes=[pltpu_vmem((2 * count,) + rest), pltpu_vmem((2 * count,) + rest)],
-    )(position, gathered, responses)
+    )(position, *parts, responses)
 
 
 def sweep_kernel(h_ref, y_ref, u_ref, out_ref, ratio_ref, s_ref):
@@ -194,17 +209,20 @@
     count = lax.axis_size(axis)
     if count & (count - 1):
         return lax.all_gather(part, axis)
+    if count == 1:
+        return part[None]
     mine = lax.axis_index(axis)
     held = part[None]
     step = 1
-    while step < count:
+    while 2 * step < count:
         other = lax.ppermute(held, axis, [(i, i ^ step) for i in range(count)])
         lower = (mine // step) % 2 == 0
         held = jnp.where(
             lower, jnp.concatenate([held, other], 0), jnp.concatenate([other, held], 0)
         )
         step *= 2
-    return held
+    other = lax.ppermute(held, axis, [(i, i ^ step) for i in range(count)])
+    return held, other
 
 
 def distributed_solve(h_lines, d_lines, axis, doubling, edges=None):

time: 50.4 us -> 50.3 us (level)
  other arithmetic: 3.57 us -> 2.87 us
  local copies, waits for them, and re-layouts: 5.72 us -> 6.35 us
    select_n x3 -> x2, other arithmetic: 0.71 us -> 0.03 us  [doubling_gather(): jnp.where(lower, jnp.concatenate([held, other], 0), jnp.concatenate([othe...]
    unnamed x11 -> x15, local copies, waits for them, and re-layouts: 1.38 us -> 2.01 us
where the time goes in v18:
time: 50.3 us; the launch traced here: 49.9 us
  starting transfers between devices  14.5 us (29%)
  Pallas kernels  12 us (24%)
  blocking collectives  7.57 us (15%)
  waiting for transfers between devices  6.51 us (13%)
  local copies, waits for them, and re-layouts  6.35 us (13%)
  other arithmetic  2.87 us (6%)
    ppermute x3, starting transfers between devices, doubling_gather(): other = lax.ppermute(held, axis, [(i, i ^ step) for i in range(count)])  8.38 us
    all_gather x1, blocking collectives, distributed_solve(): gathered = lax.all_gather(reduced, axis)  7.57 us
    ppermute x3, waiting for transfers between devices, doubling_gather(): other = lax.ppermute(held, axis, [(i, i ^ step) for i in range(count)])  6.14 us
    pallas_call x2, Pallas kernels, partition_call(): pl.pallas_call(partition_kernel, out_shape=(jax.ShapeDtypeStruct((3, n) +...  5.61 us
    ppermute x1, starting transfers between devices, halos(): low = lax.ppermute(last, axis, forward)  4.84 us
    pallas_call x2, Pallas kernels, finish_call(): pl.pallas_call(finish_kernel, out_shape=jax.ShapeDtypeStruct((n,) + rest,...  4.24 us
    pallas_call x1, Pallas kernels, sweep_call(): pl.pallas_call(sweep_kernel, out_shape=jax.ShapeDtypeStruct(h_lines.shape...  2.12 us
    unnamed x15, local copies, waits for them, and re-layouts  2.01 us
  transfers between devices with their start and end apart: 5, of which 4 were waited for; matrix products, arithmetic and copies ran while one was open for 6% of the time, Pallas kernels for 0%

profile of v18, /device:TPU:0, one launch (start us, length us, event | category | flops | bytes accessed | tf_op | source)
XLA Modules:
  0.0 49.9 jit_solution(9320544289852091104)
XLA Ops:
  0.0 1.2 %fusion.11 = (f32[16,32,1]{2,1,0:T(8,128)S(1)}, f32[16,32,1]{2,1,0:T(8,128)S(1)}) fusion(f32[16,32,128]{2,1,0:T(8,128)} %u_ref.1), kind=kLoop, calls=%fused_computation.21 | loop fusion | bytes 8192 | tf_op jit(solution)/shard_map/slice | solution.py:16
  1.3 4.8 %collective-permute-start = (f32[16,32]{1,0:T(8,128)S(1)}, f32[16,32]{1,0:T(8,128)S(1)}, u32[]{:S(2)}, u32[]{:S(2)}) collective-permute-start(f32[16,32]{1,0:T(8,128)S(1)} %bitcast.31), channel_id=1, source_target_pairs={{0,1},{1,2},{2,3},{3,4},{4,5},{5,6},{6,7},{8,9},{9,10},{10,11},{11... | collective-permute-start | bytes 6152 | tf_op jit(solution)/shard_map/ppermute | solution.py:18
  6.3 1.3 %collective-permute-start.1 = (f32[16,32]{1,0:T(8,128)S(1)}, f32[16,32]{1,0:T(8,128)S(1)}, u32[]{:S(2)}, u32[]{:S(2)}) collective-permute-start(f32[16,32]{1,0:T(8,128)S(1)} %bitcast.33), channel_id=1, source_target_pairs={{1,0},{2,1},{3,2},{4,3},{5,4},{6,5},{7,6},{9,8},{10,9},{11,10},{12... | collective-permute-start | bytes 6152 | tf_op jit(solution)/shard_map/ppermute | solution.py:19
  8.0 0.9 %copy-done.2 = f32[16,32,128]{2,1,0:T(8,128)S(1)} copy-done((f32[16,32,128]{2,1,0:T(8,128)S(1)}, f32[16,32,128]{2,1,0:T(8,128)}, u32[]{:S(2)}) %copy-start.2) | copy-done | bytes 262168
  9.0 0.6 %pad_maximum_fusion.refs_0_ = f32[2,16,128]{2,1,0:T(8,128)} fusion(f32[1,16,128]{2,1,0:T(8,128)S(1)} %get-tuple-element.16, f32[1,16,128]{2,1,0:T(8,128)S(1)} %get-tuple-element.15), kind=kLoop, calls=%fused_computation.17 | loop fusion | flops 4096 | bytes 32768 | tf_op jit(solution)/shard_map/stack | solution.py:274
  9.6 0.9 %copy.50.h_ref = f32[32,16,128]{2,1,0:T(8,128)} copy(f32[32,16,128]{2,0,1:T(8,128)S(1)} %get-tuple-element.23) | data formatting | bytes 524288 | tf_op jit(solution)/shard_map/transpose | solution.py:268
  10.5 0.8 %copy.52.h_ref = f32[128,4,128]{2,1,0:T(4,128)} copy(f32[128,4,128]{0,2,1:T(8,128)S(1)} %bitcast.26) | data formatting | bytes 524288 | tf_op jit(solution)/shard_map/reshape | solution.py:280
  11.5 0.4 collective-permute-done.1
  12.1 1.2 %fusion.5 = (f32[32,16,128]{2,1,0:T(8,128)}, f32[16,32,128]{2,0,1:T(8,128)S(1)}) fusion(f32[16,32,128]{2,0,1:T(8,128)S(1)} %copy.40, f32[16,31,128]{2,0,1:T(8,128)S(1)} %get-tuple-element.22, f32[16,31,128]{2,0,1:T(8,128)S(1)} %get-tuple-element.21, f32[16,32,128]{2,1,0:T(8,128)S(1)} %copy-done.2, f32[16,32,1]{2,0,1:T(8,128)S(1)} %copy.46, ...), kind=kLoop, calls=%fused_computation.7 | loop fusion | flops 1245184 | bytes 2342912 | tf_op jit(solution)/shard_map/transpose | solution.py:265
  13.3 2.3 %shard_map.28 = (f32[3,32,16,128]{3,2,1,0:T(8,128)}, f32[5,2,16,128]{3,2,1,0:T(8,128)}) custom-call(f32[32,16,128]{2,1,0:T(8,128)} %copy.50.h_ref, f32[32,16,128]{2,1,0:T(8,128)} %get-tuple-element.13.d_ref, f32[2,16,128]{2,1,0:T(8,128)} %pad_maximum_fusion.refs_0_), custom_call_target="tpu_custom_call" | custom-call | tf_op jit(solution)/shard_map/pallas_call | solution.py:82
  15.5 7.6 %all-gather = f32[20,2,16,128]{3,2,1,0:T(8,128)} all-gather(f32[5,2,16,128]{3,2,1,0:T(8,128)} %get-tuple-element.9), channel_id=2, replica_groups=mesh['gx'=4,'gy'=8] {'gx'}, dimensions={0}, use_global_device_ids=true | all-gather | bytes 409600 | tf_op jit(solution)/shard_map/all_gather | solution.py:233
  23.1 2.1 %shard_map.29 = f32[32,16,128]{2,1,0:T(8,128)} custom-call(s32[1]{0:T(128)} %bitcast.3.position_ref, f32[4,5,2,16,128]{4,3,2,1,0:T(8,128)} %bitcast.27, f32[3,32,16,128]{3,2,1,0:T(8,128)} %get-tuple-element.10.refs_0_), custom_call_target="tpu_custom_call" | custom-call | tf_op jit(solution)/shard_map/pallas_call | solution.py:155
  25.2 1.0 %fusion.8 = f32[128,16,32]{0,1,2:T(8,128)S(1)} fusion(f32[32,16,128]{2,1,0:T(8,128)} %shard_map.29, f32[16,32,128]{2,0,1:T(8,128)S(1)} %get-tuple-element.14), kind=kLoop, calls=%fused_computation.12 | loop fusion | flops 131072 | bytes 786432 | tf_op jit(solution)/shard_map/transpose | solution.py:279
  26.2 0.8 %copy.53.d_ref = f32[128,4,128]{2,1,0:T(4,128)} copy(f32[128,4,128]{0,2,1:T(8,128)S(1)} %bitcast.28) | data formatting | bytes 524288 | tf_op jit(solution)/shard_map/reshape | solution.py:279
  27.1 3.3 %shard_map.30 = (f32[3,128,4,128]{3,2,1,0:T(4,128)}, f32[4,2,4,128]{3,2,1,0:T(4,128)}) custom-call(f32[128,4,128]{2,1,0:T(4,128)} %copy.52.h_ref, f32[128,4,128]{2,1,0:T(4,128)} %copy.53.d_ref), custom_call_target="tpu_custom_call" | custom-call | tf_op jit(solution)/shard_map/pallas_call | solution.py:82
  30.4 2.5 %collective-permute-start.2 = (f32[1,4,2,4,128]{4,3,2,1,0:T(4,128)}, f32[1,4,2,4,128]{4,3,2,1,0:T(4,128)S(1)}, u32[]{:S(2)}, u32[]{:S(2)}) collective-permute-start(f32[1,4,2,4,128]{4,3,2,1,0:T(4,128)} %bitcast.29), channel_id=1, source_target_pairs={{0,1},{1,0},{2,3},{3,2},{4,5},{5,4},{6,7},{7,6},{8,9},{9,8},{10,11... | collective-permute-start | bytes 49160 | tf_op jit(solution)/shard_map/ppermute | solution.py:218
  32.9 2.0 %collective-permute-done.2 = f32[1,4,2,4,128]{4,3,2,1,0:T(4,128)S(1)} collective-permute-done((f32[1,4,2,4,128]{4,3,2,1,0:T(4,128)}, f32[1,4,2,4,128]{4,3,2,1,0:T(4,128)S(1)}, u32[]{:S(2)}, u32[]{:S(2)}) %collective-permute-start.2) | collective-permute-done | bytes 16416 | tf_op jit(solution)/shard_map/ppermute | solution.py:218
  34.9 2.8 %collective-permute-start.3 = (f32[2,4,2,4,128]{4,3,2,1,0:T(4,128)S(1)}, f32[2,4,2,4,128]{4,3,2,1,0:T(4,128)S(1)}, u32[]{:S(2)}, u32[]{:S(2)}) collective-permute-start(f32[2,4,2,4,128]{4,3,2,1,0:T(4,128)S(1)} %maximum_select_fusion.1), channel_id=1, source_target_pairs={{0,2},{1,3},{2,0},{3,1},{4,6},{5,7},{6,4},{7,5},{8,10},{9,11},{10,... | collective-permute-start | bytes 98312 | tf_op jit(solution)/shard_map/ppermute | solution.py:218
  37.7 1.9 %collective-permute-done.3 = f32[2,4,2,4,128]{4,3,2,1,0:T(4,128)S(1)} collective-permute-done((f32[2,4,2,4,128]{4,3,2,1,0:T(4,128)S(1)}, f32[2,4,2,4,128]{4,3,2,1,0:T(4,128)S(1)}, u32[]{:S(2)}, u32[]{:S(2)}) %collective-permute-start.3) | collective-permute-done | bytes 32800 | tf_op jit(solution)/shard_map/ppermute | solution.py:218
  39.6 3.1 %collective-permute-start.4 = (f32[4,4,2,4,128]{4,3,2,1,0:T(4,128)S(1)}, f32[4,4,2,4,128]{4,3,2,1,0:T(4,128)S(1)}, u32[]{:S(2)}, u32[]{:S(2)}) collective-permute-start(f32[4,4,2,4,128]{4,3,2,1,0:T(4,128)S(1)} %maximum_select_fusion.g_ref), channel_id=1, source_target_pairs={{0,4},{1,5},{2,6},{3,7},{4,0},{5,1},{6,2},{7,3},{8,12},{9,13},{10,... | collective-permute-start | bytes 196616 | tf_op jit(solution)/shard_map/ppermute | solution.py:224
  42.7 2.2 %collective-permute-done.4.refs_0_ = f32[4,4,2,4,128]{4,3,2,1,0:T(4,128)S(1)} collective-permute-done((f32[4,4,2,4,128]{4,3,2,1,0:T(4,128)S(1)}, f32[4,4,2,4,128]{4,3,2,1,0:T(4,128)S(1)}, u32[]{:S(2)}, u32[]{:S(2)}) %collective-permute-start.4) | collective-permute-done | bytes 65568 | tf_op jit(solution)/shard_map/ppermute | solution.py:224
  45.0 0.6 %copy-done.4 = f32[4,4,2,4,128]{4,3,2,1,0:T(4,128)} copy-done((f32[4,4,2,4,128]{4,3,2,1,0:T(4,128)}, f32[4,4,2,4,128]{4,3,2,1,0:T(4,128)S(1)}, u32[]{:S(2)}) %copy-start.4) | copy-done | bytes 65560
  45.6 2.2 %shard_map.31.y_ref = f32[128,4,128]{2,1,0:T(4,128)} custom-call(s32[1]{0:T(128)} %bitcast.position_ref, f32[4,4,2,4,128]{4,3,2,1,0:T(4,128)} %copy-done.3, f32[4,4,2,4,128]{4,3,2,1,0:T(4,128)} %copy-done.4, f32[3,128,4,128]{3,2,1,0:T(4,128)} %get-tuple-element.12.refs_1_), custom_call_target="tpu_custom_call" | custom-call | tf_op jit(solution)/shard_map/pallas_call | solution.py:155
  47.8 2.1 %shard_map.32 = f32[16,32,128]{2,1,0:T(8,128)} custom-call(f32[16,32,128]{2,1,0:T(8,128)} %copy-done.1, f32[128,4,128]{2,1,0:T(4,128)} %shard_map.31.y_ref, f32[16,32,128]{2,1,0:T(8,128)} %u_ref.1), custom_call_target="tpu_custom_call" | custom-call | tf_op jit(solution)/shard_map/pallas_call | solution.py:201
  (23 shorter events, 1.2 us)
Async XLA Ops:
  1.2 6.5 %copy-start = (f32[16,32,128]{2,1,0:T(8,128)S(1)}, f32[16,32,128]{2,1,0:T(8,128)}, u32[]{:S(2)}) copy-start(f32[16,32,128]{2,1,0:T(8,128)} %u_ref.1) | copy-start | bytes 786436
  1.3 10.0 %collective-permute-start = (f32[16,32]{1,0:T(8,128)S(1)}, f32[16,32]{1,0:T(8,128)S(1)}, u32[]{:S(2)}, u32[]{:S(2)}) collective-permute-start(f32[16,32]{1,0:T(8,128)S(1)} %bitcast.31), channel_id=1, source_target_pairs={{0,1},{1,2},{2,3},{3,4},{4,5},{5,6},{6,7},{8,9},{9,10},{10,11},{11... | collective-permute-start | bytes 6152 | tf_op jit(solution)/shard_map/ppermute | solution.py:18
  6.3 5.5 %collective-permute-start.1 = (f32[16,32]{1,0:T(8,128)S(1)}, f32[16,32]{1,0:T(8,128)S(1)}, u32[]{:S(2)}, u32[]{:S(2)}) collective-permute-start(f32[16,32]{1,0:T(8,128)S(1)} %bitcast.33), channel_id=1, source_target_pairs={{1,0},{2,1},{3,2},{4,3},{5,4},{6,5},{7,6},{9,8},{10,9},{11,10},{12... | collective-permute-start | bytes 6152 | tf_op jit(solution)/shard_map/ppermute | solution.py:19
  7.9 1.0 %copy-start.2 = (f32[16,32,128]{2,1,0:T(8,128)S(1)}, f32[16,32,128]{2,1,0:T(8,128)}, u32[]{:S(2)}) copy-start(f32[16,32,128]{2,1,0:T(8,128)} %param.3) | copy-start | bytes 786436
  8.9 1.5 %copy-start.1 = (f32[16,32,128]{2,1,0:T(8,128)}, f32[16,32,128]{2,1,0:T(8,128)S(1)}, u32[]{:S(2)}) copy-start(f32[16,32,128]{2,1,0:T(8,128)S(1)} %get-tuple-element.24.h_ref) | copy-start | bytes 786436
  30.4 4.5 %copy-start.5 = (f32[4,2,4,128]{3,2,1,0:T(4,128)S(1)}, f32[4,2,4,128]{3,2,1,0:T(4,128)}, u32[]{:S(2)}) copy-start(f32[4,2,4,128]{3,2,1,0:T(4,128)} %get-tuple-element.11) | copy-start | bytes 49156
  30.4 4.4 %collective-permute-start.2 = (f32[1,4,2,4,128]{4,3,2,1,0:T(4,128)}, f32[1,4,2,4,128]{4,3,2,1,0:T(4,128)S(1)}, u32[]{:S(2)}, u32[]{:S(2)}) collective-permute-start(f32[1,4,2,4,128]{4,3,2,1,0:T(4,128)} %bitcast.29), channel_id=1, source_target_pairs={{0,1},{1,0},{2,3},{3,2},{4,5},{5,4},{6,7},{7,6},{8,9},{9,8},{10,11... | collective-permute-start | bytes 49160 | tf_op jit(solution)/shard_map/ppermute | solution.py:218
  34.9 4.7 %collective-permute-start.3 = (f32[2,4,2,4,128]{4,3,2,1,0:T(4,128)S(1)}, f32[2,4,2,4,128]{4,3,2,1,0:T(4,128)S(1)}, u32[]{:S(2)}, u32[]{:S(2)}) collective-permute-start(f32[2,4,2,4,128]{4,3,2,1,0:T(4,128)S(1)} %maximum_select_fusion.1), channel_id=1, source_target_pairs={{0,2},{1,3},{2,0},{3,1},{4,6},{5,7},{6,4},{7,5},{8,10},{9,11},{10,... | collective-permute-start | bytes 98312 | tf_op jit(solution)/shard_map/ppermute | solution.py:218
  39.6 5.4 %copy-start.3 = (f32[4,4,2,4,128]{4,3,2,1,0:T(4,128)}, f32[4,4,2,4,128]{4,3,2,1,0:T(4,128)S(1)}, u32[]{:S(2)}) copy-start(f32[4,4,2,4,128]{4,3,2,1,0:T(4,128)S(1)} %maximum_select_fusion.g_ref) | copy-start | bytes 196612
  39.6 5.3 %collective-permute-start.4 = (f32[4,4,2,4,128]{4,3,2,1,0:T(4,128)S(1)}, f32[4,4,2,4,128]{4,3,2,1,0:T(4,128)S(1)}, u32[]{:S(2)}, u32[]{:S(2)}) collective-permute-start(f32[4,4,2,4,128]{4,3,2,1,0:T(4,128)S(1)} %maximum_select_fusion.g_ref), channel_id=1, source_target_pairs={{0,4},{1,5},{2,6},{3,7},{4,0},{5,1},{6,2},{7,3},{8,12},{9,13},{10,... | collective-permute-start | bytes 196616 | tf_op jit(solution)/shard_map/ppermute | solution.py:224
  45.0 0.6 %copy-start.4 = (f32[4,4,2,4,128]{4,3,2,1,0:T(4,128)}, f32[4,4,2,4,128]{4,3,2,1,0:T(4,128)S(1)}, u32[]{:S(2)}) copy-start(f32[4,4,2,4,128]{4,3,2,1,0:T(4,128)S(1)} %collective-permute-done.4.refs_0_) | copy-start | bytes 196612
